TPU v7x, 32 devices: a whole 2x2x4 slice. The times are simulated.
32 devices in a mesh: seq: 8 (over z, x), win: 4 (over y, core).
Axes of the slice: x: 2, y: 2, z: 4, core: 2. Of those that a mesh axis runs over, the one named last changes fastest.
Arguments:
- inputs: bfloat16 [4, 3072, 1536], P('win', 'seq'), may hold values from -6 to 6
- cotangent: bfloat16 [4, 3072, 1536], P('win', 'seq'), may hold values from -6 to 6
- w_dilated: bfloat16 [2, 1536, 3, 768], P(None, ('seq', 'win')), may hold values from -0.09375 to 0.09375
- w_mix: bfloat16 [2, 1536, 768], P(None, ('seq', 'win')), may hold values from -0.21875 to 0.21875
- in_scale: float32 [2, 1536], replicated, may hold values from 0.1 to 1.9
- in_shift: float32 [2, 1536], replicated, may hold values from -3 to 3
- mid_scale: float32 [2, 768], replicated, may hold values from 0.1 to 1.9
- mid_shift: float32 [2, 768], replicated, may hold values from -3 to 3
Outputs:
- output: bfloat16 [4, 3072, 1536], P('win', 'seq')
- input_gradient: float32 [4, 3072, 1536], P('win', 'seq')
- dilated_weight_gradient: float32 [2, 1536, 3, 768], P(None, ('seq', 'win'))
- grad_mix: float32 [2, 1536, 768], P(None, ('seq', 'win'))
All inputs are finite; a program needn't handle non-finite values.
Results may differ from a plain program's by a relative error of at most 0.034.
Values may be sent and summed in bfloat16 or wider, within the bound.
No kernel may reach another device: no remote copies, remote signals or barrier semaphores. Data moves between devices by JAX's collectives and lax.ppermute only.
A program may use at most 192 MiB of HBM per device.

v0:
```python
import math

import jax
import jax.numpy as jnp
from jax import lax
from jax.sharding import PartitionSpec as P

dilation_steps = (8, 16)


def padded_2(block, sides, width):
    for axis, dim in sides:
        count = lax.axis_size(axis)
        forward = [(i, i + 1) for i in range(count - 1)]
        backward = [(target, source) for source, target in forward]
        low = lax.ppermute(
            lax.slice_in_dim(block, block.shape[dim] - width, None, axis=dim), axis, forward
        )
        high = lax.ppermute(lax.slice_in_dim(block, 0, width, axis=dim), axis, backward)
        block = jnp.concatenate([low, block, high], axis=dim)
    return block


def gelu_value(values):
    return jax.nn.gelu(values, approximate=True)


def gelu_back(pre_values, upstream_gradient):
    return jax.vjp(gelu_value, pre_values)[1](upstream_gradient)[0]


def dilated_conv(padded, w_conv, dilation, out_rows):
    hidden = jnp.dot(padded[0:out_rows], w_conv[:, 0, :], preferred_element_type=jnp.float32)
    for kernel_tap in (1, 2):
        lower = kernel_tap * dilation
        hidden = hidden + jnp.dot(
            padded[lower : lower + out_rows],
            w_conv[:, kernel_tap, :],
            preferred_element_type=jnp.float32,
        )
    return hidden


def fetch_weights(residual_block_index, w_dilated, w_mix):
    return (
        lax.all_gather(w_dilated[residual_block_index], ("seq", "win"), axis=0, tiled=True),
        lax.all_gather(w_mix[residual_block_index], ("seq", "win"), axis=0, tiled=True),
    )


def weight_gradient_list(padded, d_hidden, cot_here, middle, dilation, inverse_square_root):
    row_count = d_hidden.shape[0]
    sliced = padded
    kernel_taps = [
        jnp.einsum(
            "pc,pe->ce",
            sliced[kernel_tap * dilation : kernel_tap * dilation + row_count],
            d_hidden,
            preferred_element_type=jnp.float32,
        )
        for kernel_tap in range(3)
    ]
    seq_dilated = lax.psum_scatter(
        (jnp.stack(kernel_taps, axis=1) * inverse_square_root).astype(jnp.bfloat16),
        "seq",
        scatter_dimension=0,
        tiled=True,
    )
    sliced = cot_here
    seq_mixed = lax.psum_scatter(
        (
            jnp.einsum("pc,pe->ce", sliced, middle, preferred_element_type=jnp.float32)
            * inverse_square_root
        ).astype(jnp.bfloat16),
        "seq",
        scatter_dimension=0,
        tiled=True,
    )
    return (
        lax.psum_scatter(seq_dilated, "win", scatter_dimension=0, tiled=True).astype(jnp.float32),
        lax.psum_scatter(seq_mixed, "win", scatter_dimension=0, tiled=True).astype(jnp.float32),
    )


def per_device(inputs, cotangent, w_dilated, w_mix, in_scale, in_shift, mid_scale, mid_shift):
    x_local = inputs[0]
    cot_local = cotangent[0]
    row_count = x_local.shape[0]
    window_len = lax.axis_size("seq") * row_count
    inverse_square_root = 1.0 / math.sqrt(lax.axis_size("win") * inputs.shape[0] * window_len)
    residual_block_count = len(dilation_steps)
    saved = []
    stream = x_local.astype(jnp.float32)
    for residual_block_index in range(residual_block_count):
        dilation = dilation_steps[residual_block_index]
        w_conv, w_out = fetch_weights(residual_block_index, w_dilated, w_mix)
        pre_in = stream * in_scale[residual_block_index] + in_shift[residual_block_index]
        activated = gelu_value(pre_in).astype(jnp.bfloat16)
        padded = padded_2(activated, (("seq", 0),), dilation)
        pre_mid = (
            dilated_conv(padded, w_conv, dilation, row_count) * mid_scale[residual_block_index]
            + mid_shift[residual_block_index]
        )
        middle = gelu_value(pre_mid).astype(jnp.bfloat16)
        stream = stream + jnp.einsum("pe,ce->pc", middle, w_out, preferred_element_type=jnp.float32)
        saved.append((w_conv, w_out, pre_in, padded, pre_mid, middle))
    output = stream.astype(jnp.bfloat16)
    upstream_gradient = cot_local.astype(jnp.float32)
    dilated_weight_gradients = [None] * residual_block_count
    mixing_weight_gradients = [None] * residual_block_count
    for residual_block_index in reversed(range(residual_block_count)):
        dilation = dilation_steps[residual_block_index]
        w_conv, w_out, pre_in, padded, pre_mid, middle = saved[residual_block_index]
        cot_here = upstream_gradient.astype(jnp.bfloat16)
        d_mid = jnp.dot(cot_here, w_out, preferred_element_type=jnp.float32)
        d_hidden = (gelu_back(pre_mid, d_mid) * mid_scale[residual_block_index]).astype(
            jnp.bfloat16
        )
        d_pad = padded_2(d_hidden, (("seq", 0),), dilation)
        d_act = jnp.einsum(
            "pe,ce->pc",
            d_pad[2 * dilation : 2 * dilation + row_count],
            w_conv[:, 0, :],
            preferred_element_type=jnp.float32,
        )
        for kernel_tap in (1, 2):
            lower = (2 - kernel_tap) * dilation
            d_act = d_act + jnp.einsum(
                "pe,ce->pc",
                d_pad[lower : lower + row_count],
                w_conv[:, kernel_tap, :],
                preferred_element_type=jnp.float32,
            )
        (
            dilated_weight_gradients[residual_block_index],
            mixing_weight_gradients[residual_block_index],
        ) = weight_gradient_list(padded, d_hidden, cot_here, middle, dilation, inverse_square_root)
        upstream_gradient = (
            upstream_gradient + gelu_back(pre_in, d_act) * in_scale[residual_block_index]
        )
    return (
        output[None],
        upstream_gradient[None],
        jnp.stack(dilated_weight_gradients),
        jnp.stack(mixing_weight_gradients),
    )


def solution(mesh):
    in_specs = (
        P("win", "seq", None),
        P("win", "seq", None),
        P(None, ("seq", "win"), None, None),
        P(None, ("seq", "win"), None),
        P(),
        P(),
        P(),
        P(),
    )
    out_specs = (
        P("win", "seq", None),
        P("win", "seq", None),
        P(None, ("seq", "win"), None, None),
        P(None, ("seq", "win"), None),
    )
    return jax.shard_map(
        per_device, mesh=mesh, in_specs=in_specs, out_specs=out_specs, check_vma=False
    )
```

profile of v0, /device:TPU:0, one launch (start us, length us, event | category | flops | bytes accessed | tf_op | source)
XLA Modules:
  0.0 793.3 jit_solution(16933065255860855362)
XLA Ops:
  16.0 4.8 collective-permute-start
  23.4 63.5 %all-gather.9.cloned.1.call-done = bf16[1,1536,3,768]{3,1,2,0:T(8,128)(2,1)} async-done(((bf16[1,48,3,768]{3,1,2,0:T(8,128)(2,1)}), bf16[1,1536,3,768]{3,1,2,0:T(8,128)(2,1)}) %all-gather.9.cloned.1.call-update) | async-done | bytes 7077904 | tf_op jit(solution)/shard_map/all_gather | solution.py:46
  86.9 3.5 fusion.48
  93.8 52.4 %all-gather.11.cloned.1.call-done = bf16[1,1536,768]{2,1,0:T(8,128)(2,1)} async-done(((bf16[1,48,768]{2,1,0:T(8,128)(2,1)}), bf16[1,1536,768]{2,1,0:T(8,128)(2,1)}) %all-gather.11.cloned.1.call-update) | async-done | bytes 2359312 | tf_op jit(solution)/shard_map/all_gather | solution.py:47
  146.2 5.2 multiply_convert_fusion.2
  152.0 3.9 collective-permute-start.2
  157.2 64.0 %all-gather.13.cloned.1.call-done = bf16[1,1536,3,768]{3,1,2,0:T(8,128)(2,1)} async-done(((bf16[1,48,3,768]{3,1,2,0:T(8,128)(2,1)}), bf16[1,1536,3,768]{3,1,2,0:T(8,128)(2,1)}) %all-gather.13.cloned.1.call-update) | async-done | bytes 7077904 | tf_op jit(solution)/shard_map/all_gather | solution.py:46
  233.9 45.9 %all-gather.15.cloned.1.call-done = bf16[1,1536,768]{2,1,0:T(8,128)(2,1)} async-done(((bf16[1,48,768]{2,1,0:T(8,128)(2,1)}), bf16[1,1536,768]{2,1,0:T(8,128)(2,1)}) %all-gather.15.cloned.1.call-update) | async-done | bytes 2359312 | tf_op jit(solution)/shard_map/all_gather | solution.py:47
  279.9 3.9 fusion.79
  296.0 4.2 fusion.38
  311.1 3.8 fusion.1
  315.6 4.3 fusion.71
  324.2 3.9 fusion
  328.1 23.1 %reduce-scatter.21.cloned.1.call-done = bf16[192,768]{1,0:T(8,128)(2,1)} async-done(((bf16[1536,768]{1,0:T(8,128)(2,1)}), bf16[192,768]{1,0:T(8,128)(2,1)}) %reduce-scatter.21.cloned.1.call-update) | async-done | bytes 294928 | tf_op jit(solution)/shard_map/reduce_scatter | solution.py:70
  351.3 71.5 %reduce-scatter.17.cloned.1.call-done = bf16[192,768]{1,0:T(8,128)(2,1)} async-done(((bf16[1536,768]{1,0:T(8,128)(2,1)}), bf16[192,768]{1,0:T(8,128)(2,1)}) %reduce-scatter.17.cloned.1.call-update) | async-done | bytes 294928 | tf_op jit(solution)/shard_map/reduce_scatter | solution.py:70
  422.8 131.7 %reduce-scatter.13.cloned.1.call-done = bf16[192,3,768]{2,0,1:T(8,128)(2,1)} async-done(((bf16[1536,3,768]{2,0,1:T(8,128)(2,1)}), bf16[192,3,768]{2,0,1:T(8,128)(2,1)}) %reduce-scatter.13.cloned.1.call-update) | async-done | bytes 884752 | tf_op jit(solution)/shard_map/reduce_scatter | solution.py:63
  554.6 4.6 fusion.7
  559.2 127.6 %reduce-scatter.9.cloned.1.call-done = bf16[192,3,768]{2,0,1:T(8,128)(2,1)} async-done(((bf16[1536,3,768]{2,0,1:T(8,128)(2,1)}), bf16[192,3,768]{2,0,1:T(8,128)(2,1)}) %reduce-scatter.9.cloned.1.call-update) | async-done | bytes 884752 | tf_op jit(solution)/shard_map/reduce_scatter | solution.py:63
  686.8 3.4 collective-permute-start.7
  698.7 5.7 fusion.30
  704.4 4.2 reduce-scatter.23.cloned.1.call-done
  708.7 22.8 %reduce-scatter.19.cloned.1.call-done = bf16[48,768]{1,0:T(8,128)(2,1)} async-done(((bf16[192,768]{1,0:T(8,128)(2,1)}), bf16[48,768]{1,0:T(8,128)(2,1)}) %reduce-scatter.19.cloned.1.call-update) | async-done | bytes 73744 | tf_op jit(solution)/shard_map/reduce_scatter | solution.py:81
  733.1 24.8 %reduce-scatter.15.cloned.1.call-done = bf16[48,3,768]{2,0,1:T(8,128)(2,1)} async-done(((bf16[192,3,768]{2,0,1:T(8,128)(2,1)}), bf16[48,3,768]{2,0,1:T(8,128)(2,1)}) %reduce-scatter.15.cloned.1.call-update) | async-done | bytes 221200 | tf_op jit(solution)/shard_map/reduce_scatter | solution.py:80
  757.9 26.5 %reduce-scatter.11.cloned.1.call-done = bf16[48,3,768]{2,0,1:T(8,128)(2,1)} async-done(((bf16[192,3,768]{2,0,1:T(8,128)(2,1)}), bf16[48,3,768]{2,0,1:T(8,128)(2,1)}) %reduce-scatter.11.cloned.1.call-update) | async-done | bytes 221200 | tf_op jit(solution)/shard_map/reduce_scatter | solution.py:80
  (115 shorter events, 69.4 us)
Async XLA Ops:
  7.2 15.0 %copy-start.5 = (f32[2,768]{1,0:T(2,128)S(1)}, f32[2,768]{1,0:T(2,128)}, u32[]{:S(2)}) copy-start(f32[2,768]{1,0:T(2,128)} %param.14) | copy-start | bytes 18436
  7.2 15.6 %copy-start.6 = (f32[2,768]{1,0:T(2,128)S(1)}, f32[2,768]{1,0:T(2,128)}, u32[]{:S(2)}) copy-start(f32[2,768]{1,0:T(2,128)} %param.15) | copy-start | bytes 18436
  7.2 79.7 %all-gather.9.cloned.1.call-start = ((), (), s32[]{:S(2)}) async-start(), calls=%async_computation.16 | async-start | bytes 7299072 | tf_op jit(solution)/shard_map/all_gather | solution.py:46
  9.2 137.0 %all-gather.11.cloned.1.call-start = ((), (), s32[]{:S(2)}) async-start(), calls=%async_computation.17 | async-start | bytes 2433024 | tf_op jit(solution)/shard_map/all_gather | solution.py:47
  10.8 210.4 %all-gather.13.cloned.1.call-start = ((), (), s32[]{:S(2)}) async-start(), calls=%async_computation.18 | async-start | bytes 7299072 | tf_op jit(solution)/shard_map/all_gather | solution.py:46
  11.6 268.3 %all-gather.15.cloned.1.call-start = ((), (), s32[]{:S(2)}) async-start(), calls=%async_computation.19 | async-start | bytes 2433024 | tf_op jit(solution)/shard_map/all_gather | solution.py:47
  12.2 339.1 %reduce-scatter.21.cloned.1.call-start = ((), (), s32[]{:S(2)}) async-start(), calls=%async_computation.14 | async-start | bytes 2654208 | tf_op jit(solution)/shard_map/reduce_scatter | solution.py:70
  16.0 75.7 %collective-permute-start = (bf16[8,1536]{1,0:T(8,128)(2,1)S(1)}, bf16[8,1536]{1,0:T(8,128)(2,1)S(1)}, u32[]{:S(2)}, u32[]{:S(2)}) collective-permute-start(bf16[8,1536]{1,0:T(8,128)(2,1)S(1)} %get-tuple-element.14), channel_id=1, source_target_pairs={{0,4},{4,8},{8,12},{12,16},{16,20},{20,24},{24,28},{1,5},{5,9},{9,... | collective-permute-start | bytes 73736 | tf_op jit(solution)/shard_map/ppermute | solution.py:16
  20.8 69.6 %collective-permute-start.1 = (bf16[8,1536]{1,0:T(8,128)(2,1)S(1)}, bf16[8,1536]{1,0:T(8,128)(2,1)S(1)}, u32[]{:S(2)}, u32[]{:S(2)}) collective-permute-start(bf16[8,1536]{1,0:T(8,128)(2,1)S(1)} %get-tuple-element.15), channel_id=1, source_target_pairs={{4,0},{8,4},{12,8},{16,12},{20,16},{24,20},{28,24},{5,1},{9,5},{13... | collective-permute-start | bytes 73736 | tf_op jit(solution)/shard_map/ppermute | solution.py:19
  22.8 68.9 %copy-start.7 = (f32[768]{0:T(1024)}, f32[768]{0:T(1024)S(1)}, u32[]{:S(2)}) copy-start(f32[768]{0:T(1024)S(1)} %get-tuple-element.9) | copy-start | bytes 9220
  152.0 74.7 %collective-permute-start.2 = (bf16[16,1536]{1,0:T(8,128)(2,1)}, bf16[16,1536]{1,0:T(8,128)(2,1)}, u32[]{:S(2)}, u32[]{:S(2)}) collective-permute-start(bf16[16,1536]{1,0:T(8,128)(2,1)} %get-tuple-element.12), channel_id=1, source_target_pairs={{0,4},{4,8},{8,12},{12,16},{16,20},{20,24},{24,28},{1,5},{5,9},{9,... | collective-permute-start | bytes 147464 | tf_op jit(solution)/shard_map/ppermute | solution.py:16
  156.0 68.0 %collective-permute-start.3 = (bf16[16,1536]{1,0:T(8,128)(2,1)}, bf16[16,1536]{1,0:T(8,128)(2,1)}, u32[]{:S(2)}, u32[]{:S(2)}) collective-permute-start(bf16[16,1536]{1,0:T(8,128)(2,1)} %get-tuple-element.13), channel_id=1, source_target_pairs={{4,0},{8,4},{12,8},{16,12},{20,16},{24,20},{28,24},{5,1},{9,5},{13... | collective-permute-start | bytes 147464 | tf_op jit(solution)/shard_map/ppermute | solution.py:19
  233.7 189.1 %reduce-scatter.17.cloned.1.call-start = ((), (), s32[]{:S(2)}) async-start(), calls=%async_computation.12 | async-start | bytes 2654208 | tf_op jit(solution)/shard_map/reduce_scatter | solution.py:70
  283.8 7.7 collective-permute-start.5
  290.0 6.0 collective-permute-start.4
  304.7 249.8 %reduce-scatter.13.cloned.1.call-start = ((), (), s32[]{:S(2)}) async-start(), calls=%async_computation.10 | async-start | bytes 7962624 | tf_op jit(solution)/shard_map/reduce_scatter | solution.py:63
  314.9 371.8 %reduce-scatter.9.cloned.1.call-start = ((), (), s32[]{:S(2)}) async-start(), calls=%async_computation.8 | async-start | bytes 7962624 | tf_op jit(solution)/shard_map/reduce_scatter | solution.py:63
  328.1 226.5 %copy-start.20 = (f32[384,768]{1,0:T(8,128)S(1)}, f32[384,768]{1,0:T(8,128)}, u32[]{:S(2)}) copy-start(f32[384,768]{1,0:T(8,128)} %copy-done.19) | copy-start | bytes 3538948
  328.1 380.6 %reduce-scatter.23.cloned.1.call-start = ((), (), s32[]{:S(2)}) async-start(), calls=%async_computation.15 | async-start | bytes 368640 | tf_op jit(solution)/shard_map/reduce_scatter | solution.py:81
  351.2 380.2 %reduce-scatter.19.cloned.1.call-start = ((), (), s32[]{:S(2)}) async-start(), calls=%async_computation.13 | async-start | bytes 368640 | tf_op jit(solution)/shard_map/reduce_scatter | solution.py:81
  422.8 335.1 %reduce-scatter.15.cloned.1.call-start = ((), (), s32[]{:S(2)}) async-start(), calls=%async_computation.11 | async-start | bytes 1105920 | tf_op jit(solution)/shard_map/reduce_scatter | solution.py:80
  554.6 229.9 %reduce-scatter.11.cloned.1.call-start = ((), (), s32[]{:S(2)}) async-start(), calls=%async_computation.9 | async-start | bytes 1105920 | tf_op jit(solution)/shard_map/reduce_scatter | solution.py:80
  686.8 7.6 collective-permute-start.7
  693.0 5.7 collective-permute-start.6
  (20 other events, 84.3 us)
Sparse Core Ops, SparseCore 0:
  11.5 75.3 all-gather.8
  90.4 55.8 all-gather.10
  149.7 71.5 all-gather.12
  224.0 55.8 all-gather.14
  283.2 67.9 reduce-scatter.20
  354.6 68.1 reduce-scatter.16
  426.4 128.0 reduce-scatter.12
  558.7 128.0 reduce-scatter.8
  689.3 19.3 reduce-scatter.22
  711.1 20.2 reduce-scatter.18
  734.0 23.8 reduce-scatter.14
  760.5 23.8 reduce-scatter.10
where the time goes:
time: 794 us; the launch traced here: 793 us
  waiting for transfers between devices  662 us (83%)
  matrix products  70.6 us (9%)
  starting transfers between devices  21.9 us (3%)
  between operations  14.7 us (2%)
  other arithmetic  12.3 us (2%)
  local copies, waits for them, and re-layouts  11.3 us (1%)
    reduce_scatter x2, waiting for transfers between devices, weight_gradient_list(): lax.psum_scatter((jnp.stack(kernel_taps, axis=1) * inverse_square_root).a...  259 us
    all_gather x2, waiting for transfers between devices, fetch_weights(): lax.all_gather(w_dilated[residual_block_index], ('seq', 'win'), axis=0, t...  127 us
    all_gather x2, waiting for transfers between devices, fetch_weights(): lax.all_gather(w_mix[residual_block_index], ('seq', 'win'), axis=0, tiled...  98.3 us
    reduce_scatter x2, waiting for transfers between devices, weight_gradient_list(): lax.psum_scatter((jnp.einsum('pc,pe->ce', sliced, middle, preferred_eleme...  94.5 us
    reduce_scatter x2, waiting for transfers between devices, weight_gradient_list(): lax.psum_scatter(seq_dilated, 'win', scatter_dimension=0, tiled=True)  51.3 us
    reduce_scatter x2, waiting for transfers between devices, weight_gradient_list(): lax.psum_scatter(seq_mixed, 'win', scatter_dimension=0, tiled=True)  27 us
  transfers between devices with their start and end apart: 20, of which 14 were waited for; matrix products, arithmetic and copies ran while one was open for 11% of the time, Pallas kernels for 0%

commit v1 on v0

--- a/solution.py
+++ b/solution.py
@@ -41,45 +41,42 @@
     return hidden
 
 
-def fetch_weights(residual_block_index, w_dilated, w_mix):
-    return (
-        lax.all_gather(w_dilated[residual_block_index], ("seq", "win"), axis=0, tiled=True),
-        lax.all_gather(w_mix[residual_block_index], ("seq", "win"), axis=0, tiled=True),
+def fetch_weights(w_dilated, w_mix):
+    blocks, rows, taps, c2 = w_dilated.shape
+    local = jnp.concatenate(
+        [w_dilated.reshape(blocks, rows, taps * c2).transpose(1, 0, 2).reshape(rows, -1),
+         w_mix.transpose(1, 0, 2).reshape(rows, -1)],
+        axis=1,
     )
+    gathered = lax.all_gather(local, ("seq", "win"), axis=0, tiled=True)
+    full_rows = gathered.shape[0]
+    split = blocks * taps * c2
+    return [
+        (
+            gathered[:, b * taps * c2 : (b + 1) * taps * c2].reshape(full_rows, taps, c2),
+            gathered[:, split + b * c2 : split + (b + 1) * c2],
+        )
+        for b in range(blocks)
+    ]
 
 
-def weight_gradient_list(padded, d_hidden, cot_here, middle, dilation, inverse_square_root):
+def weight_gradient_terms(padded, d_hidden, cot_here, middle, dilation, inverse_square_root):
     row_count = d_hidden.shape[0]
-    sliced = padded
     kernel_taps = [
         jnp.einsum(
             "pc,pe->ce",
-            sliced[kernel_tap * dilation : kernel_tap * dilation + row_count],
+            padded[kernel_tap * dilation : kernel_tap * dilation + row_count],
             d_hidden,
             preferred_element_type=jnp.float32,
         )
         for kernel_tap in range(3)
     ]
-    seq_dilated = lax.psum_scatter(
-        (jnp.stack(kernel_taps, axis=1) * inverse_square_root).astype(jnp.bfloat16),
-        "seq",
-        scatter_dimension=0,
-        tiled=True,
-    )
-    sliced = cot_here
-    seq_mixed = lax.psum_scatter(
-        (
-            jnp.einsum("pc,pe->ce", sliced, middle, preferred_element_type=jnp.float32)
-            * inverse_square_root
-        ).astype(jnp.bfloat16),
-        "seq",
-        scatter_dimension=0,
-        tiled=True,
-    )
-    return (
-        lax.psum_scatter(seq_dilated, "win", scatter_dimension=0, tiled=True).astype(jnp.float32),
-        lax.psum_scatter(seq_mixed, "win", scatter_dimension=0, tiled=True).astype(jnp.float32),
-    )
+    dilated = (jnp.concatenate(kernel_taps, axis=1) * inverse_square_root).astype(jnp.bfloat16)
+    mixed = (
+        jnp.einsum("pc,pe->ce", cot_here, middle, preferred_element_type=jnp.float32)
+        * inverse_square_root
+    ).astype(jnp.bfloat16)
+    return dilated, mixed
 
 
 def per_device(inputs, cotangent, w_dilated, w_mix, in_scale, in_shift, mid_scale, mid_shift):
@@ -90,10 +87,11 @@
     inverse_square_root = 1.0 / math.sqrt(lax.axis_size("win") * inputs.shape[0] * window_len)
     residual_block_count = len(dilation_steps)
     saved = []
+    weights = fetch_weights(w_dilated, w_mix)
     stream = x_local.astype(jnp.float32)
     for residual_block_index in range(residual_block_count):
         dilation = dilation_steps[residual_block_index]
-        w_conv, w_out = fetch_weights(residual_block_index, w_dilated, w_mix)
+        w_conv, w_out = weights[residual_block_index]
         pre_in = stream * in_scale[residual_block_index] + in_shift[residual_block_index]
         activated = gelu_value(pre_in).astype(jnp.bfloat16)
         padded = padded_2(activated, (("seq", 0),), dilation)
@@ -134,15 +132,24 @@
         (
             dilated_weight_gradients[residual_block_index],
             mixing_weight_gradients[residual_block_index],
-        ) = weight_gradient_list(padded, d_hidden, cot_here, middle, dilation, inverse_square_root)
+        ) = weight_gradient_terms(padded, d_hidden, cot_here, middle, dilation, inverse_square_root)
         upstream_gradient = (
             upstream_gradient + gelu_back(pre_in, d_act) * in_scale[residual_block_index]
         )
+    summed = lax.psum_scatter(
+        jnp.concatenate(dilated_weight_gradients + mixing_weight_gradients, axis=1),
+        ("seq", "win"),
+        scatter_dimension=0,
+        tiled=True,
+    ).astype(jnp.float32)
+    own_rows = summed.shape[0]
+    taps, c2 = w_dilated.shape[2], w_dilated.shape[3]
+    split = residual_block_count * taps * c2
     return (
         output[None],
         upstream_gradient[None],
-        jnp.stack(dilated_weight_gradients),
-        jnp.stack(mixing_weight_gradients),
+        summed[:, :split].reshape(own_rows, residual_block_count, taps, c2).transpose(1, 0, 2, 3),
+        summed[:, split:].reshape(own_rows, residual_block_count, c2).transpose(1, 0, 2),
     )
 
 

time: 794 us -> 502 us (0.63)
  waiting for transfers between devices: 662 us -> 308 us
  local copies, waits for them, and re-layouts: 11.3 us -> 63.7 us
  other arithmetic: 12.3 us -> 27.4 us
  matrix products: 70.6 us -> 61.1 us
    reduce_scatter x8 -> x0, waiting for transfers between devices: 432 us -> none  [the longest x2 259 us: weight_gradient_list(): lax.psum_scatter((jnp.stack(kernel_taps, axis=1) * inverse_square_root).a...]
    unnamed x12 -> x3, waiting for transfers between devices: 1.37 us -> 181 us
    all_gather x4 -> x1, waiting for transfers between devices: 226 us -> 121 us  [fetch_weights(): gathered = lax.all_gather(local, ('seq', 'win'), axis=0, tiled=True)]
    slice x4 -> x5, local copies, waits for them, and re-layouts: 5.52 us -> 31.7 us  [the longest x3 30.6 us: fetch_weights(): gathered[:, b * taps * c2:(b + 1) * taps * c2].reshape(full_rows, taps, c2)]
    unnamed x48 -> x31, local copies, waits for them, and re-layouts: 3.1 us -> 27.3 us
    concatenate x0 -> x2, other arithmetic: none -> 17.8 us  [the longest x1 17 us: per_device(): jnp.concatenate(dilated_weight_gradients + mixing_weight_gradients, axis=1)]
  transfers between devices with their start and end apart: 20 -> 10, of which waited for: 14 -> 5; matrix products, arithmetic and copies ran while one was open for 11% -> 14% of each run, Pallas kernels for 0% -> 0%
where the time goes in v1:
time: 502 us; the launch traced here: 500 us
  waiting for transfers between devices  308 us (61%)
  local copies, waits for them, and re-layouts  63.7 us (13%)
  matrix products  61.1 us (12%)
  other arithmetic  27.4 us (5%)
  starting transfers between devices  25.2 us (5%)
  between operations  14.5 us (3%)
    unnamed x3, waiting for transfers between devices  181 us
    all_gather x1, waiting for transfers between devices, fetch_weights(): gathered = lax.all_gather(local, ('seq', 'win'), axis=0, tiled=True)  121 us
    slice x3, local copies, waits for them, and re-layouts, fetch_weights(): gathered[:, b * taps * c2:(b + 1) * taps * c2].reshape(full_rows, taps, c2)  30.6 us
    unnamed x31, local copies, waits for them, and re-layouts  27.3 us
    ppermute x4, starting transfers between devices, padded_2(): lax.ppermute(lax.slice_in_dim(block, block.shape[dim] - width, None, axis...  19.5 us
    concatenate x1, other arithmetic, per_device(): jnp.concatenate(dilated_weight_gradients + mixing_weight_gradients, axis=1)  17 us
    dot_general x4, matrix products, dilated_conv(): jnp.dot(padded[lower:lower + out_rows], w_conv[:, kernel_tap, :], preferr...  10.4 us
  transfers between devices with their start and end apart: 10, of which 5 were waited for; matrix products, arithmetic and copies ran while one was open for 14% of the time, Pallas kernels for 0%

profile of v1, /device:TPU:0, one launch (start us, length us, event | category | flops | bytes accessed | tf_op | source)
XLA Modules:
  0.0 499.8 jit_solution(18363902650150961037)
XLA Ops:
  12.7 5.5 %collective-permute-start = (bf16[8,1536]{1,0:T(8,128)(2,1)S(1)}, bf16[8,1536]{1,0:T(8,128)(2,1)S(1)}, u32[]{:S(2)}, u32[]{:S(2)}) collective-permute-start(bf16[8,1536]{1,0:T(8,128)(2,1)S(1)} %get-tuple-element.16), channel_id=1, source_target_pairs={{0,4},{4,8},{8,12},{12,16},{16,20},{20,24},{24,28},{1,5},{5,9},{9,... | collective-permute-start | bytes 73736 | tf_op jit(solution)/shard_map/ppermute | solution.py:16
  18.2 120.7 %all-gather.2.cloned.1.call-done = bf16[1536,6144]{1,0:T(8,128)(2,1)} async-done(((bf16[48,6144]{1,0:T(8,128)(2,1)}), bf16[1536,6144]{1,0:T(8,128)(2,1)}) %all-gather.2.cloned.1.call-update) | async-done | bytes 18874384 | tf_op jit(solution)/shard_map/all_gather | solution.py:51
  138.9 10.1 %fusion.125 = (bf16[1536,2304]{1,0:T(8,128)(2,1)}, bf16[1536,2304]{1,0:T(8,128)(2,1)}) fusion(bf16[1536,6144]{1,0:T(8,128)(2,1)} %all-gather.2.cloned.1.call-done), kind=kLoop, calls=%fused_computation.163 | loop fusion | bytes 28311552 | tf_op jit(solution)/shard_map/slice | solution.py:56
  149.0 10.2 %copy.30 = bf16[1536,2304]{0,1:T(8,128)(2,1)} copy(bf16[1536,2304]{1,0:T(8,128)(2,1)} %get-tuple-element.13) | data formatting | bytes 14155776 | tf_op jit(solution)/shard_map/slice | solution.py:56
  159.2 4.4 fusion.42
  163.6 3.8 fusion.44
  167.4 10.3 %copy.34 = bf16[1536,2304]{0,1:T(8,128)(2,1)} copy(bf16[1536,2304]{1,0:T(8,128)(2,1)} %get-tuple-element.12) | data formatting | bytes 14155776 | tf_op jit(solution)/shard_map/slice | solution.py:56
  177.7 3.6 fusion.66
  181.3 3.6 multiply_convert_fusion.2
  187.4 4.7 collective-permute-start.2
  195.0 3.0 fusion.2
  197.9 3.3 fusion.82
  202.7 4.2 collective-permute-start.5
  209.9 4.3 fusion.1
  217.9 4.3 collective-permute-done.4
  224.9 2.9 multiply_convert_fusion.1
  227.9 3.3 fusion.74
  235.5 4.3 fusion
  239.7 17.0 %pad_maximum_fusion = bf16[1536,6144]{0,1:T(8,128)(2,1)} fusion(bf16[1536,768]{0,1:T(8,128)(2,1)} %fusion.2, bf16[1536,768]{0,1:T(8,128)(2,1)} %multiply_convert_fusion.1, bf16[1536,2304]{0,1:T(8,128)(2,1)} %fusion.1, bf16[1536,2304]{0,1:T(8,128)(2,1)} %fusion), kind=kLoop, calls=%fused_computation | loop fusion | flops 75497472 | bytes 37748736 | tf_op jit(solution)/shard_map/concatenate | solution.py:140
  256.7 24.7 %copy.40 = bf16[1536,6144]{1,0:T(8,128)(2,1)} copy(bf16[1536,6144]{0,1:T(8,128)(2,1)} %pad_maximum_fusion) | data formatting | bytes 37748736
  282.7 4.6 fusion.7
  287.3 5.1 %collective-permute-start.7 = (bf16[8,768]{1,0:T(8,128)(2,1)S(1)}, bf16[8,768]{1,0:T(8,128)(2,1)S(1)}, u32[]{:S(2)}, u32[]{:S(2)}) collective-permute-start(bf16[8,768]{1,0:T(8,128)(2,1)S(1)} %get-tuple-element.19), channel_id=1, source_target_pairs={{0,4},{4,8},{8,12},{12,16},{16,20},{20,24},{24,28},{1,5},{5,9},{9,... | collective-permute-start | bytes 36872 | tf_op jit(solution)/shard_map/ppermute | solution.py:16
  301.2 5.9 %fusion.30 = f32[1,384,1536]{2,1,0:T(8,128)} fusion(f32[384,1536]{1,0:T(8,128)S(1)} %copy-done.8, bf16[1,384,1536]{2,1,0:T(8,128)(2,1)S(1)} %copy-done.1, f32[384,1536]{1,0:T(8,128)S(1)} %fusion.43, f32[384,1536]{1,0:T(8,128)S(1)} %fusion.41, bf16[1536,3,768]{0,2,1:T(8,128)(2,1)} %bitcast.154, f32[1536]{0:T(1024)S(1)} %get-tuple-element.7, ...), kind=kOutput, calls=%fused_computation.46 | convolution fusion | flops 922484736 | bytes 13590528 | tf_op jit(solution)/shard_map/pe,ce->pc/dot_general | solution.py:118
  307.1 180.9 %reduce-scatter.4.cloned.1.call-done = bf16[48,6144]{1,0:T(8,128)(2,1)} async-done(((bf16[1536,6144]{1,0:T(8,128)(2,1)}), bf16[48,6144]{1,0:T(8,128)(2,1)}) %reduce-scatter.4.cloned.1.call-update) | async-done | bytes 589840
  (75 shorter events, 40.5 us)
Async XLA Ops:
  7.2 3.1 copy-start.2
  7.2 3.1 copy-start.3
  7.2 3.2 copy-start.1
  7.2 131.7 %all-gather.2.cloned.1.call-start = ((), (), s32[]{:S(2)}) async-start(), calls=%async_computation.1 | async-start | bytes 19464192 | tf_op jit(solution)/shard_map/all_gather | solution.py:51
  9.3 8.8 %copy-start.4 = (f32[2,768]{1,0:T(2,128)S(1)}, f32[2,768]{1,0:T(2,128)}, u32[]{:S(2)}) copy-start(f32[2,768]{1,0:T(2,128)} %param.15) | copy-start | bytes 18436
  9.4 8.8 %copy-start.5 = (f32[2,768]{1,0:T(2,128)S(1)}, f32[2,768]{1,0:T(2,128)}, u32[]{:S(2)}) copy-start(f32[2,768]{1,0:T(2,128)} %param.14) | copy-start | bytes 18436
  10.2 477.8 %reduce-scatter.4.cloned.1.call-start = ((), (), s32[]{:S(2)}) async-start(), calls=%async_computation.2 | async-start | bytes 19464192
  11.4 152.2 %collective-permute-start.1 = (bf16[8,1536]{1,0:T(8,128)(2,1)S(1)}, bf16[8,1536]{1,0:T(8,128)(2,1)S(1)}, u32[]{:S(2)}, u32[]{:S(2)}) collective-permute-start(bf16[8,1536]{1,0:T(8,128)(2,1)S(1)} %get-tuple-element.17), channel_id=1, source_target_pairs={{4,0},{8,4},{12,8},{16,12},{20,16},{24,20},{28,24},{5,1},{9,5},{13... | collective-permute-start | bytes 73736 | tf_op jit(solution)/shard_map/ppermute | solution.py:19
  12.7 165.0 %collective-permute-start = (bf16[8,1536]{1,0:T(8,128)(2,1)S(1)}, bf16[8,1536]{1,0:T(8,128)(2,1)S(1)}, u32[]{:S(2)}, u32[]{:S(2)}) collective-permute-start(bf16[8,1536]{1,0:T(8,128)(2,1)S(1)} %get-tuple-element.16), channel_id=1, source_target_pairs={{0,4},{4,8},{8,12},{12,16},{16,20},{20,24},{24,28},{1,5},{5,9},{9,... | collective-permute-start | bytes 73736 | tf_op jit(solution)/shard_map/ppermute | solution.py:16
  177.7 8.6 %slice-start = ((s8[7077888]{0:T(1024)(128)(4,1)}), s8[4194304]{0:T(1024)(128)(4,1)S(1)}, s32[]{:S(2)}) async-start(s8[7077888]{0:T(1024)(128)(4,1)} %bitcast.155), calls=%async_computation.3 | async-start | bytes 8388608
  181.3 5.0 slice-start.1
  185.0 37.3 %copy-start.9 = (f32[384,1536]{1,0:T(8,128)}, f32[384,1536]{1,0:T(8,128)S(1)}, u32[]{:S(2)}) copy-start(f32[384,1536]{1,0:T(8,128)S(1)} %get-tuple-element.23) | copy-start | bytes 7077892
  185.0 7.2 %collective-permute-start.3 = (bf16[16,1536]{1,0:T(8,128)(2,1)S(1)}, bf16[16,1536]{1,0:T(8,128)(2,1)S(1)}, u32[]{:S(2)}, u32[]{:S(2)}) collective-permute-start(bf16[16,1536]{1,0:T(8,128)(2,1)S(1)} %get-tuple-element.15), channel_id=1, source_target_pairs={{4,0},{8,4},{12,8},{16,12},{20,16},{24,20},{28,24},{5,1},{9,5},{13... | collective-permute-start | bytes 147464 | tf_op jit(solution)/shard_map/ppermute | solution.py:19
  187.4 6.3 %collective-permute-start.2 = (bf16[16,1536]{1,0:T(8,128)(2,1)S(1)}, bf16[16,1536]{1,0:T(8,128)(2,1)S(1)}, u32[]{:S(2)}, u32[]{:S(2)}) collective-permute-start(bf16[16,1536]{1,0:T(8,128)(2,1)S(1)} %get-tuple-element.14), channel_id=1, source_target_pairs={{0,4},{4,8},{8,12},{12,16},{16,20},{20,24},{24,28},{1,5},{5,9},{9,... | collective-permute-start | bytes 147464 | tf_op jit(solution)/shard_map/ppermute | solution.py:16
  193.7 1.3 copy-start.6
  195.0 3.0 copy-start.10
  202.7 14.1 %collective-permute-start.5 = (bf16[16,768]{1,0:T(8,128)(2,1)S(1)}, bf16[16,768]{1,0:T(8,128)(2,1)S(1)}, u32[]{:S(2)}, u32[]{:S(2)}) collective-permute-start(bf16[16,768]{1,0:T(8,128)(2,1)S(1)} %get-tuple-element.21), channel_id=1, source_target_pairs={{0,4},{4,8},{8,12},{12,16},{16,20},{20,24},{24,28},{1,5},{5,9},{9,... | collective-permute-start | bytes 73736 | tf_op jit(solution)/shard_map/ppermute | solution.py:16
  215.3 6.9 %collective-permute-start.4 = (bf16[16,768]{1,0:T(8,128)(2,1)S(1)}, bf16[16,768]{1,0:T(8,128)(2,1)S(1)}, u32[]{:S(2)}, u32[]{:S(2)}) collective-permute-start(bf16[16,768]{1,0:T(8,128)(2,1)S(1)} %get-tuple-element.20), channel_id=1, source_target_pairs={{4,0},{8,4},{12,8},{16,12},{20,16},{24,20},{28,24},{5,1},{9,5},{13... | collective-permute-start | bytes 73736 | tf_op jit(solution)/shard_map/ppermute | solution.py:19
  224.9 2.9 copy-start.7
  281.5 1.3 copy-start.11
  287.3 9.6 %collective-permute-start.7 = (bf16[8,768]{1,0:T(8,128)(2,1)S(1)}, bf16[8,768]{1,0:T(8,128)(2,1)S(1)}, u32[]{:S(2)}, u32[]{:S(2)}) collective-permute-start(bf16[8,768]{1,0:T(8,128)(2,1)S(1)} %get-tuple-element.19), channel_id=1, source_target_pairs={{0,4},{4,8},{8,12},{12,16},{16,20},{20,24},{24,28},{1,5},{5,9},{9,... | collective-permute-start | bytes 36872 | tf_op jit(solution)/shard_map/ppermute | solution.py:16
  295.3 5.9 %copy-start.8 = (f32[384,1536]{1,0:T(8,128)S(1)}, f32[384,1536]{1,0:T(8,128)}, u32[]{:S(2)}) copy-start(f32[384,1536]{1,0:T(8,128)} %copy-done.7) | copy-start | bytes 7077892
  295.3 5.9 %collective-permute-start.6 = (bf16[8,768]{1,0:T(8,128)(2,1)S(1)}, bf16[8,768]{1,0:T(8,128)(2,1)S(1)}, u32[]{:S(2)}, u32[]{:S(2)}) collective-permute-start(bf16[8,768]{1,0:T(8,128)(2,1)S(1)} %get-tuple-element.18), channel_id=1, source_target_pairs={{4,0},{8,4},{12,8},{16,12},{20,16},{24,20},{28,24},{5,1},{9,5},{13... | collective-permute-start | bytes 36872 | tf_op jit(solution)/shard_map/ppermute | solution.py:19
  490.0 1.7 copy-start
Sparse Core Ops, SparseCore 0:
  11.5 127.3 all-gather.1
  281.6 206.4 reduce-scatter.3

commit v2 on v1

--- a/solution.py
+++ b/solution.py
@@ -3,6 +3,7 @@
 import jax
 import jax.numpy as jnp
 from jax import lax
+from jax.experimental import pallas as pl
 from jax.sharding import PartitionSpec as P
 
 dilation_steps = (8, 16)
@@ -60,23 +61,39 @@
     ]
 
 
-def weight_gradient_terms(padded, d_hidden, cot_here, middle, dilation, inverse_square_root):
-    row_count = d_hidden.shape[0]
-    kernel_taps = [
-        jnp.einsum(
-            "pc,pe->ce",
-            padded[kernel_tap * dilation : kernel_tap * dilation + row_count],
-            d_hidden,
-            preferred_element_type=jnp.float32,
-        )
-        for kernel_tap in range(3)
-    ]
-    dilated = (jnp.concatenate(kernel_taps, axis=1) * inverse_square_root).astype(jnp.bfloat16)
-    mixed = (
-        jnp.einsum("pc,pe->ce", cot_here, middle, preferred_element_type=jnp.float32)
-        * inverse_square_root
-    ).astype(jnp.bfloat16)
-    return dilated, mixed
+def shifted_taps(d_hidden, dilation):
+    return jnp.concatenate(
+        [jnp.pad(d_hidden, ((k * dilation, (2 - k) * dilation), (0, 0))) for k in range(3)], axis=1
+    )
+
+
+def gradient_kernel(scale, widths, *refs):
+    out_ref = refs[-1]
+    start = 0
+    for pair in range(len(widths)):
+        lhs = refs[2 * pair][...]
+        rhs = refs[2 * pair + 1][...]
+        term = jnp.dot(lhs, rhs, preferred_element_type=jnp.float32) * scale
+        out_ref[:, start : start + widths[pair]] = term.astype(out_ref.dtype)
+        start += widths[pair]
+
+
+def weight_gradient_buffer(pairs, inverse_square_root, row_tile=256):
+    rows = pairs[0][0].shape[0]
+    widths = tuple(rhs.shape[1] for _, rhs in pairs)
+    in_specs = []
+    operands = []
+    for lhs, rhs in pairs:
+        in_specs.append(pl.BlockSpec((row_tile, lhs.shape[1]), lambda i: (i, 0)))
+        in_specs.append(pl.BlockSpec(rhs.shape, lambda i: (0, 0)))
+        operands += [lhs, rhs]
+    return pl.pallas_call(
+        lambda *refs: gradient_kernel(inverse_square_root, widths, *refs),
+        grid=(rows // row_tile,),
+        in_specs=in_specs,
+        out_specs=pl.BlockSpec((row_tile, sum(widths)), lambda i: (i, 0)),
+        out_shape=jax.ShapeDtypeStruct((rows, sum(widths)), jnp.bfloat16),
+    )(*operands)
 
 
 def per_device(inputs, cotangent, w_dilated, w_mix, in_scale, in_shift, mid_scale, mid_shift):
@@ -129,15 +146,13 @@
                 w_conv[:, kernel_tap, :],
                 preferred_element_type=jnp.float32,
             )
-        (
-            dilated_weight_gradients[residual_block_index],
-            mixing_weight_gradients[residual_block_index],
-        ) = weight_gradient_terms(padded, d_hidden, cot_here, middle, dilation, inverse_square_root)
+        dilated_weight_gradients[residual_block_index] = (padded.T, shifted_taps(d_hidden, dilation))
+        mixing_weight_gradients[residual_block_index] = (cot_here.T, middle)
         upstream_gradient = (
             upstream_gradient + gelu_back(pre_in, d_act) * in_scale[residual_block_index]
         )
     summed = lax.psum_scatter(
-        jnp.concatenate(dilated_weight_gradients + mixing_weight_gradients, axis=1),
+        weight_gradient_buffer(dilated_weight_gradients + mixing_weight_gradients, inverse_square_root),
         ("seq", "win"),
         scatter_dimension=0,
         tiled=True,

time: 502 us -> 488 us (0.972); the launches traced: 500 us -> 479 us
  local copies, waits for them, and re-layouts: 63.7 us -> 47.2 us
  other arithmetic: 27.4 us -> 11.6 us
  Pallas kernels: 0 us -> 15.6 us
  matrix products: 61.1 us -> 51.3 us
    unnamed x3 -> x2, waiting for transfers between devices: 181 us -> 0.03 us
    reduce_scatter x0 -> x1, waiting for transfers between devices: none -> 178 us  [per_device(): lax.psum_scatter(weight_gradient_buffer(dilated_weight_gradients + mixing...]
    unnamed x31 -> x49, local copies, waits for them, and re-layouts: 27.3 us -> 9.46 us
    all_gather x1, waiting for transfers between devices: 121 us -> 104 us  [fetch_weights(): gathered = lax.all_gather(local, ('seq', 'win'), axis=0, tiled=True)]
    pallas_call x0 -> x1, Pallas kernels: none -> 15.6 us  [weight_gradient_buffer(): pl.pallas_call(lambda *refs: gradient_kernel(inverse_square_root, widths,...]
    ppermute x4, waiting for transfers between devices: 0.45 us -> 16 us  [padded_2(): lax.ppermute(lax.slice_in_dim(block, block.shape[dim] - width, None, axis...]
    dot_general x8 -> x0, matrix products: 14.6 us -> none  [the longest x6 8.72 us: weight_gradient_terms(): jnp.einsum('pc,pe->ce', padded[kernel_tap * dilation:kernel_tap * dilatio...]
    concatenate x1 -> x2, other arithmetic: 17 us -> 2.8 us  [shifted_taps(): jnp.concatenate([jnp.pad(d_hidden, ((k * dilation, (2 - k) * dilation), (...]
  transfers between devices with their start and end apart: 10 -> 10, of which waited for: 5 -> 8; matrix products, arithmetic and copies ran while one was open for 14% -> 8% of each run, Pallas kernels for 0% -> 0%
where the time goes in v2:
time: 488 us; the launch traced here: 479 us
  waiting for transfers between devices  313 us (64%)
  matrix products  51.3 us (11%)
  local copies, waits for them, and re-layouts  47.2 us (10%)
  starting transfers between devices  25.3 us (5%)
  Pallas kernels  15.6 us (3%)
  between operations  14.9 us (3%)
  other arithmetic  11.6 us (2%)
    reduce_scatter x1, waiting for transfers between devices, per_device(): lax.psum_scatter(weight_gradient_buffer(dilated_weight_gradients + mixing...  178 us
    all_gather x1, waiting for transfers between devices, fetch_weights(): gathered = lax.all_gather(local, ('seq', 'win'), axis=0, tiled=True)  104 us
    slice x3, local copies, waits for them, and re-layouts, fetch_weights(): gathered[:, b * taps * c2:(b + 1) * taps * c2].reshape(full_rows, taps, c2)  30.6 us
    ppermute x4, starting transfers between devices, padded_2(): lax.ppermute(lax.slice_in_dim(block, block.shape[dim] - width, None, axis...  19.4 us
    ppermute x4, waiting for transfers between devices, padded_2(): lax.ppermute(lax.slice_in_dim(block, block.shape[dim] - width, None, axis...  16 us
    pallas_call x1, Pallas kernels, weight_gradient_buffer(): pl.pallas_call(lambda *refs: gradient_kernel(inverse_square_root, widths,...  15.6 us
    ppermute x4, waiting for transfers between devices, padded_2(): lax.ppermute(lax.slice_in_dim(block, 0, width, axis=dim), axis, backward)  15.2 us
    dot_general x4, matrix products, dilated_conv(): jnp.dot(padded[lower:lower + out_rows], w_conv[:, kernel_tap, :], preferr...  10.9 us
  transfers between devices with their start and end apart: 10, of which 8 were waited for; matrix products, arithmetic and copies ran while one was open for 8% of the time, Pallas kernels for 0%

profile of v2, /device:TPU:0, one launch (start us, length us, event | category | flops | bytes accessed | tf_op | source)
XLA Modules:
  0.0 479.0 jit_solution(13926427675389160798)
XLA Ops:
  15.4 6.2 %collective-permute-start = (bf16[8,1536]{0,1:T(8,128)(2,1)}, bf16[8,1536]{0,1:T(8,128)(2,1)}, u32[]{:S(2)}, u32[]{:S(2)}) collective-permute-start(bf16[8,1536]{0,1:T(8,128)(2,1)} %get-tuple-element.24), channel_id=1, source_target_pairs={{0,4},{4,8},{8,12},{12,16},{16,20},{20,24},{24,28},{1,5},{5,9},{9,... | collective-permute-start | bytes 73736 | tf_op jit(solution)/shard_map/ppermute | solution.py:17
  24.0 7.7 %collective-permute-done.1 = bf16[8,1536]{0,1:T(8,128)(2,1)} collective-permute-done((bf16[8,1536]{0,1:T(8,128)(2,1)}, bf16[8,1536]{0,1:T(8,128)(2,1)}, u32[]{:S(2)}, u32[]{:S(2)}) %collective-permute-start.1) | collective-permute-done | bytes 24608 | tf_op jit(solution)/shard_map/ppermute | solution.py:20
  31.7 9.4 %collective-permute-done = bf16[8,1536]{0,1:T(8,128)(2,1)} collective-permute-done((bf16[8,1536]{0,1:T(8,128)(2,1)}, bf16[8,1536]{0,1:T(8,128)(2,1)}, u32[]{:S(2)}, u32[]{:S(2)}) %collective-permute-start) | collective-permute-done | bytes 24608 | tf_op jit(solution)/shard_map/ppermute | solution.py:17
  44.4 103.9 %all-gather.2.cloned.1.call-done = bf16[1536,6144]{1,0:T(8,128)(2,1)} async-done(((bf16[48,6144]{1,0:T(8,128)(2,1)}), bf16[1536,6144]{1,0:T(8,128)(2,1)}) %all-gather.2.cloned.1.call-update) | async-done | bytes 18874384 | tf_op jit(solution)/shard_map/all_gather | solution.py:52
  148.3 10.0 %fusion.128 = (bf16[1536,2304]{1,0:T(8,128)(2,1)}, bf16[1536,2304]{1,0:T(8,128)(2,1)}) fusion(bf16[1536,6144]{1,0:T(8,128)(2,1)} %all-gather.2.cloned.1.call-done), kind=kLoop, calls=%fused_computation.173 | loop fusion | bytes 28311552 | tf_op jit(solution)/shard_map/slice | solution.py:57
  158.3 10.3 %copy.30 = bf16[1536,2304]{0,1:T(8,128)(2,1)} copy(bf16[1536,2304]{1,0:T(8,128)(2,1)} %get-tuple-element.21) | data formatting | bytes 14155776 | tf_op jit(solution)/shard_map/slice | solution.py:57
  168.6 4.6 fusion.47
  173.2 10.3 %copy.35 = bf16[1536,2304]{0,1:T(8,128)(2,1)} copy(bf16[1536,2304]{1,0:T(8,128)(2,1)} %get-tuple-element.20) | data formatting | bytes 14155776 | tf_op jit(solution)/shard_map/slice | solution.py:57
  183.5 3.5 fusion.49
  187.1 3.7 multiply_convert_fusion.2
  190.8 3.9 multiply_convert_fusion
  197.6 4.6 collective-permute-start.2
  202.2 5.9 %collective-permute-done.3 = bf16[16,1536]{0,1:T(8,128)(2,1)S(1)} collective-permute-done((bf16[16,1536]{0,1:T(8,128)(2,1)S(1)}, bf16[16,1536]{0,1:T(8,128)(2,1)S(1)}, u32[]{:S(2)}, u32[]{:S(2)}) %collective-permute-start.3) | collective-permute-done | bytes 49184 | tf_op jit(solution)/shard_map/ppermute | solution.py:20
  209.8 6.6 %collective-permute-done.2 = bf16[16,1536]{0,1:T(8,128)(2,1)S(1)} collective-permute-done((bf16[16,1536]{0,1:T(8,128)(2,1)S(1)}, bf16[16,1536]{0,1:T(8,128)(2,1)S(1)}, u32[]{:S(2)}, u32[]{:S(2)}) %collective-permute-start.2) | collective-permute-done | bytes 49184 | tf_op jit(solution)/shard_map/ppermute | solution.py:17
  225.2 4.4 collective-permute-start.5
  235.3 3.5 fusion.43
  240.1 3.4 fusion.83
  244.9 15.6 %shard_map.111 = bf16[1536,6144]{1,0:T(8,128)(2,1)} custom-call(bf16[1536,400]{1,0:T(8,128)(2,1)} %maximum_bitcast_fusion.refs_0_, bf16[400,2304]{1,0:T(8,128)(2,1)} %fusion.64.refs_1_, bf16[1536,416]{1,0:T(8,128)(2,1)} %maximum_bitcast_fusion.1.refs_2_, bf16[416,2304]{1,0:T(8,128)(2,1)} %fusion.62.refs_3_, bf16[1536,384]{1,0:T(8,128)(2,1)} %convert_bitcast_fusion.1.refs_4_, ...), custom_call_target="tpu_custom_call" | custom-call | tf_op jit(solution)/shard_map/pallas_call | solution.py:90
  261.6 3.8 fusion.12
  266.8 4.2 collective-permute-start.7
  271.1 3.3 fusion.46
  276.0 3.3 fusion.48
  280.3 6.7 %fusion.35 = f32[1,384,1536]{1,2,0:T(8,128)} fusion(f32[384,1536]{0,1:T(8,128)S(1)} %copy-done.3, bf16[1,384,1536]{1,2,0:T(8,128)(2,1)S(1)} %copy.26, f32[384,1536]{0,1:T(8,128)S(1)} %fusion.48, f32[384,1536]{0,1:T(8,128)S(1)} %fusion.46, bf16[1536,3,768]{0,2,1:T(8,128)(2,1)} %bitcast.159, f32[1536]{0:T(1024)S(1)} %get-tuple-element.15, ...), kind=kOutput, calls=%fused_computation.54 | convolution fusion | flops 922484736 | bytes 13590528 | tf_op jit(solution)/shard_map/pe,ce->pc/dot_general | solution.py:135
  290.2 177.8 %reduce-scatter.2.cloned.1.call-done = bf16[48,6144]{1,0:T(8,128)(2,1)} async-done(((bf16[1536,6144]{1,0:T(8,128)(2,1)}), bf16[48,6144]{1,0:T(8,128)(2,1)}) %reduce-scatter.2.cloned.1.call-update) | async-done | bytes 589840 | tf_op jit(solution)/shard_map/reduce_scatter | solution.py:154
  (88 shorter events, 47.2 us)
Async XLA Ops:
  7.2 141.1 %all-gather.2.cloned.1.call-start = ((), (), s32[]{:S(2)}) async-start(), calls=%async_computation.1 | async-start | bytes 19464192 | tf_op jit(solution)/shard_map/all_gather | solution.py:52
  10.2 457.8 %reduce-scatter.2.cloned.1.call-start = ((), (), s32[]{:S(2)}) async-start(), calls=%async_computation.2 | async-start | bytes 19464192 | tf_op jit(solution)/shard_map/reduce_scatter | solution.py:154
  11.0 10.6 %copy-start.12 = (f32[2,768]{1,0:T(2,128)S(1)}, f32[2,768]{1,0:T(2,128)}, u32[]{:S(2)}) copy-start(f32[2,768]{1,0:T(2,128)} %param.15) | copy-start | bytes 18436
  11.1 10.6 %copy-start.13 = (f32[2,768]{1,0:T(2,128)S(1)}, f32[2,768]{1,0:T(2,128)}, u32[]{:S(2)}) copy-start(f32[2,768]{1,0:T(2,128)} %param.14) | copy-start | bytes 18436
  14.1 17.6 %collective-permute-start.1 = (bf16[8,1536]{0,1:T(8,128)(2,1)}, bf16[8,1536]{0,1:T(8,128)(2,1)}, u32[]{:S(2)}, u32[]{:S(2)}) collective-permute-start(bf16[8,1536]{0,1:T(8,128)(2,1)} %get-tuple-element.25), channel_id=1, source_target_pairs={{4,0},{8,4},{12,8},{16,12},{20,16},{24,20},{28,24},{5,1},{9,5},{13... | collective-permute-start | bytes 73736 | tf_op jit(solution)/shard_map/ppermute | solution.py:20
  15.4 25.8 %collective-permute-start = (bf16[8,1536]{0,1:T(8,128)(2,1)}, bf16[8,1536]{0,1:T(8,128)(2,1)}, u32[]{:S(2)}, u32[]{:S(2)}) collective-permute-start(bf16[8,1536]{0,1:T(8,128)(2,1)} %get-tuple-element.24), channel_id=1, source_target_pairs={{0,4},{4,8},{8,12},{12,16},{16,20},{20,24},{24,28},{1,5},{5,9},{9,... | collective-permute-start | bytes 73736 | tf_op jit(solution)/shard_map/ppermute | solution.py:17
  24.0 211.3 %copy-start = (bf16[1,384,1536]{1,2,0:T(8,128)(2,1)}, bf16[1,384,1536]{1,2,0:T(8,128)(2,1)S(1)}, u32[]{:S(2)}) copy-start(bf16[1,384,1536]{1,2,0:T(8,128)(2,1)S(1)} %copy.40) | copy-start | bytes 3538948
  183.5 3.5 copy-start.19
  187.1 3.7 copy-start.10
  187.1 3.7 copy-start.11
  187.1 9.3 %slice-start = ((s8[7077888]{0:T(1024)(128)(4,1)}), s8[4194304]{0:T(1024)(128)(4,1)S(1)}, s32[]{:S(2)}) async-start(s8[7077888]{0:T(1024)(128)(4,1)} %bitcast.160), calls=%async_computation.3 | async-start | bytes 8388608
  190.8 3.9 copy-start.6
  190.8 5.6 %slice-start.1 = ((s8[7077888]{0:T(1024)(128)(4,1)}), s8[2883584]{0:T(1024)(128)(4,1)S(1)}, s32[]{:S(2)}) async-start(s8[7077888]{0:T(1024)(128)(4,1)} %bitcast.160), calls=%async_computation.4 | async-start | bytes 5767168
  194.7 40.6 %copy-start.18 = (f32[384,1536]{0,1:T(8,128)}, f32[384,1536]{0,1:T(8,128)S(1)}, u32[]{:S(2)}) copy-start(f32[384,1536]{0,1:T(8,128)S(1)} %get-tuple-element.33) | copy-start | bytes 7077892
  194.9 13.2 %collective-permute-start.3 = (bf16[16,1536]{0,1:T(8,128)(2,1)S(1)}, bf16[16,1536]{0,1:T(8,128)(2,1)S(1)}, u32[]{:S(2)}, u32[]{:S(2)}) collective-permute-start(bf16[16,1536]{0,1:T(8,128)(2,1)S(1)} %get-tuple-element.23), channel_id=1, source_target_pairs={{4,0},{8,4},{12,8},{16,12},{20,16},{24,20},{28,24},{5,1},{9,5},{13... | collective-permute-start | bytes 147464 | tf_op jit(solution)/shard_map/ppermute | solution.py:20
  197.6 18.8 %copy-start.15 = (f32[768]{0:T(1024)S(1)}, f32[768]{0:T(1024)}, u32[]{:S(2)}) copy-start(f32[768]{0:T(1024)} %get-tuple-element.39) | copy-start | bytes 9220
  197.6 18.8 %copy-start.16 = (f32[768]{0:T(1024)S(1)}, f32[768]{0:T(1024)}, u32[]{:S(2)}) copy-start(f32[768]{0:T(1024)} %get-tuple-element.18) | copy-start | bytes 9220
  197.6 18.8 %collective-permute-start.2 = (bf16[16,1536]{0,1:T(8,128)(2,1)S(1)}, bf16[16,1536]{0,1:T(8,128)(2,1)S(1)}, u32[]{:S(2)}, u32[]{:S(2)}) collective-permute-start(bf16[16,1536]{0,1:T(8,128)(2,1)S(1)} %get-tuple-element.22), channel_id=1, source_target_pairs={{0,4},{4,8},{8,12},{12,16},{16,20},{20,24},{24,28},{1,5},{5,9},{9,... | collective-permute-start | bytes 147464 | tf_op jit(solution)/shard_map/ppermute | solution.py:17
  225.2 8.0 %collective-permute-start.5 = (bf16[16,768]{1,0:T(8,128)(2,1)S(1)}, bf16[16,768]{1,0:T(8,128)(2,1)S(1)}, u32[]{:S(2)}, u32[]{:S(2)}) collective-permute-start(bf16[16,768]{1,0:T(8,128)(2,1)S(1)} %get-tuple-element.29), channel_id=1, source_target_pairs={{0,4},{4,8},{8,12},{12,16},{16,20},{20,24},{24,28},{1,5},{5,9},{9,... | collective-permute-start | bytes 73736 | tf_op jit(solution)/shard_map/ppermute | solution.py:17
  229.6 5.7 %collective-permute-start.4 = (bf16[16,768]{1,0:T(8,128)(2,1)S(1)}, bf16[16,768]{1,0:T(8,128)(2,1)S(1)}, u32[]{:S(2)}, u32[]{:S(2)}) collective-permute-start(bf16[16,768]{1,0:T(8,128)(2,1)S(1)} %get-tuple-element.28), channel_id=1, source_target_pairs={{4,0},{8,4},{12,8},{16,12},{20,16},{24,20},{28,24},{5,1},{9,5},{13... | collective-permute-start | bytes 73736 | tf_op jit(solution)/shard_map/ppermute | solution.py:20
  238.8 4.7 copy-start.2
  266.8 9.1 %collective-permute-start.7 = (bf16[8,768]{1,0:T(8,128)(2,1)S(1)}, bf16[8,768]{1,0:T(8,128)(2,1)S(1)}, u32[]{:S(2)}, u32[]{:S(2)}) collective-permute-start(bf16[8,768]{1,0:T(8,128)(2,1)S(1)} %get-tuple-element.27), channel_id=1, source_target_pairs={{0,4},{4,8},{8,12},{12,16},{16,20},{20,24},{24,28},{1,5},{5,9},{9,... | collective-permute-start | bytes 36872 | tf_op jit(solution)/shard_map/ppermute | solution.py:17
  274.4 5.9 %copy-start.3 = (f32[384,1536]{0,1:T(8,128)S(1)}, f32[384,1536]{0,1:T(8,128)}, u32[]{:S(2)}) copy-start(f32[384,1536]{0,1:T(8,128)} %copy-done.2) | copy-start | bytes 7077892
  274.4 5.9 %collective-permute-start.6 = (bf16[8,768]{1,0:T(8,128)(2,1)S(1)}, bf16[8,768]{1,0:T(8,128)(2,1)S(1)}, u32[]{:S(2)}, u32[]{:S(2)}) collective-permute-start(bf16[8,768]{1,0:T(8,128)(2,1)S(1)} %get-tuple-element.26), channel_id=1, source_target_pairs={{4,0},{8,4},{12,8},{16,12},{20,16},{24,20},{28,24},{5,1},{9,5},{13... | collective-permute-start | bytes 36872 | tf_op jit(solution)/shard_map/ppermute | solution.py:20
  (8 other events, 19.1 us)
Sparse Core Ops, SparseCore 0:
  11.5 136.7 all-gather.1
  260.6 207.3 reduce-scatter.1

commit v3 on v2

--- a/solution.py
+++ b/solution.py
@@ -30,16 +30,63 @@
     return jax.vjp(gelu_value, pre_values)[1](upstream_gradient)[0]
 
 
-def dilated_conv(padded, w_conv, dilation, out_rows):
-    hidden = jnp.dot(padded[0:out_rows], w_conv[:, 0, :], preferred_element_type=jnp.float32)
+def conv_forward_kernel(dilation, out_rows, act_ref, w_ref, scale_ref, shift_ref, out_ref):
+    width = out_ref.shape[1]
+    hidden = jnp.dot(act_ref[0:out_rows, :], w_ref[:, 0:width], preferred_element_type=jnp.float32)
     for kernel_tap in (1, 2):
         lower = kernel_tap * dilation
         hidden = hidden + jnp.dot(
-            padded[lower : lower + out_rows],
-            w_conv[:, kernel_tap, :],
+            act_ref[lower : lower + out_rows, :],
+            w_ref[:, kernel_tap * width : (kernel_tap + 1) * width],
             preferred_element_type=jnp.float32,
         )
-    return hidden
+    out_ref[...] = hidden * scale_ref[...] + shift_ref[...]
+
+
+def conv_backward_kernel(dilation, out_rows, grad_ref, w_ref, out_ref):
+    width = grad_ref.shape[1]
+    numbers = (((1,), (1,)), ((), ()))
+    total = None
+    for kernel_tap in range(3):
+        lower = (2 - kernel_tap) * dilation
+        term = lax.dot_general(
+            grad_ref[lower : lower + out_rows, :],
+            w_ref[:, kernel_tap * width : (kernel_tap + 1) * width],
+            numbers,
+            preferred_element_type=jnp.float32,
+        )
+        total = term if total is None else total + term
+    out_ref[...] = total
+
+
+def conv_forward(padded, gathered, block, c2, scale, shift, dilation, out_rows):
+    rows = gathered.shape[0]
+    return pl.pallas_call(
+        lambda *refs: conv_forward_kernel(dilation, out_rows, *refs),
+        grid=(1,),
+        in_specs=[
+            pl.BlockSpec(padded.shape, lambda i: (0, 0)),
+            pl.BlockSpec((rows, 3 * c2), lambda i: (0, block)),
+            pl.BlockSpec((1, c2), lambda i: (0, 0)),
+            pl.BlockSpec((1, c2), lambda i: (0, 0)),
+        ],
+        out_specs=pl.BlockSpec((out_rows, c2), lambda i: (0, 0)),
+        out_shape=jax.ShapeDtypeStruct((out_rows, c2), jnp.float32),
+    )(padded, gathered, scale.reshape(1, c2), shift.reshape(1, c2))
+
+
+def conv_backward(d_pad, gathered, block, c2, dilation, out_rows):
+    rows = gathered.shape[0]
+    return pl.pallas_call(
+        lambda *refs: conv_backward_kernel(dilation, out_rows, *refs),
+        grid=(1,),
+        in_specs=[
+            pl.BlockSpec(d_pad.shape, lambda i: (0, 0)),
+            pl.BlockSpec((rows, 3 * c2), lambda i: (0, block)),
+        ],
+        out_specs=pl.BlockSpec((out_rows, rows), lambda i: (0, 0)),
+        out_shape=jax.ShapeDtypeStruct((out_rows, rows), jnp.float32),
+    )(d_pad, gathered)
 
 
 def fetch_weights(w_dilated, w_mix):
@@ -50,15 +97,8 @@
         axis=1,
     )
     gathered = lax.all_gather(local, ("seq", "win"), axis=0, tiled=True)
-    full_rows = gathered.shape[0]
     split = blocks * taps * c2
-    return [
-        (
-            gathered[:, b * taps * c2 : (b + 1) * taps * c2].reshape(full_rows, taps, c2),
-            gathered[:, split + b * c2 : split + (b + 1) * c2],
-        )
-        for b in range(blocks)
-    ]
+    return gathered, [gathered[:, split + b * c2 : split + (b + 1) * c2] for b in range(blocks)]
 
 
 def shifted_taps(d_hidden, dilation):
@@ -104,48 +144,42 @@
     inverse_square_root = 1.0 / math.sqrt(lax.axis_size("win") * inputs.shape[0] * window_len)
     residual_block_count = len(dilation_steps)
     saved = []
-    weights = fetch_weights(w_dilated, w_mix)
+    gathered, mixing_weights = fetch_weights(w_dilated, w_mix)
+    c2 = w_dilated.shape[3]
     stream = x_local.astype(jnp.float32)
     for residual_block_index in range(residual_block_count):
         dilation = dilation_steps[residual_block_index]
-        w_conv, w_out = weights[residual_block_index]
+        w_out = mixing_weights[residual_block_index]
         pre_in = stream * in_scale[residual_block_index] + in_shift[residual_block_index]
         activated = gelu_value(pre_in).astype(jnp.bfloat16)
         padded = padded_2(activated, (("seq", 0),), dilation)
-        pre_mid = (
-            dilated_conv(padded, w_conv, dilation, row_count) * mid_scale[residual_block_index]
-            + mid_shift[residual_block_index]
+        pre_mid = conv_forward(
+            padded,
+            gathered,
+            residual_block_index,
+            c2,
+            mid_scale[residual_block_index],
+            mid_shift[residual_block_index],
+            dilation,
+            row_count,
         )
         middle = gelu_value(pre_mid).astype(jnp.bfloat16)
         stream = stream + jnp.einsum("pe,ce->pc", middle, w_out, preferred_element_type=jnp.float32)
-        saved.append((w_conv, w_out, pre_in, padded, pre_mid, middle))
+        saved.append((w_out, pre_in, padded, pre_mid, middle))
     output = stream.astype(jnp.bfloat16)
     upstream_gradient = cot_local.astype(jnp.float32)
     dilated_weight_gradients = [None] * residual_block_count
     mixing_weight_gradients = [None] * residual_block_count
     for residual_block_index in reversed(range(residual_block_count)):
         dilation = dilation_steps[residual_block_index]
-        w_conv, w_out, pre_in, padded, pre_mid, middle = saved[residual_block_index]
+        w_out, pre_in, padded, pre_mid, middle = saved[residual_block_index]
         cot_here = upstream_gradient.astype(jnp.bfloat16)
         d_mid = jnp.dot(cot_here, w_out, preferred_element_type=jnp.float32)
         d_hidden = (gelu_back(pre_mid, d_mid) * mid_scale[residual_block_index]).astype(
             jnp.bfloat16
         )
         d_pad = padded_2(d_hidden, (("seq", 0),), dilation)
-        d_act = jnp.einsum(
-            "pe,ce->pc",
-            d_pad[2 * dilation : 2 * dilation + row_count],
-            w_conv[:, 0, :],
-            preferred_element_type=jnp.float32,
-        )
-        for kernel_tap in (1, 2):
-            lower = (2 - kernel_tap) * dilation
-            d_act = d_act + jnp.einsum(
-                "pe,ce->pc",
-                d_pad[lower : lower + row_count],
-                w_conv[:, kernel_tap, :],
-                preferred_element_type=jnp.float32,
-            )
+        d_act = conv_backward(d_pad, gathered, residual_block_index, c2, dilation, row_count)
         dilated_weight_gradients[residual_block_index] = (padded.T, shifted_taps(d_hidden, dilation))
         mixing_weight_gradients[residual_block_index] = (cot_here.T, middle)
         upstream_gradient = (

time: 488 us -> 469 us (0.961); the launches traced: 479 us -> 468 us
  matrix products: 51.3 us -> 16.7 us
  Pallas kernels: 15.6 us -> 46 us
  other arithmetic: 11.6 us -> 30.6 us
  local copies, waits for them, and re-layouts: 47.2 us -> 29.1 us
  waiting for transfers between devices: 313 us -> 303 us
    dot_general x12 -> x0, matrix products: 37 us -> none  [the longest x4 10.9 us: dilated_conv(): jnp.dot(padded[lower:lower + out_rows], w_conv[:, kernel_tap, :], preferr...]
    pallas_call x0 -> x4, Pallas kernels: none -> 30.4 us  [the longest x2 15.8 us: conv_backward(): pl.pallas_call(lambda *refs: conv_backward_kernel(dilation, out_rows, *re...]
    slice x6 -> x1, local copies, waits for them, and re-layouts: 31.3 us -> 1.22 us  [per_device(): mid_scale[residual_block_index]]
    concatenate x0 -> x4, other arithmetic: none -> 7.82 us  [padded_2(): block = jnp.concatenate([low, block, high], axis=dim)]
    pallas_call x0 -> x2, local copies, waits for them, and re-layouts: none -> 5.27 us  [conv_backward(): pl.pallas_call(lambda *refs: conv_backward_kernel(dilation, out_rows, *re...]
    concatenate x0 -> x2, local copies, waits for them, and re-layouts: none -> 5.04 us  [padded_2(): block = jnp.concatenate([low, block, high], axis=dim)]
  transfers between devices with their start and end apart: 10 -> 10, of which waited for: 8 -> 6; matrix products, arithmetic and copies ran while one was open for 8% -> 8% of each run, Pallas kernels for 0% -> 2%
where the time goes in v3:
time: 469 us; the launch traced here: 468 us
  waiting for transfers between devices  303 us (65%)
  Pallas kernels  46 us (10%)
  other arithmetic  30.6 us (7%)
  local copies, waits for them, and re-layouts  29.1 us (6%)
  starting transfers between devices  27.6 us (6%)
  matrix products  16.7 us (4%)
  between operations  14.4 us (3%)
    reduce_scatter x1, waiting for transfers between devices, per_device(): lax.psum_scatter(weight_gradient_buffer(dilated_weight_gradients + mixing...  173 us
    all_gather x1, waiting for transfers between devices, fetch_weights(): gathered = lax.all_gather(local, ('seq', 'win'), axis=0, tiled=True)  101 us
    ppermute x4, starting transfers between devices, padded_2(): lax.ppermute(lax.slice_in_dim(block, block.shape[dim] - width, None, axis...  22.3 us
    ppermute x4, waiting for transfers between devices, padded_2(): lax.ppermute(lax.slice_in_dim(block, block.shape[dim] - width, None, axis...  17.7 us
    pallas_call x2, Pallas kernels, conv_backward(): pl.pallas_call(lambda *refs: conv_backward_kernel(dilation, out_rows, *re...  15.8 us
    pallas_call x1, Pallas kernels, weight_gradient_buffer(): pl.pallas_call(lambda *refs: gradient_kernel(inverse_square_root, widths,...  15.6 us
    pallas_call x2, Pallas kernels, conv_forward(): pl.pallas_call(lambda *refs: conv_forward_kernel(dilation, out_rows, *ref...  14.6 us
    ppermute x4, waiting for transfers between devices, padded_2(): lax.ppermute(lax.slice_in_dim(block, 0, width, axis=dim), axis, backward)  11.1 us
  transfers between devices with their start and end apart: 10, of which 6 were waited for; matrix products, arithmetic and copies ran while one was open for 8% of the time, Pallas kernels for 2%

profile of v3, /device:TPU:0, one launch (start us, length us, event | category | flops | bytes accessed | tf_op | source)
XLA Modules:
  0.0 467.7 jit_solution(1562837005714750885)
XLA Ops:
  15.4 6.2 %collective-permute-start = (bf16[8,1536]{0,1:T(8,128)(2,1)}, bf16[8,1536]{0,1:T(8,128)(2,1)}, u32[]{:S(2)}, u32[]{:S(2)}) collective-permute-start(bf16[8,1536]{0,1:T(8,128)(2,1)} %get-tuple-element.22), channel_id=1, source_target_pairs={{0,4},{4,8},{8,12},{12,16},{16,20},{20,24},{24,28},{1,5},{5,9},{9,... | collective-permute-start | bytes 73736 | tf_op jit(solution)/shard_map/ppermute | solution.py:17
  24.6 7.2 %collective-permute-done.1 = bf16[8,1536]{0,1:T(8,128)(2,1)} collective-permute-done((bf16[8,1536]{0,1:T(8,128)(2,1)}, bf16[8,1536]{0,1:T(8,128)(2,1)}, u32[]{:S(2)}, u32[]{:S(2)}) %collective-permute-start.1) | collective-permute-done | bytes 24608 | tf_op jit(solution)/shard_map/ppermute | solution.py:20
  31.7 9.4 %collective-permute-done = bf16[8,1536]{0,1:T(8,128)(2,1)} collective-permute-done((bf16[8,1536]{0,1:T(8,128)(2,1)}, bf16[8,1536]{0,1:T(8,128)(2,1)}, u32[]{:S(2)}, u32[]{:S(2)}) %collective-permute-start) | collective-permute-done | bytes 24608 | tf_op jit(solution)/shard_map/ppermute | solution.py:17
  41.1 3.2 pad_maximum_fusion
  46.9 101.4 %all-gather.2.cloned.1.call-done.refs_1_ = bf16[1536,6144]{1,0:T(8,128)(2,1)} async-done(((bf16[48,6144]{1,0:T(8,128)(2,1)}), bf16[1536,6144]{1,0:T(8,128)(2,1)}) %all-gather.2.cloned.1.call-update) | async-done | bytes 18874384 | tf_op jit(solution)/shard_map/all_gather | solution.py:99
  148.3 7.3 %shard_map.111 = f32[384,768]{1,0:T(8,128)} custom-call(bf16[400,1536]{1,0:T(8,128)(2,1)} %copy.31.refs_0_, bf16[1536,6144]{1,0:T(8,128)(2,1)} %all-gather.2.cloned.1.call-done.refs_1_, f32[1,768]{1,0:T(1,128)} %get-tuple-element.29.refs_2_, f32[1,768]{1,0:T(1,128)} %get-tuple-element.36.refs_3_), custom_call_target="tpu_custom_call" | custom-call | tf_op jit(solution)/shard_map/pallas_call | solution.py:64
  157.2 5.4 %multiply_convert_fusion = (bf16[384,1536]{0,1:T(8,128)(2,1)S(1)}, f32[384,1536]{0,1:T(8,128)}) fusion(f32[1536]{0:T(1024)} %get-tuple-element.14, f32[1536]{0:T(1024)} %get-tuple-element.35, bf16[384,768]{1,0:T(8,128)(2,1)S(1)} %multiply_convert_fusion.2.refs_5_, bf16[1536,6144]{1,0:T(8,128)(2,1)} %all-gather.2.cloned.1.call-done.refs_1_, ...), kind=kOutput, calls=%fused_computation.48 | convolution fusion | flops 913637376 | bytes 7684096 | tf_op jit(solution)/shard_map/pe,ce->pc/dot_general | solution.py:167
  164.1 4.8 %collective-permute-start.2 = (bf16[16,1536]{0,1:T(8,128)(2,1)S(1)}, bf16[16,1536]{0,1:T(8,128)(2,1)S(1)}, u32[]{:S(2)}, u32[]{:S(2)}) collective-permute-start(bf16[16,1536]{0,1:T(8,128)(2,1)S(1)} %get-tuple-element.20), channel_id=1, source_target_pairs={{0,4},{4,8},{8,12},{12,16},{16,20},{20,24},{24,28},{1,5},{5,9},{9,... | collective-permute-start | bytes 147464 | tf_op jit(solution)/shard_map/ppermute | solution.py:17
  168.8 3.2 fusion.79.refs_0_
  172.1 3.9 collective-permute-done.3
  176.0 8.3 %collective-permute-done.2 = bf16[16,1536]{0,1:T(8,128)(2,1)S(1)} collective-permute-done((bf16[16,1536]{0,1:T(8,128)(2,1)S(1)}, bf16[16,1536]{0,1:T(8,128)(2,1)S(1)}, u32[]{:S(2)}, u32[]{:S(2)}) %collective-permute-start.2) | collective-permute-done | bytes 49184 | tf_op jit(solution)/shard_map/ppermute | solution.py:17
  189.6 7.4 %shard_map.112 = f32[384,768]{1,0:T(8,128)} custom-call(bf16[416,1536]{1,0:T(8,128)(2,1)} %copy.33.refs_0_, bf16[1536,6144]{1,0:T(8,128)(2,1)} %all-gather.2.cloned.1.call-done.refs_1_, f32[1,768]{1,0:T(1,128)} %get-tuple-element.28.refs_2_, f32[1,768]{1,0:T(1,128)} %get-tuple-element.37.refs_3_), custom_call_target="tpu_custom_call" | custom-call | tf_op jit(solution)/shard_map/pallas_call | solution.py:64
  197.0 3.6 fusion.61
  203.6 5.2 %collective-permute-start.4 = (bf16[16,768]{1,0:T(8,128)(2,1)S(1)}, bf16[16,768]{1,0:T(8,128)(2,1)S(1)}, u32[]{:S(2)}, u32[]{:S(2)}) collective-permute-start(bf16[16,768]{1,0:T(8,128)(2,1)S(1)} %get-tuple-element.26), channel_id=1, source_target_pairs={{0,4},{4,8},{8,12},{12,16},{16,20},{20,24},{24,28},{1,5},{5,9},{9,... | collective-permute-start | bytes 73736 | tf_op jit(solution)/shard_map/ppermute | solution.py:17
  213.2 7.6 %shard_map.113 = f32[384,1536]{1,0:T(8,128)} custom-call(bf16[416,768]{1,0:T(8,128)(2,1)} %pad_maximum_fusion.2.refs_0_, bf16[1536,6144]{1,0:T(8,128)(2,1)} %all-gather.2.cloned.1.call-done.refs_1_), custom_call_target="tpu_custom_call" | custom-call | tf_op jit(solution)/shard_map/pallas_call | solution.py:80
  223.9 4.9 %convert_bitcast_fusion = (bf16[1536,384]{1,0:T(8,128)(2,1)}, f32[384,1536]{0,1:T(8,128)S(1)}) fusion(f32[384,1536]{0,1:T(8,128)} %copy.36, f32[1536]{0:T(1024)S(1)} %copy-done.15, f32[384,1536]{0,1:T(8,128)} %get-tuple-element.33, f32[1536]{0:T(1024)S(1)} %copy-done.16, bf16[1,384,1536]{1,2,0:T(8,128)(2,1)S(1)} %copy.35), kind=kLoop, calls=%fused_computation.89 | loop fusion | flops 14745600 | bytes 9449472 | tf_op jit(solution)/shard_map/transpose | solution.py:184
  230.2 3.4 fusion.53
  235.0 15.6 %shard_map.115 = bf16[1536,6144]{1,0:T(8,128)(2,1)} custom-call(bf16[1536,400]{1,0:T(8,128)(2,1)} %fusion.79.refs_0_, bf16[400,2304]{1,0:T(8,128)(2,1)} %fusion.42.refs_1_, bf16[1536,416]{1,0:T(8,128)(2,1)} %fusion.78.refs_2_, bf16[416,2304]{1,0:T(8,128)(2,1)} %fusion.40.refs_3_, bf16[1536,384]{1,0:T(8,128)(2,1)} %get-tuple-element.18.refs_4_, ...), custom_call_target="tpu_custom_call" | custom-call | tf_op jit(solution)/shard_map/pallas_call | solution.py:130
  252.6 6.1 %collective-permute-start.6 = (bf16[8,768]{1,0:T(8,128)(2,1)}, bf16[8,768]{1,0:T(8,128)(2,1)}, u32[]{:S(2)}, u32[]{:S(2)}) collective-permute-start(bf16[8,768]{1,0:T(8,128)(2,1)} %get-tuple-element.24), channel_id=1, source_target_pairs={{0,4},{4,8},{8,12},{12,16},{16,20},{20,24},{24,28},{1,5},{5,9},{9,... | collective-permute-start | bytes 36872 | tf_op jit(solution)/shard_map/ppermute | solution.py:17
  258.6 4.2 fusion.9
  265.9 8.2 %shard_map.114 = f32[384,1536]{1,0:T(8,128)} custom-call(bf16[400,768]{1,0:T(8,128)(2,1)} %pad_maximum_fusion.3.refs_0_, bf16[1536,6144]{1,0:T(8,128)(2,1)} %all-gather.2.cloned.1.call-done.refs_1_), custom_call_target="tpu_custom_call" | custom-call | tf_op jit(solution)/shard_map/pallas_call | solution.py:80
  276.2 4.6 fusion.24
  280.8 3.2 copy.42
  284.0 173.1 %reduce-scatter.2.cloned.1.call-done = bf16[48,6144]{1,0:T(8,128)(2,1)} async-done(((bf16[1536,6144]{1,0:T(8,128)(2,1)}), bf16[48,6144]{1,0:T(8,128)(2,1)}) %reduce-scatter.2.cloned.1.call-update) | async-done | bytes 589840 | tf_op jit(solution)/shard_map/reduce_scatter | solution.py:188
  (87 shorter events, 46.0 us)
Async XLA Ops:
  7.2 141.1 %all-gather.2.cloned.1.call-start = ((), (), s32[]{:S(2)}) async-start(), calls=%async_computation.1 | async-start | bytes 19464192 | tf_op jit(solution)/shard_map/all_gather | solution.py:99
  10.2 446.9 %reduce-scatter.2.cloned.1.call-start = ((), (), s32[]{:S(2)}) async-start(), calls=%async_computation.2 | async-start | bytes 19464192 | tf_op jit(solution)/shard_map/reduce_scatter | solution.py:188
  11.0 10.6 %copy-start.19 = (f32[2,768]{1,0:T(2,128)S(1)}, f32[2,768]{1,0:T(2,128)}, u32[]{:S(2)}) copy-start(f32[2,768]{1,0:T(2,128)} %param.14) | copy-start | bytes 18436
  11.1 10.6 %copy-start.20 = (f32[2,768]{1,0:T(2,128)S(1)}, f32[2,768]{1,0:T(2,128)}, u32[]{:S(2)}) copy-start(f32[2,768]{1,0:T(2,128)} %param.15) | copy-start | bytes 18436
  14.1 17.6 %collective-permute-start.1 = (bf16[8,1536]{0,1:T(8,128)(2,1)}, bf16[8,1536]{0,1:T(8,128)(2,1)}, u32[]{:S(2)}, u32[]{:S(2)}) collective-permute-start(bf16[8,1536]{0,1:T(8,128)(2,1)} %get-tuple-element.23), channel_id=1, source_target_pairs={{4,0},{8,4},{12,8},{16,12},{20,16},{24,20},{28,24},{5,1},{9,5},{13... | collective-permute-start | bytes 73736 | tf_op jit(solution)/shard_map/ppermute | solution.py:20
  15.4 25.8 %collective-permute-start = (bf16[8,1536]{0,1:T(8,128)(2,1)}, bf16[8,1536]{0,1:T(8,128)(2,1)}, u32[]{:S(2)}, u32[]{:S(2)}) collective-permute-start(bf16[8,1536]{0,1:T(8,128)(2,1)} %get-tuple-element.22), channel_id=1, source_target_pairs={{0,4},{4,8},{8,12},{12,16},{16,20},{20,24},{24,28},{1,5},{5,9},{9,... | collective-permute-start | bytes 73736 | tf_op jit(solution)/shard_map/ppermute | solution.py:17
  24.6 199.3 %copy-start = (bf16[1,384,1536]{1,2,0:T(8,128)(2,1)}, bf16[1,384,1536]{1,2,0:T(8,128)(2,1)S(1)}, u32[]{:S(2)}) copy-start(bf16[1,384,1536]{1,2,0:T(8,128)(2,1)S(1)} %copy.35) | copy-start | bytes 3538948
  157.2 5.4 %copy-start.7 = (bf16[384,768]{1,0:T(8,128)(2,1)}, bf16[384,768]{1,0:T(8,128)(2,1)S(1)}, u32[]{:S(2)}) copy-start(bf16[384,768]{1,0:T(8,128)(2,1)S(1)} %multiply_convert_fusion.2.refs_5_) | copy-start | bytes 1769476
  162.6 21.7 %copy-start.2 = (bf16[384,1536]{0,1:T(8,128)(2,1)}, bf16[384,1536]{0,1:T(8,128)(2,1)S(1)}, u32[]{:S(2)}) copy-start(bf16[384,1536]{0,1:T(8,128)(2,1)S(1)} %get-tuple-element.32) | copy-start | bytes 3538948
  162.8 13.2 %collective-permute-start.3 = (bf16[16,1536]{0,1:T(8,128)(2,1)S(1)}, bf16[16,1536]{0,1:T(8,128)(2,1)S(1)}, u32[]{:S(2)}, u32[]{:S(2)}) collective-permute-start(bf16[16,1536]{0,1:T(8,128)(2,1)S(1)} %get-tuple-element.21), channel_id=1, source_target_pairs={{4,0},{8,4},{12,8},{16,12},{20,16},{24,20},{28,24},{5,1},{9,5},{13... | collective-permute-start | bytes 147464 | tf_op jit(solution)/shard_map/ppermute | solution.py:20
  164.1 20.1 %collective-permute-start.2 = (bf16[16,1536]{0,1:T(8,128)(2,1)S(1)}, bf16[16,1536]{0,1:T(8,128)(2,1)S(1)}, u32[]{:S(2)}, u32[]{:S(2)}) collective-permute-start(bf16[16,1536]{0,1:T(8,128)(2,1)S(1)} %get-tuple-element.20), channel_id=1, source_target_pairs={{0,4},{4,8},{8,12},{12,16},{16,20},{20,24},{24,28},{1,5},{5,9},{9,... | collective-permute-start | bytes 147464 | tf_op jit(solution)/shard_map/ppermute | solution.py:17
  176.0 8.3 %copy-start.9 = (bf16[16,1536]{0,1:T(8,128)(2,1)}, bf16[16,1536]{0,1:T(8,128)(2,1)S(1)}, u32[]{:S(2)}) copy-start(bf16[16,1536]{0,1:T(8,128)(2,1)S(1)} %collective-permute-done.3) | copy-start | bytes 147460
  189.6 7.4 %copy-start.14 = (bf16[1,384,1536]{2,1,0:T(8,128)(2,1)S(1)}, bf16[1,384,1536]{2,1,0:T(8,128)(2,1)}, u32[]{:S(2)}) copy-start(bf16[1,384,1536]{2,1,0:T(8,128)(2,1)} %param.9) | copy-start | bytes 3538948
  200.6 8.3 %copy-start.3 = (bf16[384,1536]{0,1:T(8,128)(2,1)S(1)}, bf16[384,1536]{0,1:T(8,128)(2,1)}, u32[]{:S(2)}) copy-start(bf16[384,1536]{0,1:T(8,128)(2,1)} %copy-done.2) | copy-start | bytes 3538948
  200.6 8.3 %copy-start.10 = (bf16[16,1536]{0,1:T(8,128)(2,1)S(1)}, bf16[16,1536]{0,1:T(8,128)(2,1)}, u32[]{:S(2)}) copy-start(bf16[16,1536]{0,1:T(8,128)(2,1)} %copy-done.9) | copy-start | bytes 147460
  200.7 8.2 %copy-start.12 = (bf16[16,1536]{0,1:T(8,128)(2,1)S(1)}, bf16[16,1536]{0,1:T(8,128)(2,1)}, u32[]{:S(2)}) copy-start(bf16[16,1536]{0,1:T(8,128)(2,1)} %copy-done.11) | copy-start | bytes 147460
  202.2 8.8 %copy-start.4 = (f32[384,768]{1,0:T(8,128)S(1)}, f32[384,768]{1,0:T(8,128)}, u32[]{:S(2)}) copy-start(f32[384,768]{1,0:T(8,128)} %shard_map.112) | copy-start | bytes 3538948
  202.2 10.0 %collective-permute-start.5 = (bf16[16,768]{1,0:T(8,128)(2,1)S(1)}, bf16[16,768]{1,0:T(8,128)(2,1)S(1)}, u32[]{:S(2)}, u32[]{:S(2)}) collective-permute-start(bf16[16,768]{1,0:T(8,128)(2,1)S(1)} %get-tuple-element.27), channel_id=1, source_target_pairs={{4,0},{8,4},{12,8},{16,12},{20,16},{24,20},{28,24},{5,1},{9,5},{13... | collective-permute-start | bytes 73736 | tf_op jit(solution)/shard_map/ppermute | solution.py:20
  203.6 8.6 %collective-permute-start.4 = (bf16[16,768]{1,0:T(8,128)(2,1)S(1)}, bf16[16,768]{1,0:T(8,128)(2,1)S(1)}, u32[]{:S(2)}, u32[]{:S(2)}) collective-permute-start(bf16[16,768]{1,0:T(8,128)(2,1)S(1)} %get-tuple-element.26), channel_id=1, source_target_pairs={{0,4},{4,8},{8,12},{12,16},{16,20},{20,24},{24,28},{1,5},{5,9},{9,... | collective-permute-start | bytes 73736 | tf_op jit(solution)/shard_map/ppermute | solution.py:17
  223.8 6.3 %copy-start.5 = (f32[384,768]{1,0:T(8,128)S(1)}, f32[384,768]{1,0:T(8,128)}, u32[]{:S(2)}) copy-start(f32[384,768]{1,0:T(8,128)} %shard_map.111) | copy-start | bytes 3538948
  223.9 6.3 %copy-start.21 = (f32[768]{0:T(1024)S(1)}, f32[768]{0:T(1024)}, u32[]{:S(2)}) copy-start(f32[768]{0:T(1024)} %get-tuple-element.16) | copy-start | bytes 9220
  250.6 8.0 %copy-start.8 = (bf16[384,768]{1,0:T(8,128)(2,1)S(1)}, bf16[384,768]{1,0:T(8,128)(2,1)}, u32[]{:S(2)}) copy-start(bf16[384,768]{1,0:T(8,128)(2,1)} %multiply_convert_fusion.1.refs_7_) | copy-start | bytes 1769476
  251.3 13.0 %collective-permute-start.7 = (bf16[8,768]{1,0:T(8,128)(2,1)}, bf16[8,768]{1,0:T(8,128)(2,1)}, u32[]{:S(2)}, u32[]{:S(2)}) collective-permute-start(bf16[8,768]{1,0:T(8,128)(2,1)} %get-tuple-element.25), channel_id=1, source_target_pairs={{4,0},{8,4},{12,8},{16,12},{20,16},{24,20},{28,24},{5,1},{9,5},{13... | collective-permute-start | bytes 36872 | tf_op jit(solution)/shard_map/ppermute | solution.py:20
  252.6 11.7 %collective-permute-start.6 = (bf16[8,768]{1,0:T(8,128)(2,1)}, bf16[8,768]{1,0:T(8,128)(2,1)}, u32[]{:S(2)}, u32[]{:S(2)}) collective-permute-start(bf16[8,768]{1,0:T(8,128)(2,1)} %get-tuple-element.24), channel_id=1, source_target_pairs={{0,4},{4,8},{8,12},{12,16},{16,20},{20,24},{24,28},{1,5},{5,9},{9,... | collective-permute-start | bytes 36872 | tf_op jit(solution)/shard_map/ppermute | solution.py:17
  (8 other events, 16.8 us)
Sparse Core Ops, SparseCore 0:
  11.5 136.7 all-gather.1
  250.8 206.3 reduce-scatter.1

commit v4 on v3

--- a/solution.py
+++ b/solution.py
@@ -146,26 +146,42 @@
     saved = []
     gathered, mixing_weights = fetch_weights(w_dilated, w_mix)
     c2 = w_dilated.shape[3]
-    stream = x_local.astype(jnp.float32)
+    remaining = sum(dilation_steps)
+    first_row = lax.axis_index("seq") * row_count
+    stream = padded_2(x_local, (("seq", 0),), remaining).astype(jnp.float32)
     for residual_block_index in range(residual_block_count):
         dilation = dilation_steps[residual_block_index]
         w_out = mixing_weights[residual_block_index]
         pre_in = stream * in_scale[residual_block_index] + in_shift[residual_block_index]
-        activated = gelu_value(pre_in).astype(jnp.bfloat16)
-        padded = padded_2(activated, (("seq", 0),), dilation)
+        position = first_row - remaining + lax.broadcasted_iota(jnp.int32, (pre_in.shape[0], 1), 0)
+        inside = (position >= 0) & (position < window_len)
+        activated = jnp.where(inside, gelu_value(pre_in), 0.0).astype(jnp.bfloat16)
+        out_rows = row_count + 2 * (remaining - dilation)
         pre_mid = conv_forward(
-            padded,
+            activated,
             gathered,
             residual_block_index,
             c2,
             mid_scale[residual_block_index],
             mid_shift[residual_block_index],
             dilation,
-            row_count,
+            out_rows,
         )
         middle = gelu_value(pre_mid).astype(jnp.bfloat16)
-        stream = stream + jnp.einsum("pe,ce->pc", middle, w_out, preferred_element_type=jnp.float32)
-        saved.append((w_out, pre_in, padded, pre_mid, middle))
+        stream = stream[dilation : dilation + out_rows] + jnp.einsum(
+            "pe,ce->pc", middle, w_out, preferred_element_type=jnp.float32
+        )
+        own = remaining - dilation
+        saved.append(
+            (
+                w_out,
+                pre_in[remaining : remaining + row_count],
+                activated[own : own + row_count + 2 * dilation],
+                pre_mid[own : own + row_count],
+                middle[own : own + row_count],
+            )
+        )
+        remaining -= dilation
     output = stream.astype(jnp.bfloat16)
     upstream_gradient = cot_local.astype(jnp.float32)
     dilated_weight_gradients = [None] * residual_block_count

time: 469 us -> 440 us (0.938)
  waiting for transfers between devices: 303 us -> 286 us
  starting transfers between devices: 27.6 us -> 19.2 us
  other arithmetic: 30.6 us -> 24.7 us
    ppermute x4 -> x3, waiting for transfers between devices: 11.1 us -> 1.71 us  [padded_2(): lax.ppermute(lax.slice_in_dim(block, 0, width, axis=dim), axis, backward)]
    ppermute x4 -> x3, starting transfers between devices: 22.3 us -> 15.1 us  [padded_2(): lax.ppermute(lax.slice_in_dim(block, block.shape[dim] - width, None, axis...]
    concatenate x4 -> x2, other arithmetic: 7.82 us -> 1.74 us  [padded_2(): block = jnp.concatenate([low, block, high], axis=dim)]
    transpose x2 -> x0, other arithmetic: 5.37 us -> none  [per_device(): dilated_weight_gradients[residual_block_index] = (padded.T, shifted_taps(...]
    concatenate x2 -> x0, local copies, waits for them, and re-layouts: 5.04 us -> none  [padded_2(): block = jnp.concatenate([low, block, high], axis=dim)]
    ppermute x4 -> x3, waiting for transfers between devices: 17.7 us -> 12.8 us  [padded_2(): lax.ppermute(lax.slice_in_dim(block, block.shape[dim] - width, None, axis...]
    unnamed x49 -> x41, local copies, waits for them, and re-layouts: 10.5 us -> 10.8 us
  transfers between devices with their start and end apart: 10 -> 8, of which waited for: 6 -> 4; matrix products, arithmetic and copies ran while one was open for 8% -> 8% of each run, Pallas kernels for 2% -> 2%
where the time goes in v4:
time: 440 us; the launch traced here: 439 us
  waiting for transfers between devices  286 us (65%)
  Pallas kernels  46.3 us (11%)
  local copies, waits for them, and re-layouts  29.1 us (7%)
  other arithmetic  24.7 us (6%)
  matrix products  19.3 us (4%)
  starting transfers between devices  19.2 us (4%)
  between operations  14.3 us (3%)
    reduce_scatter x1, waiting for transfers between devices, per_device(): lax.psum_scatter(weight_gradient_buffer(dilated_weight_gradients + mixing...  174 us
    all_gather x1, waiting for transfers between devices, fetch_weights(): gathered = lax.all_gather(local, ('seq', 'win'), axis=0, tiled=True)  97.7 us
    pallas_call x2, Pallas kernels, conv_backward(): pl.pallas_call(lambda *refs: conv_backward_kernel(dilation, out_rows, *re...  15.7 us
    pallas_call x1, Pallas kernels, weight_gradient_buffer(): pl.pallas_call(lambda *refs: gradient_kernel(inverse_square_root, widths,...  15.6 us
    ppermute x3, starting transfers between devices, padded_2(): lax.ppermute(lax.slice_in_dim(block, block.shape[dim] - width, None, axis...  15.1 us
    pallas_call x2, Pallas kernels, conv_forward(): pl.pallas_call(lambda *refs: conv_forward_kernel(dilation, out_rows, *ref...  14.9 us
    ppermute x3, waiting for transfers between devices, padded_2(): lax.ppermute(lax.slice_in_dim(block, block.shape[dim] - width, None, axis...  12.8 us
    dot_general x2, matrix products, per_device(): jnp.einsum('pe,ce->pc', middle, w_out, preferred_element_type=jnp.float32)  12.3 us
  transfers between devices with their start and end apart: 8, of which 4 were waited for; matrix products, arithmetic and copies ran while one was open for 8% of the time, Pallas kernels for 2%

profile of v4, /device:TPU:0, one launch (start us, length us, event | category | flops | bytes accessed | tf_op | source)
XLA Modules:
  0.0 439.1 jit_solution(4596906174267122340)
XLA Ops:
  12.5 5.5 %collective-permute-start = (bf16[24,1536]{0,1:T(8,128)(2,1)S(1)}, bf16[24,1536]{0,1:T(8,128)(2,1)S(1)}, u32[]{:S(2)}, u32[]{:S(2)}) collective-permute-start(bf16[24,1536]{0,1:T(8,128)(2,1)S(1)} %get-tuple-element.24), channel_id=1, source_target_pairs={{0,4},{4,8},{8,12},{12,16},{16,20},{20,24},{24,28},{1,5},{5,9},{9,... | collective-permute-start | bytes 221192 | tf_op jit(solution)/shard_map/ppermute | solution.py:17
  18.1 2.4 copy.39
  25.2 12.8 %collective-permute-done = bf16[24,1536]{0,1:T(8,128)(2,1)S(1)} collective-permute-done((bf16[24,1536]{0,1:T(8,128)(2,1)S(1)}, bf16[24,1536]{0,1:T(8,128)(2,1)S(1)}, u32[]{:S(2)}, u32[]{:S(2)}) %collective-permute-start) | collective-permute-done | bytes 73760 | tf_op jit(solution)/shard_map/ppermute | solution.py:17
  38.0 3.7 multiply_add_fusion.1
  43.1 2.5 maximum_convert_fusion
  45.6 1.9 slice_bitcast_fusion.refs_0_
  47.5 97.7 %all-gather.2.cloned.1.call-done.refs_1_ = bf16[1536,6144]{1,0:T(8,128)(2,1)} async-done(((bf16[48,6144]{1,0:T(8,128)(2,1)}), bf16[1536,6144]{1,0:T(8,128)(2,1)}) %all-gather.2.cloned.1.call-update) | async-done | bytes 18874384 | tf_op jit(solution)/shard_map/all_gather | solution.py:99
  145.2 7.6 %shard_map.111 = f32[416,768]{1,0:T(8,128)} custom-call(bf16[432,1536]{1,0:T(8,128)(2,1)} %copy.35.refs_0_, bf16[1536,6144]{1,0:T(8,128)(2,1)} %all-gather.2.cloned.1.call-done.refs_1_, f32[1,768]{1,0:T(1,128)} %get-tuple-element.31.refs_2_, f32[1,768]{1,0:T(1,128)} %get-tuple-element.33.refs_3_), custom_call_target="tpu_custom_call" | custom-call | tf_op jit(solution)/shard_map/pallas_call | solution.py:64
  154.5 7.8 %fusion.25 = (bf16[416,1536]{0,1:T(8,128)(2,1)S(1)}, f32[416,1536]{0,1:T(8,128)}, f32[416,1536]{0,1:T(8,128)}) fusion(pred[416]{0:T(512)(128)(4,1)S(1)} %copy-done.17, f32[1536]{0:T(1024)S(1)} %copy-done.12, f32[1536]{0:T(1024)S(1)} %get-tuple-element.36, bf16[416,768]{1,0:T(8,128)(2,1)S(1)} %fusion.73, ...), kind=kOutput, calls=%fused_computation.39 | convolution fusion | flops 989773824 | bytes 12546464 | tf_op jit(solution)/shard_map/pe,ce->pc/dot_general | solution.py:171
  163.9 7.3 %shard_map.112 = f32[384,768]{1,0:T(8,128)} custom-call(bf16[416,1536]{1,0:T(8,128)(2,1)} %copy.37.refs_0_, bf16[1536,6144]{1,0:T(8,128)(2,1)} %all-gather.2.cloned.1.call-done.refs_1_, f32[1,768]{1,0:T(1,128)} %get-tuple-element.30.refs_2_, f32[1,768]{1,0:T(1,128)} %get-tuple-element.32.refs_3_), custom_call_target="tpu_custom_call" | custom-call | tf_op jit(solution)/shard_map/pallas_call | solution.py:64
  171.2 3.6 fusion.81
  177.6 4.5 %collective-permute-start.2 = (bf16[16,768]{1,0:T(8,128)(2,1)S(1)}, bf16[16,768]{1,0:T(8,128)(2,1)S(1)}, u32[]{:S(2)}, u32[]{:S(2)}) collective-permute-start(bf16[16,768]{1,0:T(8,128)(2,1)S(1)} %get-tuple-element.28), channel_id=1, source_target_pairs={{0,4},{4,8},{8,12},{12,16},{16,20},{20,24},{24,28},{1,5},{5,9},{9,... | collective-permute-start | bytes 73736 | tf_op jit(solution)/shard_map/ppermute | solution.py:17
  185.1 7.6 %shard_map.113 = f32[384,1536]{1,0:T(8,128)} custom-call(bf16[416,768]{1,0:T(8,128)(2,1)} %pad_maximum_fusion.refs_0_, bf16[1536,6144]{1,0:T(8,128)(2,1)} %all-gather.2.cloned.1.call-done.refs_1_), custom_call_target="tpu_custom_call" | custom-call | tf_op jit(solution)/shard_map/pallas_call | solution.py:80
  192.6 2.1 copy.40
  194.8 4.8 %convert_bitcast_fusion = (bf16[1536,384]{1,0:T(8,128)(2,1)}, f32[384,1536]{0,1:T(8,128)S(1)}) fusion(f32[1536]{0:T(1024)S(1)} %get-tuple-element.36, f32[384,1536]{0,1:T(8,128)S(1)} %copy.40, f32[416,1536]{0,1:T(8,128)} %get-tuple-element.21, bf16[1,384,1536]{1,2,0:T(8,128)(2,1)S(1)} %copy-done), kind=kLoop, calls=%fused_computation.112 | loop fusion | flops 13565952 | bytes 9443328 | tf_op jit(solution)/shard_map/transpose | solution.py:200
  201.0 3.4 fusion.89
  205.8 15.6 %shard_map.115 = bf16[1536,6144]{1,0:T(8,128)(2,1)} custom-call(bf16[1536,400]{1,0:T(8,128)(2,1)} %slice_bitcast_fusion.refs_0_, bf16[400,2304]{1,0:T(8,128)(2,1)} %fusion.62.refs_1_, bf16[1536,416]{1,0:T(8,128)(2,1)} %bitcast.50, bf16[416,2304]{1,0:T(8,128)(2,1)} %fusion.60.refs_3_, bf16[1536,384]{1,0:T(8,128)(2,1)} %get-tuple-element.18.refs_4_, ...), custom_call_target="tpu_custom_call" | custom-call | tf_op jit(solution)/shard_map/pallas_call | solution.py:130
  222.9 5.1 %collective-permute-start.4 = (bf16[8,768]{1,0:T(8,128)(2,1)S(1)}, bf16[8,768]{1,0:T(8,128)(2,1)S(1)}, u32[]{:S(2)}, u32[]{:S(2)}) collective-permute-start(bf16[8,768]{1,0:T(8,128)(2,1)S(1)} %get-tuple-element.26), channel_id=1, source_target_pairs={{0,4},{4,8},{8,12},{12,16},{16,20},{20,24},{24,28},{1,5},{5,9},{9,... | collective-permute-start | bytes 36872 | tf_op jit(solution)/shard_map/ppermute | solution.py:17
  228.0 4.5 %fusion.50 = bf16[1,384,1536]{1,2,0:T(8,128)(2,1)S(1)} fusion(bf16[384,768]{1,0:T(8,128)(2,1)S(1)} %copy-done.7, bf16[1536,6144]{1,0:T(8,128)(2,1)} %all-gather.2.cloned.1.call-done.refs_1_, f32[416,1536]{0,1:T(8,128)} %get-tuple-element.34), kind=kOutput, calls=%fused_computation.66 | convolution fusion | flops 907149312 | bytes 6488064 | tf_op jit(solution)/shard_map/pe,ce->pc/dot_general | solution.py:171
  234.9 8.2 %shard_map.114 = f32[384,1536]{1,0:T(8,128)} custom-call(bf16[400,768]{1,0:T(8,128)(2,1)} %pad_maximum_fusion.1.refs_0_, bf16[1536,6144]{1,0:T(8,128)(2,1)} %all-gather.2.cloned.1.call-done.refs_1_), custom_call_target="tpu_custom_call" | custom-call | tf_op jit(solution)/shard_map/pallas_call | solution.py:80
  243.1 3.3 copy.42
  246.7 4.8 %fusion.42 = f32[1,384,1536]{1,2,0:T(8,128)} fusion(f32[384,1536]{0,1:T(8,128)} %copy-done.2, f32[384,1536]{0,1:T(8,128)} %copy.42, f32[432,1536]{0,1:T(8,128)S(1)} %copy-done.1, f32[1536]{0:T(1024)S(1)} %get-tuple-element.35), kind=kLoop, calls=%fused_computation.59 | loop fusion | flops 12386304 | bytes 9443328 | tf_op jit(solution)/shard_map/broadcast_in_dim | solution.py:215
  251.5 3.2 copy.46
  254.8 173.8 %reduce-scatter.2.cloned.1.call-done = bf16[48,6144]{1,0:T(8,128)(2,1)} async-done(((bf16[1536,6144]{1,0:T(8,128)(2,1)}), bf16[48,6144]{1,0:T(8,128)(2,1)}) %reduce-scatter.2.cloned.1.call-update) | async-done | bytes 589840 | tf_op jit(solution)/shard_map/reduce_scatter | solution.py:204
  (76 shorter events, 31.0 us)
Async XLA Ops:
  7.2 3.1 copy-start.8
  7.2 138.0 %all-gather.2.cloned.1.call-start = ((), (), s32[]{:S(2)}) async-start(), calls=%async_computation.1 | async-start | bytes 19464192 | tf_op jit(solution)/shard_map/all_gather | solution.py:99
  10.2 418.4 %reduce-scatter.2.cloned.1.call-start = ((), (), s32[]{:S(2)}) async-start(), calls=%async_computation.2 | async-start | bytes 19464192 | tf_op jit(solution)/shard_map/reduce_scatter | solution.py:204
  11.0 10.1 %copy-start.10 = (f32[2,1536]{1,0:T(2,128)S(1)}, f32[2,1536]{1,0:T(2,128)}, u32[]{:S(2)}) copy-start(f32[2,1536]{1,0:T(2,128)} %param.13) | copy-start | bytes 36868
  11.0 10.0 %copy-start.11 = (f32[2,1536]{1,0:T(2,128)S(1)}, f32[2,1536]{1,0:T(2,128)}, u32[]{:S(2)}) copy-start(f32[2,1536]{1,0:T(2,128)} %param.12) | copy-start | bytes 36868
  11.0 10.7 %copy-start.14 = (f32[2,768]{1,0:T(2,128)S(1)}, f32[2,768]{1,0:T(2,128)}, u32[]{:S(2)}) copy-start(f32[2,768]{1,0:T(2,128)} %param.14) | copy-start | bytes 18436
  11.0 11.9 %copy-start.13 = (f32[2,768]{1,0:T(2,128)S(1)}, f32[2,768]{1,0:T(2,128)}, u32[]{:S(2)}) copy-start(f32[2,768]{1,0:T(2,128)} %param.15) | copy-start | bytes 18436
  11.2 14.0 %collective-permute-start.1 = (bf16[24,1536]{0,1:T(8,128)(2,1)S(1)}, bf16[24,1536]{0,1:T(8,128)(2,1)S(1)}, u32[]{:S(2)}, u32[]{:S(2)}) collective-permute-start(bf16[24,1536]{0,1:T(8,128)(2,1)S(1)} %get-tuple-element.25), channel_id=1, source_target_pairs={{4,0},{8,4},{12,8},{16,12},{20,16},{24,20},{28,24},{5,1},{9,5},{13... | collective-permute-start | bytes 221192 | tf_op jit(solution)/shard_map/ppermute | solution.py:20
  12.5 25.4 %collective-permute-start = (bf16[24,1536]{0,1:T(8,128)(2,1)S(1)}, bf16[24,1536]{0,1:T(8,128)(2,1)S(1)}, u32[]{:S(2)}, u32[]{:S(2)}) collective-permute-start(bf16[24,1536]{0,1:T(8,128)(2,1)S(1)} %get-tuple-element.24), channel_id=1, source_target_pairs={{0,4},{4,8},{8,12},{12,16},{16,20},{20,24},{24,28},{1,5},{5,9},{9,... | collective-permute-start | bytes 221192 | tf_op jit(solution)/shard_map/ppermute | solution.py:17
  145.2 9.3 %copy-start.12 = (f32[1536]{0:T(1024)S(1)}, f32[1536]{0:T(1024)}, u32[]{:S(2)}) copy-start(f32[1536]{0:T(1024)} %get-tuple-element.14) | copy-start | bytes 18436
  145.2 9.3 %copy-start.17 = (pred[416]{0:T(512)(128)(4,1)S(1)}, pred[416]{0:T(512)(128)(4,1)}, u32[]{:S(2)}) copy-start(pred[416]{0:T(512)(128)(4,1)} %fusion.103) | copy-start | bytes 1252
  162.3 8.9 %copy-start.3 = (bf16[416,1536]{0,1:T(8,128)(2,1)}, bf16[416,1536]{0,1:T(8,128)(2,1)S(1)}, u32[]{:S(2)}) copy-start(bf16[416,1536]{0,1:T(8,128)(2,1)S(1)} %get-tuple-element.20) | copy-start | bytes 3833860
  163.9 7.3 %copy-start.9 = (bf16[1,384,1536]{2,1,0:T(8,128)(2,1)S(1)}, bf16[1,384,1536]{2,1,0:T(8,128)(2,1)}, u32[]{:S(2)}) copy-start(bf16[1,384,1536]{2,1,0:T(8,128)(2,1)} %param.9) | copy-start | bytes 3538948
  163.9 7.3 %copy-start.16 = (f32[768]{0:T(1024)S(1)}, f32[768]{0:T(1024)}, u32[]{:S(2)}) copy-start(f32[768]{0:T(1024)} %get-tuple-element.17) | copy-start | bytes 9220
  174.8 7.3 %copy-start.5 = (f32[384,768]{1,0:T(8,128)S(1)}, f32[384,768]{1,0:T(8,128)}, u32[]{:S(2)}) copy-start(f32[384,768]{1,0:T(8,128)} %shard_map.112) | copy-start | bytes 3538948
  176.3 7.9 %collective-permute-start.3 = (bf16[16,768]{1,0:T(8,128)(2,1)S(1)}, bf16[16,768]{1,0:T(8,128)(2,1)S(1)}, u32[]{:S(2)}, u32[]{:S(2)}) collective-permute-start(bf16[16,768]{1,0:T(8,128)(2,1)S(1)} %get-tuple-element.29), channel_id=1, source_target_pairs={{4,0},{8,4},{12,8},{16,12},{20,16},{24,20},{28,24},{5,1},{9,5},{13... | collective-permute-start | bytes 73736 | tf_op jit(solution)/shard_map/ppermute | solution.py:20
  177.6 6.6 %collective-permute-start.2 = (bf16[16,768]{1,0:T(8,128)(2,1)S(1)}, bf16[16,768]{1,0:T(8,128)(2,1)S(1)}, u32[]{:S(2)}, u32[]{:S(2)}) collective-permute-start(bf16[16,768]{1,0:T(8,128)(2,1)S(1)} %get-tuple-element.28), channel_id=1, source_target_pairs={{0,4},{4,8},{8,12},{12,16},{16,20},{20,24},{24,28},{1,5},{5,9},{9,... | collective-permute-start | bytes 73736 | tf_op jit(solution)/shard_map/ppermute | solution.py:17
  192.6 2.1 copy-start
  194.8 6.2 %copy-start.4 = (f32[416,768]{1,0:T(8,128)S(1)}, f32[416,768]{1,0:T(8,128)}, u32[]{:S(2)}) copy-start(f32[416,768]{1,0:T(8,128)} %shard_map.111) | copy-start | bytes 3833860
  194.8 6.2 %copy-start.15 = (f32[768]{0:T(1024)S(1)}, f32[768]{0:T(1024)}, u32[]{:S(2)}) copy-start(f32[768]{0:T(1024)} %get-tuple-element.16) | copy-start | bytes 9220
  221.5 6.6 %copy-start.7 = (bf16[384,768]{1,0:T(8,128)(2,1)S(1)}, bf16[384,768]{1,0:T(8,128)(2,1)}, u32[]{:S(2)}) copy-start(bf16[384,768]{1,0:T(8,128)(2,1)} %multiply_convert_fusion.refs_7_) | copy-start | bytes 1769476
  221.5 12.5 %collective-permute-start.5 = (bf16[8,768]{1,0:T(8,128)(2,1)S(1)}, bf16[8,768]{1,0:T(8,128)(2,1)S(1)}, u32[]{:S(2)}, u32[]{:S(2)}) collective-permute-start(bf16[8,768]{1,0:T(8,128)(2,1)S(1)} %get-tuple-element.27), channel_id=1, source_target_pairs={{4,0},{8,4},{12,8},{16,12},{20,16},{24,20},{28,24},{5,1},{9,5},{13... | collective-permute-start | bytes 36872 | tf_op jit(solution)/shard_map/ppermute | solution.py:20
  222.9 11.1 %collective-permute-start.4 = (bf16[8,768]{1,0:T(8,128)(2,1)S(1)}, bf16[8,768]{1,0:T(8,128)(2,1)S(1)}, u32[]{:S(2)}, u32[]{:S(2)}) collective-permute-start(bf16[8,768]{1,0:T(8,128)(2,1)S(1)} %get-tuple-element.26), channel_id=1, source_target_pairs={{0,4},{4,8},{8,12},{12,16},{16,20},{20,24},{24,28},{1,5},{5,9},{9,... | collective-permute-start | bytes 36872 | tf_op jit(solution)/shard_map/ppermute | solution.py:17
  243.1 3.6 copy-start.1
  (2 other events, 3.3 us)
Sparse Core Ops, SparseCore 0:
  11.5 133.6 all-gather.1
  221.6 206.9 reduce-scatter.1

commit v5 on v4

--- a/solution.py
+++ b/solution.py
@@ -89,6 +89,49 @@
     )(d_pad, gathered)
 
 
+def mix_forward_kernel(dilation, middle_ref, w_ref, stream_ref, out_ref):
+    rows = out_ref.shape[0]
+    mixed = lax.dot_general(
+        middle_ref[...], w_ref[...], (((1,), (1,)), ((), ())), preferred_element_type=jnp.float32
+    )
+    out_ref[...] = stream_ref[dilation : dilation + rows, :] + mixed
+
+
+def mix_forward(middle, gathered, column_block, stream, dilation):
+    rows, c2 = middle.shape
+    channels = gathered.shape[0]
+    return pl.pallas_call(
+        lambda *refs: mix_forward_kernel(dilation, *refs),
+        grid=(1,),
+        in_specs=[
+            pl.BlockSpec(middle.shape, lambda i: (0, 0)),
+            pl.BlockSpec((channels, c2), lambda i: (0, column_block)),
+            pl.BlockSpec(stream.shape, lambda i: (0, 0)),
+        ],
+        out_specs=pl.BlockSpec((rows, channels), lambda i: (0, 0)),
+        out_shape=jax.ShapeDtypeStruct((rows, channels), jnp.float32),
+    )(middle, gathered, stream)
+
+
+def mix_backward_kernel(cot_ref, w_ref, out_ref):
+    out_ref[...] = jnp.dot(cot_ref[...], w_ref[...], preferred_element_type=jnp.float32)
+
+
+def mix_backward(cot_here, gathered, column_block, c2):
+    rows = cot_here.shape[0]
+    channels = gathered.shape[0]
+    return pl.pallas_call(
+        mix_backward_kernel,
+        grid=(1,),
+        in_specs=[
+            pl.BlockSpec(cot_here.shape, lambda i: (0, 0)),
+            pl.BlockSpec((channels, c2), lambda i: (0, column_block)),
+        ],
+        out_specs=pl.BlockSpec((rows, c2), lambda i: (0, 0)),
+        out_shape=jax.ShapeDtypeStruct((rows, c2), jnp.float32),
+    )(cot_here, gathered)
+
+
 def fetch_weights(w_dilated, w_mix):
     blocks, rows, taps, c2 = w_dilated.shape
     local = jnp.concatenate(
@@ -146,6 +189,7 @@
     saved = []
     gathered, mixing_weights = fetch_weights(w_dilated, w_mix)
     c2 = w_dilated.shape[3]
+    mix_column = residual_block_count * w_dilated.shape[2]
     remaining = sum(dilation_steps)
     first_row = lax.axis_index("seq") * row_count
     stream = padded_2(x_local, (("seq", 0),), remaining).astype(jnp.float32)
@@ -168,9 +212,7 @@
             out_rows,
         )
         middle = gelu_value(pre_mid).astype(jnp.bfloat16)
-        stream = stream[dilation : dilation + out_rows] + jnp.einsum(
-            "pe,ce->pc", middle, w_out, preferred_element_type=jnp.float32
-        )
+        stream = mix_forward(middle, gathered, mix_column + residual_block_index, stream, dilation)
         own = remaining - dilation
         saved.append(
             (
@@ -190,7 +232,7 @@
         dilation = dilation_steps[residual_block_index]
         w_out, pre_in, padded, pre_mid, middle = saved[residual_block_index]
         cot_here = upstream_gradient.astype(jnp.bfloat16)
-        d_mid = jnp.dot(cot_here, w_out, preferred_element_type=jnp.float32)
+        d_mid = mix_backward(cot_here, gathered, mix_column + residual_block_index, c2)
         d_hidden = (gelu_back(pre_mid, d_mid) * mid_scale[residual_block_index]).astype(
             jnp.bfloat16
         )

time: 440 us -> 454 us (1.032)
  matrix products: 19.3 us -> 0 us
  Pallas kernels: 46.3 us -> 65.2 us
  other arithmetic: 24.7 us -> 37 us
  local copies, waits for them, and re-layouts: 29.1 us -> 38.6 us
  waiting for transfers between devices: 286 us -> 279 us
    dot_general x4 -> x0, matrix products: 19.3 us -> none  [the longest x2 12.3 us: per_device(): jnp.einsum('pe,ce->pc', middle, w_out, preferred_element_type=jnp.float32)]
    pallas_call x0 -> x4, Pallas kernels: none -> 18.9 us  [the longest x2 10.5 us: mix_forward(): pl.pallas_call(lambda *refs: mix_forward_kernel(dilation, *refs), grid=(1...]
    convert_element_type x0 -> x4, other arithmetic: none -> 14.4 us  [the longest x1 5.25 us: per_device(): cot_here = upstream_gradient.astype(jnp.bfloat16)]
    convert_element_type x0 -> x2, local copies, waits for them, and re-layouts: none -> 4.9 us  [the longest x1 3.46 us: per_device(): stream = padded_2(x_local, (('seq', 0),), remaining).astype(jnp.float32)]
    transpose x1 -> x0, other arithmetic: 4.79 us -> none  [per_device(): mixing_weight_gradients[residual_block_index] = (cot_here.T, middle)]
    unnamed x41 -> x32, local copies, waits for them, and re-layouts: 10.8 us -> 7.66 us
  transfers between devices with their start and end apart: 8 -> 8, of which waited for: 4 -> 4; matrix products, arithmetic and copies ran while one was open for 8% -> 9% of each run, Pallas kernels for 2% -> 3%
where the time goes in v5:
time: 454 us; the launch traced here: 453 us
  waiting for transfers between devices  279 us (61%)
  Pallas kernels  65.2 us (14%)
  local copies, waits for them, and re-layouts  38.6 us (9%)
  other arithmetic  37 us (8%)
  starting transfers between devices  19 us (4%)
  between operations  14.2 us (3%)
    reduce_scatter x1, waiting for transfers between devices, per_device(): lax.psum_scatter(weight_gradient_buffer(dilated_weight_gradients + mixing...  172 us
    all_gather x1, waiting for transfers between devices, fetch_weights(): gathered = lax.all_gather(local, ('seq', 'win'), axis=0, tiled=True)  94.2 us
    pallas_call x2, Pallas kernels, conv_backward(): pl.pallas_call(lambda *refs: conv_backward_kernel(dilation, out_rows, *re...  15.7 us
    pallas_call x1, Pallas kernels, weight_gradient_buffer(): pl.pallas_call(lambda *refs: gradient_kernel(inverse_square_root, widths,...  15.6 us
    ppermute x3, starting transfers between devices, padded_2(): lax.ppermute(lax.slice_in_dim(block, block.shape[dim] - width, None, axis...  15.1 us
    pallas_call x2, Pallas kernels, conv_forward(): pl.pallas_call(lambda *refs: conv_forward_kernel(dilation, out_rows, *ref...  15 us
    ppermute x3, waiting for transfers between devices, padded_2(): lax.ppermute(lax.slice_in_dim(block, block.shape[dim] - width, None, axis...  11.9 us
    pallas_call x2, Pallas kernels, mix_forward(): pl.pallas_call(lambda *refs: mix_forward_kernel(dilation, *refs), grid=(1...  10.5 us
  transfers between devices with their start and end apart: 8, of which 4 were waited for; matrix products, arithmetic and copies ran while one was open for 9% of the time, Pallas kernels for 3%

profile of v5, /device:TPU:0, one launch (start us, length us, event | category | flops | bytes accessed | tf_op | source)
XLA Modules:
  0.0 453.4 jit_solution(13694116384075123743)
XLA Ops:
  13.2 5.5 %collective-permute-start = (bf16[24,1536]{0,1:T(8,128)(2,1)S(1)}, bf16[24,1536]{0,1:T(8,128)(2,1)S(1)}, u32[]{:S(2)}, u32[]{:S(2)}) collective-permute-start(bf16[24,1536]{0,1:T(8,128)(2,1)S(1)} %get-tuple-element.26), channel_id=1, source_target_pairs={{0,4},{4,8},{8,12},{12,16},{16,20},{20,24},{24,28},{1,5},{5,9},{9,... | collective-permute-start | bytes 221192 | tf_op jit(solution)/shard_map/ppermute | solution.py:17
  27.0 11.9 %collective-permute-done = bf16[24,1536]{0,1:T(8,128)(2,1)S(1)} collective-permute-done((bf16[24,1536]{0,1:T(8,128)(2,1)S(1)}, bf16[24,1536]{0,1:T(8,128)(2,1)S(1)}, u32[]{:S(2)}, u32[]{:S(2)}) %collective-permute-start) | collective-permute-done | bytes 73760 | tf_op jit(solution)/shard_map/ppermute | solution.py:17
  38.9 3.7 multiply_add_fusion.1
  46.5 3.5 copy.37.refs_2_
  51.8 94.2 %all-gather.2.cloned.1.call-done.refs_1_.w_ref = bf16[1536,6144]{1,0:T(8,128)(2,1)} async-done(((bf16[48,6144]{1,0:T(8,128)(2,1)}), bf16[1536,6144]{1,0:T(8,128)(2,1)}) %all-gather.2.cloned.1.call-update) | async-done | bytes 18874384 | tf_op jit(solution)/shard_map/all_gather | solution.py:142
  146.0 7.7 %shard_map.111 = f32[416,768]{1,0:T(8,128)} custom-call(bf16[432,1536]{1,0:T(8,128)(2,1)} %copy.36.refs_0_, bf16[1536,6144]{1,0:T(8,128)(2,1)} %all-gather.2.cloned.1.call-done.refs_1_.w_ref, f32[1,768]{1,0:T(1,128)} %get-tuple-element.33.refs_2_, f32[1,768]{1,0:T(1,128)} %get-tuple-element.35.refs_3_), custom_call_target="tpu_custom_call" | custom-call | tf_op jit(solution)/shard_map/pallas_call | solution.py:64
  156.2 5.3 %shard_map.112.refs_2_ = f32[416,1536]{1,0:T(8,128)} custom-call(bf16[416,768]{1,0:T(8,128)(2,1)} %fusion.54.refs_0_, bf16[1536,6144]{1,0:T(8,128)(2,1)} %all-gather.2.cloned.1.call-done.refs_1_.w_ref, f32[432,1536]{1,0:T(8,128)} %copy.37.refs_2_), custom_call_target="tpu_custom_call" | custom-call | tf_op jit(solution)/shard_map/pallas_call | solution.py:103
  161.5 3.5 copy.38
  165.0 4.1 fusion.25
  170.6 4.2 shard_map.115
  174.8 7.3 %shard_map.113 = f32[384,768]{1,0:T(8,128)} custom-call(bf16[416,1536]{1,0:T(8,128)(2,1)} %copy.39.refs_0_, bf16[1536,6144]{1,0:T(8,128)(2,1)} %all-gather.2.cloned.1.call-done.refs_1_.w_ref, f32[1,768]{1,0:T(1,128)} %get-tuple-element.32.refs_2_, f32[1,768]{1,0:T(1,128)} %get-tuple-element.34.refs_3_), custom_call_target="tpu_custom_call" | custom-call | tf_op jit(solution)/shard_map/pallas_call | solution.py:64
  186.5 4.5 %collective-permute-start.2 = (bf16[16,768]{1,0:T(8,128)(2,1)S(1)}, bf16[16,768]{1,0:T(8,128)(2,1)S(1)}, u32[]{:S(2)}, u32[]{:S(2)}) collective-permute-start(bf16[16,768]{1,0:T(8,128)(2,1)S(1)} %get-tuple-element.30), channel_id=1, source_target_pairs={{0,4},{4,8},{8,12},{12,16},{16,20},{20,24},{24,28},{1,5},{5,9},{9,... | collective-permute-start | bytes 73736 | tf_op jit(solution)/shard_map/ppermute | solution.py:17
  194.3 7.6 %shard_map.116 = f32[384,1536]{1,0:T(8,128)} custom-call(bf16[416,768]{1,0:T(8,128)(2,1)} %pad_maximum_fusion.refs_0_, bf16[1536,6144]{1,0:T(8,128)(2,1)} %all-gather.2.cloned.1.call-done.refs_1_.w_ref), custom_call_target="tpu_custom_call" | custom-call | tf_op jit(solution)/shard_map/pallas_call | solution.py:80
  201.9 3.2 copy.42
  205.0 5.2 %fusion.77 = (bf16[384,1536]{0,1:T(8,128)(2,1)S(1)}, f32[384,1536]{0,1:T(8,128)}) fusion(f32[1536]{0:T(1024)S(1)} %get-tuple-element.37, f32[384,1536]{0,1:T(8,128)} %copy.42, f32[416,1536]{0,1:T(8,128)} %get-tuple-element.21, bf16[1,384,1536]{1,2,0:T(8,128)(2,1)S(1)} %copy-done.2), kind=kLoop, calls=%fused_computation.116 | loop fusion | flops 13565952 | bytes 9443328 | tf_op jit(solution)/shard_map/convert_element_type | solution.py:234
  212.8 4.2 shard_map.117
  220.4 15.6 %shard_map.119 = bf16[1536,6144]{1,0:T(8,128)(2,1)} custom-call(bf16[1536,400]{1,0:T(8,128)(2,1)} %slice_bitcast_fusion.refs_0_, bf16[400,2304]{1,0:T(8,128)(2,1)} %fusion.46.refs_1_, bf16[1536,416]{1,0:T(8,128)(2,1)} %bitcast.38, bf16[416,2304]{1,0:T(8,128)(2,1)} %fusion.44.refs_3_, bf16[1536,384]{1,0:T(8,128)(2,1)} %bitcast.40, ...), custom_call_target="tpu_custom_call" | custom-call | tf_op jit(solution)/shard_map/pallas_call | solution.py:173
  236.1 5.1 %shard_map.114 = f32[384,1536]{1,0:T(8,128)} custom-call(bf16[384,768]{1,0:T(8,128)(2,1)} %get-tuple-element.25.refs_0_.refs_7_, bf16[1536,6144]{1,0:T(8,128)(2,1)} %all-gather.2.cloned.1.call-done.refs_1_.w_ref, f32[416,1536]{1,0:T(8,128)} %shard_map.112.refs_2_), custom_call_target="tpu_custom_call" | custom-call | tf_op jit(solution)/shard_map/pallas_call | solution.py:103
  242.5 5.1 %collective-permute-start.4 = (bf16[8,768]{1,0:T(8,128)(2,1)S(1)}, bf16[8,768]{1,0:T(8,128)(2,1)S(1)}, u32[]{:S(2)}, u32[]{:S(2)}) collective-permute-start(bf16[8,768]{1,0:T(8,128)(2,1)S(1)} %get-tuple-element.28), channel_id=1, source_target_pairs={{0,4},{4,8},{8,12},{12,16},{16,20},{20,24},{24,28},{1,5},{5,9},{9,... | collective-permute-start | bytes 36872 | tf_op jit(solution)/shard_map/ppermute | solution.py:17
  251.5 8.2 %shard_map.118 = f32[384,1536]{1,0:T(8,128)} custom-call(bf16[400,768]{1,0:T(8,128)(2,1)} %pad_maximum_fusion.1.refs_0_, bf16[1536,6144]{1,0:T(8,128)(2,1)} %all-gather.2.cloned.1.call-done.refs_1_.w_ref), custom_call_target="tpu_custom_call" | custom-call | tf_op jit(solution)/shard_map/pallas_call | solution.py:80
  259.6 3.3 copy.45
  263.0 4.9 %fusion.42 = f32[1,384,1536]{1,2,0:T(8,128)} fusion(f32[384,1536]{0,1:T(8,128)} %get-tuple-element.19, f32[384,1536]{0,1:T(8,128)} %copy.45, f32[432,1536]{0,1:T(8,128)S(1)} %copy-done.4, f32[1536]{0:T(1024)S(1)} %get-tuple-element.36), kind=kLoop, calls=%fused_computation.58 | loop fusion | flops 12386304 | bytes 9443328 | tf_op jit(solution)/shard_map/broadcast_in_dim | solution.py:257
  267.9 3.2 copy.48
  271.1 171.8 %reduce-scatter.2.cloned.1.call-done = bf16[48,6144]{1,0:T(8,128)(2,1)} async-done(((bf16[1536,6144]{1,0:T(8,128)(2,1)}), bf16[48,6144]{1,0:T(8,128)(2,1)}) %reduce-scatter.2.cloned.1.call-update) | async-done | bytes 589840 | tf_op jit(solution)/shard_map/reduce_scatter | solution.py:246
  (73 shorter events, 46.7 us)
Async XLA Ops:
  7.2 3.1 copy-start.9
  7.2 138.8 %all-gather.2.cloned.1.call-start = ((), (), s32[]{:S(2)}) async-start(), calls=%async_computation.1 | async-start | bytes 19464192 | tf_op jit(solution)/shard_map/all_gather | solution.py:142
  10.2 8.6 %copy-start.6 = (bf16[1,384,1536]{2,1,0:T(8,128)(2,1)S(1)}, bf16[1,384,1536]{2,1,0:T(8,128)(2,1)}, u32[]{:S(2)}) copy-start(bf16[1,384,1536]{2,1,0:T(8,128)(2,1)} %param.9) | copy-start | bytes 3538948
  10.2 432.7 %reduce-scatter.2.cloned.1.call-start = ((), (), s32[]{:S(2)}) async-start(), calls=%async_computation.2 | async-start | bytes 19464192 | tf_op jit(solution)/shard_map/reduce_scatter | solution.py:246
  11.9 15.1 %collective-permute-start.1 = (bf16[24,1536]{0,1:T(8,128)(2,1)}, bf16[24,1536]{0,1:T(8,128)(2,1)S(1)}, u32[]{:S(2)}, u32[]{:S(2)}) collective-permute-start(bf16[24,1536]{0,1:T(8,128)(2,1)} %get-tuple-element.27), channel_id=1, source_target_pairs={{4,0},{8,4},{12,8},{16,12},{20,16},{24,20},{28,24},{5,1},{9,5},{13... | collective-permute-start | bytes 221192 | tf_op jit(solution)/shard_map/ppermute | solution.py:20
  13.2 25.7 %collective-permute-start = (bf16[24,1536]{0,1:T(8,128)(2,1)S(1)}, bf16[24,1536]{0,1:T(8,128)(2,1)S(1)}, u32[]{:S(2)}, u32[]{:S(2)}) collective-permute-start(bf16[24,1536]{0,1:T(8,128)(2,1)S(1)} %get-tuple-element.26), channel_id=1, source_target_pairs={{0,4},{4,8},{8,12},{12,16},{16,20},{20,24},{24,28},{1,5},{5,9},{9,... | collective-permute-start | bytes 221192 | tf_op jit(solution)/shard_map/ppermute | solution.py:17
  161.5 3.5 copy-start.10
  161.5 3.5 copy-start.13
  169.1 5.7 %copy-start = (bf16[416,1536]{0,1:T(8,128)(2,1)}, bf16[416,1536]{0,1:T(8,128)(2,1)S(1)}, u32[]{:S(2)}) copy-start(bf16[416,1536]{0,1:T(8,128)(2,1)S(1)} %get-tuple-element.20) | copy-start | bytes 3833860
  174.8 7.3 %copy-start.7 = (f32[384,768]{1,0:T(8,128)S(1)}, f32[384,768]{1,0:T(8,128)}, u32[]{:S(2)}) copy-start(f32[384,768]{1,0:T(8,128)} %shard_map.115) | copy-start | bytes 3538948
  174.8 7.3 %copy-start.12 = (f32[768]{0:T(1024)S(1)}, f32[768]{0:T(1024)}, u32[]{:S(2)}) copy-start(f32[768]{0:T(1024)} %get-tuple-element.17) | copy-start | bytes 9220
  182.1 10.4 %copy-start.5 = (bf16[416,768]{1,0:T(8,128)(2,1)S(1)}, bf16[416,768]{1,0:T(8,128)(2,1)}, u32[]{:S(2)}) copy-start(bf16[416,768]{1,0:T(8,128)(2,1)} %fusion.54.refs_0_) | copy-start | bytes 1916932
  185.2 8.2 %collective-permute-start.3 = (bf16[16,768]{1,0:T(8,128)(2,1)S(1)}, bf16[16,768]{1,0:T(8,128)(2,1)S(1)}, u32[]{:S(2)}, u32[]{:S(2)}) collective-permute-start(bf16[16,768]{1,0:T(8,128)(2,1)S(1)} %get-tuple-element.31), channel_id=1, source_target_pairs={{4,0},{8,4},{12,8},{16,12},{20,16},{24,20},{28,24},{5,1},{9,5},{13... | collective-permute-start | bytes 73736 | tf_op jit(solution)/shard_map/ppermute | solution.py:20
  186.5 7.0 %collective-permute-start.2 = (bf16[16,768]{1,0:T(8,128)(2,1)S(1)}, bf16[16,768]{1,0:T(8,128)(2,1)S(1)}, u32[]{:S(2)}, u32[]{:S(2)}) collective-permute-start(bf16[16,768]{1,0:T(8,128)(2,1)S(1)} %get-tuple-element.30), channel_id=1, source_target_pairs={{0,4},{4,8},{8,12},{12,16},{16,20},{20,24},{24,28},{1,5},{5,9},{9,... | collective-permute-start | bytes 73736 | tf_op jit(solution)/shard_map/ppermute | solution.py:17
  201.9 3.2 copy-start.2
  210.3 1.0 copy-start.3
  212.8 4.2 copy-start.1
  212.8 4.2 copy-start.11
  241.2 9.4 %collective-permute-start.5 = (bf16[8,768]{1,0:T(8,128)(2,1)S(1)}, bf16[8,768]{1,0:T(8,128)(2,1)S(1)}, u32[]{:S(2)}, u32[]{:S(2)}) collective-permute-start(bf16[8,768]{1,0:T(8,128)(2,1)S(1)} %get-tuple-element.29), channel_id=1, source_target_pairs={{4,0},{8,4},{12,8},{16,12},{20,16},{24,20},{28,24},{5,1},{9,5},{13... | collective-permute-start | bytes 36872 | tf_op jit(solution)/shard_map/ppermute | solution.py:20
  242.5 8.1 %collective-permute-start.4 = (bf16[8,768]{1,0:T(8,128)(2,1)S(1)}, bf16[8,768]{1,0:T(8,128)(2,1)S(1)}, u32[]{:S(2)}, u32[]{:S(2)}) collective-permute-start(bf16[8,768]{1,0:T(8,128)(2,1)S(1)} %get-tuple-element.28), channel_id=1, source_target_pairs={{0,4},{4,8},{8,12},{12,16},{16,20},{20,24},{24,28},{1,5},{5,9},{9,... | collective-permute-start | bytes 36872 | tf_op jit(solution)/shard_map/ppermute | solution.py:17
  259.6 3.4 copy-start.4
  444.0 1.9 copy-start.8
Sparse Core Ops, SparseCore 0:
  11.5 134.4 all-gather.1
  236.2 206.6 reduce-scatter.1

commit v6 on v4

--- a/solution.py
+++ b/solution.py
@@ -31,46 +31,55 @@
 
 
 def conv_forward_kernel(dilation, out_rows, act_ref, w_ref, scale_ref, shift_ref, out_ref):
-    width = out_ref.shape[1]
-    hidden = jnp.dot(act_ref[0:out_rows, :], w_ref[:, 0:width], preferred_element_type=jnp.float32)
-    for kernel_tap in (1, 2):
-        lower = kernel_tap * dilation
-        hidden = hidden + jnp.dot(
-            act_ref[lower : lower + out_rows, :],
-            w_ref[:, kernel_tap * width : (kernel_tap + 1) * width],
-            preferred_element_type=jnp.float32,
-        )
-    out_ref[...] = hidden * scale_ref[...] + shift_ref[...]
+    tap = pl.program_id(0)
+    for kernel_tap in range(3):
+
+        @pl.when(tap == kernel_tap)
+        def _():
+            lower = kernel_tap * dilation
+            term = jnp.dot(
+                act_ref[lower : lower + out_rows, :], w_ref[...], preferred_element_type=jnp.float32
+            )
+            if kernel_tap == 0:
+                out_ref[...] = term
+            elif kernel_tap == 1:
+                out_ref[...] = out_ref[...] + term
+            else:
+                out_ref[...] = (out_ref[...] + term) * scale_ref[...] + shift_ref[...]
 
 
 def conv_backward_kernel(dilation, out_rows, grad_ref, w_ref, out_ref):
-    width = grad_ref.shape[1]
+    tap = pl.program_id(0)
     numbers = (((1,), (1,)), ((), ()))
-    total = None
     for kernel_tap in range(3):
-        lower = (2 - kernel_tap) * dilation
-        term = lax.dot_general(
-            grad_ref[lower : lower + out_rows, :],
-            w_ref[:, kernel_tap * width : (kernel_tap + 1) * width],
-            numbers,
-            preferred_element_type=jnp.float32,
-        )
-        total = term if total is None else total + term
-    out_ref[...] = total
+
+        @pl.when(tap == kernel_tap)
+        def _():
+            lower = (2 - kernel_tap) * dilation
+            term = lax.dot_general(
+                grad_ref[lower : lower + out_rows, :],
+                w_ref[...],
+                numbers,
+                preferred_element_type=jnp.float32,
+            )
+            if kernel_tap == 0:
+                out_ref[...] = term
+            else:
+                out_ref[...] = out_ref[...] + term
 
 
 def conv_forward(padded, gathered, block, c2, scale, shift, dilation, out_rows):
     rows = gathered.shape[0]
     return pl.pallas_call(
         lambda *refs: conv_forward_kernel(dilation, out_rows, *refs),
-        grid=(1,),
+        grid=(3,),
         in_specs=[
-            pl.BlockSpec(padded.shape, lambda i: (0, 0)),
-            pl.BlockSpec((rows, 3 * c2), lambda i: (0, block)),
-            pl.BlockSpec((1, c2), lambda i: (0, 0)),
-            pl.BlockSpec((1, c2), lambda i: (0, 0)),
+            pl.BlockSpec(padded.shape, lambda k: (0, 0)),
+            pl.BlockSpec((rows, c2), lambda k: (0, 3 * block + k)),
+            pl.BlockSpec((1, c2), lambda k: (0, 0)),
+            pl.BlockSpec((1, c2), lambda k: (0, 0)),
         ],
-        out_specs=pl.BlockSpec((out_rows, c2), lambda i: (0, 0)),
+        out_specs=pl.BlockSpec((out_rows, c2), lambda k: (0, 0)),
         out_shape=jax.ShapeDtypeStruct((out_rows, c2), jnp.float32),
     )(padded, gathered, scale.reshape(1, c2), shift.reshape(1, c2))
 
@@ -79,12 +88,12 @@
     rows = gathered.shape[0]
     return pl.pallas_call(
         lambda *refs: conv_backward_kernel(dilation, out_rows, *refs),
-        grid=(1,),
+        grid=(3,),
         in_specs=[
-            pl.BlockSpec(d_pad.shape, lambda i: (0, 0)),
-            pl.BlockSpec((rows, 3 * c2), lambda i: (0, block)),
+            pl.BlockSpec(d_pad.shape, lambda k: (0, 0)),
+            pl.BlockSpec((rows, c2), lambda k: (0, 3 * block + k)),
         ],
-        out_specs=pl.BlockSpec((out_rows, rows), lambda i: (0, 0)),
+        out_specs=pl.BlockSpec((out_rows, rows), lambda k: (0, 0)),
         out_shape=jax.ShapeDtypeStruct((out_rows, rows), jnp.float32),
     )(d_pad, gathered)
 

time: 440 us -> 439 us (level)
  no operation moved by 1% of the time
where the time goes in v6:
time: 439 us; the launch traced here: 438 us
  waiting for transfers between devices  287 us (65%)
  Pallas kernels  44.5 us (10%)
  local copies, waits for them, and re-layouts  29.2 us (7%)
  other arithmetic  24.8 us (6%)
  matrix products  19.3 us (4%)
  starting transfers between devices  19 us (4%)
  between operations  14.3 us (3%)
    reduce_scatter x1, waiting for transfers between devices, per_device(): lax.psum_scatter(weight_gradient_buffer(dilated_weight_gradients + mixing...  175 us
    all_gather x1, waiting for transfers between devices, fetch_weights(): gathered = lax.all_gather(local, ('seq', 'win'), axis=0, tiled=True)  97.7 us
    pallas_call x1, Pallas kernels, weight_gradient_buffer(): pl.pallas_call(lambda *refs: gradient_kernel(inverse_square_root, widths,...  15.6 us
    ppermute x3, starting transfers between devices, padded_2(): lax.ppermute(lax.slice_in_dim(block, block.shape[dim] - width, None, axis...  14.9 us
    pallas_call x2, Pallas kernels, conv_backward(): pl.pallas_call(lambda *refs: conv_backward_kernel(dilation, out_rows, *re...  14.7 us
    pallas_call x2, Pallas kernels, conv_forward(): pl.pallas_call(lambda *refs: conv_forward_kernel(dilation, out_rows, *ref...  14.1 us
    ppermute x3, waiting for transfers between devices, padded_2(): lax.ppermute(lax.slice_in_dim(block, block.shape[dim] - width, None, axis...  12.8 us
    dot_general x2, matrix products, per_device(): jnp.einsum('pe,ce->pc', middle, w_out, preferred_element_type=jnp.float32)  12.3 us
  transfers between devices with their start and end apart: 8, of which 4 were waited for; matrix products, arithmetic and copies ran while one was open for 8% of the time, Pallas kernels for 2%

profile of v6, /device:TPU:0, one launch (start us, length us, event | category | flops | bytes accessed | tf_op | source)
XLA Modules:
  0.0 437.9 jit_solution(17995318725759528748)
XLA Ops:
  12.5 5.5 %collective-permute-start = (bf16[24,1536]{0,1:T(8,128)(2,1)S(1)}, bf16[24,1536]{0,1:T(8,128)(2,1)S(1)}, u32[]{:S(2)}, u32[]{:S(2)}) collective-permute-start(bf16[24,1536]{0,1:T(8,128)(2,1)S(1)} %get-tuple-element.24), channel_id=1, source_target_pairs={{0,4},{4,8},{8,12},{12,16},{16,20},{20,24},{24,28},{1,5},{5,9},{9,... | collective-permute-start | bytes 221192 | tf_op jit(solution)/shard_map/ppermute | solution.py:17
  18.1 2.4 copy.39
  25.2 12.8 %collective-permute-done = bf16[24,1536]{0,1:T(8,128)(2,1)S(1)} collective-permute-done((bf16[24,1536]{0,1:T(8,128)(2,1)S(1)}, bf16[24,1536]{0,1:T(8,128)(2,1)S(1)}, u32[]{:S(2)}, u32[]{:S(2)}) %collective-permute-start) | collective-permute-done | bytes 73760 | tf_op jit(solution)/shard_map/ppermute | solution.py:17
  38.0 3.7 multiply_add_fusion.1
  43.1 2.5 maximum_convert_fusion
  45.6 1.9 slice_bitcast_fusion.refs_0_
  47.5 97.7 %all-gather.2.cloned.1.call-done.refs_1_ = bf16[1536,6144]{1,0:T(8,128)(2,1)} async-done(((bf16[48,6144]{1,0:T(8,128)(2,1)}), bf16[1536,6144]{1,0:T(8,128)(2,1)}) %all-gather.2.cloned.1.call-update) | async-done | bytes 18874384 | tf_op jit(solution)/shard_map/all_gather | solution.py:108
  145.2 7.2 %shard_map.111 = f32[416,768]{1,0:T(8,128)} custom-call(bf16[432,1536]{1,0:T(8,128)(2,1)} %copy.35.refs_0_, bf16[1536,6144]{1,0:T(8,128)(2,1)} %all-gather.2.cloned.1.call-done.refs_1_, f32[1,768]{1,0:T(1,128)} %get-tuple-element.31.refs_2_, f32[1,768]{1,0:T(1,128)} %get-tuple-element.33.refs_3_), custom_call_target="tpu_custom_call" | custom-call | tf_op jit(solution)/shard_map/pallas_call | solution.py:73
  154.1 7.8 %fusion.25 = (bf16[416,1536]{0,1:T(8,128)(2,1)S(1)}, f32[416,1536]{0,1:T(8,128)}, f32[416,1536]{0,1:T(8,128)}) fusion(pred[416]{0:T(512)(128)(4,1)S(1)} %copy-done.17, f32[1536]{0:T(1024)S(1)} %copy-done.12, f32[1536]{0:T(1024)S(1)} %get-tuple-element.36, bf16[416,768]{1,0:T(8,128)(2,1)S(1)} %fusion.73, ...), kind=kOutput, calls=%fused_computation.39 | convolution fusion | flops 989773824 | bytes 12546464 | tf_op jit(solution)/shard_map/pe,ce->pc/dot_general | solution.py:180
  163.4 7.0 %shard_map.112 = f32[384,768]{1,0:T(8,128)} custom-call(bf16[416,1536]{1,0:T(8,128)(2,1)} %copy.37.refs_0_, bf16[1536,6144]{1,0:T(8,128)(2,1)} %all-gather.2.cloned.1.call-done.refs_1_, f32[1,768]{1,0:T(1,128)} %get-tuple-element.30.refs_2_, f32[1,768]{1,0:T(1,128)} %get-tuple-element.32.refs_3_), custom_call_target="tpu_custom_call" | custom-call | tf_op jit(solution)/shard_map/pallas_call | solution.py:73
  170.4 3.6 fusion.81
  176.8 4.5 %collective-permute-start.2 = (bf16[16,768]{1,0:T(8,128)(2,1)S(1)}, bf16[16,768]{1,0:T(8,128)(2,1)S(1)}, u32[]{:S(2)}, u32[]{:S(2)}) collective-permute-start(bf16[16,768]{1,0:T(8,128)(2,1)S(1)} %get-tuple-element.28), channel_id=1, source_target_pairs={{0,4},{4,8},{8,12},{12,16},{16,20},{20,24},{24,28},{1,5},{5,9},{9,... | collective-permute-start | bytes 73736 | tf_op jit(solution)/shard_map/ppermute | solution.py:17
  184.3 7.1 %shard_map.113 = f32[384,1536]{1,0:T(8,128)} custom-call(bf16[416,768]{1,0:T(8,128)(2,1)} %pad_maximum_fusion.refs_0_, bf16[1536,6144]{1,0:T(8,128)(2,1)} %all-gather.2.cloned.1.call-done.refs_1_), custom_call_target="tpu_custom_call" | custom-call | tf_op jit(solution)/shard_map/pallas_call | solution.py:89
  191.4 2.1 copy.40
  193.6 4.8 %convert_bitcast_fusion = (bf16[1536,384]{1,0:T(8,128)(2,1)}, f32[384,1536]{0,1:T(8,128)S(1)}) fusion(f32[1536]{0:T(1024)S(1)} %get-tuple-element.36, f32[384,1536]{0,1:T(8,128)S(1)} %copy.40, f32[416,1536]{0,1:T(8,128)} %get-tuple-element.21, bf16[1,384,1536]{1,2,0:T(8,128)(2,1)S(1)} %copy-done), kind=kLoop, calls=%fused_computation.112 | loop fusion | flops 13565952 | bytes 9443328 | tf_op jit(solution)/shard_map/transpose | solution.py:209
  199.8 3.4 fusion.89
  204.6 15.6 %shard_map.115 = bf16[1536,6144]{1,0:T(8,128)(2,1)} custom-call(bf16[1536,400]{1,0:T(8,128)(2,1)} %slice_bitcast_fusion.refs_0_, bf16[400,2304]{1,0:T(8,128)(2,1)} %fusion.62.refs_1_, bf16[1536,416]{1,0:T(8,128)(2,1)} %bitcast.50, bf16[416,2304]{1,0:T(8,128)(2,1)} %fusion.60.refs_3_, bf16[1536,384]{1,0:T(8,128)(2,1)} %get-tuple-element.18.refs_4_, ...), custom_call_target="tpu_custom_call" | custom-call | tf_op jit(solution)/shard_map/pallas_call | solution.py:139
  221.7 4.9 %collective-permute-start.4 = (bf16[8,768]{1,0:T(8,128)(2,1)S(1)}, bf16[8,768]{1,0:T(8,128)(2,1)S(1)}, u32[]{:S(2)}, u32[]{:S(2)}) collective-permute-start(bf16[8,768]{1,0:T(8,128)(2,1)S(1)} %get-tuple-element.26), channel_id=1, source_target_pairs={{0,4},{4,8},{8,12},{12,16},{16,20},{20,24},{24,28},{1,5},{5,9},{9,... | collective-permute-start | bytes 36872 | tf_op jit(solution)/shard_map/ppermute | solution.py:17
  226.6 4.5 %fusion.50 = bf16[1,384,1536]{1,2,0:T(8,128)(2,1)S(1)} fusion(bf16[384,768]{1,0:T(8,128)(2,1)S(1)} %copy-done.7, bf16[1536,6144]{1,0:T(8,128)(2,1)} %all-gather.2.cloned.1.call-done.refs_1_, f32[416,1536]{0,1:T(8,128)} %get-tuple-element.34), kind=kOutput, calls=%fused_computation.66 | convolution fusion | flops 907149312 | bytes 6488064 | tf_op jit(solution)/shard_map/pe,ce->pc/dot_general | solution.py:180
  233.7 7.6 %shard_map.114 = f32[384,1536]{1,0:T(8,128)} custom-call(bf16[400,768]{1,0:T(8,128)(2,1)} %pad_maximum_fusion.1.refs_0_, bf16[1536,6144]{1,0:T(8,128)(2,1)} %all-gather.2.cloned.1.call-done.refs_1_), custom_call_target="tpu_custom_call" | custom-call | tf_op jit(solution)/shard_map/pallas_call | solution.py:89
  241.2 3.3 copy.42
  244.8 4.9 %fusion.42 = f32[1,384,1536]{1,2,0:T(8,128)} fusion(f32[384,1536]{0,1:T(8,128)} %copy-done.2, f32[384,1536]{0,1:T(8,128)} %copy.42, f32[432,1536]{0,1:T(8,128)S(1)} %copy-done.1, f32[1536]{0:T(1024)S(1)} %get-tuple-element.35), kind=kLoop, calls=%fused_computation.59 | loop fusion | flops 12386304 | bytes 9443328 | tf_op jit(solution)/shard_map/broadcast_in_dim | solution.py:224
  249.6 3.2 copy.46
  252.8 174.6 %reduce-scatter.2.cloned.1.call-done = bf16[48,6144]{1,0:T(8,128)(2,1)} async-done(((bf16[1536,6144]{1,0:T(8,128)(2,1)}), bf16[48,6144]{1,0:T(8,128)(2,1)}) %reduce-scatter.2.cloned.1.call-update) | async-done | bytes 589840 | tf_op jit(solution)/shard_map/reduce_scatter | solution.py:213
  (76 shorter events, 31.1 us)
Async XLA Ops:
  7.2 3.1 copy-start.8
  7.2 138.0 %all-gather.2.cloned.1.call-start = ((), (), s32[]{:S(2)}) async-start(), calls=%async_computation.1 | async-start | bytes 19464192 | tf_op jit(solution)/shard_map/all_gather | solution.py:108
  10.2 417.2 %reduce-scatter.2.cloned.1.call-start = ((), (), s32[]{:S(2)}) async-start(), calls=%async_computation.2 | async-start | bytes 19464192 | tf_op jit(solution)/shard_map/reduce_scatter | solution.py:213
  11.0 10.1 %copy-start.10 = (f32[2,1536]{1,0:T(2,128)S(1)}, f32[2,1536]{1,0:T(2,128)}, u32[]{:S(2)}) copy-start(f32[2,1536]{1,0:T(2,128)} %param.13) | copy-start | bytes 36868
  11.0 10.0 %copy-start.11 = (f32[2,1536]{1,0:T(2,128)S(1)}, f32[2,1536]{1,0:T(2,128)}, u32[]{:S(2)}) copy-start(f32[2,1536]{1,0:T(2,128)} %param.12) | copy-start | bytes 36868
  11.0 10.7 %copy-start.14 = (f32[2,768]{1,0:T(2,128)S(1)}, f32[2,768]{1,0:T(2,128)}, u32[]{:S(2)}) copy-start(f32[2,768]{1,0:T(2,128)} %param.14) | copy-start | bytes 18436
  11.0 11.9 %copy-start.13 = (f32[2,768]{1,0:T(2,128)S(1)}, f32[2,768]{1,0:T(2,128)}, u32[]{:S(2)}) copy-start(f32[2,768]{1,0:T(2,128)} %param.15) | copy-start | bytes 18436
  11.2 14.0 %collective-permute-start.1 = (bf16[24,1536]{0,1:T(8,128)(2,1)S(1)}, bf16[24,1536]{0,1:T(8,128)(2,1)S(1)}, u32[]{:S(2)}, u32[]{:S(2)}) collective-permute-start(bf16[24,1536]{0,1:T(8,128)(2,1)S(1)} %get-tuple-element.25), channel_id=1, source_target_pairs={{4,0},{8,4},{12,8},{16,12},{20,16},{24,20},{28,24},{5,1},{9,5},{13... | collective-permute-start | bytes 221192 | tf_op jit(solution)/shard_map/ppermute | solution.py:20
  12.5 25.4 %collective-permute-start = (bf16[24,1536]{0,1:T(8,128)(2,1)S(1)}, bf16[24,1536]{0,1:T(8,128)(2,1)S(1)}, u32[]{:S(2)}, u32[]{:S(2)}) collective-permute-start(bf16[24,1536]{0,1:T(8,128)(2,1)S(1)} %get-tuple-element.24), channel_id=1, source_target_pairs={{0,4},{4,8},{8,12},{12,16},{16,20},{20,24},{24,28},{1,5},{5,9},{9,... | collective-permute-start | bytes 221192 | tf_op jit(solution)/shard_map/ppermute | solution.py:17
  145.2 8.9 %copy-start.12 = (f32[1536]{0:T(1024)S(1)}, f32[1536]{0:T(1024)}, u32[]{:S(2)}) copy-start(f32[1536]{0:T(1024)} %get-tuple-element.14) | copy-start | bytes 18436
  145.2 8.9 %copy-start.17 = (pred[416]{0:T(512)(128)(4,1)S(1)}, pred[416]{0:T(512)(128)(4,1)}, u32[]{:S(2)}) copy-start(pred[416]{0:T(512)(128)(4,1)} %fusion.103) | copy-start | bytes 1252
  161.9 8.6 %copy-start.3 = (bf16[416,1536]{0,1:T(8,128)(2,1)}, bf16[416,1536]{0,1:T(8,128)(2,1)S(1)}, u32[]{:S(2)}) copy-start(bf16[416,1536]{0,1:T(8,128)(2,1)S(1)} %get-tuple-element.20) | copy-start | bytes 3833860
  163.4 7.0 %copy-start.9 = (bf16[1,384,1536]{2,1,0:T(8,128)(2,1)S(1)}, bf16[1,384,1536]{2,1,0:T(8,128)(2,1)}, u32[]{:S(2)}) copy-start(bf16[1,384,1536]{2,1,0:T(8,128)(2,1)} %param.9) | copy-start | bytes 3538948
  163.4 7.0 %copy-start.16 = (f32[768]{0:T(1024)S(1)}, f32[768]{0:T(1024)}, u32[]{:S(2)}) copy-start(f32[768]{0:T(1024)} %get-tuple-element.17) | copy-start | bytes 9220
  174.0 7.3 %copy-start.5 = (f32[384,768]{1,0:T(8,128)S(1)}, f32[384,768]{1,0:T(8,128)}, u32[]{:S(2)}) copy-start(f32[384,768]{1,0:T(8,128)} %shard_map.112) | copy-start | bytes 3538948
  175.5 7.9 %collective-permute-start.3 = (bf16[16,768]{1,0:T(8,128)(2,1)S(1)}, bf16[16,768]{1,0:T(8,128)(2,1)S(1)}, u32[]{:S(2)}, u32[]{:S(2)}) collective-permute-start(bf16[16,768]{1,0:T(8,128)(2,1)S(1)} %get-tuple-element.29), channel_id=1, source_target_pairs={{4,0},{8,4},{12,8},{16,12},{20,16},{24,20},{28,24},{5,1},{9,5},{13... | collective-permute-start | bytes 73736 | tf_op jit(solution)/shard_map/ppermute | solution.py:20
  176.8 6.6 %collective-permute-start.2 = (bf16[16,768]{1,0:T(8,128)(2,1)S(1)}, bf16[16,768]{1,0:T(8,128)(2,1)S(1)}, u32[]{:S(2)}, u32[]{:S(2)}) collective-permute-start(bf16[16,768]{1,0:T(8,128)(2,1)S(1)} %get-tuple-element.28), channel_id=1, source_target_pairs={{0,4},{4,8},{8,12},{12,16},{16,20},{20,24},{24,28},{1,5},{5,9},{9,... | collective-permute-start | bytes 73736 | tf_op jit(solution)/shard_map/ppermute | solution.py:17
  191.4 2.1 copy-start
  193.6 6.2 %copy-start.4 = (f32[416,768]{1,0:T(8,128)S(1)}, f32[416,768]{1,0:T(8,128)}, u32[]{:S(2)}) copy-start(f32[416,768]{1,0:T(8,128)} %shard_map.111) | copy-start | bytes 3833860
  193.6 6.2 %copy-start.15 = (f32[768]{0:T(1024)S(1)}, f32[768]{0:T(1024)}, u32[]{:S(2)}) copy-start(f32[768]{0:T(1024)} %get-tuple-element.16) | copy-start | bytes 9220
  220.3 6.3 %copy-start.7 = (bf16[384,768]{1,0:T(8,128)(2,1)S(1)}, bf16[384,768]{1,0:T(8,128)(2,1)}, u32[]{:S(2)}) copy-start(bf16[384,768]{1,0:T(8,128)(2,1)} %multiply_convert_fusion.refs_7_) | copy-start | bytes 1769476
  220.3 12.5 %collective-permute-start.5 = (bf16[8,768]{1,0:T(8,128)(2,1)S(1)}, bf16[8,768]{1,0:T(8,128)(2,1)S(1)}, u32[]{:S(2)}, u32[]{:S(2)}) collective-permute-start(bf16[8,768]{1,0:T(8,128)(2,1)S(1)} %get-tuple-element.27), channel_id=1, source_target_pairs={{4,0},{8,4},{12,8},{16,12},{20,16},{24,20},{28,24},{5,1},{9,5},{13... | collective-permute-start | bytes 36872 | tf_op jit(solution)/shard_map/ppermute | solution.py:20
  221.7 11.1 %collective-permute-start.4 = (bf16[8,768]{1,0:T(8,128)(2,1)S(1)}, bf16[8,768]{1,0:T(8,128)(2,1)S(1)}, u32[]{:S(2)}, u32[]{:S(2)}) collective-permute-start(bf16[8,768]{1,0:T(8,128)(2,1)S(1)} %get-tuple-element.26), channel_id=1, source_target_pairs={{0,4},{4,8},{8,12},{12,16},{16,20},{20,24},{24,28},{1,5},{5,9},{9,... | collective-permute-start | bytes 36872 | tf_op jit(solution)/shard_map/ppermute | solution.py:17
  241.2 3.5 copy-start.1
  (2 other events, 3.3 us)
Sparse Core Ops, SparseCore 0:
  11.5 133.6 all-gather.1
  220.4 206.9 reduce-scatter.1

commit v7 on v6

--- a/solution.py
+++ b/solution.py
@@ -116,33 +116,44 @@
     )
 
 
-def gradient_kernel(scale, widths, *refs):
-    out_ref = refs[-1]
-    start = 0
-    for pair in range(len(widths)):
+def gradient_kernel(scale, layout, count, *refs):
+    out_refs = refs[2 * count :]
+    for pair, (target, start, width) in enumerate(layout):
         lhs = refs[2 * pair][...]
         rhs = refs[2 * pair + 1][...]
         term = jnp.dot(lhs, rhs, preferred_element_type=jnp.float32) * scale
-        out_ref[:, start : start + widths[pair]] = term.astype(out_ref.dtype)
-        start += widths[pair]
-
-
-def weight_gradient_buffer(pairs, inverse_square_root, row_tile=256):
-    rows = pairs[0][0].shape[0]
-    widths = tuple(rhs.shape[1] for _, rhs in pairs)
+        out_refs[target][:, start : start + width] = term.astype(out_refs[target].dtype)
+
+
+def weight_gradient_buffers(groups, inverse_square_root, row_tile=256):
+    rows = groups[0][0][0].shape[0]
+    layout = []
     in_specs = []
     operands = []
-    for lhs, rhs in pairs:
-        in_specs.append(pl.BlockSpec((row_tile, lhs.shape[1]), lambda i: (i, 0)))
-        in_specs.append(pl.BlockSpec(rhs.shape, lambda i: (0, 0)))
-        operands += [lhs, rhs]
+    widths = []
+    for target, group in enumerate(groups):
+        start = 0
+        for lhs, rhs in group:
+            layout.append((target, start, rhs.shape[1]))
+            start += rhs.shape[1]
+            in_specs.append(pl.BlockSpec((row_tile, lhs.shape[1]), lambda i: (i, 0)))
+            in_specs.append(pl.BlockSpec(rhs.shape, lambda i: (0, 0)))
+            operands += [lhs, rhs]
+        widths.append(start)
     return pl.pallas_call(
-        lambda *refs: gradient_kernel(inverse_square_root, widths, *refs),
+        lambda *refs: gradient_kernel(inverse_square_root, tuple(layout), len(layout), *refs),
         grid=(rows // row_tile,),
         in_specs=in_specs,
-        out_specs=pl.BlockSpec((row_tile, sum(widths)), lambda i: (i, 0)),
-        out_shape=jax.ShapeDtypeStruct((rows, sum(widths)), jnp.bfloat16),
+        out_specs=[pl.BlockSpec((row_tile, w), lambda i: (i, 0)) for w in widths],
+        out_shape=[jax.ShapeDtypeStruct((rows, w), jnp.bfloat16) for w in widths],
     )(*operands)
+
+
+def scatter_by_exchange(buffer, axes):
+    count = lax.axis_size(axes)
+    pieces = buffer.reshape(count, buffer.shape[0] // count, buffer.shape[1])
+    received = lax.all_to_all(pieces, axes, 0, 0, tiled=False)
+    return jnp.sum(received.astype(jnp.float32), axis=0)
 
 
 def per_device(inputs, cotangent, w_dilated, w_mix, in_scale, in_shift, mid_scale, mid_shift):
@@ -210,20 +221,29 @@
         upstream_gradient = (
             upstream_gradient + gelu_back(pre_in, d_act) * in_scale[residual_block_index]
         )
-    summed = lax.psum_scatter(
-        weight_gradient_buffer(dilated_weight_gradients + mixing_weight_gradients, inverse_square_root),
-        ("seq", "win"),
-        scatter_dimension=0,
-        tiled=True,
+    first, second = weight_gradient_buffers(
+        [
+            [dilated_weight_gradients[0]] + mixing_weight_gradients,
+            dilated_weight_gradients[1:],
+        ],
+        inverse_square_root,
+    )
+    summed_first = lax.psum_scatter(
+        first, ("seq", "win"), scatter_dimension=0, tiled=True
     ).astype(jnp.float32)
-    own_rows = summed.shape[0]
+    summed_second = scatter_by_exchange(second, ("seq", "win"))
+    own_rows = summed_first.shape[0]
     taps, c2 = w_dilated.shape[2], w_dilated.shape[3]
-    split = residual_block_count * taps * c2
+    width = taps * c2
+    dilated = jnp.stack(
+        [summed_first[:, :width], summed_second[:, :width]]
+    ).reshape(residual_block_count, own_rows, taps, c2)
+    mixing = summed_first[:, width:].reshape(own_rows, residual_block_count, c2).transpose(1, 0, 2)
     return (
         output[None],
         upstream_gradient[None],
-        summed[:, :split].reshape(own_rows, residual_block_count, taps, c2).transpose(1, 0, 2, 3),
-        summed[:, split:].reshape(own_rows, residual_block_count, c2).transpose(1, 0, 2),
+        dilated,
+        mixing,
     )
 
 

time: 439 us -> 471 us (1.073)
  the two profiles are of different devices: /device:TPU:0 before, /device:TPU:21 now
where the time goes in v7:
time: 471 us
  waiting for transfers between devices  314 us (67%)
  Pallas kernels  43.4 us (9%)
  other arithmetic  29 us (6%)
  local copies, waits for them, and re-layouts  28.4 us (6%)
  starting transfers between devices  22.4 us (5%)
  matrix products  19.2 us (4%)
  between operations  14.4 us (3%)
    ppermute x3, waiting for transfers between devices, padded_2(): lax.ppermute(lax.slice_in_dim(block, 0, width, axis=dim), axis, backward)  209 us
    all_gather x1, waiting for transfers between devices, fetch_weights(): gathered = lax.all_gather(local, ('seq', 'win'), axis=0, tiled=True)  96.8 us
    pallas_call x1, Pallas kernels, weight_gradient_buffers(): pl.pallas_call(lambda *refs: gradient_kernel(inverse_square_root, tuple(l...  15 us
    pallas_call x2, Pallas kernels, conv_backward(): pl.pallas_call(lambda *refs: conv_backward_kernel(dilation, out_rows, *re...  14.3 us
    pallas_call x2, Pallas kernels, conv_forward(): pl.pallas_call(lambda *refs: conv_forward_kernel(dilation, out_rows, *ref...  14.1 us
    dot_general x2, matrix products, per_device(): jnp.einsum('pe,ce->pc', middle, w_out, preferred_element_type=jnp.float32)  12.1 us
    unnamed x41, local copies, waits for them, and re-layouts  10.4 us
  transfers between devices with their start and end apart: 9, of which 5 were waited for; matrix products, arithmetic and copies ran while one was open for 9% of the time, Pallas kernels for 2%

profile of v7, /device:TPU:21, one launch (start us, length us, event | category | flops | bytes accessed | tf_op | source)
XLA Modules:
  0.0 470.6 jit_solution(8496698960586937609)
XLA Ops:
  11.2 3.0 collective-permute-start.1
  22.0 12.7 %collective-permute-done.1 = bf16[24,1536]{0,1:T(8,128)(2,1)S(1)} collective-permute-done((bf16[24,1536]{0,1:T(8,128)(2,1)S(1)}, bf16[24,1536]{0,1:T(8,128)(2,1)S(1)}, u32[]{:S(2)}, u32[]{:S(2)}) %collective-permute-start.1) | collective-permute-done | bytes 73760 | tf_op jit(solution)/shard_map/ppermute | solution.py:20
  36.7 3.7 multiply_add_fusion.1
  41.9 2.5 maximum_convert_fusion
  46.3 96.8 %all-gather.2.cloned.1.call-done.refs_1_ = bf16[1536,6144]{1,0:T(8,128)(2,1)} async-done(((bf16[48,6144]{1,0:T(8,128)(2,1)}), bf16[1536,6144]{1,0:T(8,128)(2,1)}) %all-gather.2.cloned.1.call-update) | async-done | bytes 18874384 | tf_op jit(solution)/shard_map/all_gather | solution.py:108
  143.1 7.1 %shard_map.111 = f32[416,768]{1,0:T(8,128)} custom-call(bf16[432,1536]{1,0:T(8,128)(2,1)} %copy.35.refs_0_, bf16[1536,6144]{1,0:T(8,128)(2,1)} %all-gather.2.cloned.1.call-done.refs_1_, f32[1,768]{1,0:T(1,128)} %get-tuple-element.35.refs_2_, f32[1,768]{1,0:T(1,128)} %get-tuple-element.37.refs_3_), custom_call_target="tpu_custom_call" | custom-call | tf_op jit(solution)/shard_map/pallas_call | solution.py:73
  151.9 7.8 %fusion.25 = (bf16[416,1536]{0,1:T(8,128)(2,1)S(1)}, f32[416,1536]{0,1:T(8,128)}, f32[416,1536]{0,1:T(8,128)}) fusion(pred[416]{0:T(512)(128)(4,1)S(1)} %copy-done.17, f32[1536]{0:T(1024)S(1)} %copy-done.12, f32[1536]{0:T(1024)S(1)} %get-tuple-element.40, bf16[416,768]{1,0:T(8,128)(2,1)S(1)} %fusion.73, ...), kind=kOutput, calls=%fused_computation.40 | convolution fusion | flops 989773824 | bytes 12546464 | tf_op jit(solution)/shard_map/pe,ce->pc/dot_general | solution.py:191
  161.3 7.0 %shard_map.112 = f32[384,768]{1,0:T(8,128)} custom-call(bf16[416,1536]{1,0:T(8,128)(2,1)} %copy.37.refs_0_, bf16[1536,6144]{1,0:T(8,128)(2,1)} %all-gather.2.cloned.1.call-done.refs_1_, f32[1,768]{1,0:T(1,128)} %get-tuple-element.34.refs_2_, f32[1,768]{1,0:T(1,128)} %get-tuple-element.36.refs_3_), custom_call_target="tpu_custom_call" | custom-call | tf_op jit(solution)/shard_map/pallas_call | solution.py:73
  168.3 3.6 fusion.81
  175.3 3.4 collective-permute-start.2
  181.6 7.1 %shard_map.113 = f32[384,1536]{1,0:T(8,128)} custom-call(bf16[416,768]{1,0:T(8,128)(2,1)} %pad_maximum_fusion.1.refs_0_, bf16[1536,6144]{1,0:T(8,128)(2,1)} %all-gather.2.cloned.1.call-done.refs_1_), custom_call_target="tpu_custom_call" | custom-call | tf_op jit(solution)/shard_map/pallas_call | solution.py:89
  190.9 4.8 %convert_bitcast_fusion = (bf16[1536,384]{1,0:T(8,128)(2,1)}, f32[384,1536]{0,1:T(8,128)S(1)}) fusion(f32[1536]{0:T(1024)S(1)} %get-tuple-element.40, f32[384,1536]{0,1:T(8,128)S(1)} %copy.40, f32[416,1536]{0,1:T(8,128)} %get-tuple-element.25, bf16[1,384,1536]{1,2,0:T(8,128)(2,1)S(1)} %copy-done), kind=kLoop, calls=%fused_computation.114 | loop fusion | flops 13565952 | bytes 9443328 | tf_op jit(solution)/shard_map/transpose | solution.py:220
  197.1 3.4 fusion.89
  201.9 15.0 %shard_map.115 = (bf16[1536,3840]{1,0:T(8,128)(2,1)}, bf16[1536,2304]{1,0:T(8,128)(2,1)}) custom-call(bf16[1536,400]{1,0:T(8,128)(2,1)} %slice_bitcast_fusion.refs_0_, bf16[400,2304]{1,0:T(8,128)(2,1)} %fusion.62.refs_1_, bf16[1536,384]{1,0:T(8,128)(2,1)} %get-tuple-element.22.refs_2_, bf16[384,768]{1,0:T(8,128)(2,1)} %slice.126.refs_3_, ...), custom_call_target="tpu_custom_call" | custom-call | tf_op jit(solution)/shard_map/pallas_call | solution.py:143
  216.9 6.5 %all-to-all-start = ((bf16[32,48,2304]{2,1,0:T(8,128)(2,1)}), bf16[32,48,2304]{2,1,0:T(8,128)(2,1)}, u32[]{:S(2)}, u32[]{:S(2)}) async-start(bf16[32,48,2304]{2,1,0:T(8,128)(2,1)} %bitcast.50), calls=%async_computation.1 | async-start | bytes 14155776 | tf_op jit(solution)/shard_map/all_to_all | solution.py:155
  223.4 3.1 collective-permute-start.5
  228.7 4.4 fusion.50
  234.8 196.0 %collective-permute-done.5 = bf16[8,768]{1,0:T(8,128)(2,1)S(1)} collective-permute-done((bf16[8,768]{1,0:T(8,128)(2,1)S(1)}, bf16[8,768]{1,0:T(8,128)(2,1)S(1)}, u32[]{:S(2)}, u32[]{:S(2)}) %collective-permute-start.5) | collective-permute-done | bytes 12320 | tf_op jit(solution)/shard_map/ppermute | solution.py:20
  430.8 6.2 %collective-permute-done.4 = bf16[8,768]{1,0:T(8,128)(2,1)S(1)} collective-permute-done((bf16[8,768]{1,0:T(8,128)(2,1)S(1)}, bf16[8,768]{1,0:T(8,128)(2,1)S(1)}, u32[]{:S(2)}, u32[]{:S(2)}) %collective-permute-start.4) | collective-permute-done | bytes 12320 | tf_op jit(solution)/shard_map/ppermute | solution.py:17
  437.9 7.1 %shard_map.114 = f32[384,1536]{1,0:T(8,128)} custom-call(bf16[400,768]{1,0:T(8,128)(2,1)} %pad_maximum_fusion.2.refs_0_, bf16[1536,6144]{1,0:T(8,128)(2,1)} %all-gather.2.cloned.1.call-done.refs_1_), custom_call_target="tpu_custom_call" | custom-call | tf_op jit(solution)/shard_map/pallas_call | solution.py:89
  445.0 3.2 copy.42
  448.2 4.6 fusion.42
  452.9 3.0 copy.46
  455.9 4.2 convert_reduce_fusion
  (81 shorter events, 39.9 us)
Async XLA Ops:
  7.2 3.1 copy-start.8
  7.2 135.9 %all-gather.2.cloned.1.call-start = ((), (), s32[]{:S(2)}) async-start(), calls=%async_computation.2 | async-start | bytes 19464192 | tf_op jit(solution)/shard_map/all_gather | solution.py:108
  10.2 450.2 %reduce-scatter.2.cloned.1.call-start = ((), (), s32[]{:S(2)}) async-start(), calls=%async_computation.3 | async-start | bytes 12165120 | tf_op jit(solution)/shard_map/reduce_scatter | solution.py:231
  11.0 8.5 %copy-start.10 = (f32[2,1536]{1,0:T(2,128)S(1)}, f32[2,1536]{1,0:T(2,128)}, u32[]{:S(2)}) copy-start(f32[2,1536]{1,0:T(2,128)} %param.13) | copy-start | bytes 36868
  11.0 8.5 %copy-start.11 = (f32[2,1536]{1,0:T(2,128)S(1)}, f32[2,1536]{1,0:T(2,128)}, u32[]{:S(2)}) copy-start(f32[2,1536]{1,0:T(2,128)} %param.12) | copy-start | bytes 36868
  11.0 9.1 %copy-start.14 = (f32[2,768]{1,0:T(2,128)S(1)}, f32[2,768]{1,0:T(2,128)}, u32[]{:S(2)}) copy-start(f32[2,768]{1,0:T(2,128)} %param.14) | copy-start | bytes 18436
  11.0 10.3 %copy-start.13 = (f32[2,768]{1,0:T(2,128)S(1)}, f32[2,768]{1,0:T(2,128)}, u32[]{:S(2)}) copy-start(f32[2,768]{1,0:T(2,128)} %param.15) | copy-start | bytes 18436
  11.2 23.4 %collective-permute-start.1 = (bf16[24,1536]{0,1:T(8,128)(2,1)S(1)}, bf16[24,1536]{0,1:T(8,128)(2,1)S(1)}, u32[]{:S(2)}, u32[]{:S(2)}) collective-permute-start(bf16[24,1536]{0,1:T(8,128)(2,1)S(1)} %get-tuple-element.29), channel_id=1, source_target_pairs={{4,0},{8,4},{12,8},{16,12},{20,16},{24,20},{28,24},{5,1},{9,5},{13... | collective-permute-start | bytes 221192 | tf_op jit(solution)/shard_map/ppermute | solution.py:20
  14.3 22.5 %collective-permute-start = (bf16[24,1536]{0,1:T(8,128)(2,1)S(1)}, bf16[24,1536]{0,1:T(8,128)(2,1)S(1)}, u32[]{:S(2)}, u32[]{:S(2)}) collective-permute-start(bf16[24,1536]{0,1:T(8,128)(2,1)S(1)} %get-tuple-element.28), channel_id=1, source_target_pairs={{0,4},{4,8},{8,12},{12,16},{16,20},{20,24},{24,28},{1,5},{5,9},{9,... | collective-permute-start | bytes 221192 | tf_op jit(solution)/shard_map/ppermute | solution.py:17
  143.1 8.8 %copy-start.12 = (f32[1536]{0:T(1024)S(1)}, f32[1536]{0:T(1024)}, u32[]{:S(2)}) copy-start(f32[1536]{0:T(1024)} %get-tuple-element.18) | copy-start | bytes 18436
  143.1 8.8 %copy-start.17 = (pred[416]{0:T(512)(128)(4,1)S(1)}, pred[416]{0:T(512)(128)(4,1)}, u32[]{:S(2)}) copy-start(pred[416]{0:T(512)(128)(4,1)} %fusion.103) | copy-start | bytes 1252
  159.7 8.6 %copy-start.3 = (bf16[416,1536]{0,1:T(8,128)(2,1)}, bf16[416,1536]{0,1:T(8,128)(2,1)S(1)}, u32[]{:S(2)}) copy-start(bf16[416,1536]{0,1:T(8,128)(2,1)S(1)} %get-tuple-element.24) | copy-start | bytes 3833860
  161.3 7.0 %copy-start.9 = (bf16[1,384,1536]{2,1,0:T(8,128)(2,1)S(1)}, bf16[1,384,1536]{2,1,0:T(8,128)(2,1)}, u32[]{:S(2)}) copy-start(bf16[1,384,1536]{2,1,0:T(8,128)(2,1)} %param.9) | copy-start | bytes 3538948
  161.3 7.0 %copy-start.16 = (f32[768]{0:T(1024)S(1)}, f32[768]{0:T(1024)}, u32[]{:S(2)}) copy-start(f32[768]{0:T(1024)} %get-tuple-element.21) | copy-start | bytes 9220
  171.9 6.8 %copy-start.5 = (f32[384,768]{1,0:T(8,128)S(1)}, f32[384,768]{1,0:T(8,128)}, u32[]{:S(2)}) copy-start(f32[384,768]{1,0:T(8,128)} %shard_map.112) | copy-start | bytes 3538948
  173.3 7.4 %collective-permute-start.3 = (bf16[16,768]{1,0:T(8,128)(2,1)S(1)}, bf16[16,768]{1,0:T(8,128)(2,1)S(1)}, u32[]{:S(2)}, u32[]{:S(2)}) collective-permute-start(bf16[16,768]{1,0:T(8,128)(2,1)S(1)} %get-tuple-element.33), channel_id=1, source_target_pairs={{4,0},{8,4},{12,8},{16,12},{20,16},{24,20},{28,24},{5,1},{9,5},{13... | collective-permute-start | bytes 73736 | tf_op jit(solution)/shard_map/ppermute | solution.py:20
  175.3 5.5 %collective-permute-start.2 = (bf16[16,768]{1,0:T(8,128)(2,1)S(1)}, bf16[16,768]{1,0:T(8,128)(2,1)S(1)}, u32[]{:S(2)}, u32[]{:S(2)}) collective-permute-start(bf16[16,768]{1,0:T(8,128)(2,1)S(1)} %get-tuple-element.32), channel_id=1, source_target_pairs={{0,4},{4,8},{8,12},{12,16},{16,20},{20,24},{24,28},{1,5},{5,9},{9,... | collective-permute-start | bytes 73736 | tf_op jit(solution)/shard_map/ppermute | solution.py:17
  190.9 6.2 %copy-start.4 = (f32[416,768]{1,0:T(8,128)S(1)}, f32[416,768]{1,0:T(8,128)}, u32[]{:S(2)}) copy-start(f32[416,768]{1,0:T(8,128)} %shard_map.111) | copy-start | bytes 3833860
  190.9 6.2 %copy-start.15 = (f32[768]{0:T(1024)S(1)}, f32[768]{0:T(1024)}, u32[]{:S(2)}) copy-start(f32[768]{0:T(1024)} %get-tuple-element.20) | copy-start | bytes 9220
  216.9 11.8 %copy-start.6 = (bf16[384,768]{1,0:T(8,128)(2,1)S(1)}, bf16[384,768]{1,0:T(8,128)(2,1)}, u32[]{:S(2)}) copy-start(bf16[384,768]{1,0:T(8,128)(2,1)} %multiply_convert_fusion.refs_5_) | copy-start | bytes 1769476
  216.9 239.0 %all-to-all-start = ((bf16[32,48,2304]{2,1,0:T(8,128)(2,1)}), bf16[32,48,2304]{2,1,0:T(8,128)(2,1)}, u32[]{:S(2)}, u32[]{:S(2)}) async-start(bf16[32,48,2304]{2,1,0:T(8,128)(2,1)} %bitcast.50), calls=%async_computation.1 | async-start | bytes 14155776 | tf_op jit(solution)/shard_map/all_to_all | solution.py:155
  223.4 207.4 %collective-permute-start.5 = (bf16[8,768]{1,0:T(8,128)(2,1)S(1)}, bf16[8,768]{1,0:T(8,128)(2,1)S(1)}, u32[]{:S(2)}, u32[]{:S(2)}) collective-permute-start(bf16[8,768]{1,0:T(8,128)(2,1)S(1)} %get-tuple-element.31), channel_id=1, source_target_pairs={{4,0},{8,4},{12,8},{16,12},{20,16},{24,20},{28,24},{5,1},{9,5},{13... | collective-permute-start | bytes 36872 | tf_op jit(solution)/shard_map/ppermute | solution.py:20
  226.5 210.5 %collective-permute-start.4 = (bf16[8,768]{1,0:T(8,128)(2,1)S(1)}, bf16[8,768]{1,0:T(8,128)(2,1)S(1)}, u32[]{:S(2)}, u32[]{:S(2)}) collective-permute-start(bf16[8,768]{1,0:T(8,128)(2,1)S(1)} %get-tuple-element.30), channel_id=1, source_target_pairs={{0,4},{4,8},{8,12},{12,16},{16,20},{20,24},{24,28},{1,5},{5,9},{9,... | collective-permute-start | bytes 36872 | tf_op jit(solution)/shard_map/ppermute | solution.py:17
  445.0 3.2 copy-start.1
  (3 other events, 4.9 us)
Sparse Core Ops, SparseCore 0:
  11.5 131.5 all-gather.1
  217.0 209.7 reduce-scatter.1

commit v8 on v6

--- a/solution.py
+++ b/solution.py
@@ -7,6 +7,8 @@
 from jax.sharding import PartitionSpec as P
 
 dilation_steps = (8, 16)
+WIN = ("y", "core")
+ALL = ("seq", "y", "core")
 
 
 def padded_2(block, sides, width):
@@ -105,7 +107,7 @@
          w_mix.transpose(1, 0, 2).reshape(rows, -1)],
         axis=1,
     )
-    gathered = lax.all_gather(local, ("seq", "win"), axis=0, tiled=True)
+    gathered = lax.all_gather(local, ALL, axis=0, tiled=True)
     split = blocks * taps * c2
     return gathered, [gathered[:, split + b * c2 : split + (b + 1) * c2] for b in range(blocks)]
 
@@ -145,12 +147,20 @@
     )(*operands)
 
 
+def own_first(rows_by_channel):
+    cores = lax.axis_size("core")
+    core = lax.axis_index("core")
+    grouped = rows_by_channel.reshape(-1, cores, rows_by_channel.shape[0] // (cores * lax.axis_size(("seq", "y"))), rows_by_channel.shape[1])
+    order = (core + jnp.arange(cores)) % cores
+    return jnp.take(grouped, order, axis=1).transpose(1, 0, 2, 3).reshape(rows_by_channel.shape)
+
+
 def per_device(inputs, cotangent, w_dilated, w_mix, in_scale, in_shift, mid_scale, mid_shift):
     x_local = inputs[0]
     cot_local = cotangent[0]
     row_count = x_local.shape[0]
     window_len = lax.axis_size("seq") * row_count
-    inverse_square_root = 1.0 / math.sqrt(lax.axis_size("win") * inputs.shape[0] * window_len)
+    inverse_square_root = 1.0 / math.sqrt(lax.axis_size("y") * lax.axis_size("core") * inputs.shape[0] * window_len)
     residual_block_count = len(dilation_steps)
     saved = []
     gathered, mixing_weights = fetch_weights(w_dilated, w_mix)
@@ -205,17 +215,16 @@
         )
         d_pad = padded_2(d_hidden, (("seq", 0),), dilation)
         d_act = conv_backward(d_pad, gathered, residual_block_index, c2, dilation, row_count)
-        dilated_weight_gradients[residual_block_index] = (padded.T, shifted_taps(d_hidden, dilation))
-        mixing_weight_gradients[residual_block_index] = (cot_here.T, middle)
+        dilated_weight_gradients[residual_block_index] = (own_first(padded.T), shifted_taps(d_hidden, dilation))
+        mixing_weight_gradients[residual_block_index] = (own_first(cot_here.T), middle)
         upstream_gradient = (
             upstream_gradient + gelu_back(pre_in, d_act) * in_scale[residual_block_index]
         )
-    summed = lax.psum_scatter(
-        weight_gradient_buffer(dilated_weight_gradients + mixing_weight_gradients, inverse_square_root),
-        ("seq", "win"),
-        scatter_dimension=0,
-        tiled=True,
-    ).astype(jnp.float32)
+    buffer = weight_gradient_buffer(dilated_weight_gradients + mixing_weight_gradients, inverse_square_root)
+    half = buffer.shape[0] // lax.axis_size("core")
+    partner = lax.ppermute(buffer[half:], "core", [(0, 1), (1, 0)])
+    paired = (buffer[:half].astype(jnp.float32) + partner.astype(jnp.float32)).astype(jnp.bfloat16)
+    summed = lax.psum_scatter(paired, ("seq", "y"), scatter_dimension=0, tiled=True).astype(jnp.float32)
     own_rows = summed.shape[0]
     taps, c2 = w_dilated.shape[2], w_dilated.shape[3]
     split = residual_block_count * taps * c2
@@ -228,22 +237,24 @@
 
 
 def solution(mesh):
+    win = mesh.shape["win"]
+    grid = jax.sharding.Mesh(mesh.devices.reshape(mesh.shape["seq"], win // 2, 2), ALL)
     in_specs = (
-        P("win", "seq", None),
-        P("win", "seq", None),
-        P(None, ("seq", "win"), None, None),
-        P(None, ("seq", "win"), None),
+        P(WIN, "seq", None),
+        P(WIN, "seq", None),
+        P(None, ALL, None, None),
+        P(None, ALL, None),
         P(),
         P(),
         P(),
         P(),
     )
     out_specs = (
-        P("win", "seq", None),
-        P("win", "seq", None),
-        P(None, ("seq", "win"), None, None),
-        P(None, ("seq", "win"), None),
+        P(WIN, "seq", None),
+        P(WIN, "seq", None),
+        P(None, ALL, None, None),
+        P(None, ALL, None),
     )
     return jax.shard_map(
-        per_device, mesh=mesh, in_specs=in_specs, out_specs=out_specs, check_vma=False
-    )
+        per_device, mesh=grid, in_specs=in_specs, out_specs=out_specs, check_vma=False
+    )

time: 439 us -> 434 us (0.989)
  waiting for transfers between devices: 287 us -> 266 us
  other arithmetic: 24.8 us -> 34.9 us
  local copies, waits for them, and re-layouts: 29.2 us -> 37.6 us
    reduce_scatter x1, waiting for transfers between devices: 175 us -> 146 us  [per_device(): lax.psum_scatter(paired, ('seq', 'y'), scatter_dimension=0, tiled=True)]
    ppermute x0 -> x1, waiting for transfers between devices: none -> 14.9 us  [per_device(): partner = lax.ppermute(buffer[half:], 'core', [(0, 1), (1, 0)])]
    ppermute x3, waiting for transfers between devices: 12.8 us -> 0.01 us  [padded_2(): lax.ppermute(lax.slice_in_dim(block, block.shape[dim] - width, None, axis...]
    convert_element_type x0 -> x1, other arithmetic: none -> 8.94 us  [per_device(): (buffer[:half].astype(jnp.float32) + partner.astype(jnp.float32)).astype(...]
    slice x1, local copies, waits for them, and re-layouts: 0.6 us -> 8.51 us  [per_device(): partner = lax.ppermute(buffer[half:], 'core', [(0, 1), (1, 0)])]
    unnamed x41 -> x53, local copies, waits for them, and re-layouts: 10.9 us -> 3.42 us
    all_gather x1, waiting for transfers between devices: 97.7 us -> 105 us  [fetch_weights(): gathered = lax.all_gather(local, ALL, axis=0, tiled=True)]
    gather x0 -> x4, local copies, waits for them, and re-layouts: none -> 6.62 us  [own_first(): jnp.take(grouped, order, axis=1).transpose(1, 0, 2, 3)]
  transfers between devices with their start and end apart: 8 -> 9, of which waited for: 4 -> 3; matrix products, arithmetic and copies ran while one was open for 8% -> 8% of each run, Pallas kernels for 2% -> 2%
where the time goes in v8:
time: 434 us; the launch traced here: 433 us
  waiting for transfers between devices  266 us (61%)
  Pallas kernels  44.2 us (10%)
  local copies, waits for them, and re-layouts  37.6 us (9%)
  other arithmetic  34.9 us (8%)
  matrix products  18.6 us (4%)
  starting transfers between devices  17.1 us (4%)
  between operations  14.5 us (3%)
    reduce_scatter x1, waiting for transfers between devices, per_device(): lax.psum_scatter(paired, ('seq', 'y'), scatter_dimension=0, tiled=True)  146 us
    all_gather x1, waiting for transfers between devices, fetch_weights(): gathered = lax.all_gather(local, ALL, axis=0, tiled=True)  105 us
    pallas_call x1, Pallas kernels, weight_gradient_buffer(): pl.pallas_call(lambda *refs: gradient_kernel(inverse_square_root, widths,...  15.6 us
    ppermute x1, waiting for transfers between devices, per_device(): partner = lax.ppermute(buffer[half:], 'core', [(0, 1), (1, 0)])  14.9 us
    pallas_call x2, Pallas kernels, conv_backward(): pl.pallas_call(lambda *refs: conv_backward_kernel(dilation, out_rows, *re...  14.5 us
    pallas_call x2, Pallas kernels, conv_forward(): pl.pallas_call(lambda *refs: conv_forward_kernel(dilation, out_rows, *ref...  14.1 us
    ppermute x3, starting transfers between devices, padded_2(): lax.ppermute(lax.slice_in_dim(block, block.shape[dim] - width, None, axis...  12.7 us
    dot_general x2, matrix products, per_device(): jnp.einsum('pe,ce->pc', middle, w_out, preferred_element_type=jnp.float32)  11.4 us
  transfers between devices with their start and end apart: 9, of which 3 were waited for; matrix products, arithmetic and copies ran while one was open for 8% of the time, Pallas kernels for 2%

profile of v8, /device:TPU:0, one launch (start us, length us, event | category | flops | bytes accessed | tf_op | source)
XLA Modules:
  0.0 432.9 jit_solution(146240149217100739)
XLA Ops:
  10.4 4.8 %collective-permute-start = (bf16[24,1536]{1,0:T(8,128)(2,1)S(1)}, bf16[24,1536]{1,0:T(8,128)(2,1)S(1)}, u32[]{:S(2)}, u32[]{:S(2)}) collective-permute-start(bf16[24,1536]{1,0:T(8,128)(2,1)S(1)} %get-tuple-element.21), channel_id=1, source_target_pairs={{0,4},{4,8},{8,12},{12,16},{16,20},{20,24},{24,28},{1,5},{5,9},{9,... | collective-permute-start | bytes 221192 | tf_op jit(solution)/shard_map/ppermute | solution.py:19
  19.5 1.7 gather_fusion.3
  22.6 3.1 multiply_add_fusion
  29.8 2.1 gather_fusion
  33.8 105.1 %all-gather.2.cloned.1.call-done.refs_1_ = bf16[1536,6144]{1,0:T(8,128)(2,1)} async-done(((bf16[48,6144]{1,0:T(8,128)(2,1)}), bf16[1536,6144]{1,0:T(8,128)(2,1)}) %all-gather.2.cloned.1.call-update) | async-done | bytes 18874384 | tf_op jit(solution)/shard_map/all_gather | solution.py:110
  138.9 7.1 %shard_map.111 = f32[416,768]{1,0:T(8,128)} custom-call(bf16[432,1536]{1,0:T(8,128)(2,1)} %copy-done, bf16[1536,6144]{1,0:T(8,128)(2,1)} %all-gather.2.cloned.1.call-done.refs_1_, f32[1,768]{1,0:T(1,128)} %get-tuple-element.28.refs_2_, f32[1,768]{1,0:T(1,128)} %get-tuple-element.36.refs_3_), custom_call_target="tpu_custom_call" | custom-call | tf_op jit(solution)/shard_map/pallas_call | solution.py:75
  147.7 6.5 %fusion.27 = (bf16[416,1536]{1,0:T(8,128)(2,1)}, f32[416,1536]{1,0:T(8,128)}, f32[416,1536]{1,0:T(8,128)}) fusion(pred[416]{0:T(512)(128)(4,1)S(1)} %fusion.98, f32[1536]{0:T(1024)S(1)} %get-tuple-element.11, f32[1536]{0:T(1024)S(1)} %get-tuple-element.35, bf16[416,768]{1,0:T(8,128)(2,1)S(1)} %fusion.68, ...), kind=kOutput, calls=%fused_computation.48 | convolution fusion | flops 989773824 | bytes 11956640 | tf_op jit(solution)/shard_map/pe,ce->pc/dot_general | solution.py:190
  154.2 7.0 %shard_map.112 = f32[384,768]{1,0:T(8,128)} custom-call(bf16[416,1536]{1,0:T(8,128)(2,1)} %get-tuple-element.17.refs_0_, bf16[1536,6144]{1,0:T(8,128)(2,1)} %all-gather.2.cloned.1.call-done.refs_1_, f32[1,768]{1,0:T(1,128)} %get-tuple-element.27.refs_2_, f32[1,768]{1,0:T(1,128)} %get-tuple-element.37.refs_3_), custom_call_target="tpu_custom_call" | custom-call | tf_op jit(solution)/shard_map/pallas_call | solution.py:75
  161.2 3.6 fusion.76
  166.3 3.3 collective-permute-start.2
  177.1 7.2 %shard_map.113 = f32[384,1536]{1,0:T(8,128)} custom-call(bf16[416,768]{1,0:T(8,128)(2,1)} %pad_maximum_fusion.refs_0_, bf16[1536,6144]{1,0:T(8,128)(2,1)} %all-gather.2.cloned.1.call-done.refs_1_), custom_call_target="tpu_custom_call" | custom-call | tf_op jit(solution)/shard_map/pallas_call | solution.py:91
  184.3 4.3 convert_bitcast_fusion
  188.6 2.4 copy.22
  192.1 2.2 gather_fusion.2
  194.4 3.6 fusion.84
  201.8 15.6 %shard_map.115 = bf16[1536,6144]{1,0:T(8,128)(2,1)} custom-call(bf16[1536,400]{1,0:T(8,128)(2,1)} %bitcast.64, bf16[400,2304]{1,0:T(8,128)(2,1)} %fusion.57.refs_1_, bf16[1536,416]{1,0:T(8,128)(2,1)} %bitcast.65, bf16[416,2304]{1,0:T(8,128)(2,1)} %fusion.55.refs_3_, bf16[1536,384]{1,0:T(8,128)(2,1)} %bitcast.74, bf16[384,768]{1,0:T(8,128)(2,1)} %slice.140.refs_5_, ...), custom_call_target="tpu_custom_call" | custom-call | tf_op jit(solution)/shard_map/pallas_call | solution.py:141
  217.4 8.5 %slice.142 = bf16[768,6144]{1,0:T(8,128)(2,1)} slice(bf16[1536,6144]{1,0:T(8,128)(2,1)} %shard_map.115), slice={[768:1536], [0:6144]} | slice | bytes 18874368 | tf_op jit(solution)/shard_map/slice | solution.py:225
  225.9 14.9 %collective-permute-done.6 = bf16[768,6144]{1,0:T(8,128)(2,1)S(1)} collective-permute-done((bf16[768,6144]{1,0:T(8,128)(2,1)}, bf16[768,6144]{1,0:T(8,128)(2,1)S(1)}, u32[]{:S(2)}, u32[]{:S(2)}) %collective-permute-start.6) | collective-permute-done | bytes 9437216 | tf_op jit(solution)/shard_map/ppermute | solution.py:225
  240.8 8.9 %add_convert_fusion = bf16[768,6144]{1,0:T(8,128)(2,1)} fusion(bf16[768,6144]{1,0:T(8,128)(2,1)S(1)} %collective-permute-done.6, bf16[1536,6144]{1,0:T(8,128)(2,1)} %shard_map.115), kind=kLoop, calls=%fused_computation.4 | loop fusion | flops 18874368 | bytes 28311552 | tf_op jit(solution)/shard_map/convert_element_type | solution.py:226
  250.8 4.5 %collective-permute-start.4 = (bf16[8,768]{1,0:T(8,128)(2,1)S(1)}, bf16[8,768]{1,0:T(8,128)(2,1)S(1)}, u32[]{:S(2)}, u32[]{:S(2)}) collective-permute-start(bf16[8,768]{1,0:T(8,128)(2,1)S(1)} %get-tuple-element.23), channel_id=1, source_target_pairs={{0,4},{4,8},{8,12},{12,16},{16,20},{20,24},{24,28},{1,5},{5,9},{9,... | collective-permute-start | bytes 36872 | tf_op jit(solution)/shard_map/ppermute | solution.py:19
  256.9 4.9 %fusion.18 = bf16[1,384,1536]{2,1,0:T(8,128)(2,1)} fusion(bf16[384,768]{1,0:T(8,128)(2,1)S(1)} %copy-done.17, f32[416,1536]{1,0:T(8,128)} %get-tuple-element.33, bf16[1536,6144]{1,0:T(8,128)(2,1)} %all-gather.2.cloned.1.call-done.refs_1_), kind=kOutput, calls=%fused_computation.39 | convolution fusion | flops 907149312 | bytes 6488064 | tf_op jit(solution)/shard_map/pe,ce->pc/dot_general | solution.py:190
  262.7 7.3 %shard_map.114 = f32[384,1536]{1,0:T(8,128)} custom-call(bf16[400,768]{1,0:T(8,128)(2,1)} %pad_maximum_fusion.1.refs_0_, bf16[1536,6144]{1,0:T(8,128)(2,1)} %all-gather.2.cloned.1.call-done.refs_1_), custom_call_target="tpu_custom_call" | custom-call | tf_op jit(solution)/shard_map/pallas_call | solution.py:91
  270.0 5.5 %fusion.44 = f32[1,384,1536]{2,1,0:T(8,128)} fusion(f32[384,1536]{1,0:T(8,128)} %copy-done.2, f32[384,1536]{1,0:T(8,128)} %shard_map.114, f32[432,1536]{1,0:T(8,128)S(1)} %copy-done.1, f32[1536]{0:T(1024)S(1)} %get-tuple-element.34), kind=kLoop, calls=%fused_computation.67 | loop fusion | flops 12386304 | bytes 9443328 | tf_op jit(solution)/shard_map/broadcast_in_dim | solution.py:233
  275.5 146.0 %reduce-scatter.2.cloned.1.call-done = bf16[48,6144]{1,0:T(8,128)(2,1)} async-done(((bf16[768,6144]{1,0:T(8,128)(2,1)}), bf16[48,6144]{1,0:T(8,128)(2,1)}) %reduce-scatter.2.cloned.1.call-update) | async-done | bytes 589840 | tf_op jit(solution)/shard_map/reduce_scatter | solution.py:227
  (107 shorter events, 38.3 us)
Async XLA Ops:
  7.2 131.7 %all-gather.2.cloned.1.call-start = ((), (), s32[]{:S(2)}) async-start(), calls=%async_computation.1 | async-start | bytes 19464192 | tf_op jit(solution)/shard_map/all_gather | solution.py:110
  8.2 8.3 %copy-start.8 = (bf16[1,384,1536]{2,1,0:T(8,128)(2,1)S(1)}, bf16[1,384,1536]{2,1,0:T(8,128)(2,1)}, u32[]{:S(2)}) copy-start(bf16[1,384,1536]{2,1,0:T(8,128)(2,1)} %param.11) | copy-start | bytes 3538948
  10.3 411.2 %reduce-scatter.2.cloned.1.call-start = ((), (), s32[]{:S(2)}) async-start(), calls=%async_computation.2 | async-start | bytes 10027008 | tf_op jit(solution)/shard_map/reduce_scatter | solution.py:227
  10.4 12.2 %collective-permute-start = (bf16[24,1536]{1,0:T(8,128)(2,1)S(1)}, bf16[24,1536]{1,0:T(8,128)(2,1)S(1)}, u32[]{:S(2)}, u32[]{:S(2)}) collective-permute-start(bf16[24,1536]{1,0:T(8,128)(2,1)S(1)} %get-tuple-element.21), channel_id=1, source_target_pairs={{0,4},{4,8},{8,12},{12,16},{16,20},{20,24},{24,28},{1,5},{5,9},{9,... | collective-permute-start | bytes 221192 | tf_op jit(solution)/shard_map/ppermute | solution.py:19
  15.2 7.4 %collective-permute-start.1 = (bf16[24,1536]{1,0:T(8,128)(2,1)S(1)}, bf16[24,1536]{1,0:T(8,128)(2,1)S(1)}, u32[]{:S(2)}, u32[]{:S(2)}) collective-permute-start(bf16[24,1536]{1,0:T(8,128)(2,1)S(1)} %get-tuple-element.22), channel_id=1, source_target_pairs={{4,0},{8,4},{12,8},{16,12},{20,16},{24,20},{28,24},{5,1},{9,5},{13... | collective-permute-start | bytes 221192 | tf_op jit(solution)/shard_map/ppermute | solution.py:22
  18.0 3.3 copy-start.19
  18.0 3.4 copy-start.21
  18.0 3.4 copy-start.22
  21.2 151.4 %copy-start.23 = (pred[2]{0:T(512)(128)(4,1)}, pred[2]{0:T(512)(128)(4,1)S(1)}, u32[]{:S(2)}) copy-start(pred[2]{0:T(512)(128)(4,1)S(1)} %compare_and_fusion) | copy-start | bytes 10
  147.7 6.5 %copy-start.15 = (bf16[416,768]{1,0:T(8,128)(2,1)}, bf16[416,768]{1,0:T(8,128)(2,1)S(1)}, u32[]{:S(2)}) copy-start(bf16[416,768]{1,0:T(8,128)(2,1)S(1)} %fusion.68) | copy-start | bytes 1916932
  154.2 7.0 %copy-start.9 = (bf16[1,384,1536]{2,1,0:T(8,128)(2,1)S(1)}, bf16[1,384,1536]{2,1,0:T(8,128)(2,1)}, u32[]{:S(2)}) copy-start(bf16[1,384,1536]{2,1,0:T(8,128)(2,1)} %param.11) | copy-start | bytes 3538948
  164.8 6.3 %copy-start.11 = (bf16[384,768]{1,0:T(8,128)(2,1)}, bf16[384,768]{1,0:T(8,128)(2,1)S(1)}, u32[]{:S(2)}) copy-start(bf16[384,768]{1,0:T(8,128)(2,1)S(1)} %fusion.76) | copy-start | bytes 1769476
  164.8 6.3 %copy-start.5 = (bf16[416,1536]{1,0:T(8,128)(2,1)S(1)}, bf16[416,1536]{1,0:T(8,128)(2,1)}, u32[]{:S(2)}) copy-start(bf16[416,1536]{1,0:T(8,128)(2,1)} %get-tuple-element.17.refs_0_) | copy-start | bytes 3833860
  166.3 9.9 %collective-permute-start.2 = (bf16[16,768]{1,0:T(8,128)(2,1)S(1)}, bf16[16,768]{1,0:T(8,128)(2,1)S(1)}, u32[]{:S(2)}, u32[]{:S(2)}) collective-permute-start(bf16[16,768]{1,0:T(8,128)(2,1)S(1)} %get-tuple-element.25), channel_id=1, source_target_pairs={{0,4},{4,8},{8,12},{12,16},{16,20},{20,24},{24,28},{1,5},{5,9},{9,... | collective-permute-start | bytes 73736 | tf_op jit(solution)/shard_map/ppermute | solution.py:19
  169.6 6.6 %collective-permute-start.3 = (bf16[16,768]{1,0:T(8,128)(2,1)S(1)}, bf16[16,768]{1,0:T(8,128)(2,1)S(1)}, u32[]{:S(2)}, u32[]{:S(2)}) collective-permute-start(bf16[16,768]{1,0:T(8,128)(2,1)S(1)} %get-tuple-element.26), channel_id=1, source_target_pairs={{4,0},{8,4},{12,8},{16,12},{20,16},{24,20},{28,24},{5,1},{9,5},{13... | collective-permute-start | bytes 73736 | tf_op jit(solution)/shard_map/ppermute | solution.py:22
  177.1 7.2 %copy-start.10 = (bf16[1,384,1536]{2,1,0:T(8,128)(2,1)S(1)}, bf16[1,384,1536]{2,1,0:T(8,128)(2,1)}, u32[]{:S(2)}) copy-start(bf16[1,384,1536]{2,1,0:T(8,128)(2,1)} %param.11) | copy-start | bytes 3538948
  188.6 5.8 %copy-start.2 = (f32[384,1536]{1,0:T(8,128)}, f32[384,1536]{1,0:T(8,128)S(1)}, u32[]{:S(2)}) copy-start(f32[384,1536]{1,0:T(8,128)S(1)} %get-tuple-element.16) | copy-start | bytes 7077892
  191.0 3.4 copy-start.25
  197.9 3.9 copy-start.13
  225.9 14.9 %collective-permute-start.6 = (bf16[768,6144]{1,0:T(8,128)(2,1)}, bf16[768,6144]{1,0:T(8,128)(2,1)S(1)}, u32[]{:S(2)}, u32[]{:S(2)}) collective-permute-start(bf16[768,6144]{1,0:T(8,128)(2,1)} %slice.142), channel_id=1, source_target_pairs={{0,1},{1,0},{2,3},{3,2},{4,5},{5,4},{6,7},{7,6},{8,9},{9,8},{10,11... | collective-permute-start | bytes 28311560 | tf_op jit(solution)/shard_map/ppermute | solution.py:225
  249.7 7.1 %copy-start.17 = (bf16[384,768]{1,0:T(8,128)(2,1)S(1)}, bf16[384,768]{1,0:T(8,128)(2,1)}, u32[]{:S(2)}) copy-start(bf16[384,768]{1,0:T(8,128)(2,1)} %multiply_convert_fusion.refs_7_) | copy-start | bytes 1769476
  250.8 11.0 %collective-permute-start.4 = (bf16[8,768]{1,0:T(8,128)(2,1)S(1)}, bf16[8,768]{1,0:T(8,128)(2,1)S(1)}, u32[]{:S(2)}, u32[]{:S(2)}) collective-permute-start(bf16[8,768]{1,0:T(8,128)(2,1)S(1)} %get-tuple-element.23), channel_id=1, source_target_pairs={{0,4},{4,8},{8,12},{12,16},{16,20},{20,24},{24,28},{1,5},{5,9},{9,... | collective-permute-start | bytes 36872 | tf_op jit(solution)/shard_map/ppermute | solution.py:19
  255.4 6.5 %collective-permute-start.5 = (bf16[8,768]{1,0:T(8,128)(2,1)S(1)}, bf16[8,768]{1,0:T(8,128)(2,1)S(1)}, u32[]{:S(2)}, u32[]{:S(2)}) collective-permute-start(bf16[8,768]{1,0:T(8,128)(2,1)S(1)} %get-tuple-element.24), channel_id=1, source_target_pairs={{4,0},{8,4},{12,8},{16,12},{20,16},{24,20},{28,24},{5,1},{9,5},{13... | collective-permute-start | bytes 36872 | tf_op jit(solution)/shard_map/ppermute | solution.py:22
  262.7 7.3 %copy-start.1 = (f32[432,1536]{1,0:T(8,128)S(1)}, f32[432,1536]{1,0:T(8,128)}, u32[]{:S(2)}) copy-start(f32[432,1536]{1,0:T(8,128)} %get-tuple-element.19) | copy-start | bytes 7962628
  (11 other events, 24.4 us)
Sparse Core Ops, SparseCore 0:
  11.5 127.3 all-gather.1
  249.9 171.5 reduce-scatter.1

commit v9 on v8

--- a/solution.py
+++ b/solution.py
@@ -129,21 +129,20 @@
         start += widths[pair]
 
 
-def weight_gradient_buffer(pairs, inverse_square_root, row_tile=256):
-    rows = pairs[0][0].shape[0]
+def weight_gradient_buffer(pairs, inverse_square_root, first_tile, tiles, row_tile=256):
     widths = tuple(rhs.shape[1] for _, rhs in pairs)
     in_specs = []
     operands = []
     for lhs, rhs in pairs:
-        in_specs.append(pl.BlockSpec((row_tile, lhs.shape[1]), lambda i: (i, 0)))
+        in_specs.append(pl.BlockSpec((row_tile, lhs.shape[1]), lambda i: (i + first_tile, 0)))
         in_specs.append(pl.BlockSpec(rhs.shape, lambda i: (0, 0)))
         operands += [lhs, rhs]
     return pl.pallas_call(
         lambda *refs: gradient_kernel(inverse_square_root, widths, *refs),
-        grid=(rows // row_tile,),
+        grid=(tiles,),
         in_specs=in_specs,
         out_specs=pl.BlockSpec((row_tile, sum(widths)), lambda i: (i, 0)),
-        out_shape=jax.ShapeDtypeStruct((rows, sum(widths)), jnp.bfloat16),
+        out_shape=jax.ShapeDtypeStruct((tiles * row_tile, sum(widths)), jnp.bfloat16),
     )(*operands)
 
 
@@ -220,10 +219,13 @@
         upstream_gradient = (
             upstream_gradient + gelu_back(pre_in, d_act) * in_scale[residual_block_index]
         )
-    buffer = weight_gradient_buffer(dilated_weight_gradients + mixing_weight_gradients, inverse_square_root)
-    half = buffer.shape[0] // lax.axis_size("core")
-    partner = lax.ppermute(buffer[half:], "core", [(0, 1), (1, 0)])
-    paired = (buffer[:half].astype(jnp.float32) + partner.astype(jnp.float32)).astype(jnp.bfloat16)
+    pairs = dilated_weight_gradients + mixing_weight_gradients
+    row_tile = 256
+    tiles = pairs[0][0].shape[0] // (row_tile * lax.axis_size("core"))
+    partner_rows = weight_gradient_buffer(pairs, inverse_square_root, tiles, tiles, row_tile)
+    partner = lax.ppermute(partner_rows, "core", [(0, 1), (1, 0)])
+    own_rows = weight_gradient_buffer(pairs, inverse_square_root, 0, tiles, row_tile)
+    paired = (own_rows.astype(jnp.float32) + partner.astype(jnp.float32)).astype(jnp.bfloat16)
     summed = lax.psum_scatter(paired, ("seq", "y"), scatter_dimension=0, tiled=True).astype(jnp.float32)
     own_rows = summed.shape[0]
     taps, c2 = w_dilated.shape[2], w_dilated.shape[3]

time: 434 us -> 418 us (0.963)
  local copies, waits for them, and re-layouts: 37.6 us -> 25 us
  waiting for transfers between devices: 266 us -> 254 us
  Pallas kernels: 44.2 us -> 48.7 us
    ppermute x1, waiting for transfers between devices: 14.9 us -> 4.87 us  [per_device(): partner = lax.ppermute(partner_rows, 'core', [(0, 1), (1, 0)])]
    slice x1 -> x0, local copies, waits for them, and re-layouts: 8.51 us -> none  [per_device(): partner = lax.ppermute(buffer[half:], 'core', [(0, 1), (1, 0)])]
    pallas_call x1 -> x2, Pallas kernels: 15.6 us -> 20.1 us  [weight_gradient_buffer(): pl.pallas_call(lambda *refs: gradient_kernel(inverse_square_root, widths,...]
  transfers between devices with their start and end apart: 9 -> 9, of which waited for: 3 -> 3; matrix products, arithmetic and copies ran while one was open for 8% -> 8% of each run, Pallas kernels for 2% -> 4%
where the time goes in v9:
time: 418 us; the launch traced here: 417 us
  waiting for transfers between devices  254 us (61%)
  Pallas kernels  48.7 us (12%)
  other arithmetic  37.8 us (9%)
  local copies, waits for them, and re-layouts  25 us (6%)
  starting transfers between devices  19.2 us (5%)
  matrix products  17.9 us (4%)
  between operations  14.5 us (3%)
    reduce_scatter x1, waiting for transfers between devices, per_device(): lax.psum_scatter(paired, ('seq', 'y'), scatter_dimension=0, tiled=True)  145 us
    all_gather x1, waiting for transfers between devices, fetch_weights(): gathered = lax.all_gather(local, ALL, axis=0, tiled=True)  104 us
    pallas_call x2, Pallas kernels, weight_gradient_buffer(): pl.pallas_call(lambda *refs: gradient_kernel(inverse_square_root, widths,...  20.1 us
    ppermute x3, starting transfers between devices, padded_2(): lax.ppermute(lax.slice_in_dim(block, block.shape[dim] - width, None, axis...  15.3 us
    pallas_call x2, Pallas kernels, conv_backward(): pl.pallas_call(lambda *refs: conv_backward_kernel(dilation, out_rows, *re...  14.5 us
    pallas_call x2, Pallas kernels, conv_forward(): pl.pallas_call(lambda *refs: conv_forward_kernel(dilation, out_rows, *ref...  14.1 us
    convert_element_type x1, other arithmetic, per_device(): (own_rows.astype(jnp.float32) + partner.astype(jnp.float32)).astype(jnp.b...  12.3 us
    dot_general x2, matrix products, per_device(): jnp.einsum('pe,ce->pc', middle, w_out, preferred_element_type=jnp.float32)  11 us
  transfers between devices with their start and end apart: 9, of which 3 were waited for; matrix products, arithmetic and copies ran while one was open for 8% of the time, Pallas kernels for 4%

profile of v9, /device:TPU:0, one launch (start us, length us, event | category | flops | bytes accessed | tf_op | source)
XLA Modules:
  0.0 417.4 jit_solution(12655716021924368391)
XLA Ops:
  11.7 5.5 %collective-permute-start = (bf16[24,1536]{1,0:T(8,128)(2,1)S(1)}, bf16[24,1536]{1,0:T(8,128)(2,1)S(1)}, u32[]{:S(2)}, u32[]{:S(2)}) collective-permute-start(bf16[24,1536]{1,0:T(8,128)(2,1)S(1)} %get-tuple-element.21), channel_id=1, source_target_pairs={{0,4},{4,8},{8,12},{12,16},{16,20},{20,24},{24,28},{1,5},{5,9},{9,... | collective-permute-start | bytes 221192 | tf_op jit(solution)/shard_map/ppermute | solution.py:19
  20.1 1.8 gather_fusion.3
  23.3 3.1 multiply_add_fusion
  30.4 2.1 gather_fusion
  34.4 104.5 %all-gather.2.cloned.1.call-done.refs_1_ = bf16[1536,6144]{1,0:T(8,128)(2,1)} async-done(((bf16[48,6144]{1,0:T(8,128)(2,1)}), bf16[1536,6144]{1,0:T(8,128)(2,1)}) %all-gather.2.cloned.1.call-update) | async-done | bytes 18874384 | tf_op jit(solution)/shard_map/all_gather | solution.py:110
  138.9 7.1 %shard_map.111 = f32[416,768]{1,0:T(8,128)} custom-call(bf16[432,1536]{1,0:T(8,128)(2,1)} %copy-done, bf16[1536,6144]{1,0:T(8,128)(2,1)} %all-gather.2.cloned.1.call-done.refs_1_, f32[1,768]{1,0:T(1,128)} %get-tuple-element.28.refs_2_, f32[1,768]{1,0:T(1,128)} %get-tuple-element.36.refs_3_), custom_call_target="tpu_custom_call" | custom-call | tf_op jit(solution)/shard_map/pallas_call | solution.py:75
  146.0 1.7 fusion.68
  147.7 6.5 %fusion.27 = (bf16[416,1536]{1,0:T(8,128)(2,1)}, f32[416,1536]{1,0:T(8,128)}, f32[416,1536]{1,0:T(8,128)}) fusion(pred[416]{0:T(512)(128)(4,1)S(1)} %fusion.98, f32[1536]{0:T(1024)S(1)} %get-tuple-element.11, f32[1536]{0:T(1024)S(1)} %get-tuple-element.35, bf16[416,768]{1,0:T(8,128)(2,1)S(1)} %fusion.68, ...), kind=kOutput, calls=%fused_computation.48 | convolution fusion | flops 989773824 | bytes 11956640 | tf_op jit(solution)/shard_map/pe,ce->pc/dot_general | solution.py:189
  154.2 7.0 %shard_map.112 = f32[384,768]{1,0:T(8,128)} custom-call(bf16[416,1536]{1,0:T(8,128)(2,1)} %get-tuple-element.17.refs_0_, bf16[1536,6144]{1,0:T(8,128)(2,1)} %all-gather.2.cloned.1.call-done.refs_1_, f32[1,768]{1,0:T(1,128)} %get-tuple-element.27.refs_2_, f32[1,768]{1,0:T(1,128)} %get-tuple-element.37.refs_3_), custom_call_target="tpu_custom_call" | custom-call | tf_op jit(solution)/shard_map/pallas_call | solution.py:75
  161.2 3.6 fusion.76
  167.7 4.7 %collective-permute-start.2 = (bf16[16,768]{1,0:T(8,128)(2,1)S(1)}, bf16[16,768]{1,0:T(8,128)(2,1)S(1)}, u32[]{:S(2)}, u32[]{:S(2)}) collective-permute-start(bf16[16,768]{1,0:T(8,128)(2,1)S(1)} %get-tuple-element.25), channel_id=1, source_target_pairs={{0,4},{4,8},{8,12},{12,16},{16,20},{20,24},{24,28},{1,5},{5,9},{9,... | collective-permute-start | bytes 73736 | tf_op jit(solution)/shard_map/ppermute | solution.py:19
  178.4 7.2 %shard_map.113 = f32[384,1536]{1,0:T(8,128)} custom-call(bf16[416,768]{1,0:T(8,128)(2,1)} %pad_maximum_fusion.refs_0_, bf16[1536,6144]{1,0:T(8,128)(2,1)} %all-gather.2.cloned.1.call-done.refs_1_), custom_call_target="tpu_custom_call" | custom-call | tf_op jit(solution)/shard_map/pallas_call | solution.py:91
  185.6 3.6 convert_bitcast_fusion
  190.6 3.3 fusion.84
  197.3 1.8 broadcast_select_fusion.2
  199.1 9.9 %shard_map.116 = bf16[768,6144]{1,0:T(8,128)(2,1)} custom-call(bf16[1536,400]{1,0:T(8,128)(2,1)} %bitcast.62, bf16[400,2304]{1,0:T(8,128)(2,1)} %fusion.57.refs_1_, bf16[1536,416]{1,0:T(8,128)(2,1)} %bitcast.64, bf16[416,2304]{1,0:T(8,128)(2,1)} %fusion.55.refs_3_, bf16[1536,384]{1,0:T(8,128)(2,1)} %bitcast.68, bf16[384,768]{1,0:T(8,128)(2,1)} %slice.132.refs_5_, ...), custom_call_target="tpu_custom_call" | custom-call | tf_op jit(solution)/shard_map/pallas_call | solution.py:140
  209.0 10.1 %shard_map.115 = bf16[768,6144]{1,0:T(8,128)(2,1)} custom-call(bf16[1536,400]{1,0:T(8,128)(2,1)} %bitcast.63, bf16[400,2304]{1,0:T(8,128)(2,1)} %fusion.57.refs_1_, bf16[1536,416]{1,0:T(8,128)(2,1)} %bitcast.65, bf16[416,2304]{1,0:T(8,128)(2,1)} %fusion.55.refs_3_, bf16[1536,384]{1,0:T(8,128)(2,1)} %bitcast.69, bf16[384,768]{1,0:T(8,128)(2,1)} %slice.132.refs_5_, ...), custom_call_target="tpu_custom_call" | custom-call | tf_op jit(solution)/shard_map/pallas_call | solution.py:140
  219.2 4.9 %collective-permute-done.6 = bf16[768,6144]{1,0:T(8,128)(2,1)} collective-permute-done((bf16[768,6144]{1,0:T(8,128)(2,1)}, bf16[768,6144]{1,0:T(8,128)(2,1)}, u32[]{:S(2)}, u32[]{:S(2)}) %collective-permute-start.6) | collective-permute-done | bytes 9437216 | tf_op jit(solution)/shard_map/ppermute | solution.py:226
  224.0 12.3 %add_convert_fusion = bf16[768,6144]{1,0:T(8,128)(2,1)} fusion(bf16[768,6144]{1,0:T(8,128)(2,1)} %collective-permute-done.6, bf16[768,6144]{1,0:T(8,128)(2,1)} %shard_map.115), kind=kLoop, calls=%fused_computation.4 | loop fusion | flops 18874368 | bytes 28311552 | tf_op jit(solution)/shard_map/convert_element_type | solution.py:228
  238.7 5.1 %collective-permute-start.4 = (bf16[8,768]{1,0:T(8,128)(2,1)S(1)}, bf16[8,768]{1,0:T(8,128)(2,1)S(1)}, u32[]{:S(2)}, u32[]{:S(2)}) collective-permute-start(bf16[8,768]{1,0:T(8,128)(2,1)S(1)} %get-tuple-element.23), channel_id=1, source_target_pairs={{0,4},{4,8},{8,12},{12,16},{16,20},{20,24},{24,28},{1,5},{5,9},{9,... | collective-permute-start | bytes 36872 | tf_op jit(solution)/shard_map/ppermute | solution.py:19
  243.7 4.5 %fusion.18 = bf16[1,384,1536]{2,1,0:T(8,128)(2,1)} fusion(bf16[384,768]{1,0:T(8,128)(2,1)S(1)} %copy-done.5, f32[416,1536]{1,0:T(8,128)} %get-tuple-element.33, bf16[1536,6144]{1,0:T(8,128)(2,1)} %all-gather.2.cloned.1.call-done.refs_1_), kind=kOutput, calls=%fused_computation.39 | convolution fusion | flops 907149312 | bytes 6488064 | tf_op jit(solution)/shard_map/pe,ce->pc/dot_general | solution.py:189
  249.2 7.3 %shard_map.114 = f32[384,1536]{1,0:T(8,128)} custom-call(bf16[400,768]{1,0:T(8,128)(2,1)} %pad_maximum_fusion.1.refs_0_, bf16[1536,6144]{1,0:T(8,128)(2,1)} %all-gather.2.cloned.1.call-done.refs_1_), custom_call_target="tpu_custom_call" | custom-call | tf_op jit(solution)/shard_map/pallas_call | solution.py:91
  256.5 5.6 %fusion.44 = f32[1,384,1536]{2,1,0:T(8,128)} fusion(f32[384,1536]{1,0:T(8,128)} %copy-done.2, f32[384,1536]{1,0:T(8,128)} %shard_map.114, f32[432,1536]{1,0:T(8,128)S(1)} %copy-done.1, f32[1536]{0:T(1024)S(1)} %get-tuple-element.34), kind=kLoop, calls=%fused_computation.67 | loop fusion | flops 12386304 | bytes 9443328 | tf_op jit(solution)/shard_map/broadcast_in_dim | solution.py:235
  262.1 144.8 %reduce-scatter.2.cloned.1.call-done = bf16[48,6144]{1,0:T(8,128)(2,1)} async-done(((bf16[768,6144]{1,0:T(8,128)(2,1)}), bf16[48,6144]{1,0:T(8,128)(2,1)}) %reduce-scatter.2.cloned.1.call-update) | async-done | bytes 589840 | tf_op jit(solution)/shard_map/reduce_scatter | solution.py:229
  (111 shorter events, 35.0 us)
Async XLA Ops:
  7.2 131.7 %all-gather.2.cloned.1.call-start = ((), (), s32[]{:S(2)}) async-start(), calls=%async_computation.1 | async-start | bytes 19464192 | tf_op jit(solution)/shard_map/all_gather | solution.py:110
  8.2 8.9 %copy-start.10 = (bf16[1,384,1536]{2,1,0:T(8,128)(2,1)S(1)}, bf16[1,384,1536]{2,1,0:T(8,128)(2,1)}, u32[]{:S(2)}) copy-start(bf16[1,384,1536]{2,1,0:T(8,128)(2,1)} %param.11) | copy-start | bytes 3538948
  10.3 396.6 %reduce-scatter.2.cloned.1.call-start = ((), (), s32[]{:S(2)}) async-start(), calls=%async_computation.2 | async-start | bytes 10027008 | tf_op jit(solution)/shard_map/reduce_scatter | solution.py:229
  10.4 12.9 %collective-permute-start.1 = (bf16[24,1536]{1,0:T(8,128)(2,1)S(1)}, bf16[24,1536]{1,0:T(8,128)(2,1)S(1)}, u32[]{:S(2)}, u32[]{:S(2)}) collective-permute-start(bf16[24,1536]{1,0:T(8,128)(2,1)S(1)} %get-tuple-element.22), channel_id=1, source_target_pairs={{4,0},{8,4},{12,8},{16,12},{20,16},{24,20},{28,24},{5,1},{9,5},{13... | collective-permute-start | bytes 221192 | tf_op jit(solution)/shard_map/ppermute | solution.py:22
  11.7 11.6 %collective-permute-start = (bf16[24,1536]{1,0:T(8,128)(2,1)S(1)}, bf16[24,1536]{1,0:T(8,128)(2,1)S(1)}, u32[]{:S(2)}, u32[]{:S(2)}) collective-permute-start(bf16[24,1536]{1,0:T(8,128)(2,1)S(1)} %get-tuple-element.21), channel_id=1, source_target_pairs={{0,4},{4,8},{8,12},{12,16},{16,20},{20,24},{24,28},{1,5},{5,9},{9,... | collective-permute-start | bytes 221192 | tf_op jit(solution)/shard_map/ppermute | solution.py:19
  18.6 3.3 copy-start.20
  18.6 3.3 copy-start.21
  18.6 3.4 copy-start.23
  18.6 3.4 copy-start.24
  21.9 152.0 %copy-start.25 = (pred[2]{0:T(512)(128)(4,1)}, pred[2]{0:T(512)(128)(4,1)S(1)}, u32[]{:S(2)}) copy-start(pred[2]{0:T(512)(128)(4,1)S(1)} %compare_and_fusion) | copy-start | bytes 10
  147.7 6.5 %copy-start.17 = (bf16[416,768]{1,0:T(8,128)(2,1)}, bf16[416,768]{1,0:T(8,128)(2,1)S(1)}, u32[]{:S(2)}) copy-start(bf16[416,768]{1,0:T(8,128)(2,1)S(1)} %fusion.68) | copy-start | bytes 1916932
  154.2 7.0 %copy-start.11 = (bf16[1,384,1536]{2,1,0:T(8,128)(2,1)S(1)}, bf16[1,384,1536]{2,1,0:T(8,128)(2,1)}, u32[]{:S(2)}) copy-start(bf16[1,384,1536]{2,1,0:T(8,128)(2,1)} %param.11) | copy-start | bytes 3538948
  164.8 7.6 %copy-start.13 = (bf16[384,768]{1,0:T(8,128)(2,1)}, bf16[384,768]{1,0:T(8,128)(2,1)S(1)}, u32[]{:S(2)}) copy-start(bf16[384,768]{1,0:T(8,128)(2,1)S(1)} %fusion.76) | copy-start | bytes 1769476
  164.8 7.6 %copy-start.6 = (bf16[416,1536]{1,0:T(8,128)(2,1)S(1)}, bf16[416,1536]{1,0:T(8,128)(2,1)}, u32[]{:S(2)}) copy-start(bf16[416,1536]{1,0:T(8,128)(2,1)} %get-tuple-element.17.refs_0_) | copy-start | bytes 3833860
  166.4 11.1 %collective-permute-start.3 = (bf16[16,768]{1,0:T(8,128)(2,1)S(1)}, bf16[16,768]{1,0:T(8,128)(2,1)S(1)}, u32[]{:S(2)}, u32[]{:S(2)}) collective-permute-start(bf16[16,768]{1,0:T(8,128)(2,1)S(1)} %get-tuple-element.26), channel_id=1, source_target_pairs={{4,0},{8,4},{12,8},{16,12},{20,16},{24,20},{28,24},{5,1},{9,5},{13... | collective-permute-start | bytes 73736 | tf_op jit(solution)/shard_map/ppermute | solution.py:22
  167.7 9.8 %collective-permute-start.2 = (bf16[16,768]{1,0:T(8,128)(2,1)S(1)}, bf16[16,768]{1,0:T(8,128)(2,1)S(1)}, u32[]{:S(2)}, u32[]{:S(2)}) collective-permute-start(bf16[16,768]{1,0:T(8,128)(2,1)S(1)} %get-tuple-element.25), channel_id=1, source_target_pairs={{0,4},{4,8},{8,12},{12,16},{16,20},{20,24},{24,28},{1,5},{5,9},{9,... | collective-permute-start | bytes 73736 | tf_op jit(solution)/shard_map/ppermute | solution.py:19
  178.4 7.2 %copy-start.12 = (bf16[1,384,1536]{2,1,0:T(8,128)(2,1)S(1)}, bf16[1,384,1536]{2,1,0:T(8,128)(2,1)}, u32[]{:S(2)}) copy-start(bf16[1,384,1536]{2,1,0:T(8,128)(2,1)} %param.11) | copy-start | bytes 3538948
  185.6 5.0 %copy-start.7 = (f32[416,768]{1,0:T(8,128)S(1)}, f32[416,768]{1,0:T(8,128)}, u32[]{:S(2)}) copy-start(f32[416,768]{1,0:T(8,128)} %shard_map.111) | copy-start | bytes 3833860
  185.6 5.0 %copy-start.27 = (f32[768]{0:T(1024)S(1)}, f32[768]{0:T(1024)}, u32[]{:S(2)}) copy-start(f32[768]{0:T(1024)} %get-tuple-element.13) | copy-start | bytes 9220
  209.0 15.0 %collective-permute-start.6 = (bf16[768,6144]{1,0:T(8,128)(2,1)}, bf16[768,6144]{1,0:T(8,128)(2,1)}, u32[]{:S(2)}, u32[]{:S(2)}) collective-permute-start(bf16[768,6144]{1,0:T(8,128)(2,1)} %shard_map.116), channel_id=1, source_target_pairs={{0,1},{1,0},{2,3},{3,2},{4,5},{5,4},{6,7},{7,6},{8,9},{9,8},{10,11... | collective-permute-start | bytes 28311560 | tf_op jit(solution)/shard_map/ppermute | solution.py:226
  236.3 7.4 %copy-start.5 = (bf16[384,768]{1,0:T(8,128)(2,1)S(1)}, bf16[384,768]{1,0:T(8,128)(2,1)}, u32[]{:S(2)}) copy-start(bf16[384,768]{1,0:T(8,128)(2,1)} %multiply_convert_fusion.refs_7_) | copy-start | bytes 1769476
  237.4 10.9 %collective-permute-start.5 = (bf16[8,768]{1,0:T(8,128)(2,1)S(1)}, bf16[8,768]{1,0:T(8,128)(2,1)S(1)}, u32[]{:S(2)}, u32[]{:S(2)}) collective-permute-start(bf16[8,768]{1,0:T(8,128)(2,1)S(1)} %get-tuple-element.24), channel_id=1, source_target_pairs={{4,0},{8,4},{12,8},{16,12},{20,16},{24,20},{28,24},{5,1},{9,5},{13... | collective-permute-start | bytes 36872 | tf_op jit(solution)/shard_map/ppermute | solution.py:22
  238.7 9.6 %collective-permute-start.4 = (bf16[8,768]{1,0:T(8,128)(2,1)S(1)}, bf16[8,768]{1,0:T(8,128)(2,1)S(1)}, u32[]{:S(2)}, u32[]{:S(2)}) collective-permute-start(bf16[8,768]{1,0:T(8,128)(2,1)S(1)} %get-tuple-element.23), channel_id=1, source_target_pairs={{0,4},{4,8},{8,12},{12,16},{16,20},{20,24},{24,28},{1,5},{5,9},{9,... | collective-permute-start | bytes 36872 | tf_op jit(solution)/shard_map/ppermute | solution.py:19
  249.2 7.3 %copy-start.1 = (f32[432,1536]{1,0:T(8,128)S(1)}, f32[432,1536]{1,0:T(8,128)}, u32[]{:S(2)}) copy-start(f32[432,1536]{1,0:T(8,128)} %get-tuple-element.19) | copy-start | bytes 7962628
  (13 other events, 24.0 us)
Sparse Core Ops, SparseCore 0:
  11.5 127.3 all-gather.1
  236.4 170.3 reduce-scatter.1

commit v10 on v9

--- a/solution.py
+++ b/solution.py
@@ -118,31 +118,47 @@
     )
 
 
-def gradient_kernel(scale, widths, *refs):
+def gradient_kernel(scale, layout, count, *refs):
     out_ref = refs[-1]
-    start = 0
-    for pair in range(len(widths)):
+    partner_refs = refs[2 * count : -1]
+    for pair, (start, width, source, offset) in enumerate(layout):
         lhs = refs[2 * pair][...]
         rhs = refs[2 * pair + 1][...]
-        term = jnp.dot(lhs, rhs, preferred_element_type=jnp.float32) * scale
-        out_ref[:, start : start + widths[pair]] = term.astype(out_ref.dtype)
-        start += widths[pair]
-
-
-def weight_gradient_buffer(pairs, inverse_square_root, first_tile, tiles, row_tile=256):
-    widths = tuple(rhs.shape[1] for _, rhs in pairs)
+        term = (jnp.dot(lhs, rhs, preferred_element_type=jnp.float32) * scale).astype(out_ref.dtype)
+        if source is not None:
+            term = (
+                term.astype(jnp.float32)
+                + partner_refs[source][:, offset : offset + width].astype(jnp.float32)
+            ).astype(out_ref.dtype)
+        out_ref[:, start : start + width] = term
+
+
+def weight_gradient_buffer(pairs, inverse_square_root, first_tile, tiles, partners=(), row_tile=256):
+    widths = [rhs.shape[1] for _, rhs in pairs]
+    layout = []
+    start = 0
+    for pair, width in enumerate(widths):
+        if partners:
+            source, offset = (0, start) if start < partners[0].shape[1] else (1, start - partners[0].shape[1])
+        else:
+            source, offset = None, 0
+        layout.append((start, width, source, offset))
+        start += width
     in_specs = []
     operands = []
     for lhs, rhs in pairs:
         in_specs.append(pl.BlockSpec((row_tile, lhs.shape[1]), lambda i: (i + first_tile, 0)))
         in_specs.append(pl.BlockSpec(rhs.shape, lambda i: (0, 0)))
         operands += [lhs, rhs]
+    for partner in partners:
+        in_specs.append(pl.BlockSpec((row_tile, partner.shape[1]), lambda i: (i, 0)))
+        operands.append(partner)
     return pl.pallas_call(
-        lambda *refs: gradient_kernel(inverse_square_root, widths, *refs),
+        lambda *refs: gradient_kernel(inverse_square_root, tuple(layout), len(pairs), *refs),
         grid=(tiles,),
         in_specs=in_specs,
-        out_specs=pl.BlockSpec((row_tile, sum(widths)), lambda i: (i, 0)),
-        out_shape=jax.ShapeDtypeStruct((tiles * row_tile, sum(widths)), jnp.bfloat16),
+        out_specs=pl.BlockSpec((row_tile, start), lambda i: (i, 0)),
+        out_shape=jax.ShapeDtypeStruct((tiles * row_tile, start), jnp.bfloat16),
     )(*operands)
 
 
@@ -203,6 +219,8 @@
     output = stream.astype(jnp.bfloat16)
     upstream_gradient = cot_local.astype(jnp.float32)
     dilated_weight_gradients = [None] * residual_block_count
+    partners = [None] * residual_block_count
+    row_tile = 256
     mixing_weight_gradients = [None] * residual_block_count
     for residual_block_index in reversed(range(residual_block_count)):
         dilation = dilation_steps[residual_block_index]
@@ -216,25 +234,24 @@
         d_act = conv_backward(d_pad, gathered, residual_block_index, c2, dilation, row_count)
         dilated_weight_gradients[residual_block_index] = (own_first(padded.T), shifted_taps(d_hidden, dilation))
         mixing_weight_gradients[residual_block_index] = (own_first(cot_here.T), middle)
+        block_pairs = [dilated_weight_gradients[residual_block_index], mixing_weight_gradients[residual_block_index]]
+        tiles = padded.shape[1] // (row_tile * lax.axis_size("core"))
+        partner_rows = weight_gradient_buffer(block_pairs, inverse_square_root, tiles, tiles, (), row_tile)
+        partners[residual_block_index] = lax.ppermute(partner_rows, "core", [(0, 1), (1, 0)])
         upstream_gradient = (
             upstream_gradient + gelu_back(pre_in, d_act) * in_scale[residual_block_index]
         )
-    pairs = dilated_weight_gradients + mixing_weight_gradients
-    row_tile = 256
-    tiles = pairs[0][0].shape[0] // (row_tile * lax.axis_size("core"))
-    partner_rows = weight_gradient_buffer(pairs, inverse_square_root, tiles, tiles, row_tile)
-    partner = lax.ppermute(partner_rows, "core", [(0, 1), (1, 0)])
-    own_rows = weight_gradient_buffer(pairs, inverse_square_root, 0, tiles, row_tile)
-    paired = (own_rows.astype(jnp.float32) + partner.astype(jnp.float32)).astype(jnp.bfloat16)
+    pairs = [p for b in range(residual_block_count) for p in (dilated_weight_gradients[b], mixing_weight_gradients[b])]
+    paired = weight_gradient_buffer(pairs, inverse_square_root, 0, tiles, tuple(partners), row_tile)
     summed = lax.psum_scatter(paired, ("seq", "y"), scatter_dimension=0, tiled=True).astype(jnp.float32)
     own_rows = summed.shape[0]
     taps, c2 = w_dilated.shape[2], w_dilated.shape[3]
-    split = residual_block_count * taps * c2
+    per_block = summed.reshape(own_rows, residual_block_count, (taps + 1) * c2).transpose(1, 0, 2)
     return (
         output[None],
         upstream_gradient[None],
-        summed[:, :split].reshape(own_rows, residual_block_count, taps, c2).transpose(1, 0, 2, 3),
-        summed[:, split:].reshape(own_rows, residual_block_count, c2).transpose(1, 0, 2),
+        per_block[:, :, : taps * c2].reshape(residual_block_count, own_rows, taps, c2),
+        per_block[:, :, taps * c2 :],
     )
 
 

time: 418 us -> 416 us (level)
  other arithmetic: 37.8 us -> 26.6 us
  Pallas kernels: 48.7 us -> 55.4 us
    convert_element_type x1 -> x0, other arithmetic: 12.3 us -> none  [per_device(): (own_rows.astype(jnp.float32) + partner.astype(jnp.float32)).astype(jnp.b...]
    pallas_call x2 -> x3, Pallas kernels: 20.1 us -> 26.7 us  [weight_gradient_buffer(): pl.pallas_call(lambda *refs: gradient_kernel(inverse_square_root, tuple(l...]
  transfers between devices with their start and end apart: 9 -> 10, of which waited for: 3 -> 4; matrix products, arithmetic and copies ran while one was open for 8% -> 8% of each run, Pallas kernels for 4% -> 3%
where the time goes in v10:
time: 416 us; the launch traced here: 415 us
  waiting for transfers between devices  257 us (62%)
  Pallas kernels  55.4 us (13%)
  other arithmetic  26.6 us (6%)
  local copies, waits for them, and re-layouts  23.3 us (6%)
  starting transfers between devices  19.7 us (5%)
  matrix products  17.9 us (4%)
  between operations  14.5 us (3%)
    reduce_scatter x1, waiting for transfers between devices, per_device(): lax.psum_scatter(paired, ('seq', 'y'), scatter_dimension=0, tiled=True)  145 us
    all_gather x1, waiting for transfers between devices, fetch_weights(): gathered = lax.all_gather(local, ALL, axis=0, tiled=True)  104 us
    pallas_call x3, Pallas kernels, weight_gradient_buffer(): pl.pallas_call(lambda *refs: gradient_kernel(inverse_square_root, tuple(l...  26.7 us
    ppermute x3, starting transfers between devices, padded_2(): lax.ppermute(lax.slice_in_dim(block, block.shape[dim] - width, None, axis...  15.3 us
    pallas_call x2, Pallas kernels, conv_backward(): pl.pallas_call(lambda *refs: conv_backward_kernel(dilation, out_rows, *re...  14.6 us
    pallas_call x2, Pallas kernels, conv_forward(): pl.pallas_call(lambda *refs: conv_forward_kernel(dilation, out_rows, *ref...  14.1 us
    dot_general x2, matrix products, per_device(): jnp.einsum('pe,ce->pc', middle, w_out, preferred_element_type=jnp.float32)  11 us
  transfers between devices with their start and end apart: 10, of which 4 were waited for; matrix products, arithmetic and copies ran while one was open for 8% of the time, Pallas kernels for 3%

profile of v10, /device:TPU:0, one launch (start us, length us, event | category | flops | bytes accessed | tf_op | source)
XLA Modules:
  0.0 414.7 jit_solution(13928675153599720951)
XLA Ops:
  11.7 5.5 %collective-permute-start = (bf16[24,1536]{1,0:T(8,128)(2,1)S(1)}, bf16[24,1536]{1,0:T(8,128)(2,1)S(1)}, u32[]{:S(2)}, u32[]{:S(2)}) collective-permute-start(bf16[24,1536]{1,0:T(8,128)(2,1)S(1)} %get-tuple-element.21), channel_id=1, source_target_pairs={{0,4},{4,8},{8,12},{12,16},{16,20},{20,24},{24,28},{1,5},{5,9},{9,... | collective-permute-start | bytes 221192 | tf_op jit(solution)/shard_map/ppermute | solution.py:19
  20.1 1.8 gather_fusion.3
  23.3 3.1 multiply_add_fusion
  30.5 2.1 gather_fusion
  34.4 104.4 %all-gather.2.cloned.1.call-done.refs_1_ = bf16[1536,6144]{1,0:T(8,128)(2,1)} async-done(((bf16[48,6144]{1,0:T(8,128)(2,1)}), bf16[1536,6144]{1,0:T(8,128)(2,1)}) %all-gather.2.cloned.1.call-update) | async-done | bytes 18874384 | tf_op jit(solution)/shard_map/all_gather | solution.py:110
  138.9 7.1 %shard_map.111 = f32[416,768]{1,0:T(8,128)} custom-call(bf16[432,1536]{1,0:T(8,128)(2,1)} %copy-done, bf16[1536,6144]{1,0:T(8,128)(2,1)} %all-gather.2.cloned.1.call-done.refs_1_, f32[1,768]{1,0:T(1,128)} %get-tuple-element.28.refs_2_, f32[1,768]{1,0:T(1,128)} %get-tuple-element.36.refs_3_), custom_call_target="tpu_custom_call" | custom-call | tf_op jit(solution)/shard_map/pallas_call | solution.py:75
  146.0 1.7 fusion.68
  147.7 6.5 %fusion.27 = (bf16[416,1536]{1,0:T(8,128)(2,1)}, f32[416,1536]{1,0:T(8,128)}, f32[416,1536]{1,0:T(8,128)}) fusion(pred[416]{0:T(512)(128)(4,1)S(1)} %fusion.98, f32[1536]{0:T(1024)S(1)} %get-tuple-element.11, f32[1536]{0:T(1024)S(1)} %get-tuple-element.35, bf16[416,768]{1,0:T(8,128)(2,1)S(1)} %fusion.68, ...), kind=kOutput, calls=%fused_computation.47 | convolution fusion | flops 989773824 | bytes 11956640 | tf_op jit(solution)/shard_map/pe,ce->pc/dot_general | solution.py:205
  154.2 7.0 %shard_map.112 = f32[384,768]{1,0:T(8,128)} custom-call(bf16[416,1536]{1,0:T(8,128)(2,1)} %get-tuple-element.17.refs_0_, bf16[1536,6144]{1,0:T(8,128)(2,1)} %all-gather.2.cloned.1.call-done.refs_1_, f32[1,768]{1,0:T(1,128)} %get-tuple-element.27.refs_2_, f32[1,768]{1,0:T(1,128)} %get-tuple-element.37.refs_3_), custom_call_target="tpu_custom_call" | custom-call | tf_op jit(solution)/shard_map/pallas_call | solution.py:75
  161.2 3.6 fusion.76
  167.6 4.7 %collective-permute-start.2 = (bf16[16,768]{1,0:T(8,128)(2,1)S(1)}, bf16[16,768]{1,0:T(8,128)(2,1)S(1)}, u32[]{:S(2)}, u32[]{:S(2)}) collective-permute-start(bf16[16,768]{1,0:T(8,128)(2,1)S(1)} %get-tuple-element.25), channel_id=1, source_target_pairs={{0,4},{4,8},{8,12},{12,16},{16,20},{20,24},{24,28},{1,5},{5,9},{9,... | collective-permute-start | bytes 73736 | tf_op jit(solution)/shard_map/ppermute | solution.py:19
  178.3 7.2 %shard_map.113 = f32[384,1536]{1,0:T(8,128)} custom-call(bf16[416,768]{1,0:T(8,128)(2,1)} %pad_maximum_fusion.refs_0_, bf16[1536,6144]{1,0:T(8,128)(2,1)} %all-gather.2.cloned.1.call-done.refs_1_), custom_call_target="tpu_custom_call" | custom-call | tf_op jit(solution)/shard_map/pallas_call | solution.py:91
  185.6 3.6 convert_bitcast_fusion
  190.6 3.3 fusion.84
  197.3 1.7 broadcast_select_fusion.2
  199.1 6.4 %shard_map.115 = bf16[768,3072]{1,0:T(8,128)(2,1)} custom-call(bf16[1536,400]{1,0:T(8,128)(2,1)} %bitcast.67, bf16[400,2304]{1,0:T(8,128)(2,1)} %fusion.57.refs_1_, bf16[1536,384]{1,0:T(8,128)(2,1)} %bitcast.71, bf16[384,768]{1,0:T(8,128)(2,1)} %slice.132.refs_3_), custom_call_target="tpu_custom_call" | custom-call | tf_op jit(solution)/shard_map/pallas_call | solution.py:156
  205.5 6.4 %shard_map.116 = bf16[768,3072]{1,0:T(8,128)(2,1)} custom-call(bf16[1536,416]{1,0:T(8,128)(2,1)} %bitcast.65, bf16[416,2304]{1,0:T(8,128)(2,1)} %fusion.55.refs_1_.refs_5_, bf16[1536,384]{1,0:T(8,128)(2,1)} %bitcast.69, bf16[384,768]{1,0:T(8,128)(2,1)} %multiply_convert_fusion.refs_3_.refs_7_), custom_call_target="tpu_custom_call" | custom-call | tf_op jit(solution)/shard_map/pallas_call | solution.py:156
  213.7 6.7 %collective-permute-done.7.refs_9_ = bf16[768,3072]{1,0:T(8,128)(2,1)} collective-permute-done((bf16[768,3072]{1,0:T(8,128)(2,1)}, bf16[768,3072]{1,0:T(8,128)(2,1)}, u32[]{:S(2)}, u32[]{:S(2)}) %collective-permute-start.7) | collective-permute-done | bytes 4718624 | tf_op jit(solution)/shard_map/ppermute | solution.py:240
  220.5 13.9 %shard_map.117 = bf16[768,6144]{1,0:T(8,128)(2,1)} custom-call(bf16[1536,400]{1,0:T(8,128)(2,1)} %bitcast.68, bf16[400,2304]{1,0:T(8,128)(2,1)} %fusion.57.refs_1_, bf16[1536,384]{1,0:T(8,128)(2,1)} %bitcast.72, bf16[384,768]{1,0:T(8,128)(2,1)} %slice.132.refs_3_, bf16[1536,416]{1,0:T(8,128)(2,1)} %bitcast.66, bf16[416,2304]{1,0:T(8,128)(2,1)} %fusion.55.refs_1_.refs_5_, ...), custom_call_target="tpu_custom_call" | custom-call | tf_op jit(solution)/shard_map/pallas_call | solution.py:156
  236.7 5.1 %collective-permute-start.4 = (bf16[8,768]{1,0:T(8,128)(2,1)S(1)}, bf16[8,768]{1,0:T(8,128)(2,1)S(1)}, u32[]{:S(2)}, u32[]{:S(2)}) collective-permute-start(bf16[8,768]{1,0:T(8,128)(2,1)S(1)} %get-tuple-element.23), channel_id=1, source_target_pairs={{0,4},{4,8},{8,12},{12,16},{16,20},{20,24},{24,28},{1,5},{5,9},{9,... | collective-permute-start | bytes 36872 | tf_op jit(solution)/shard_map/ppermute | solution.py:19
  241.8 4.5 %fusion.18 = bf16[1,384,1536]{2,1,0:T(8,128)(2,1)} fusion(bf16[384,768]{1,0:T(8,128)(2,1)S(1)} %copy-done.5, f32[416,1536]{1,0:T(8,128)} %get-tuple-element.33, bf16[1536,6144]{1,0:T(8,128)(2,1)} %all-gather.2.cloned.1.call-done.refs_1_), kind=kOutput, calls=%fused_computation.38 | convolution fusion | flops 907149312 | bytes 6488064 | tf_op jit(solution)/shard_map/pe,ce->pc/dot_general | solution.py:205
  247.2 7.4 %shard_map.114 = f32[384,1536]{1,0:T(8,128)} custom-call(bf16[400,768]{1,0:T(8,128)(2,1)} %pad_maximum_fusion.1.refs_0_, bf16[1536,6144]{1,0:T(8,128)(2,1)} %all-gather.2.cloned.1.call-done.refs_1_), custom_call_target="tpu_custom_call" | custom-call | tf_op jit(solution)/shard_map/pallas_call | solution.py:91
  254.6 5.6 %fusion.44 = f32[1,384,1536]{2,1,0:T(8,128)} fusion(f32[384,1536]{1,0:T(8,128)} %copy-done.2, f32[384,1536]{1,0:T(8,128)} %shard_map.114, f32[432,1536]{1,0:T(8,128)S(1)} %copy-done.1, f32[1536]{0:T(1024)S(1)} %get-tuple-element.34), kind=kLoop, calls=%fused_computation.66 | loop fusion | flops 12386304 | bytes 9443328 | tf_op jit(solution)/shard_map/broadcast_in_dim | solution.py:252
  260.2 144.7 %reduce-scatter.2.cloned.1.call-done = bf16[48,6144]{1,0:T(8,128)(2,1)} async-done(((bf16[768,6144]{1,0:T(8,128)(2,1)}), bf16[48,6144]{1,0:T(8,128)(2,1)}) %reduce-scatter.2.cloned.1.call-update) | async-done | bytes 589840 | tf_op jit(solution)/shard_map/reduce_scatter | solution.py:246
  (111 shorter events, 36.2 us)
Async XLA Ops:
  7.2 131.7 %all-gather.2.cloned.1.call-start = ((), (), s32[]{:S(2)}) async-start(), calls=%async_computation.1 | async-start | bytes 19464192 | tf_op jit(solution)/shard_map/all_gather | solution.py:110
  8.2 8.9 %copy-start.10 = (bf16[1,384,1536]{2,1,0:T(8,128)(2,1)S(1)}, bf16[1,384,1536]{2,1,0:T(8,128)(2,1)}, u32[]{:S(2)}) copy-start(bf16[1,384,1536]{2,1,0:T(8,128)(2,1)} %param.11) | copy-start | bytes 3538948
  10.3 394.6 %reduce-scatter.2.cloned.1.call-start = ((), (), s32[]{:S(2)}) async-start(), calls=%async_computation.2 | async-start | bytes 10027008 | tf_op jit(solution)/shard_map/reduce_scatter | solution.py:246
  10.4 12.9 %collective-permute-start.1 = (bf16[24,1536]{1,0:T(8,128)(2,1)S(1)}, bf16[24,1536]{1,0:T(8,128)(2,1)S(1)}, u32[]{:S(2)}, u32[]{:S(2)}) collective-permute-start(bf16[24,1536]{1,0:T(8,128)(2,1)S(1)} %get-tuple-element.22), channel_id=1, source_target_pairs={{4,0},{8,4},{12,8},{16,12},{20,16},{24,20},{28,24},{5,1},{9,5},{13... | collective-permute-start | bytes 221192 | tf_op jit(solution)/shard_map/ppermute | solution.py:22
  11.7 11.6 %collective-permute-start = (bf16[24,1536]{1,0:T(8,128)(2,1)S(1)}, bf16[24,1536]{1,0:T(8,128)(2,1)S(1)}, u32[]{:S(2)}, u32[]{:S(2)}) collective-permute-start(bf16[24,1536]{1,0:T(8,128)(2,1)S(1)} %get-tuple-element.21), channel_id=1, source_target_pairs={{0,4},{4,8},{8,12},{12,16},{16,20},{20,24},{24,28},{1,5},{5,9},{9,... | collective-permute-start | bytes 221192 | tf_op jit(solution)/shard_map/ppermute | solution.py:19
  18.6 3.3 copy-start.20
  18.6 3.4 copy-start.22
  18.6 3.4 copy-start.23
  21.9 152.0 %copy-start.24 = (pred[2]{0:T(512)(128)(4,1)}, pred[2]{0:T(512)(128)(4,1)S(1)}, u32[]{:S(2)}) copy-start(pred[2]{0:T(512)(128)(4,1)S(1)} %compare_and_fusion) | copy-start | bytes 10
  147.7 6.5 %copy-start.17 = (bf16[416,768]{1,0:T(8,128)(2,1)}, bf16[416,768]{1,0:T(8,128)(2,1)S(1)}, u32[]{:S(2)}) copy-start(bf16[416,768]{1,0:T(8,128)(2,1)S(1)} %fusion.68) | copy-start | bytes 1916932
  154.2 7.0 %copy-start.11 = (bf16[1,384,1536]{2,1,0:T(8,128)(2,1)S(1)}, bf16[1,384,1536]{2,1,0:T(8,128)(2,1)}, u32[]{:S(2)}) copy-start(bf16[1,384,1536]{2,1,0:T(8,128)(2,1)} %param.11) | copy-start | bytes 3538948
  164.8 7.5 %copy-start.13 = (bf16[384,768]{1,0:T(8,128)(2,1)}, bf16[384,768]{1,0:T(8,128)(2,1)S(1)}, u32[]{:S(2)}) copy-start(bf16[384,768]{1,0:T(8,128)(2,1)S(1)} %fusion.76) | copy-start | bytes 1769476
  164.8 7.5 %copy-start.6 = (bf16[416,1536]{1,0:T(8,128)(2,1)S(1)}, bf16[416,1536]{1,0:T(8,128)(2,1)}, u32[]{:S(2)}) copy-start(bf16[416,1536]{1,0:T(8,128)(2,1)} %get-tuple-element.17.refs_0_) | copy-start | bytes 3833860
  166.3 11.1 %collective-permute-start.3 = (bf16[16,768]{1,0:T(8,128)(2,1)S(1)}, bf16[16,768]{1,0:T(8,128)(2,1)S(1)}, u32[]{:S(2)}, u32[]{:S(2)}) collective-permute-start(bf16[16,768]{1,0:T(8,128)(2,1)S(1)} %get-tuple-element.26), channel_id=1, source_target_pairs={{4,0},{8,4},{12,8},{16,12},{20,16},{24,20},{28,24},{5,1},{9,5},{13... | collective-permute-start | bytes 73736 | tf_op jit(solution)/shard_map/ppermute | solution.py:22
  167.6 9.8 %collective-permute-start.2 = (bf16[16,768]{1,0:T(8,128)(2,1)S(1)}, bf16[16,768]{1,0:T(8,128)(2,1)S(1)}, u32[]{:S(2)}, u32[]{:S(2)}) collective-permute-start(bf16[16,768]{1,0:T(8,128)(2,1)S(1)} %get-tuple-element.25), channel_id=1, source_target_pairs={{0,4},{4,8},{8,12},{12,16},{16,20},{20,24},{24,28},{1,5},{5,9},{9,... | collective-permute-start | bytes 73736 | tf_op jit(solution)/shard_map/ppermute | solution.py:19
  178.3 7.2 %copy-start.12 = (bf16[1,384,1536]{2,1,0:T(8,128)(2,1)S(1)}, bf16[1,384,1536]{2,1,0:T(8,128)(2,1)}, u32[]{:S(2)}) copy-start(bf16[1,384,1536]{2,1,0:T(8,128)(2,1)} %param.11) | copy-start | bytes 3538948
  185.6 5.0 %copy-start.7 = (f32[416,768]{1,0:T(8,128)S(1)}, f32[416,768]{1,0:T(8,128)}, u32[]{:S(2)}) copy-start(f32[416,768]{1,0:T(8,128)} %shard_map.111) | copy-start | bytes 3833860
  185.6 5.0 %copy-start.26 = (f32[768]{0:T(1024)S(1)}, f32[768]{0:T(1024)}, u32[]{:S(2)}) copy-start(f32[768]{0:T(1024)} %get-tuple-element.13) | copy-start | bytes 9220
  205.5 8.3 %collective-permute-start.6 = (bf16[768,3072]{1,0:T(8,128)(2,1)}, bf16[768,3072]{1,0:T(8,128)(2,1)}, u32[]{:S(2)}, u32[]{:S(2)}) collective-permute-start(bf16[768,3072]{1,0:T(8,128)(2,1)} %shard_map.115), channel_id=1, source_target_pairs={{0,1},{1,0},{2,3},{3,2},{4,5},{5,4},{6,7},{7,6},{8,9},{9,8},{10,11... | collective-permute-start | bytes 14155784 | tf_op jit(solution)/shard_map/ppermute | solution.py:240
  211.9 8.6 %collective-permute-start.7 = (bf16[768,3072]{1,0:T(8,128)(2,1)}, bf16[768,3072]{1,0:T(8,128)(2,1)}, u32[]{:S(2)}, u32[]{:S(2)}) collective-permute-start(bf16[768,3072]{1,0:T(8,128)(2,1)} %shard_map.116), channel_id=1, source_target_pairs={{0,1},{1,0},{2,3},{3,2},{4,5},{5,4},{6,7},{7,6},{8,9},{9,8},{10,11... | collective-permute-start | bytes 14155784 | tf_op jit(solution)/shard_map/ppermute | solution.py:240
  234.4 7.4 %copy-start.5 = (bf16[384,768]{1,0:T(8,128)(2,1)S(1)}, bf16[384,768]{1,0:T(8,128)(2,1)}, u32[]{:S(2)}) copy-start(bf16[384,768]{1,0:T(8,128)(2,1)} %multiply_convert_fusion.refs_3_.refs_7_) | copy-start | bytes 1769476
  235.4 10.9 %collective-permute-start.5 = (bf16[8,768]{1,0:T(8,128)(2,1)S(1)}, bf16[8,768]{1,0:T(8,128)(2,1)S(1)}, u32[]{:S(2)}, u32[]{:S(2)}) collective-permute-start(bf16[8,768]{1,0:T(8,128)(2,1)S(1)} %get-tuple-element.24), channel_id=1, source_target_pairs={{4,0},{8,4},{12,8},{16,12},{20,16},{24,20},{28,24},{5,1},{9,5},{13... | collective-permute-start | bytes 36872 | tf_op jit(solution)/shard_map/ppermute | solution.py:22
  236.7 9.6 %collective-permute-start.4 = (bf16[8,768]{1,0:T(8,128)(2,1)S(1)}, bf16[8,768]{1,0:T(8,128)(2,1)S(1)}, u32[]{:S(2)}, u32[]{:S(2)}) collective-permute-start(bf16[8,768]{1,0:T(8,128)(2,1)S(1)} %get-tuple-element.23), channel_id=1, source_target_pairs={{0,4},{4,8},{8,12},{12,16},{16,20},{20,24},{24,28},{1,5},{5,9},{9,... | collective-permute-start | bytes 36872 | tf_op jit(solution)/shard_map/ppermute | solution.py:19
  247.2 7.4 %copy-start.1 = (f32[432,1536]{1,0:T(8,128)S(1)}, f32[432,1536]{1,0:T(8,128)}, u32[]{:S(2)}) copy-start(f32[432,1536]{1,0:T(8,128)} %get-tuple-element.19) | copy-start | bytes 7962628
  (13 other events, 25.6 us)
Sparse Core Ops, SparseCore 0:
  11.5 127.3 all-gather.1
  234.5 170.2 reduce-scatter.1

commit v11 on v10

--- a/solution.py
+++ b/solution.py
@@ -118,47 +118,49 @@
     )
 
 
-def gradient_kernel(scale, layout, count, *refs):
+def gradient_kernel(scale, layout, count, has_partner, *refs):
     out_ref = refs[-1]
-    partner_refs = refs[2 * count : -1]
-    for pair, (start, width, source, offset) in enumerate(layout):
+    partner_ref = refs[2 * count] if has_partner else None
+    for pair, (start, width) in enumerate(layout):
         lhs = refs[2 * pair][...]
         rhs = refs[2 * pair + 1][...]
         term = (jnp.dot(lhs, rhs, preferred_element_type=jnp.float32) * scale).astype(out_ref.dtype)
-        if source is not None:
+        if has_partner:
             term = (
-                term.astype(jnp.float32)
-                + partner_refs[source][:, offset : offset + width].astype(jnp.float32)
+                term.astype(jnp.float32) + partner_ref[:, start : start + width].astype(jnp.float32)
             ).astype(out_ref.dtype)
         out_ref[:, start : start + width] = term
 
 
-def weight_gradient_buffer(pairs, inverse_square_root, first_tile, tiles, partners=(), row_tile=256):
-    widths = [rhs.shape[1] for _, rhs in pairs]
+def weight_gradient_buffer(
+    pairs, inverse_square_root, first_tile, tiles, partner=None, row_tile=256, column_block=0, into=None, blocks=1
+):
     layout = []
     start = 0
-    for pair, width in enumerate(widths):
-        if partners:
-            source, offset = (0, start) if start < partners[0].shape[1] else (1, start - partners[0].shape[1])
-        else:
-            source, offset = None, 0
-        layout.append((start, width, source, offset))
-        start += width
+    for _, rhs in pairs:
+        layout.append((start, rhs.shape[1]))
+        start += rhs.shape[1]
     in_specs = []
     operands = []
     for lhs, rhs in pairs:
         in_specs.append(pl.BlockSpec((row_tile, lhs.shape[1]), lambda i: (i + first_tile, 0)))
         in_specs.append(pl.BlockSpec(rhs.shape, lambda i: (0, 0)))
         operands += [lhs, rhs]
-    for partner in partners:
-        in_specs.append(pl.BlockSpec((row_tile, partner.shape[1]), lambda i: (i, 0)))
+    if partner is not None:
+        in_specs.append(pl.BlockSpec((row_tile, start), lambda i: (i, 0)))
         operands.append(partner)
+    aliases = {}
+    if into is not None:
+        in_specs.append(pl.BlockSpec(memory_space=pl.ANY))
+        operands.append(into)
+        aliases = {len(operands) - 1: 0}
     return pl.pallas_call(
-        lambda *refs: gradient_kernel(inverse_square_root, tuple(layout), len(pairs), *refs),
+        lambda *refs: gradient_kernel(inverse_square_root, tuple(layout), len(pairs), partner is not None, *refs),
         grid=(tiles,),
         in_specs=in_specs,
-        out_specs=pl.BlockSpec((row_tile, start), lambda i: (i, 0)),
-        out_shape=jax.ShapeDtypeStruct((tiles * row_tile, start), jnp.bfloat16),
+        out_specs=pl.BlockSpec((row_tile, start), lambda i: (i, column_block)),
+        out_shape=jax.ShapeDtypeStruct((tiles * row_tile, blocks * start), jnp.bfloat16),
+        input_output_aliases=aliases,
     )(*operands)
 
 
@@ -236,13 +238,24 @@
         mixing_weight_gradients[residual_block_index] = (own_first(cot_here.T), middle)
         block_pairs = [dilated_weight_gradients[residual_block_index], mixing_weight_gradients[residual_block_index]]
         tiles = padded.shape[1] // (row_tile * lax.axis_size("core"))
-        partner_rows = weight_gradient_buffer(block_pairs, inverse_square_root, tiles, tiles, (), row_tile)
+        partner_rows = weight_gradient_buffer(block_pairs, inverse_square_root, tiles, tiles, None, row_tile)
         partners[residual_block_index] = lax.ppermute(partner_rows, "core", [(0, 1), (1, 0)])
         upstream_gradient = (
             upstream_gradient + gelu_back(pre_in, d_act) * in_scale[residual_block_index]
         )
-    pairs = [p for b in range(residual_block_count) for p in (dilated_weight_gradients[b], mixing_weight_gradients[b])]
-    paired = weight_gradient_buffer(pairs, inverse_square_root, 0, tiles, tuple(partners), row_tile)
+    paired = None
+    for b in reversed(range(residual_block_count)):
+        paired = weight_gradient_buffer(
+            [dilated_weight_gradients[b], mixing_weight_gradients[b]],
+            inverse_square_root,
+            0,
+            tiles,
+            partners[b],
+            row_tile,
+            b,
+            paired,
+            residual_block_count,
+        )
     summed = lax.psum_scatter(paired, ("seq", "y"), scatter_dimension=0, tiled=True).astype(jnp.float32)
     own_rows = summed.shape[0]
     taps, c2 = w_dilated.shape[2], w_dilated.shape[3]

time: 416 us -> 411 us (0.988)
  waiting for transfers between devices: 257 us -> 251 us
    ppermute x2, waiting for transfers between devices: 8.08 us -> 1.31 us  [per_device(): lax.ppermute(partner_rows, 'core', [(0, 1), (1, 0)])]
    pallas_call x3 -> x4, Pallas kernels: 26.7 us -> 29.1 us  [weight_gradient_buffer(): pl.pallas_call(lambda *refs: gradient_kernel(inverse_square_root, tuple(l...]
  transfers between devices with their start and end apart: 10 -> 10, of which waited for: 4 -> 3; matrix products, arithmetic and copies ran while one was open for 8% -> 8% of each run, Pallas kernels for 3% -> 5%
where the time goes in v11:
time: 411 us
  waiting for transfers between devices  251 us (61%)
  Pallas kernels  57.9 us (14%)
  other arithmetic  26.5 us (6%)
  local copies, waits for them, and re-layouts  23.3 us (6%)
  starting transfers between devices  19.7 us (5%)
  matrix products  17.9 us (4%)
  between operations  14.5 us (4%)
    reduce_scatter x1, waiting for transfers between devices, per_device(): lax.psum_scatter(paired, ('seq', 'y'), scatter_dimension=0, tiled=True)  145 us
    all_gather x1, waiting for transfers between devices, fetch_weights(): gathered = lax.all_gather(local, ALL, axis=0, tiled=True)  104 us
    pallas_call x4, Pallas kernels, weight_gradient_buffer(): pl.pallas_call(lambda *refs: gradient_kernel(inverse_square_root, tuple(l...  29.1 us
    ppermute x3, starting transfers between devices, padded_2(): lax.ppermute(lax.slice_in_dim(block, block.shape[dim] - width, None, axis...  15.3 us
    pallas_call x2, Pallas kernels, conv_backward(): pl.pallas_call(lambda *refs: conv_backward_kernel(dilation, out_rows, *re...  14.6 us
    pallas_call x2, Pallas kernels, conv_forward(): pl.pallas_call(lambda *refs: conv_forward_kernel(dilation, out_rows, *ref...  14.1 us
    dot_general x2, matrix products, per_device(): jnp.einsum('pe,ce->pc', middle, w_out, preferred_element_type=jnp.float32)  11 us
  transfers between devices with their start and end apart: 10, of which 3 were waited for; matrix products, arithmetic and copies ran while one was open for 8% of the time, Pallas kernels for 5%

profile of v11, /device:TPU:0, one launch (start us, length us, event | category | flops | bytes accessed | tf_op | source)
XLA Modules:
  0.0 410.5 jit_solution(16642587738193370989)
XLA Ops:
  11.7 5.5 %collective-permute-start = (bf16[24,1536]{1,0:T(8,128)(2,1)S(1)}, bf16[24,1536]{1,0:T(8,128)(2,1)S(1)}, u32[]{:S(2)}, u32[]{:S(2)}) collective-permute-start(bf16[24,1536]{1,0:T(8,128)(2,1)S(1)} %get-tuple-element.21), channel_id=1, source_target_pairs={{0,4},{4,8},{8,12},{12,16},{16,20},{20,24},{24,28},{1,5},{5,9},{9,... | collective-permute-start | bytes 221192 | tf_op jit(solution)/shard_map/ppermute | solution.py:19
  20.1 1.8 gather_fusion.3
  23.3 3.0 multiply_add_fusion
  30.4 2.1 gather_fusion
  34.4 104.5 %all-gather.2.cloned.1.call-done.refs_1_ = bf16[1536,6144]{1,0:T(8,128)(2,1)} async-done(((bf16[48,6144]{1,0:T(8,128)(2,1)}), bf16[1536,6144]{1,0:T(8,128)(2,1)}) %all-gather.2.cloned.1.call-update) | async-done | bytes 18874384 | tf_op jit(solution)/shard_map/all_gather | solution.py:110
  138.9 7.1 %shard_map.111 = f32[416,768]{1,0:T(8,128)} custom-call(bf16[432,1536]{1,0:T(8,128)(2,1)} %copy-done, bf16[1536,6144]{1,0:T(8,128)(2,1)} %all-gather.2.cloned.1.call-done.refs_1_, f32[1,768]{1,0:T(1,128)} %get-tuple-element.28.refs_2_, f32[1,768]{1,0:T(1,128)} %get-tuple-element.36.refs_3_), custom_call_target="tpu_custom_call" | custom-call | tf_op jit(solution)/shard_map/pallas_call | solution.py:75
  146.0 1.7 fusion.68
  147.7 6.5 %fusion.27 = (bf16[416,1536]{1,0:T(8,128)(2,1)}, f32[416,1536]{1,0:T(8,128)}, f32[416,1536]{1,0:T(8,128)}) fusion(pred[416]{0:T(512)(128)(4,1)S(1)} %fusion.98, f32[1536]{0:T(1024)S(1)} %get-tuple-element.11, f32[1536]{0:T(1024)S(1)} %get-tuple-element.35, bf16[416,768]{1,0:T(8,128)(2,1)S(1)} %fusion.68, ...), kind=kOutput, calls=%fused_computation.47 | convolution fusion | flops 989773824 | bytes 11956640 | tf_op jit(solution)/shard_map/pe,ce->pc/dot_general | solution.py:207
  154.3 7.0 %shard_map.112 = f32[384,768]{1,0:T(8,128)} custom-call(bf16[416,1536]{1,0:T(8,128)(2,1)} %get-tuple-element.17.refs_0_, bf16[1536,6144]{1,0:T(8,128)(2,1)} %all-gather.2.cloned.1.call-done.refs_1_, f32[1,768]{1,0:T(1,128)} %get-tuple-element.27.refs_2_, f32[1,768]{1,0:T(1,128)} %get-tuple-element.37.refs_3_), custom_call_target="tpu_custom_call" | custom-call | tf_op jit(solution)/shard_map/pallas_call | solution.py:75
  161.3 3.6 fusion.76
  167.7 4.7 %collective-permute-start.2 = (bf16[16,768]{1,0:T(8,128)(2,1)S(1)}, bf16[16,768]{1,0:T(8,128)(2,1)S(1)}, u32[]{:S(2)}, u32[]{:S(2)}) collective-permute-start(bf16[16,768]{1,0:T(8,128)(2,1)S(1)} %get-tuple-element.25), channel_id=1, source_target_pairs={{0,4},{4,8},{8,12},{12,16},{16,20},{20,24},{24,28},{1,5},{5,9},{9,... | collective-permute-start | bytes 73736 | tf_op jit(solution)/shard_map/ppermute | solution.py:19
  178.4 7.2 %shard_map.113 = f32[384,1536]{1,0:T(8,128)} custom-call(bf16[416,768]{1,0:T(8,128)(2,1)} %pad_maximum_fusion.refs_0_, bf16[1536,6144]{1,0:T(8,128)(2,1)} %all-gather.2.cloned.1.call-done.refs_1_), custom_call_target="tpu_custom_call" | custom-call | tf_op jit(solution)/shard_map/pallas_call | solution.py:91
  185.7 3.6 convert_bitcast_fusion
  190.7 3.3 fusion.84
  197.4 1.7 broadcast_select_fusion.2
  199.1 6.4 %shard_map.116 = bf16[768,3072]{1,0:T(8,128)(2,1)} custom-call(bf16[1536,416]{1,0:T(8,128)(2,1)} %bitcast.65, bf16[416,2304]{1,0:T(8,128)(2,1)} %fusion.55.refs_1_, bf16[1536,384]{1,0:T(8,128)(2,1)} %bitcast.69, bf16[384,768]{1,0:T(8,128)(2,1)} %multiply_convert_fusion.refs_3_), custom_call_target="tpu_custom_call" | custom-call | tf_op jit(solution)/shard_map/pallas_call | solution.py:157
  205.6 6.5 %shard_map.115 = bf16[768,3072]{1,0:T(8,128)(2,1)} custom-call(bf16[1536,400]{1,0:T(8,128)(2,1)} %bitcast.67, bf16[400,2304]{1,0:T(8,128)(2,1)} %fusion.57.refs_1_, bf16[1536,384]{1,0:T(8,128)(2,1)} %bitcast.71, bf16[384,768]{1,0:T(8,128)(2,1)} %slice.132.refs_3_), custom_call_target="tpu_custom_call" | custom-call | tf_op jit(solution)/shard_map/pallas_call | solution.py:157
  213.8 8.1 %shard_map.117.refs_5_ = bf16[768,6144]{1,0:T(8,128)(2,1)} custom-call(bf16[1536,416]{1,0:T(8,128)(2,1)} %bitcast.66, bf16[416,2304]{1,0:T(8,128)(2,1)} %fusion.55.refs_1_, bf16[1536,384]{1,0:T(8,128)(2,1)} %bitcast.70, bf16[384,768]{1,0:T(8,128)(2,1)} %multiply_convert_fusion.refs_3_, bf16[768,3072]{1,0:T(8,128)(2,1)} %collective-permute-done.7.refs_4_), custom_call_target="tpu_custom_call" | custom-call | tf_op jit(solution)/shard_map/pallas_call | solution.py:157
  221.9 8.1 %shard_map.118 = bf16[768,6144]{1,0:T(8,128)(2,1)} custom-call(bf16[1536,400]{1,0:T(8,128)(2,1)} %bitcast.68, bf16[400,2304]{1,0:T(8,128)(2,1)} %fusion.57.refs_1_, bf16[1536,384]{1,0:T(8,128)(2,1)} %bitcast.72, bf16[384,768]{1,0:T(8,128)(2,1)} %slice.132.refs_3_, bf16[768,3072]{1,0:T(8,128)(2,1)} %collective-permute-done.6.refs_4_, ...), custom_call_target="tpu_custom_call", output_to_operand_aliasing={{}: (5, {})} | custom-call | tf_op jit(solution)/shard_map/pallas_call | solution.py:157
  232.4 5.1 %collective-permute-start.4 = (bf16[8,768]{1,0:T(8,128)(2,1)S(1)}, bf16[8,768]{1,0:T(8,128)(2,1)S(1)}, u32[]{:S(2)}, u32[]{:S(2)}) collective-permute-start(bf16[8,768]{1,0:T(8,128)(2,1)S(1)} %get-tuple-element.23), channel_id=1, source_target_pairs={{0,4},{4,8},{8,12},{12,16},{16,20},{20,24},{24,28},{1,5},{5,9},{9,... | collective-permute-start | bytes 36872 | tf_op jit(solution)/shard_map/ppermute | solution.py:19
  237.5 4.5 %fusion.18 = bf16[1,384,1536]{2,1,0:T(8,128)(2,1)} fusion(bf16[384,768]{1,0:T(8,128)(2,1)S(1)} %copy-done.5, f32[416,1536]{1,0:T(8,128)} %get-tuple-element.33, bf16[1536,6144]{1,0:T(8,128)(2,1)} %all-gather.2.cloned.1.call-done.refs_1_), kind=kOutput, calls=%fused_computation.38 | convolution fusion | flops 907149312 | bytes 6488064 | tf_op jit(solution)/shard_map/pe,ce->pc/dot_general | solution.py:207
  242.9 7.4 %shard_map.114 = f32[384,1536]{1,0:T(8,128)} custom-call(bf16[400,768]{1,0:T(8,128)(2,1)} %pad_maximum_fusion.1.refs_0_, bf16[1536,6144]{1,0:T(8,128)(2,1)} %all-gather.2.cloned.1.call-done.refs_1_), custom_call_target="tpu_custom_call" | custom-call | tf_op jit(solution)/shard_map/pallas_call | solution.py:91
  250.3 5.5 %fusion.44 = f32[1,384,1536]{2,1,0:T(8,128)} fusion(f32[384,1536]{1,0:T(8,128)} %copy-done.2, f32[384,1536]{1,0:T(8,128)} %shard_map.114, f32[432,1536]{1,0:T(8,128)S(1)} %copy-done.1, f32[1536]{0:T(1024)S(1)} %get-tuple-element.34), kind=kLoop, calls=%fused_computation.66 | loop fusion | flops 12386304 | bytes 9443328 | tf_op jit(solution)/shard_map/broadcast_in_dim | solution.py:265
  255.8 144.8 %reduce-scatter.2.cloned.1.call-done = bf16[48,6144]{1,0:T(8,128)(2,1)} async-done(((bf16[768,6144]{1,0:T(8,128)(2,1)}), bf16[48,6144]{1,0:T(8,128)(2,1)}) %reduce-scatter.2.cloned.1.call-update) | async-done | bytes 589840 | tf_op jit(solution)/shard_map/reduce_scatter | solution.py:259
  (112 shorter events, 36.3 us)
Async XLA Ops:
  7.2 131.7 %all-gather.2.cloned.1.call-start = ((), (), s32[]{:S(2)}) async-start(), calls=%async_computation.1 | async-start | bytes 19464192 | tf_op jit(solution)/shard_map/all_gather | solution.py:110
  8.2 8.9 %copy-start.10 = (bf16[1,384,1536]{2,1,0:T(8,128)(2,1)S(1)}, bf16[1,384,1536]{2,1,0:T(8,128)(2,1)}, u32[]{:S(2)}) copy-start(bf16[1,384,1536]{2,1,0:T(8,128)(2,1)} %param.11) | copy-start | bytes 3538948
  10.3 390.3 %reduce-scatter.2.cloned.1.call-start = ((), (), s32[]{:S(2)}) async-start(), calls=%async_computation.2 | async-start | bytes 10027008 | tf_op jit(solution)/shard_map/reduce_scatter | solution.py:259
  10.4 12.9 %collective-permute-start.1 = (bf16[24,1536]{1,0:T(8,128)(2,1)S(1)}, bf16[24,1536]{1,0:T(8,128)(2,1)S(1)}, u32[]{:S(2)}, u32[]{:S(2)}) collective-permute-start(bf16[24,1536]{1,0:T(8,128)(2,1)S(1)} %get-tuple-element.22), channel_id=1, source_target_pairs={{4,0},{8,4},{12,8},{16,12},{20,16},{24,20},{28,24},{5,1},{9,5},{13... | collective-permute-start | bytes 221192 | tf_op jit(solution)/shard_map/ppermute | solution.py:22
  11.7 11.6 %collective-permute-start = (bf16[24,1536]{1,0:T(8,128)(2,1)S(1)}, bf16[24,1536]{1,0:T(8,128)(2,1)S(1)}, u32[]{:S(2)}, u32[]{:S(2)}) collective-permute-start(bf16[24,1536]{1,0:T(8,128)(2,1)S(1)} %get-tuple-element.21), channel_id=1, source_target_pairs={{0,4},{4,8},{8,12},{12,16},{16,20},{20,24},{24,28},{1,5},{5,9},{9,... | collective-permute-start | bytes 221192 | tf_op jit(solution)/shard_map/ppermute | solution.py:19
  18.6 3.3 copy-start.20
  18.6 3.4 copy-start.22
  18.6 3.4 copy-start.23
  21.9 152.0 %copy-start.24 = (pred[2]{0:T(512)(128)(4,1)}, pred[2]{0:T(512)(128)(4,1)S(1)}, u32[]{:S(2)}) copy-start(pred[2]{0:T(512)(128)(4,1)S(1)} %compare_and_fusion) | copy-start | bytes 10
  147.7 6.5 %copy-start.17 = (bf16[416,768]{1,0:T(8,128)(2,1)}, bf16[416,768]{1,0:T(8,128)(2,1)S(1)}, u32[]{:S(2)}) copy-start(bf16[416,768]{1,0:T(8,128)(2,1)S(1)} %fusion.68) | copy-start | bytes 1916932
  154.3 7.0 %copy-start.11 = (bf16[1,384,1536]{2,1,0:T(8,128)(2,1)S(1)}, bf16[1,384,1536]{2,1,0:T(8,128)(2,1)}, u32[]{:S(2)}) copy-start(bf16[1,384,1536]{2,1,0:T(8,128)(2,1)} %param.11) | copy-start | bytes 3538948
  164.8 7.6 %copy-start.13 = (bf16[384,768]{1,0:T(8,128)(2,1)}, bf16[384,768]{1,0:T(8,128)(2,1)S(1)}, u32[]{:S(2)}) copy-start(bf16[384,768]{1,0:T(8,128)(2,1)S(1)} %fusion.76) | copy-start | bytes 1769476
  164.9 7.6 %copy-start.6 = (bf16[416,1536]{1,0:T(8,128)(2,1)S(1)}, bf16[416,1536]{1,0:T(8,128)(2,1)}, u32[]{:S(2)}) copy-start(bf16[416,1536]{1,0:T(8,128)(2,1)} %get-tuple-element.17.refs_0_) | copy-start | bytes 3833860
  166.4 11.2 %collective-permute-start.3 = (bf16[16,768]{1,0:T(8,128)(2,1)S(1)}, bf16[16,768]{1,0:T(8,128)(2,1)S(1)}, u32[]{:S(2)}, u32[]{:S(2)}) collective-permute-start(bf16[16,768]{1,0:T(8,128)(2,1)S(1)} %get-tuple-element.26), channel_id=1, source_target_pairs={{4,0},{8,4},{12,8},{16,12},{20,16},{24,20},{28,24},{5,1},{9,5},{13... | collective-permute-start | bytes 73736 | tf_op jit(solution)/shard_map/ppermute | solution.py:22
  167.7 9.9 %collective-permute-start.2 = (bf16[16,768]{1,0:T(8,128)(2,1)S(1)}, bf16[16,768]{1,0:T(8,128)(2,1)S(1)}, u32[]{:S(2)}, u32[]{:S(2)}) collective-permute-start(bf16[16,768]{1,0:T(8,128)(2,1)S(1)} %get-tuple-element.25), channel_id=1, source_target_pairs={{0,4},{4,8},{8,12},{12,16},{16,20},{20,24},{24,28},{1,5},{5,9},{9,... | collective-permute-start | bytes 73736 | tf_op jit(solution)/shard_map/ppermute | solution.py:19
  178.4 7.2 %copy-start.12 = (bf16[1,384,1536]{2,1,0:T(8,128)(2,1)S(1)}, bf16[1,384,1536]{2,1,0:T(8,128)(2,1)}, u32[]{:S(2)}) copy-start(bf16[1,384,1536]{2,1,0:T(8,128)(2,1)} %param.11) | copy-start | bytes 3538948
  185.7 5.0 %copy-start.7 = (f32[416,768]{1,0:T(8,128)S(1)}, f32[416,768]{1,0:T(8,128)}, u32[]{:S(2)}) copy-start(f32[416,768]{1,0:T(8,128)} %shard_map.111) | copy-start | bytes 3833860
  185.7 5.0 %copy-start.26 = (f32[768]{0:T(1024)S(1)}, f32[768]{0:T(1024)}, u32[]{:S(2)}) copy-start(f32[768]{0:T(1024)} %get-tuple-element.13) | copy-start | bytes 9220
  205.6 8.3 %collective-permute-start.7 = (bf16[768,3072]{1,0:T(8,128)(2,1)}, bf16[768,3072]{1,0:T(8,128)(2,1)}, u32[]{:S(2)}, u32[]{:S(2)}) collective-permute-start(bf16[768,3072]{1,0:T(8,128)(2,1)} %shard_map.116), channel_id=1, source_target_pairs={{0,1},{1,0},{2,3},{3,2},{4,5},{5,4},{6,7},{7,6},{8,9},{9,8},{10,11... | collective-permute-start | bytes 14155784 | tf_op jit(solution)/shard_map/ppermute | solution.py:242
  212.1 9.9 %collective-permute-start.6 = (bf16[768,3072]{1,0:T(8,128)(2,1)}, bf16[768,3072]{1,0:T(8,128)(2,1)}, u32[]{:S(2)}, u32[]{:S(2)}) collective-permute-start(bf16[768,3072]{1,0:T(8,128)(2,1)} %shard_map.115), channel_id=1, source_target_pairs={{0,1},{1,0},{2,3},{3,2},{4,5},{5,4},{6,7},{7,6},{8,9},{9,8},{10,11... | collective-permute-start | bytes 14155784 | tf_op jit(solution)/shard_map/ppermute | solution.py:242
  230.1 7.4 %copy-start.5 = (bf16[384,768]{1,0:T(8,128)(2,1)S(1)}, bf16[384,768]{1,0:T(8,128)(2,1)}, u32[]{:S(2)}) copy-start(bf16[384,768]{1,0:T(8,128)(2,1)} %multiply_convert_fusion.refs_3_) | copy-start | bytes 1769476
  231.1 10.9 %collective-permute-start.5 = (bf16[8,768]{1,0:T(8,128)(2,1)S(1)}, bf16[8,768]{1,0:T(8,128)(2,1)S(1)}, u32[]{:S(2)}, u32[]{:S(2)}) collective-permute-start(bf16[8,768]{1,0:T(8,128)(2,1)S(1)} %get-tuple-element.24), channel_id=1, source_target_pairs={{4,0},{8,4},{12,8},{16,12},{20,16},{24,20},{28,24},{5,1},{9,5},{13... | collective-permute-start | bytes 36872 | tf_op jit(solution)/shard_map/ppermute | solution.py:22
  232.4 9.6 %collective-permute-start.4 = (bf16[8,768]{1,0:T(8,128)(2,1)S(1)}, bf16[8,768]{1,0:T(8,128)(2,1)S(1)}, u32[]{:S(2)}, u32[]{:S(2)}) collective-permute-start(bf16[8,768]{1,0:T(8,128)(2,1)S(1)} %get-tuple-element.23), channel_id=1, source_target_pairs={{0,4},{4,8},{8,12},{12,16},{16,20},{20,24},{24,28},{1,5},{5,9},{9,... | collective-permute-start | bytes 36872 | tf_op jit(solution)/shard_map/ppermute | solution.py:19
  242.9 7.4 %copy-start.1 = (f32[432,1536]{1,0:T(8,128)S(1)}, f32[432,1536]{1,0:T(8,128)}, u32[]{:S(2)}) copy-start(f32[432,1536]{1,0:T(8,128)} %get-tuple-element.19) | copy-start | bytes 7962628
  (13 other events, 25.5 us)
Sparse Core Ops, SparseCore 0:
  11.5 127.3 all-gather.1
  230.2 170.3 reduce-scatter.1

commit v12 on v11

--- a/solution.py
+++ b/solution.py
@@ -222,7 +222,7 @@
     upstream_gradient = cot_local.astype(jnp.float32)
     dilated_weight_gradients = [None] * residual_block_count
     partners = [None] * residual_block_count
-    row_tile = 256
+    row_tile = 384
     mixing_weight_gradients = [None] * residual_block_count
     for residual_block_index in reversed(range(residual_block_count)):
         dilation = dilation_steps[residual_block_index]

time: 411 us -> 409 us (level)
  no operation moved by 1% of the time
where the time goes in v12:
time: 409 us; the launch traced here: 408 us
  waiting for transfers between devices  251 us (61%)
  Pallas kernels  55.4 us (14%)
  other arithmetic  26.6 us (7%)
  local copies, waits for them, and re-layouts  23.3 us (6%)
  starting transfers between devices  19.5 us (5%)
  matrix products  17.9 us (4%)
  between operations  14.5 us (4%)
    reduce_scatter x1, waiting for transfers between devices, per_device(): lax.psum_scatter(paired, ('seq', 'y'), scatter_dimension=0, tiled=True)  145 us
    all_gather x1, waiting for transfers between devices, fetch_weights(): gathered = lax.all_gather(local, ALL, axis=0, tiled=True)  104 us
    pallas_call x4, Pallas kernels, weight_gradient_buffer(): pl.pallas_call(lambda *refs: gradient_kernel(inverse_square_root, tuple(l...  26.7 us
    ppermute x3, starting transfers between devices, padded_2(): lax.ppermute(lax.slice_in_dim(block, block.shape[dim] - width, None, axis...  15.1 us
    pallas_call x2, Pallas kernels, conv_backward(): pl.pallas_call(lambda *refs: conv_backward_kernel(dilation, out_rows, *re...  14.6 us
    pallas_call x2, Pallas kernels, conv_forward(): pl.pallas_call(lambda *refs: conv_forward_kernel(dilation, out_rows, *ref...  14.1 us
    dot_general x2, matrix products, per_device(): jnp.einsum('pe,ce->pc', middle, w_out, preferred_element_type=jnp.float32)  11 us
  transfers between devices with their start and end apart: 10, of which 3 were waited for; matrix products, arithmetic and copies ran while one was open for 8% of the time, Pallas kernels for 5%

profile of v12, /device:TPU:0, one launch (start us, length us, event | category | flops | bytes accessed | tf_op | source)
XLA Modules:
  0.0 408.2 jit_solution(14467819389050733843)
XLA Ops:
  11.7 5.5 %collective-permute-start = (bf16[24,1536]{1,0:T(8,128)(2,1)S(1)}, bf16[24,1536]{1,0:T(8,128)(2,1)S(1)}, u32[]{:S(2)}, u32[]{:S(2)}) collective-permute-start(bf16[24,1536]{1,0:T(8,128)(2,1)S(1)} %get-tuple-element.21), channel_id=1, source_target_pairs={{0,4},{4,8},{8,12},{12,16},{16,20},{20,24},{24,28},{1,5},{5,9},{9,... | collective-permute-start | bytes 221192 | tf_op jit(solution)/shard_map/ppermute | solution.py:19
  20.1 1.8 gather_fusion.3
  23.3 3.0 multiply_add_fusion
  30.4 2.1 gather_fusion
  34.4 104.5 %all-gather.2.cloned.1.call-done.refs_1_ = bf16[1536,6144]{1,0:T(8,128)(2,1)} async-done(((bf16[48,6144]{1,0:T(8,128)(2,1)}), bf16[1536,6144]{1,0:T(8,128)(2,1)}) %all-gather.2.cloned.1.call-update) | async-done | bytes 18874384 | tf_op jit(solution)/shard_map/all_gather | solution.py:110
  138.9 7.1 %shard_map.111 = f32[416,768]{1,0:T(8,128)} custom-call(bf16[432,1536]{1,0:T(8,128)(2,1)} %copy-done, bf16[1536,6144]{1,0:T(8,128)(2,1)} %all-gather.2.cloned.1.call-done.refs_1_, f32[1,768]{1,0:T(1,128)} %get-tuple-element.28.refs_2_, f32[1,768]{1,0:T(1,128)} %get-tuple-element.36.refs_3_), custom_call_target="tpu_custom_call" | custom-call | tf_op jit(solution)/shard_map/pallas_call | solution.py:75
  146.0 1.7 fusion.68
  147.7 6.5 %fusion.27 = (bf16[416,1536]{1,0:T(8,128)(2,1)}, f32[416,1536]{1,0:T(8,128)}, f32[416,1536]{1,0:T(8,128)}) fusion(pred[416]{0:T(512)(128)(4,1)S(1)} %fusion.98, f32[1536]{0:T(1024)S(1)} %get-tuple-element.11, f32[1536]{0:T(1024)S(1)} %get-tuple-element.35, bf16[416,768]{1,0:T(8,128)(2,1)S(1)} %fusion.68, ...), kind=kOutput, calls=%fused_computation.47 | convolution fusion | flops 989773824 | bytes 11956640 | tf_op jit(solution)/shard_map/pe,ce->pc/dot_general | solution.py:207
  154.3 7.0 %shard_map.112 = f32[384,768]{1,0:T(8,128)} custom-call(bf16[416,1536]{1,0:T(8,128)(2,1)} %get-tuple-element.17.refs_0_, bf16[1536,6144]{1,0:T(8,128)(2,1)} %all-gather.2.cloned.1.call-done.refs_1_, f32[1,768]{1,0:T(1,128)} %get-tuple-element.27.refs_2_, f32[1,768]{1,0:T(1,128)} %get-tuple-element.37.refs_3_), custom_call_target="tpu_custom_call" | custom-call | tf_op jit(solution)/shard_map/pallas_call | solution.py:75
  161.3 3.6 fusion.76
  167.7 4.7 %collective-permute-start.2 = (bf16[16,768]{1,0:T(8,128)(2,1)S(1)}, bf16[16,768]{1,0:T(8,128)(2,1)S(1)}, u32[]{:S(2)}, u32[]{:S(2)}) collective-permute-start(bf16[16,768]{1,0:T(8,128)(2,1)S(1)} %get-tuple-element.25), channel_id=1, source_target_pairs={{0,4},{4,8},{8,12},{12,16},{16,20},{20,24},{24,28},{1,5},{5,9},{9,... | collective-permute-start | bytes 73736 | tf_op jit(solution)/shard_map/ppermute | solution.py:19
  178.4 7.2 %shard_map.113 = f32[384,1536]{1,0:T(8,128)} custom-call(bf16[416,768]{1,0:T(8,128)(2,1)} %pad_maximum_fusion.refs_0_, bf16[1536,6144]{1,0:T(8,128)(2,1)} %all-gather.2.cloned.1.call-done.refs_1_), custom_call_target="tpu_custom_call" | custom-call | tf_op jit(solution)/shard_map/pallas_call | solution.py:91
  185.7 3.6 convert_bitcast_fusion
  190.7 3.3 fusion.84
  197.4 1.7 broadcast_select_fusion.2
  199.1 6.1 %shard_map.116 = bf16[768,3072]{1,0:T(8,128)(2,1)} custom-call(bf16[1536,416]{1,0:T(8,128)(2,1)} %bitcast.65, bf16[416,2304]{1,0:T(8,128)(2,1)} %fusion.55.refs_1_, bf16[1536,384]{1,0:T(8,128)(2,1)} %bitcast.69, bf16[384,768]{1,0:T(8,128)(2,1)} %multiply_convert_fusion.refs_3_), custom_call_target="tpu_custom_call" | custom-call | tf_op jit(solution)/shard_map/pallas_call | solution.py:157
  205.2 6.1 %shard_map.115 = bf16[768,3072]{1,0:T(8,128)(2,1)} custom-call(bf16[1536,400]{1,0:T(8,128)(2,1)} %bitcast.67, bf16[400,2304]{1,0:T(8,128)(2,1)} %fusion.57.refs_1_, bf16[1536,384]{1,0:T(8,128)(2,1)} %bitcast.71, bf16[384,768]{1,0:T(8,128)(2,1)} %slice.132.refs_3_), custom_call_target="tpu_custom_call" | custom-call | tf_op jit(solution)/shard_map/pallas_call | solution.py:157
  213.5 7.1 %shard_map.117.refs_5_ = bf16[768,6144]{1,0:T(8,128)(2,1)} custom-call(bf16[1536,416]{1,0:T(8,128)(2,1)} %bitcast.66, bf16[416,2304]{1,0:T(8,128)(2,1)} %fusion.55.refs_1_, bf16[1536,384]{1,0:T(8,128)(2,1)} %bitcast.70, bf16[384,768]{1,0:T(8,128)(2,1)} %multiply_convert_fusion.refs_3_, bf16[768,3072]{1,0:T(8,128)(2,1)} %collective-permute-done.7.refs_4_), custom_call_target="tpu_custom_call" | custom-call | tf_op jit(solution)/shard_map/pallas_call | solution.py:157
  220.6 7.4 %shard_map.118 = bf16[768,6144]{1,0:T(8,128)(2,1)} custom-call(bf16[1536,400]{1,0:T(8,128)(2,1)} %bitcast.68, bf16[400,2304]{1,0:T(8,128)(2,1)} %fusion.57.refs_1_, bf16[1536,384]{1,0:T(8,128)(2,1)} %bitcast.72, bf16[384,768]{1,0:T(8,128)(2,1)} %slice.132.refs_3_, bf16[768,3072]{1,0:T(8,128)(2,1)} %collective-permute-done.6.refs_4_, ...), custom_call_target="tpu_custom_call", output_to_operand_aliasing={{}: (5, {})} | custom-call | tf_op jit(solution)/shard_map/pallas_call | solution.py:157
  230.3 4.9 %collective-permute-start.4 = (bf16[8,768]{1,0:T(8,128)(2,1)S(1)}, bf16[8,768]{1,0:T(8,128)(2,1)S(1)}, u32[]{:S(2)}, u32[]{:S(2)}) collective-permute-start(bf16[8,768]{1,0:T(8,128)(2,1)S(1)} %get-tuple-element.23), channel_id=1, source_target_pairs={{0,4},{4,8},{8,12},{12,16},{16,20},{20,24},{24,28},{1,5},{5,9},{9,... | collective-permute-start | bytes 36872 | tf_op jit(solution)/shard_map/ppermute | solution.py:19
  235.2 4.5 %fusion.18 = bf16[1,384,1536]{2,1,0:T(8,128)(2,1)} fusion(bf16[384,768]{1,0:T(8,128)(2,1)S(1)} %copy-done.5, f32[416,1536]{1,0:T(8,128)} %get-tuple-element.33, bf16[1536,6144]{1,0:T(8,128)(2,1)} %all-gather.2.cloned.1.call-done.refs_1_), kind=kOutput, calls=%fused_computation.38 | convolution fusion | flops 907149312 | bytes 6488064 | tf_op jit(solution)/shard_map/pe,ce->pc/dot_general | solution.py:207
  240.6 7.4 %shard_map.114 = f32[384,1536]{1,0:T(8,128)} custom-call(bf16[400,768]{1,0:T(8,128)(2,1)} %pad_maximum_fusion.1.refs_0_, bf16[1536,6144]{1,0:T(8,128)(2,1)} %all-gather.2.cloned.1.call-done.refs_1_), custom_call_target="tpu_custom_call" | custom-call | tf_op jit(solution)/shard_map/pallas_call | solution.py:91
  248.0 5.6 %fusion.44 = f32[1,384,1536]{2,1,0:T(8,128)} fusion(f32[384,1536]{1,0:T(8,128)} %copy-done.2, f32[384,1536]{1,0:T(8,128)} %shard_map.114, f32[432,1536]{1,0:T(8,128)S(1)} %copy-done.1, f32[1536]{0:T(1024)S(1)} %get-tuple-element.34), kind=kLoop, calls=%fused_computation.66 | loop fusion | flops 12386304 | bytes 9443328 | tf_op jit(solution)/shard_map/broadcast_in_dim | solution.py:265
  253.6 144.7 %reduce-scatter.2.cloned.1.call-done = bf16[48,6144]{1,0:T(8,128)(2,1)} async-done(((bf16[768,6144]{1,0:T(8,128)(2,1)}), bf16[48,6144]{1,0:T(8,128)(2,1)}) %reduce-scatter.2.cloned.1.call-update) | async-done | bytes 589840 | tf_op jit(solution)/shard_map/reduce_scatter | solution.py:259
  (112 shorter events, 36.6 us)
Async XLA Ops:
  7.2 131.7 %all-gather.2.cloned.1.call-start = ((), (), s32[]{:S(2)}) async-start(), calls=%async_computation.1 | async-start | bytes 19464192 | tf_op jit(solution)/shard_map/all_gather | solution.py:110
  8.2 8.9 %copy-start.10 = (bf16[1,384,1536]{2,1,0:T(8,128)(2,1)S(1)}, bf16[1,384,1536]{2,1,0:T(8,128)(2,1)}, u32[]{:S(2)}) copy-start(bf16[1,384,1536]{2,1,0:T(8,128)(2,1)} %param.11) | copy-start | bytes 3538948
  10.3 388.0 %reduce-scatter.2.cloned.1.call-start = ((), (), s32[]{:S(2)}) async-start(), calls=%async_computation.2 | async-start | bytes 10027008 | tf_op jit(solution)/shard_map/reduce_scatter | solution.py:259
  10.4 12.9 %collective-permute-start.1 = (bf16[24,1536]{1,0:T(8,128)(2,1)S(1)}, bf16[24,1536]{1,0:T(8,128)(2,1)S(1)}, u32[]{:S(2)}, u32[]{:S(2)}) collective-permute-start(bf16[24,1536]{1,0:T(8,128)(2,1)S(1)} %get-tuple-element.22), channel_id=1, source_target_pairs={{4,0},{8,4},{12,8},{16,12},{20,16},{24,20},{28,24},{5,1},{9,5},{13... | collective-permute-start | bytes 221192 | tf_op jit(solution)/shard_map/ppermute | solution.py:22
  11.7 11.6 %collective-permute-start = (bf16[24,1536]{1,0:T(8,128)(2,1)S(1)}, bf16[24,1536]{1,0:T(8,128)(2,1)S(1)}, u32[]{:S(2)}, u32[]{:S(2)}) collective-permute-start(bf16[24,1536]{1,0:T(8,128)(2,1)S(1)} %get-tuple-element.21), channel_id=1, source_target_pairs={{0,4},{4,8},{8,12},{12,16},{16,20},{20,24},{24,28},{1,5},{5,9},{9,... | collective-permute-start | bytes 221192 | tf_op jit(solution)/shard_map/ppermute | solution.py:19
  18.6 3.3 copy-start.20
  18.6 3.4 copy-start.22
  18.6 3.4 copy-start.23
  21.9 152.0 %copy-start.24 = (pred[2]{0:T(512)(128)(4,1)}, pred[2]{0:T(512)(128)(4,1)S(1)}, u32[]{:S(2)}) copy-start(pred[2]{0:T(512)(128)(4,1)S(1)} %compare_and_fusion) | copy-start | bytes 10
  147.7 6.5 %copy-start.17 = (bf16[416,768]{1,0:T(8,128)(2,1)}, bf16[416,768]{1,0:T(8,128)(2,1)S(1)}, u32[]{:S(2)}) copy-start(bf16[416,768]{1,0:T(8,128)(2,1)S(1)} %fusion.68) | copy-start | bytes 1916932
  154.3 7.0 %copy-start.11 = (bf16[1,384,1536]{2,1,0:T(8,128)(2,1)S(1)}, bf16[1,384,1536]{2,1,0:T(8,128)(2,1)}, u32[]{:S(2)}) copy-start(bf16[1,384,1536]{2,1,0:T(8,128)(2,1)} %param.11) | copy-start | bytes 3538948
  164.8 7.6 %copy-start.13 = (bf16[384,768]{1,0:T(8,128)(2,1)}, bf16[384,768]{1,0:T(8,128)(2,1)S(1)}, u32[]{:S(2)}) copy-start(bf16[384,768]{1,0:T(8,128)(2,1)S(1)} %fusion.76) | copy-start | bytes 1769476
  164.9 7.6 %copy-start.6 = (bf16[416,1536]{1,0:T(8,128)(2,1)S(1)}, bf16[416,1536]{1,0:T(8,128)(2,1)}, u32[]{:S(2)}) copy-start(bf16[416,1536]{1,0:T(8,128)(2,1)} %get-tuple-element.17.refs_0_) | copy-start | bytes 3833860
  166.4 11.2 %collective-permute-start.3 = (bf16[16,768]{1,0:T(8,128)(2,1)S(1)}, bf16[16,768]{1,0:T(8,128)(2,1)S(1)}, u32[]{:S(2)}, u32[]{:S(2)}) collective-permute-start(bf16[16,768]{1,0:T(8,128)(2,1)S(1)} %get-tuple-element.26), channel_id=1, source_target_pairs={{4,0},{8,4},{12,8},{16,12},{20,16},{24,20},{28,24},{5,1},{9,5},{13... | collective-permute-start | bytes 73736 | tf_op jit(solution)/shard_map/ppermute | solution.py:22
  167.7 9.9 %collective-permute-start.2 = (bf16[16,768]{1,0:T(8,128)(2,1)S(1)}, bf16[16,768]{1,0:T(8,128)(2,1)S(1)}, u32[]{:S(2)}, u32[]{:S(2)}) collective-permute-start(bf16[16,768]{1,0:T(8,128)(2,1)S(1)} %get-tuple-element.25), channel_id=1, source_target_pairs={{0,4},{4,8},{8,12},{12,16},{16,20},{20,24},{24,28},{1,5},{5,9},{9,... | collective-permute-start | bytes 73736 | tf_op jit(solution)/shard_map/ppermute | solution.py:19
  178.4 7.2 %copy-start.12 = (bf16[1,384,1536]{2,1,0:T(8,128)(2,1)S(1)}, bf16[1,384,1536]{2,1,0:T(8,128)(2,1)}, u32[]{:S(2)}) copy-start(bf16[1,384,1536]{2,1,0:T(8,128)(2,1)} %param.11) | copy-start | bytes 3538948
  185.7 5.0 %copy-start.7 = (f32[416,768]{1,0:T(8,128)S(1)}, f32[416,768]{1,0:T(8,128)}, u32[]{:S(2)}) copy-start(f32[416,768]{1,0:T(8,128)} %shard_map.111) | copy-start | bytes 3833860
  185.7 5.0 %copy-start.26 = (f32[768]{0:T(1024)S(1)}, f32[768]{0:T(1024)}, u32[]{:S(2)}) copy-start(f32[768]{0:T(1024)} %get-tuple-element.13) | copy-start | bytes 9220
  205.2 8.3 %collective-permute-start.7 = (bf16[768,3072]{1,0:T(8,128)(2,1)}, bf16[768,3072]{1,0:T(8,128)(2,1)}, u32[]{:S(2)}, u32[]{:S(2)}) collective-permute-start(bf16[768,3072]{1,0:T(8,128)(2,1)} %shard_map.116), channel_id=1, source_target_pairs={{0,1},{1,0},{2,3},{3,2},{4,5},{5,4},{6,7},{7,6},{8,9},{9,8},{10,11... | collective-permute-start | bytes 14155784 | tf_op jit(solution)/shard_map/ppermute | solution.py:242
  211.4 9.2 %collective-permute-start.6 = (bf16[768,3072]{1,0:T(8,128)(2,1)}, bf16[768,3072]{1,0:T(8,128)(2,1)}, u32[]{:S(2)}, u32[]{:S(2)}) collective-permute-start(bf16[768,3072]{1,0:T(8,128)(2,1)} %shard_map.115), channel_id=1, source_target_pairs={{0,1},{1,0},{2,3},{3,2},{4,5},{5,4},{6,7},{7,6},{8,9},{9,8},{10,11... | collective-permute-start | bytes 14155784 | tf_op jit(solution)/shard_map/ppermute | solution.py:242
  228.0 7.2 %copy-start.5 = (bf16[384,768]{1,0:T(8,128)(2,1)S(1)}, bf16[384,768]{1,0:T(8,128)(2,1)}, u32[]{:S(2)}) copy-start(bf16[384,768]{1,0:T(8,128)(2,1)} %multiply_convert_fusion.refs_3_) | copy-start | bytes 1769476
  229.0 10.7 %collective-permute-start.5 = (bf16[8,768]{1,0:T(8,128)(2,1)S(1)}, bf16[8,768]{1,0:T(8,128)(2,1)S(1)}, u32[]{:S(2)}, u32[]{:S(2)}) collective-permute-start(bf16[8,768]{1,0:T(8,128)(2,1)S(1)} %get-tuple-element.24), channel_id=1, source_target_pairs={{4,0},{8,4},{12,8},{16,12},{20,16},{24,20},{28,24},{5,1},{9,5},{13... | collective-permute-start | bytes 36872 | tf_op jit(solution)/shard_map/ppermute | solution.py:22
  230.3 9.4 %collective-permute-start.4 = (bf16[8,768]{1,0:T(8,128)(2,1)S(1)}, bf16[8,768]{1,0:T(8,128)(2,1)S(1)}, u32[]{:S(2)}, u32[]{:S(2)}) collective-permute-start(bf16[8,768]{1,0:T(8,128)(2,1)S(1)} %get-tuple-element.23), channel_id=1, source_target_pairs={{0,4},{4,8},{8,12},{12,16},{16,20},{20,24},{24,28},{1,5},{5,9},{9,... | collective-permute-start | bytes 36872 | tf_op jit(solution)/shard_map/ppermute | solution.py:19
  240.6 7.4 %copy-start.1 = (f32[432,1536]{1,0:T(8,128)S(1)}, f32[432,1536]{1,0:T(8,128)}, u32[]{:S(2)}) copy-start(f32[432,1536]{1,0:T(8,128)} %get-tuple-element.19) | copy-start | bytes 7962628
  (13 other events, 25.5 us)
Sparse Core Ops, SparseCore 0:
  11.5 127.3 all-gather.1
  228.1 170.1 reduce-scatter.1

commit v13 on v12

--- a/solution.py
+++ b/solution.py
@@ -222,7 +222,7 @@
     upstream_gradient = cot_local.astype(jnp.float32)
     dilated_weight_gradients = [None] * residual_block_count
     partners = [None] * residual_block_count
-    row_tile = 384
+    row_tile = 768
     mixing_weight_gradients = [None] * residual_block_count
     for residual_block_index in reversed(range(residual_block_count)):
         dilation = dilation_steps[residual_block_index]

time: 409 us -> 412 us (level)
  transfers between devices with their start and end apart: 10 -> 10, of which waited for: 3 -> 3; matrix products, arithmetic and copies ran while one was open for 8% -> 8% of each run, Pallas kernels for 5% -> 6%
where the time goes in v13:
time: 412 us
  waiting for transfers between devices  250 us (61%)
  Pallas kernels  59.5 us (14%)
  other arithmetic  26.6 us (6%)
  local copies, waits for them, and re-layouts  23.3 us (6%)
  starting transfers between devices  19.5 us (5%)
  matrix products  17.9 us (4%)
  between operations  14.5 us (4%)
    reduce_scatter x1, waiting for transfers between devices, per_device(): lax.psum_scatter(paired, ('seq', 'y'), scatter_dimension=0, tiled=True)  145 us
    all_gather x1, waiting for transfers between devices, fetch_weights(): gathered = lax.all_gather(local, ALL, axis=0, tiled=True)  104 us
    pallas_call x4, Pallas kernels, weight_gradient_buffer(): pl.pallas_call(lambda *refs: gradient_kernel(inverse_square_root, tuple(l...  30.7 us
    ppermute x3, starting transfers between devices, padded_2(): lax.ppermute(lax.slice_in_dim(block, block.shape[dim] - width, None, axis...  15.1 us
    pallas_call x2, Pallas kernels, conv_backward(): pl.pallas_call(lambda *refs: conv_backward_kernel(dilation, out_rows, *re...  14.6 us
    pallas_call x2, Pallas kernels, conv_forward(): pl.pallas_call(lambda *refs: conv_forward_kernel(dilation, out_rows, *ref...  14.1 us
    dot_general x2, matrix products, per_device(): jnp.einsum('pe,ce->pc', middle, w_out, preferred_element_type=jnp.float32)  11 us
  transfers between devices with their start and end apart: 10, of which 3 were waited for; matrix products, arithmetic and copies ran while one was open for 8% of the time, Pallas kernels for 6%

profile of v13, /device:TPU:0, one launch (start us, length us, event | category | flops | bytes accessed | tf_op | source)
XLA Modules:
  0.0 411.7 jit_solution(17484732153373420392)
XLA Ops:
  11.7 5.5 %collective-permute-start = (bf16[24,1536]{1,0:T(8,128)(2,1)S(1)}, bf16[24,1536]{1,0:T(8,128)(2,1)S(1)}, u32[]{:S(2)}, u32[]{:S(2)}) collective-permute-start(bf16[24,1536]{1,0:T(8,128)(2,1)S(1)} %get-tuple-element.21), channel_id=1, source_target_pairs={{0,4},{4,8},{8,12},{12,16},{16,20},{20,24},{24,28},{1,5},{5,9},{9,... | collective-permute-start | bytes 221192 | tf_op jit(solution)/shard_map/ppermute | solution.py:19
  20.1 1.8 gather_fusion.3
  23.3 3.0 multiply_add_fusion
  30.4 2.1 gather_fusion
  34.4 104.5 %all-gather.2.cloned.1.call-done.refs_1_ = bf16[1536,6144]{1,0:T(8,128)(2,1)} async-done(((bf16[48,6144]{1,0:T(8,128)(2,1)}), bf16[1536,6144]{1,0:T(8,128)(2,1)}) %all-gather.2.cloned.1.call-update) | async-done | bytes 18874384 | tf_op jit(solution)/shard_map/all_gather | solution.py:110
  138.9 7.1 %shard_map.111 = f32[416,768]{1,0:T(8,128)} custom-call(bf16[432,1536]{1,0:T(8,128)(2,1)} %copy-done, bf16[1536,6144]{1,0:T(8,128)(2,1)} %all-gather.2.cloned.1.call-done.refs_1_, f32[1,768]{1,0:T(1,128)} %get-tuple-element.28.refs_2_, f32[1,768]{1,0:T(1,128)} %get-tuple-element.36.refs_3_), custom_call_target="tpu_custom_call" | custom-call | tf_op jit(solution)/shard_map/pallas_call | solution.py:75
  146.0 1.7 fusion.68
  147.7 6.5 %fusion.27 = (bf16[416,1536]{1,0:T(8,128)(2,1)}, f32[416,1536]{1,0:T(8,128)}, f32[416,1536]{1,0:T(8,128)}) fusion(pred[416]{0:T(512)(128)(4,1)S(1)} %fusion.98, f32[1536]{0:T(1024)S(1)} %get-tuple-element.11, f32[1536]{0:T(1024)S(1)} %get-tuple-element.35, bf16[416,768]{1,0:T(8,128)(2,1)S(1)} %fusion.68, ...), kind=kOutput, calls=%fused_computation.47 | convolution fusion | flops 989773824 | bytes 11956640 | tf_op jit(solution)/shard_map/pe,ce->pc/dot_general | solution.py:207
  154.3 7.0 %shard_map.112 = f32[384,768]{1,0:T(8,128)} custom-call(bf16[416,1536]{1,0:T(8,128)(2,1)} %get-tuple-element.17.refs_0_, bf16[1536,6144]{1,0:T(8,128)(2,1)} %all-gather.2.cloned.1.call-done.refs_1_, f32[1,768]{1,0:T(1,128)} %get-tuple-element.27.refs_2_, f32[1,768]{1,0:T(1,128)} %get-tuple-element.37.refs_3_), custom_call_target="tpu_custom_call" | custom-call | tf_op jit(solution)/shard_map/pallas_call | solution.py:75
  161.3 3.6 fusion.76
  167.7 4.7 %collective-permute-start.2 = (bf16[16,768]{1,0:T(8,128)(2,1)S(1)}, bf16[16,768]{1,0:T(8,128)(2,1)S(1)}, u32[]{:S(2)}, u32[]{:S(2)}) collective-permute-start(bf16[16,768]{1,0:T(8,128)(2,1)S(1)} %get-tuple-element.25), channel_id=1, source_target_pairs={{0,4},{4,8},{8,12},{12,16},{16,20},{20,24},{24,28},{1,5},{5,9},{9,... | collective-permute-start | bytes 73736 | tf_op jit(solution)/shard_map/ppermute | solution.py:19
  178.4 7.2 %shard_map.113 = f32[384,1536]{1,0:T(8,128)} custom-call(bf16[416,768]{1,0:T(8,128)(2,1)} %pad_maximum_fusion.refs_0_, bf16[1536,6144]{1,0:T(8,128)(2,1)} %all-gather.2.cloned.1.call-done.refs_1_), custom_call_target="tpu_custom_call" | custom-call | tf_op jit(solution)/shard_map/pallas_call | solution.py:91
  185.7 3.6 convert_bitcast_fusion
  190.7 3.3 fusion.84
  197.4 1.7 broadcast_select_fusion.2
  199.1 6.9 %shard_map.116 = bf16[768,3072]{1,0:T(8,128)(2,1)} custom-call(bf16[1536,416]{1,0:T(8,128)(2,1)} %bitcast.65, bf16[416,2304]{1,0:T(8,128)(2,1)} %fusion.55.refs_1_, bf16[1536,384]{1,0:T(8,128)(2,1)} %bitcast.69, bf16[384,768]{1,0:T(8,128)(2,1)} %multiply_convert_fusion.refs_3_), custom_call_target="tpu_custom_call" | custom-call | tf_op jit(solution)/shard_map/pallas_call | solution.py:157
  206.0 6.9 %shard_map.115 = bf16[768,3072]{1,0:T(8,128)(2,1)} custom-call(bf16[1536,400]{1,0:T(8,128)(2,1)} %bitcast.67, bf16[400,2304]{1,0:T(8,128)(2,1)} %fusion.57.refs_1_, bf16[1536,384]{1,0:T(8,128)(2,1)} %bitcast.71, bf16[384,768]{1,0:T(8,128)(2,1)} %slice.132.refs_3_), custom_call_target="tpu_custom_call" | custom-call | tf_op jit(solution)/shard_map/pallas_call | solution.py:157
  214.3 8.5 %shard_map.117.refs_5_ = bf16[768,6144]{1,0:T(8,128)(2,1)} custom-call(bf16[1536,416]{1,0:T(8,128)(2,1)} %bitcast.66, bf16[416,2304]{1,0:T(8,128)(2,1)} %fusion.55.refs_1_, bf16[1536,384]{1,0:T(8,128)(2,1)} %bitcast.70, bf16[384,768]{1,0:T(8,128)(2,1)} %multiply_convert_fusion.refs_3_, bf16[768,3072]{1,0:T(8,128)(2,1)} %collective-permute-done.7.refs_4_), custom_call_target="tpu_custom_call" | custom-call | tf_op jit(solution)/shard_map/pallas_call | solution.py:157
  222.7 8.5 %shard_map.118 = bf16[768,6144]{1,0:T(8,128)(2,1)} custom-call(bf16[1536,400]{1,0:T(8,128)(2,1)} %bitcast.68, bf16[400,2304]{1,0:T(8,128)(2,1)} %fusion.57.refs_1_, bf16[1536,384]{1,0:T(8,128)(2,1)} %bitcast.72, bf16[384,768]{1,0:T(8,128)(2,1)} %slice.132.refs_3_, bf16[768,3072]{1,0:T(8,128)(2,1)} %collective-permute-done.6.refs_4_, ...), custom_call_target="tpu_custom_call", output_to_operand_aliasing={{}: (5, {})} | custom-call | tf_op jit(solution)/shard_map/pallas_call | solution.py:157
  233.6 4.9 %collective-permute-start.4 = (bf16[8,768]{1,0:T(8,128)(2,1)S(1)}, bf16[8,768]{1,0:T(8,128)(2,1)S(1)}, u32[]{:S(2)}, u32[]{:S(2)}) collective-permute-start(bf16[8,768]{1,0:T(8,128)(2,1)S(1)} %get-tuple-element.23), channel_id=1, source_target_pairs={{0,4},{4,8},{8,12},{12,16},{16,20},{20,24},{24,28},{1,5},{5,9},{9,... | collective-permute-start | bytes 36872 | tf_op jit(solution)/shard_map/ppermute | solution.py:19
  238.5 4.5 %fusion.18 = bf16[1,384,1536]{2,1,0:T(8,128)(2,1)} fusion(bf16[384,768]{1,0:T(8,128)(2,1)S(1)} %copy-done.5, f32[416,1536]{1,0:T(8,128)} %get-tuple-element.33, bf16[1536,6144]{1,0:T(8,128)(2,1)} %all-gather.2.cloned.1.call-done.refs_1_), kind=kOutput, calls=%fused_computation.38 | convolution fusion | flops 907149312 | bytes 6488064 | tf_op jit(solution)/shard_map/pe,ce->pc/dot_general | solution.py:207
  243.9 7.4 %shard_map.114 = f32[384,1536]{1,0:T(8,128)} custom-call(bf16[400,768]{1,0:T(8,128)(2,1)} %pad_maximum_fusion.1.refs_0_, bf16[1536,6144]{1,0:T(8,128)(2,1)} %all-gather.2.cloned.1.call-done.refs_1_), custom_call_target="tpu_custom_call" | custom-call | tf_op jit(solution)/shard_map/pallas_call | solution.py:91
  251.3 5.6 %fusion.44 = f32[1,384,1536]{2,1,0:T(8,128)} fusion(f32[384,1536]{1,0:T(8,128)} %copy-done.2, f32[384,1536]{1,0:T(8,128)} %shard_map.114, f32[432,1536]{1,0:T(8,128)S(1)} %copy-done.1, f32[1536]{0:T(1024)S(1)} %get-tuple-element.34), kind=kLoop, calls=%fused_computation.66 | loop fusion | flops 12386304 | bytes 9443328 | tf_op jit(solution)/shard_map/broadcast_in_dim | solution.py:265
  256.9 144.9 %reduce-scatter.2.cloned.1.call-done = bf16[48,6144]{1,0:T(8,128)(2,1)} async-done(((bf16[768,6144]{1,0:T(8,128)(2,1)}), bf16[48,6144]{1,0:T(8,128)(2,1)}) %reduce-scatter.2.cloned.1.call-update) | async-done | bytes 589840 | tf_op jit(solution)/shard_map/reduce_scatter | solution.py:259
  (112 shorter events, 35.8 us)
Async XLA Ops:
  7.2 131.7 %all-gather.2.cloned.1.call-start = ((), (), s32[]{:S(2)}) async-start(), calls=%async_computation.1 | async-start | bytes 19464192 | tf_op jit(solution)/shard_map/all_gather | solution.py:110
  8.2 8.9 %copy-start.10 = (bf16[1,384,1536]{2,1,0:T(8,128)(2,1)S(1)}, bf16[1,384,1536]{2,1,0:T(8,128)(2,1)}, u32[]{:S(2)}) copy-start(bf16[1,384,1536]{2,1,0:T(8,128)(2,1)} %param.11) | copy-start | bytes 3538948
  10.3 391.5 %reduce-scatter.2.cloned.1.call-start = ((), (), s32[]{:S(2)}) async-start(), calls=%async_computation.2 | async-start | bytes 10027008 | tf_op jit(solution)/shard_map/reduce_scatter | solution.py:259
  10.4 12.9 %collective-permute-start.1 = (bf16[24,1536]{1,0:T(8,128)(2,1)S(1)}, bf16[24,1536]{1,0:T(8,128)(2,1)S(1)}, u32[]{:S(2)}, u32[]{:S(2)}) collective-permute-start(bf16[24,1536]{1,0:T(8,128)(2,1)S(1)} %get-tuple-element.22), channel_id=1, source_target_pairs={{4,0},{8,4},{12,8},{16,12},{20,16},{24,20},{28,24},{5,1},{9,5},{13... | collective-permute-start | bytes 221192 | tf_op jit(solution)/shard_map/ppermute | solution.py:22
  11.7 11.6 %collective-permute-start = (bf16[24,1536]{1,0:T(8,128)(2,1)S(1)}, bf16[24,1536]{1,0:T(8,128)(2,1)S(1)}, u32[]{:S(2)}, u32[]{:S(2)}) collective-permute-start(bf16[24,1536]{1,0:T(8,128)(2,1)S(1)} %get-tuple-element.21), channel_id=1, source_target_pairs={{0,4},{4,8},{8,12},{12,16},{16,20},{20,24},{24,28},{1,5},{5,9},{9,... | collective-permute-start | bytes 221192 | tf_op jit(solution)/shard_map/ppermute | solution.py:19
  18.6 3.3 copy-start.20
  18.6 3.4 copy-start.22
  18.6 3.4 copy-start.23
  21.9 152.0 %copy-start.24 = (pred[2]{0:T(512)(128)(4,1)}, pred[2]{0:T(512)(128)(4,1)S(1)}, u32[]{:S(2)}) copy-start(pred[2]{0:T(512)(128)(4,1)S(1)} %compare_and_fusion) | copy-start | bytes 10
  147.7 6.5 %copy-start.17 = (bf16[416,768]{1,0:T(8,128)(2,1)}, bf16[416,768]{1,0:T(8,128)(2,1)S(1)}, u32[]{:S(2)}) copy-start(bf16[416,768]{1,0:T(8,128)(2,1)S(1)} %fusion.68) | copy-start | bytes 1916932
  154.3 7.0 %copy-start.11 = (bf16[1,384,1536]{2,1,0:T(8,128)(2,1)S(1)}, bf16[1,384,1536]{2,1,0:T(8,128)(2,1)}, u32[]{:S(2)}) copy-start(bf16[1,384,1536]{2,1,0:T(8,128)(2,1)} %param.11) | copy-start | bytes 3538948
  164.8 7.6 %copy-start.13 = (bf16[384,768]{1,0:T(8,128)(2,1)}, bf16[384,768]{1,0:T(8,128)(2,1)S(1)}, u32[]{:S(2)}) copy-start(bf16[384,768]{1,0:T(8,128)(2,1)S(1)} %fusion.76) | copy-start | bytes 1769476
  164.9 7.6 %copy-start.6 = (bf16[416,1536]{1,0:T(8,128)(2,1)S(1)}, bf16[416,1536]{1,0:T(8,128)(2,1)}, u32[]{:S(2)}) copy-start(bf16[416,1536]{1,0:T(8,128)(2,1)} %get-tuple-element.17.refs_0_) | copy-start | bytes 3833860
  166.4 11.2 %collective-permute-start.3 = (bf16[16,768]{1,0:T(8,128)(2,1)S(1)}, bf16[16,768]{1,0:T(8,128)(2,1)S(1)}, u32[]{:S(2)}, u32[]{:S(2)}) collective-permute-start(bf16[16,768]{1,0:T(8,128)(2,1)S(1)} %get-tuple-element.26), channel_id=1, source_target_pairs={{4,0},{8,4},{12,8},{16,12},{20,16},{24,20},{28,24},{5,1},{9,5},{13... | collective-permute-start | bytes 73736 | tf_op jit(solution)/shard_map/ppermute | solution.py:22
  167.7 9.9 %collective-permute-start.2 = (bf16[16,768]{1,0:T(8,128)(2,1)S(1)}, bf16[16,768]{1,0:T(8,128)(2,1)S(1)}, u32[]{:S(2)}, u32[]{:S(2)}) collective-permute-start(bf16[16,768]{1,0:T(8,128)(2,1)S(1)} %get-tuple-element.25), channel_id=1, source_target_pairs={{0,4},{4,8},{8,12},{12,16},{16,20},{20,24},{24,28},{1,5},{5,9},{9,... | collective-permute-start | bytes 73736 | tf_op jit(solution)/shard_map/ppermute | solution.py:19
  178.4 7.2 %copy-start.12 = (bf16[1,384,1536]{2,1,0:T(8,128)(2,1)S(1)}, bf16[1,384,1536]{2,1,0:T(8,128)(2,1)}, u32[]{:S(2)}) copy-start(bf16[1,384,1536]{2,1,0:T(8,128)(2,1)} %param.11) | copy-start | bytes 3538948
  185.7 5.0 %copy-start.7 = (f32[416,768]{1,0:T(8,128)S(1)}, f32[416,768]{1,0:T(8,128)}, u32[]{:S(2)}) copy-start(f32[416,768]{1,0:T(8,128)} %shard_map.111) | copy-start | bytes 3833860
  185.7 5.0 %copy-start.26 = (f32[768]{0:T(1024)S(1)}, f32[768]{0:T(1024)}, u32[]{:S(2)}) copy-start(f32[768]{0:T(1024)} %get-tuple-element.13) | copy-start | bytes 9220
  206.0 8.3 %collective-permute-start.7 = (bf16[768,3072]{1,0:T(8,128)(2,1)}, bf16[768,3072]{1,0:T(8,128)(2,1)}, u32[]{:S(2)}, u32[]{:S(2)}) collective-permute-start(bf16[768,3072]{1,0:T(8,128)(2,1)} %shard_map.116), channel_id=1, source_target_pairs={{0,1},{1,0},{2,3},{3,2},{4,5},{5,4},{6,7},{7,6},{8,9},{9,8},{10,11... | collective-permute-start | bytes 14155784 | tf_op jit(solution)/shard_map/ppermute | solution.py:242
  212.9 9.9 %collective-permute-start.6 = (bf16[768,3072]{1,0:T(8,128)(2,1)}, bf16[768,3072]{1,0:T(8,128)(2,1)}, u32[]{:S(2)}, u32[]{:S(2)}) collective-permute-start(bf16[768,3072]{1,0:T(8,128)(2,1)} %shard_map.115), channel_id=1, source_target_pairs={{0,1},{1,0},{2,3},{3,2},{4,5},{5,4},{6,7},{7,6},{8,9},{9,8},{10,11... | collective-permute-start | bytes 14155784 | tf_op jit(solution)/shard_map/ppermute | solution.py:242
  231.3 7.2 %copy-start.5 = (bf16[384,768]{1,0:T(8,128)(2,1)S(1)}, bf16[384,768]{1,0:T(8,128)(2,1)}, u32[]{:S(2)}) copy-start(bf16[384,768]{1,0:T(8,128)(2,1)} %multiply_convert_fusion.refs_3_) | copy-start | bytes 1769476
  232.3 10.7 %collective-permute-start.5 = (bf16[8,768]{1,0:T(8,128)(2,1)S(1)}, bf16[8,768]{1,0:T(8,128)(2,1)S(1)}, u32[]{:S(2)}, u32[]{:S(2)}) collective-permute-start(bf16[8,768]{1,0:T(8,128)(2,1)S(1)} %get-tuple-element.24), channel_id=1, source_target_pairs={{4,0},{8,4},{12,8},{16,12},{20,16},{24,20},{28,24},{5,1},{9,5},{13... | collective-permute-start | bytes 36872 | tf_op jit(solution)/shard_map/ppermute | solution.py:22
  233.6 9.4 %collective-permute-start.4 = (bf16[8,768]{1,0:T(8,128)(2,1)S(1)}, bf16[8,768]{1,0:T(8,128)(2,1)S(1)}, u32[]{:S(2)}, u32[]{:S(2)}) collective-permute-start(bf16[8,768]{1,0:T(8,128)(2,1)S(1)} %get-tuple-element.23), channel_id=1, source_target_pairs={{0,4},{4,8},{8,12},{12,16},{16,20},{20,24},{24,28},{1,5},{5,9},{9,... | collective-permute-start | bytes 36872 | tf_op jit(solution)/shard_map/ppermute | solution.py:19
  243.9 7.4 %copy-start.1 = (f32[432,1536]{1,0:T(8,128)S(1)}, f32[432,1536]{1,0:T(8,128)}, u32[]{:S(2)}) copy-start(f32[432,1536]{1,0:T(8,128)} %get-tuple-element.19) | copy-start | bytes 7962628
  (13 other events, 25.5 us)
Sparse Core Ops, SparseCore 0:
  11.5 127.3 all-gather.1
  231.4 170.3 reduce-scatter.1

commit v14 on v12

--- a/solution.py
+++ b/solution.py
@@ -233,13 +233,14 @@
             jnp.bfloat16
         )
         d_pad = padded_2(d_hidden, (("seq", 0),), dilation)
-        d_act = conv_backward(d_pad, gathered, residual_block_index, c2, dilation, row_count)
         dilated_weight_gradients[residual_block_index] = (own_first(padded.T), shifted_taps(d_hidden, dilation))
         mixing_weight_gradients[residual_block_index] = (own_first(cot_here.T), middle)
         block_pairs = [dilated_weight_gradients[residual_block_index], mixing_weight_gradients[residual_block_index]]
         tiles = padded.shape[1] // (row_tile * lax.axis_size("core"))
         partner_rows = weight_gradient_buffer(block_pairs, inverse_square_root, tiles, tiles, None, row_tile)
+        d_pad, partner_rows = lax.optimization_barrier((d_pad, partner_rows))
         partners[residual_block_index] = lax.ppermute(partner_rows, "core", [(0, 1), (1, 0)])
+        d_act = conv_backward(d_pad, gathered, residual_block_index, c2, dilation, row_count)
         upstream_gradient = (
             upstream_gradient + gelu_back(pre_in, d_act) * in_scale[residual_block_index]
         )

time: 409 us -> 415 us (1.015)
  waiting for transfers between devices: 251 us -> 259 us
    reduce_scatter x1, waiting for transfers between devices: 145 us -> 154 us  [per_device(): lax.psum_scatter(paired, ('seq', 'y'), scatter_dimension=0, tiled=True)]
  transfers between devices with their start and end apart: 10 -> 10, of which waited for: 3 -> 3; matrix products, arithmetic and copies ran while one was open for 8% -> 8% of each run, Pallas kernels for 5% -> 6%
where the time goes in v14:
time: 415 us; the launch traced here: 414 us
  waiting for transfers between devices  259 us (62%)
  Pallas kernels  55.3 us (13%)
  other arithmetic  27.2 us (7%)
  local copies, waits for them, and re-layouts  22 us (5%)
  matrix products  18 us (4%)
  starting transfers between devices  17.6 us (4%)
  between operations  14.5 us (3%)
    reduce_scatter x1, waiting for transfers between devices, per_device(): lax.psum_scatter(paired, ('seq', 'y'), scatter_dimension=0, tiled=True)  154 us
    all_gather x1, waiting for transfers between devices, fetch_weights(): gathered = lax.all_gather(local, ALL, axis=0, tiled=True)  104 us
    pallas_call x4, Pallas kernels, weight_gradient_buffer(): pl.pallas_call(lambda *refs: gradient_kernel(inverse_square_root, tuple(l...  26.5 us
    pallas_call x2, Pallas kernels, conv_backward(): pl.pallas_call(lambda *refs: conv_backward_kernel(dilation, out_rows, *re...  14.7 us
    pallas_call x2, Pallas kernels, conv_forward(): pl.pallas_call(lambda *refs: conv_forward_kernel(dilation, out_rows, *ref...  14.1 us
    ppermute x3, starting transfers between devices, padded_2(): lax.ppermute(lax.slice_in_dim(block, block.shape[dim] - width, None, axis...  12.7 us
    dot_general x2, matrix products, per_device(): jnp.einsum('pe,ce->pc', middle, w_out, preferred_element_type=jnp.float32)  10.3 us
  transfers between devices with their start and end apart: 10, of which 3 were waited for; matrix products, arithmetic and copies ran while one was open for 8% of the time, Pallas kernels for 6%

profile of v14, /device:TPU:0, one launch (start us, length us, event | category | flops | bytes accessed | tf_op | source)
XLA Modules:
  0.0 413.7 jit_solution(14217491514130876147)
XLA Ops:
  10.3 4.8 %collective-permute-start = (bf16[24,1536]{1,0:T(8,128)(2,1)S(1)}, bf16[24,1536]{1,0:T(8,128)(2,1)S(1)}, u32[]{:S(2)}, u32[]{:S(2)}) collective-permute-start(bf16[24,1536]{1,0:T(8,128)(2,1)S(1)} %get-tuple-element.29), channel_id=1, source_target_pairs={{0,4},{4,8},{8,12},{12,16},{16,20},{20,24},{24,28},{1,5},{5,9},{9,... | collective-permute-start | bytes 221192 | tf_op jit(solution)/shard_map/ppermute | solution.py:19
  16.4 1.7 copy.20
  19.4 2.1 gather_fusion.2
  23.5 3.0 multiply_add_fusion
  30.6 2.1 gather_fusion.1
  34.6 104.3 %all-gather.2.cloned.1.call-done.refs_1_ = bf16[1536,6144]{1,0:T(8,128)(2,1)} async-done(((bf16[48,6144]{1,0:T(8,128)(2,1)}), bf16[1536,6144]{1,0:T(8,128)(2,1)}) %all-gather.2.cloned.1.call-update) | async-done | bytes 18874384 | tf_op jit(solution)/shard_map/all_gather | solution.py:110
  138.9 7.1 %shard_map.111 = f32[416,768]{1,0:T(8,128)} custom-call(bf16[432,1536]{1,0:T(8,128)(2,1)} %copy-done, bf16[1536,6144]{1,0:T(8,128)(2,1)} %all-gather.2.cloned.1.call-done.refs_1_, f32[1,768]{1,0:T(1,128)} %get-tuple-element.36.refs_2_, f32[1,768]{1,0:T(1,128)} %get-tuple-element.42.refs_3_), custom_call_target="tpu_custom_call" | custom-call | tf_op jit(solution)/shard_map/pallas_call | solution.py:75
  146.0 1.7 fusion.68
  147.7 6.5 %fusion.27 = (bf16[416,1536]{1,0:T(8,128)(2,1)}, f32[416,1536]{1,0:T(8,128)}, f32[416,1536]{1,0:T(8,128)}) fusion(pred[416]{0:T(512)(128)(4,1)S(1)} %fusion.98, f32[1536]{0:T(1024)S(1)} %get-tuple-element.19, f32[1536]{0:T(1024)S(1)} %get-tuple-element.41, bf16[416,768]{1,0:T(8,128)(2,1)S(1)} %fusion.68, ...), kind=kOutput, calls=%fused_computation.47 | convolution fusion | flops 989773824 | bytes 11956640 | tf_op jit(solution)/shard_map/pe,ce->pc/dot_general | solution.py:207
  154.2 7.0 %shard_map.112 = f32[384,768]{1,0:T(8,128)} custom-call(bf16[416,1536]{1,0:T(8,128)(2,1)} %get-tuple-element.25.refs_0_, bf16[1536,6144]{1,0:T(8,128)(2,1)} %all-gather.2.cloned.1.call-done.refs_1_, f32[1,768]{1,0:T(1,128)} %get-tuple-element.35.refs_2_, f32[1,768]{1,0:T(1,128)} %get-tuple-element.43.refs_3_), custom_call_target="tpu_custom_call" | custom-call | tf_op jit(solution)/shard_map/pallas_call | solution.py:75
  161.2 3.6 fusion.76
  166.3 3.3 collective-permute-start.2
  176.3 6.2 %shard_map.113 = bf16[768,3072]{1,0:T(8,128)(2,1)} custom-call(bf16[1536,416]{1,0:T(8,128)(2,1)} %bitcast.65, bf16[416,2304]{1,0:T(8,128)(2,1)} %fusion.55.refs_1_, bf16[1536,384]{1,0:T(8,128)(2,1)} %bitcast.69, bf16[384,768]{1,0:T(8,128)(2,1)} %multiply_convert_fusion.refs_3_), custom_call_target="tpu_custom_call" | custom-call | tf_op jit(solution)/shard_map/pallas_call | solution.py:157
  183.3 7.2 %shard_map.114 = f32[384,1536]{1,0:T(8,128)} custom-call(bf16[416,768]{1,0:T(8,128)(2,1)} %pad_maximum_fusion.refs_0_, bf16[1536,6144]{1,0:T(8,128)(2,1)} %all-gather.2.cloned.1.call-done.refs_1_), custom_call_target="tpu_custom_call" | custom-call | tf_op jit(solution)/shard_map/pallas_call | solution.py:91
  190.6 3.6 convert_bitcast_fusion
  194.2 4.1 %fusion.84 = bf16[384,768]{1,0:T(8,128)(2,1)S(1)} fusion(f32[416,768]{1,0:T(8,128)S(1)} %copy-done.7, bf16[1536,6144]{1,0:T(8,128)(2,1)} %all-gather.2.cloned.1.call-done.refs_1_, f32[768]{0:T(1024)S(1)} %get-tuple-element.21, f32[384,1536]{1,0:T(8,128)S(1)} %get-tuple-element.24), kind=kOutput, calls=%fused_computation.111 | convolution fusion | flops 912752640 | bytes 6491136 | tf_op jit(solution)/shard_map/dot_general | solution.py:231
  201.4 4.5 %collective-permute-start.4 = (bf16[8,768]{1,0:T(8,128)(2,1)S(1)}, bf16[8,768]{1,0:T(8,128)(2,1)S(1)}, u32[]{:S(2)}, u32[]{:S(2)}) collective-permute-start(bf16[8,768]{1,0:T(8,128)(2,1)S(1)} %get-tuple-element.31), channel_id=1, source_target_pairs={{0,4},{4,8},{8,12},{12,16},{16,20},{20,24},{24,28},{1,5},{5,9},{9,... | collective-permute-start | bytes 36872 | tf_op jit(solution)/shard_map/ppermute | solution.py:19
  208.7 6.1 %shard_map.115 = bf16[768,3072]{1,0:T(8,128)(2,1)} custom-call(bf16[1536,400]{1,0:T(8,128)(2,1)} %bitcast.67, bf16[400,2304]{1,0:T(8,128)(2,1)} %fusion.57.refs_1_, bf16[1536,384]{1,0:T(8,128)(2,1)} %bitcast.71, bf16[384,768]{1,0:T(8,128)(2,1)} %slice.131.refs_3_), custom_call_target="tpu_custom_call" | custom-call | tf_op jit(solution)/shard_map/pallas_call | solution.py:157
  216.9 7.1 %shard_map.117.refs_5_ = bf16[768,6144]{1,0:T(8,128)(2,1)} custom-call(bf16[1536,416]{1,0:T(8,128)(2,1)} %bitcast.66, bf16[416,2304]{1,0:T(8,128)(2,1)} %fusion.55.refs_1_, bf16[1536,384]{1,0:T(8,128)(2,1)} %bitcast.70, bf16[384,768]{1,0:T(8,128)(2,1)} %multiply_convert_fusion.refs_3_, bf16[768,3072]{1,0:T(8,128)(2,1)} %collective-permute-done.7.refs_4_), custom_call_target="tpu_custom_call" | custom-call | tf_op jit(solution)/shard_map/pallas_call | solution.py:157
  224.0 7.2 %shard_map.118 = bf16[768,6144]{1,0:T(8,128)(2,1)} custom-call(bf16[1536,400]{1,0:T(8,128)(2,1)} %bitcast.68, bf16[400,2304]{1,0:T(8,128)(2,1)} %fusion.57.refs_1_, bf16[1536,384]{1,0:T(8,128)(2,1)} %bitcast.72, bf16[384,768]{1,0:T(8,128)(2,1)} %slice.131.refs_3_, bf16[768,3072]{1,0:T(8,128)(2,1)} %collective-permute-done.6.refs_4_, ...), custom_call_target="tpu_custom_call", output_to_operand_aliasing={{}: (5, {})} | custom-call | tf_op jit(solution)/shard_map/pallas_call | solution.py:157
  233.1 3.8 fusion.18
  236.9 7.5 %shard_map.116 = f32[384,1536]{1,0:T(8,128)} custom-call(bf16[400,768]{1,0:T(8,128)(2,1)} %pad_maximum_fusion.1.refs_0_, bf16[1536,6144]{1,0:T(8,128)(2,1)} %all-gather.2.cloned.1.call-done.refs_1_), custom_call_target="tpu_custom_call" | custom-call | tf_op jit(solution)/shard_map/pallas_call | solution.py:91
  244.4 5.5 %fusion.44 = f32[1,384,1536]{2,1,0:T(8,128)} fusion(f32[384,1536]{1,0:T(8,128)} %copy-done.2, f32[384,1536]{1,0:T(8,128)} %shard_map.116, f32[432,1536]{1,0:T(8,128)S(1)} %copy-done.1, f32[1536]{0:T(1024)S(1)} %get-tuple-element.40), kind=kLoop, calls=%fused_computation.66 | loop fusion | flops 12386304 | bytes 9443328 | tf_op jit(solution)/shard_map/broadcast_in_dim | solution.py:266
  249.9 154.0 %reduce-scatter.2.cloned.1.call-done = bf16[48,6144]{1,0:T(8,128)(2,1)} async-done(((bf16[768,6144]{1,0:T(8,128)(2,1)}), bf16[48,6144]{1,0:T(8,128)(2,1)}) %reduce-scatter.2.cloned.1.call-update) | async-done | bytes 589840 | tf_op jit(solution)/shard_map/reduce_scatter | solution.py:260
  (99 shorter events, 35.2 us)
Async XLA Ops:
  7.2 131.7 %all-gather.2.cloned.1.call-start = ((), (), s32[]{:S(2)}) async-start(), calls=%async_computation.1 | async-start | bytes 19464192 | tf_op jit(solution)/shard_map/all_gather | solution.py:110
  7.2 3.0 copy-start.3
  10.2 393.7 %reduce-scatter.2.cloned.1.call-start = ((), (), s32[]{:S(2)}) async-start(), calls=%async_computation.2 | async-start | bytes 10027008 | tf_op jit(solution)/shard_map/reduce_scatter | solution.py:260
  10.3 13.2 %collective-permute-start = (bf16[24,1536]{1,0:T(8,128)(2,1)S(1)}, bf16[24,1536]{1,0:T(8,128)(2,1)S(1)}, u32[]{:S(2)}, u32[]{:S(2)}) collective-permute-start(bf16[24,1536]{1,0:T(8,128)(2,1)S(1)} %get-tuple-element.29), channel_id=1, source_target_pairs={{0,4},{4,8},{8,12},{12,16},{16,20},{20,24},{24,28},{1,5},{5,9},{9,... | collective-permute-start | bytes 221192 | tf_op jit(solution)/shard_map/ppermute | solution.py:19
  15.1 8.4 %collective-permute-start.1 = (bf16[24,1536]{1,0:T(8,128)(2,1)S(1)}, bf16[24,1536]{1,0:T(8,128)(2,1)S(1)}, u32[]{:S(2)}, u32[]{:S(2)}) collective-permute-start(bf16[24,1536]{1,0:T(8,128)(2,1)S(1)} %get-tuple-element.30), channel_id=1, source_target_pairs={{4,0},{8,4},{12,8},{16,12},{20,16},{24,20},{28,24},{5,1},{9,5},{13... | collective-permute-start | bytes 221192 | tf_op jit(solution)/shard_map/ppermute | solution.py:22
  18.2 3.4 copy-start.15
  18.2 3.4 copy-start.16
  18.2 3.4 copy-start.17
  18.2 3.4 copy-start.18
  147.7 6.5 %copy-start.13 = (bf16[416,768]{1,0:T(8,128)(2,1)}, bf16[416,768]{1,0:T(8,128)(2,1)S(1)}, u32[]{:S(2)}) copy-start(bf16[416,768]{1,0:T(8,128)(2,1)S(1)} %fusion.68) | copy-start | bytes 1916932
  154.2 7.0 %copy-start.9 = (bf16[1,384,1536]{2,1,0:T(8,128)(2,1)S(1)}, bf16[1,384,1536]{2,1,0:T(8,128)(2,1)}, u32[]{:S(2)}) copy-start(bf16[1,384,1536]{2,1,0:T(8,128)(2,1)} %param.11) | copy-start | bytes 3538948
  164.8 6.3 %copy-start.11 = (bf16[384,768]{1,0:T(8,128)(2,1)}, bf16[384,768]{1,0:T(8,128)(2,1)S(1)}, u32[]{:S(2)}) copy-start(bf16[384,768]{1,0:T(8,128)(2,1)S(1)} %fusion.76) | copy-start | bytes 1769476
  164.8 6.3 %copy-start.6 = (bf16[416,1536]{1,0:T(8,128)(2,1)S(1)}, bf16[416,1536]{1,0:T(8,128)(2,1)}, u32[]{:S(2)}) copy-start(bf16[416,1536]{1,0:T(8,128)(2,1)} %get-tuple-element.25.refs_0_) | copy-start | bytes 3833860
  166.3 16.1 %collective-permute-start.2 = (bf16[16,768]{1,0:T(8,128)(2,1)S(1)}, bf16[16,768]{1,0:T(8,128)(2,1)S(1)}, u32[]{:S(2)}, u32[]{:S(2)}) collective-permute-start(bf16[16,768]{1,0:T(8,128)(2,1)S(1)} %get-tuple-element.33), channel_id=1, source_target_pairs={{0,4},{4,8},{8,12},{12,16},{16,20},{20,24},{24,28},{1,5},{5,9},{9,... | collective-permute-start | bytes 73736 | tf_op jit(solution)/shard_map/ppermute | solution.py:19
  169.7 12.8 %collective-permute-start.3 = (bf16[16,768]{1,0:T(8,128)(2,1)S(1)}, bf16[16,768]{1,0:T(8,128)(2,1)S(1)}, u32[]{:S(2)}, u32[]{:S(2)}) collective-permute-start(bf16[16,768]{1,0:T(8,128)(2,1)S(1)} %get-tuple-element.34), channel_id=1, source_target_pairs={{4,0},{8,4},{12,8},{16,12},{20,16},{24,20},{28,24},{5,1},{9,5},{13... | collective-permute-start | bytes 73736 | tf_op jit(solution)/shard_map/ppermute | solution.py:22
  176.3 6.2 %copy-start.12 = (bf16[384,768]{1,0:T(8,128)(2,1)S(1)}, bf16[384,768]{1,0:T(8,128)(2,1)}, u32[]{:S(2)}) copy-start(bf16[384,768]{1,0:T(8,128)(2,1)} %copy-done.11) | copy-start | bytes 1769476
  183.3 7.2 %copy-start.10 = (bf16[1,384,1536]{2,1,0:T(8,128)(2,1)S(1)}, bf16[1,384,1536]{2,1,0:T(8,128)(2,1)}, u32[]{:S(2)}) copy-start(bf16[1,384,1536]{2,1,0:T(8,128)(2,1)} %param.11) | copy-start | bytes 3538948
  190.6 3.6 copy-start.7
  194.1 4.2 %copy-start.2 = (f32[384,1536]{1,0:T(8,128)}, f32[384,1536]{1,0:T(8,128)S(1)}, u32[]{:S(2)}) copy-start(f32[384,1536]{1,0:T(8,128)S(1)} %get-tuple-element.24) | copy-start | bytes 7077892
  201.4 13.4 %collective-permute-start.4 = (bf16[8,768]{1,0:T(8,128)(2,1)S(1)}, bf16[8,768]{1,0:T(8,128)(2,1)S(1)}, u32[]{:S(2)}, u32[]{:S(2)}) collective-permute-start(bf16[8,768]{1,0:T(8,128)(2,1)S(1)} %get-tuple-element.31), channel_id=1, source_target_pairs={{0,4},{4,8},{8,12},{12,16},{16,20},{20,24},{24,28},{1,5},{5,9},{9,... | collective-permute-start | bytes 36872 | tf_op jit(solution)/shard_map/ppermute | solution.py:19
  205.9 8.9 %collective-permute-start.5 = (bf16[8,768]{1,0:T(8,128)(2,1)S(1)}, bf16[8,768]{1,0:T(8,128)(2,1)S(1)}, u32[]{:S(2)}, u32[]{:S(2)}) collective-permute-start(bf16[8,768]{1,0:T(8,128)(2,1)S(1)} %get-tuple-element.32), channel_id=1, source_target_pairs={{4,0},{8,4},{12,8},{16,12},{20,16},{24,20},{28,24},{5,1},{9,5},{13... | collective-permute-start | bytes 36872 | tf_op jit(solution)/shard_map/ppermute | solution.py:22
  208.7 8.3 %collective-permute-start.7 = (bf16[768,3072]{1,0:T(8,128)(2,1)}, bf16[768,3072]{1,0:T(8,128)(2,1)}, u32[]{:S(2)}, u32[]{:S(2)}) collective-permute-start(bf16[768,3072]{1,0:T(8,128)(2,1)} %shard_map.113), channel_id=1, source_target_pairs={{0,1},{1,0},{2,3},{3,2},{4,5},{5,4},{6,7},{7,6},{8,9},{9,8},{10,11... | collective-permute-start | bytes 14155784 | tf_op jit(solution)/shard_map/ppermute | solution.py:242
  215.7 8.4 %collective-permute-start.6 = (bf16[768,3072]{1,0:T(8,128)(2,1)}, bf16[768,3072]{1,0:T(8,128)(2,1)}, u32[]{:S(2)}, u32[]{:S(2)}) collective-permute-start(bf16[768,3072]{1,0:T(8,128)(2,1)} %shard_map.115), channel_id=1, source_target_pairs={{0,1},{1,0},{2,3},{3,2},{4,5},{5,4},{6,7},{7,6},{8,9},{9,8},{10,11... | collective-permute-start | bytes 14155784 | tf_op jit(solution)/shard_map/ppermute | solution.py:242
  236.9 7.5 %copy-start.1 = (f32[432,1536]{1,0:T(8,128)S(1)}, f32[432,1536]{1,0:T(8,128)}, u32[]{:S(2)}) copy-start(f32[432,1536]{1,0:T(8,128)} %get-tuple-element.27) | copy-start | bytes 7962628
  (6 other events, 11.6 us)
Sparse Core Ops, SparseCore 0:
  11.5 127.3 all-gather.1
  231.4 172.4 reduce-scatter.1

commit v15 on v14

--- a/solution.py
+++ b/solution.py
@@ -238,7 +238,8 @@
         block_pairs = [dilated_weight_gradients[residual_block_index], mixing_weight_gradients[residual_block_index]]
         tiles = padded.shape[1] // (row_tile * lax.axis_size("core"))
         partner_rows = weight_gradient_buffer(block_pairs, inverse_square_root, tiles, tiles, None, row_tile)
-        d_pad, partner_rows = lax.optimization_barrier((d_pad, partner_rows))
+        if residual_block_index > 0:
+            d_pad, partner_rows = lax.optimization_barrier((d_pad, partner_rows))
         partners[residual_block_index] = lax.ppermute(partner_rows, "core", [(0, 1), (1, 0)])
         d_act = conv_backward(d_pad, gathered, residual_block_index, c2, dilation, row_count)
         upstream_gradient = (

time: 415 us -> 408 us (0.983)
  waiting for transfers between devices: 259 us -> 251 us
    reduce_scatter x1, waiting for transfers between devices: 154 us -> 145 us  [per_device(): lax.psum_scatter(paired, ('seq', 'y'), scatter_dimension=0, tiled=True)]
  transfers between devices with their start and end apart: 10 -> 10, of which waited for: 3 -> 3; matrix products, arithmetic and copies ran while one was open for 8% -> 8% of each run, Pallas kernels for 6% -> 7%
where the time goes in v15:
time: 408 us; the launch traced here: 407 us
  waiting for transfers between devices  251 us (62%)
  Pallas kernels  55.3 us (14%)
  other arithmetic  27.2 us (7%)
  local copies, waits for them, and re-layouts  21.5 us (5%)
  starting transfers between devices  19.9 us (5%)
  matrix products  18 us (4%)
  between operations  14.5 us (4%)
    reduce_scatter x1, waiting for transfers between devices, per_device(): lax.psum_scatter(paired, ('seq', 'y'), scatter_dimension=0, tiled=True)  145 us
    all_gather x1, waiting for transfers between devices, fetch_weights(): gathered = lax.all_gather(local, ALL, axis=0, tiled=True)  104 us
    pallas_call x4, Pallas kernels, weight_gradient_buffer(): pl.pallas_call(lambda *refs: gradient_kernel(inverse_square_root, tuple(l...  26.5 us
    ppermute x3, starting transfers between devices, padded_2(): lax.ppermute(lax.slice_in_dim(block, block.shape[dim] - width, None, axis...  15.3 us
    pallas_call x2, Pallas kernels, conv_backward(): pl.pallas_call(lambda *refs: conv_backward_kernel(dilation, out_rows, *re...  14.6 us
    pallas_call x2, Pallas kernels, conv_forward(): pl.pallas_call(lambda *refs: conv_forward_kernel(dilation, out_rows, *ref...  14.1 us
    dot_general x2, matrix products, per_device(): jnp.einsum('pe,ce->pc', middle, w_out, preferred_element_type=jnp.float32)  11.2 us
  transfers between devices with their start and end apart: 10, of which 3 were waited for; matrix products, arithmetic and copies ran while one was open for 8% of the time, Pallas kernels for 7%

profile of v15, /device:TPU:0, one launch (start us, length us, event | category | flops | bytes accessed | tf_op | source)
XLA Modules:
  0.0 407.0 jit_solution(9591091502778700019)
XLA Ops:
  11.6 5.5 %collective-permute-start = (bf16[24,1536]{1,0:T(8,128)(2,1)S(1)}, bf16[24,1536]{1,0:T(8,128)(2,1)S(1)}, u32[]{:S(2)}, u32[]{:S(2)}) collective-permute-start(bf16[24,1536]{1,0:T(8,128)(2,1)S(1)} %get-tuple-element.25), channel_id=1, source_target_pairs={{0,4},{4,8},{8,12},{12,16},{16,20},{20,24},{24,28},{1,5},{5,9},{9,... | collective-permute-start | bytes 221192 | tf_op jit(solution)/shard_map/ppermute | solution.py:19
  17.1 1.7 copy.20
  20.0 2.1 gather_fusion.2
  24.1 3.0 multiply_add_fusion
  31.3 2.1 gather_fusion.1
  35.2 103.7 %all-gather.2.cloned.1.call-done.refs_1_ = bf16[1536,6144]{1,0:T(8,128)(2,1)} async-done(((bf16[48,6144]{1,0:T(8,128)(2,1)}), bf16[1536,6144]{1,0:T(8,128)(2,1)}) %all-gather.2.cloned.1.call-update) | async-done | bytes 18874384 | tf_op jit(solution)/shard_map/all_gather | solution.py:110
  138.9 7.1 %shard_map.111 = f32[416,768]{1,0:T(8,128)} custom-call(bf16[432,1536]{1,0:T(8,128)(2,1)} %copy-done, bf16[1536,6144]{1,0:T(8,128)(2,1)} %all-gather.2.cloned.1.call-done.refs_1_, f32[1,768]{1,0:T(1,128)} %get-tuple-element.32.refs_2_, f32[1,768]{1,0:T(1,128)} %get-tuple-element.38.refs_3_), custom_call_target="tpu_custom_call" | custom-call | tf_op jit(solution)/shard_map/pallas_call | solution.py:75
  146.0 1.7 fusion.68
  147.7 6.5 %fusion.27 = (bf16[416,1536]{1,0:T(8,128)(2,1)}, f32[416,1536]{1,0:T(8,128)}, f32[416,1536]{1,0:T(8,128)}) fusion(pred[416]{0:T(512)(128)(4,1)S(1)} %fusion.98, f32[1536]{0:T(1024)S(1)} %get-tuple-element.15, f32[1536]{0:T(1024)S(1)} %get-tuple-element.37, bf16[416,768]{1,0:T(8,128)(2,1)S(1)} %fusion.68, ...), kind=kOutput, calls=%fused_computation.47 | convolution fusion | flops 989773824 | bytes 11956640 | tf_op jit(solution)/shard_map/pe,ce->pc/dot_general | solution.py:207
  154.2 7.0 %shard_map.112 = f32[384,768]{1,0:T(8,128)} custom-call(bf16[416,1536]{1,0:T(8,128)(2,1)} %get-tuple-element.21.refs_0_, bf16[1536,6144]{1,0:T(8,128)(2,1)} %all-gather.2.cloned.1.call-done.refs_1_, f32[1,768]{1,0:T(1,128)} %get-tuple-element.31.refs_2_, f32[1,768]{1,0:T(1,128)} %get-tuple-element.39.refs_3_), custom_call_target="tpu_custom_call" | custom-call | tf_op jit(solution)/shard_map/pallas_call | solution.py:75
  161.2 3.6 fusion.76
  167.6 4.7 %collective-permute-start.2 = (bf16[16,768]{1,0:T(8,128)(2,1)S(1)}, bf16[16,768]{1,0:T(8,128)(2,1)S(1)}, u32[]{:S(2)}, u32[]{:S(2)}) collective-permute-start(bf16[16,768]{1,0:T(8,128)(2,1)S(1)} %get-tuple-element.29), channel_id=1, source_target_pairs={{0,4},{4,8},{8,12},{12,16},{16,20},{20,24},{24,28},{1,5},{5,9},{9,... | collective-permute-start | bytes 73736 | tf_op jit(solution)/shard_map/ppermute | solution.py:19
  177.5 6.2 %shard_map.113 = bf16[768,3072]{1,0:T(8,128)(2,1)} custom-call(bf16[1536,416]{1,0:T(8,128)(2,1)} %bitcast.65, bf16[416,2304]{1,0:T(8,128)(2,1)} %fusion.55.refs_1_, bf16[1536,384]{1,0:T(8,128)(2,1)} %bitcast.69, bf16[384,768]{1,0:T(8,128)(2,1)} %multiply_convert_fusion.refs_3_), custom_call_target="tpu_custom_call" | custom-call | tf_op jit(solution)/shard_map/pallas_call | solution.py:157
  184.5 7.2 %shard_map.114 = f32[384,1536]{1,0:T(8,128)} custom-call(bf16[416,768]{1,0:T(8,128)(2,1)} %pad_maximum_fusion.refs_0_, bf16[1536,6144]{1,0:T(8,128)(2,1)} %all-gather.2.cloned.1.call-done.refs_1_), custom_call_target="tpu_custom_call" | custom-call | tf_op jit(solution)/shard_map/pallas_call | solution.py:91
  191.7 3.6 convert_bitcast_fusion
  196.7 3.3 fusion.84
  204.3 6.1 %shard_map.116 = bf16[768,3072]{1,0:T(8,128)(2,1)} custom-call(bf16[1536,400]{1,0:T(8,128)(2,1)} %bitcast.67, bf16[400,2304]{1,0:T(8,128)(2,1)} %fusion.57.refs_1_, bf16[1536,384]{1,0:T(8,128)(2,1)} %bitcast.71, bf16[384,768]{1,0:T(8,128)(2,1)} %slice.132.refs_3_), custom_call_target="tpu_custom_call" | custom-call | tf_op jit(solution)/shard_map/pallas_call | solution.py:157
  212.5 7.1 %shard_map.117.refs_5_ = bf16[768,6144]{1,0:T(8,128)(2,1)} custom-call(bf16[1536,416]{1,0:T(8,128)(2,1)} %bitcast.66, bf16[416,2304]{1,0:T(8,128)(2,1)} %fusion.55.refs_1_, bf16[1536,384]{1,0:T(8,128)(2,1)} %bitcast.70, bf16[384,768]{1,0:T(8,128)(2,1)} %multiply_convert_fusion.refs_3_, bf16[768,3072]{1,0:T(8,128)(2,1)} %collective-permute-done.7.refs_4_), custom_call_target="tpu_custom_call" | custom-call | tf_op jit(solution)/shard_map/pallas_call | solution.py:157
  219.7 7.1 %shard_map.118 = bf16[768,6144]{1,0:T(8,128)(2,1)} custom-call(bf16[1536,400]{1,0:T(8,128)(2,1)} %bitcast.68, bf16[400,2304]{1,0:T(8,128)(2,1)} %fusion.57.refs_1_, bf16[1536,384]{1,0:T(8,128)(2,1)} %bitcast.72, bf16[384,768]{1,0:T(8,128)(2,1)} %slice.132.refs_3_, bf16[768,3072]{1,0:T(8,128)(2,1)} %collective-permute-done.6.refs_4_, ...), custom_call_target="tpu_custom_call", output_to_operand_aliasing={{}: (5, {})} | custom-call | tf_op jit(solution)/shard_map/pallas_call | solution.py:157
  228.3 5.1 %collective-permute-start.4 = (bf16[8,768]{1,0:T(8,128)(2,1)S(1)}, bf16[8,768]{1,0:T(8,128)(2,1)S(1)}, u32[]{:S(2)}, u32[]{:S(2)}) collective-permute-start(bf16[8,768]{1,0:T(8,128)(2,1)S(1)} %get-tuple-element.27), channel_id=1, source_target_pairs={{0,4},{4,8},{8,12},{12,16},{16,20},{20,24},{24,28},{1,5},{5,9},{9,... | collective-permute-start | bytes 36872 | tf_op jit(solution)/shard_map/ppermute | solution.py:19
  233.3 4.7 %fusion.18 = bf16[1,384,1536]{2,1,0:T(8,128)(2,1)} fusion(bf16[384,768]{1,0:T(8,128)(2,1)S(1)} %copy-done.5, f32[416,1536]{1,0:T(8,128)} %get-tuple-element.35, bf16[1536,6144]{1,0:T(8,128)(2,1)} %all-gather.2.cloned.1.call-done.refs_1_), kind=kOutput, calls=%fused_computation.38 | convolution fusion | flops 907149312 | bytes 6488064 | tf_op jit(solution)/shard_map/pe,ce->pc/dot_general | solution.py:207
  238.9 7.4 %shard_map.115 = f32[384,1536]{1,0:T(8,128)} custom-call(bf16[400,768]{1,0:T(8,128)(2,1)} %pad_maximum_fusion.1.refs_0_, bf16[1536,6144]{1,0:T(8,128)(2,1)} %all-gather.2.cloned.1.call-done.refs_1_), custom_call_target="tpu_custom_call" | custom-call | tf_op jit(solution)/shard_map/pallas_call | solution.py:91
  246.3 5.5 %fusion.44 = f32[1,384,1536]{2,1,0:T(8,128)} fusion(f32[384,1536]{1,0:T(8,128)} %copy-done.2, f32[384,1536]{1,0:T(8,128)} %shard_map.115, f32[432,1536]{1,0:T(8,128)S(1)} %copy-done.1, f32[1536]{0:T(1024)S(1)} %get-tuple-element.36), kind=kLoop, calls=%fused_computation.66 | loop fusion | flops 12386304 | bytes 9443328 | tf_op jit(solution)/shard_map/broadcast_in_dim | solution.py:267
  251.8 145.3 %reduce-scatter.2.cloned.1.call-done = bf16[48,6144]{1,0:T(8,128)(2,1)} async-done(((bf16[768,6144]{1,0:T(8,128)(2,1)}), bf16[48,6144]{1,0:T(8,128)(2,1)}) %reduce-scatter.2.cloned.1.call-update) | async-done | bytes 589840 | tf_op jit(solution)/shard_map/reduce_scatter | solution.py:261
  (97 shorter events, 35.3 us)
Async XLA Ops:
  7.2 131.7 %all-gather.2.cloned.1.call-start = ((), (), s32[]{:S(2)}) async-start(), calls=%async_computation.1 | async-start | bytes 19464192 | tf_op jit(solution)/shard_map/all_gather | solution.py:110
  7.2 3.0 copy-start.3
  10.2 386.9 %reduce-scatter.2.cloned.1.call-start = ((), (), s32[]{:S(2)}) async-start(), calls=%async_computation.2 | async-start | bytes 10027008 | tf_op jit(solution)/shard_map/reduce_scatter | solution.py:261
  10.3 13.8 %collective-permute-start.1 = (bf16[24,1536]{1,0:T(8,128)(2,1)S(1)}, bf16[24,1536]{1,0:T(8,128)(2,1)S(1)}, u32[]{:S(2)}, u32[]{:S(2)}) collective-permute-start(bf16[24,1536]{1,0:T(8,128)(2,1)S(1)} %get-tuple-element.26), channel_id=1, source_target_pairs={{4,0},{8,4},{12,8},{16,12},{20,16},{24,20},{28,24},{5,1},{9,5},{13... | collective-permute-start | bytes 221192 | tf_op jit(solution)/shard_map/ppermute | solution.py:22
  11.6 12.5 %collective-permute-start = (bf16[24,1536]{1,0:T(8,128)(2,1)S(1)}, bf16[24,1536]{1,0:T(8,128)(2,1)S(1)}, u32[]{:S(2)}, u32[]{:S(2)}) collective-permute-start(bf16[24,1536]{1,0:T(8,128)(2,1)S(1)} %get-tuple-element.25), channel_id=1, source_target_pairs={{0,4},{4,8},{8,12},{12,16},{16,20},{20,24},{24,28},{1,5},{5,9},{9,... | collective-permute-start | bytes 221192 | tf_op jit(solution)/shard_map/ppermute | solution.py:19
  18.8 3.4 copy-start.15
  18.8 3.4 copy-start.16
  18.8 3.4 copy-start.17
  18.8 3.4 copy-start.18
  147.7 6.5 %copy-start.13 = (bf16[416,768]{1,0:T(8,128)(2,1)}, bf16[416,768]{1,0:T(8,128)(2,1)S(1)}, u32[]{:S(2)}) copy-start(bf16[416,768]{1,0:T(8,128)(2,1)S(1)} %fusion.68) | copy-start | bytes 1916932
  154.2 7.0 %copy-start.9 = (bf16[1,384,1536]{2,1,0:T(8,128)(2,1)S(1)}, bf16[1,384,1536]{2,1,0:T(8,128)(2,1)}, u32[]{:S(2)}) copy-start(bf16[1,384,1536]{2,1,0:T(8,128)(2,1)} %param.11) | copy-start | bytes 3538948
  164.8 7.5 %copy-start.11 = (bf16[384,768]{1,0:T(8,128)(2,1)}, bf16[384,768]{1,0:T(8,128)(2,1)S(1)}, u32[]{:S(2)}) copy-start(bf16[384,768]{1,0:T(8,128)(2,1)S(1)} %fusion.76) | copy-start | bytes 1769476
  164.8 7.5 %copy-start.6 = (bf16[416,1536]{1,0:T(8,128)(2,1)S(1)}, bf16[416,1536]{1,0:T(8,128)(2,1)}, u32[]{:S(2)}) copy-start(bf16[416,1536]{1,0:T(8,128)(2,1)} %get-tuple-element.21.refs_0_) | copy-start | bytes 3833860
  166.3 17.3 %collective-permute-start.3 = (bf16[16,768]{1,0:T(8,128)(2,1)S(1)}, bf16[16,768]{1,0:T(8,128)(2,1)S(1)}, u32[]{:S(2)}, u32[]{:S(2)}) collective-permute-start(bf16[16,768]{1,0:T(8,128)(2,1)S(1)} %get-tuple-element.30), channel_id=1, source_target_pairs={{4,0},{8,4},{12,8},{16,12},{20,16},{24,20},{28,24},{5,1},{9,5},{13... | collective-permute-start | bytes 73736 | tf_op jit(solution)/shard_map/ppermute | solution.py:22
  167.6 16.0 %collective-permute-start.2 = (bf16[16,768]{1,0:T(8,128)(2,1)S(1)}, bf16[16,768]{1,0:T(8,128)(2,1)S(1)}, u32[]{:S(2)}, u32[]{:S(2)}) collective-permute-start(bf16[16,768]{1,0:T(8,128)(2,1)S(1)} %get-tuple-element.29), channel_id=1, source_target_pairs={{0,4},{4,8},{8,12},{12,16},{16,20},{20,24},{24,28},{1,5},{5,9},{9,... | collective-permute-start | bytes 73736 | tf_op jit(solution)/shard_map/ppermute | solution.py:19
  177.5 6.2 %copy-start.12 = (bf16[384,768]{1,0:T(8,128)(2,1)S(1)}, bf16[384,768]{1,0:T(8,128)(2,1)}, u32[]{:S(2)}) copy-start(bf16[384,768]{1,0:T(8,128)(2,1)} %copy-done.11) | copy-start | bytes 1769476
  184.5 7.2 %copy-start.10 = (bf16[1,384,1536]{2,1,0:T(8,128)(2,1)S(1)}, bf16[1,384,1536]{2,1,0:T(8,128)(2,1)}, u32[]{:S(2)}) copy-start(bf16[1,384,1536]{2,1,0:T(8,128)(2,1)} %param.11) | copy-start | bytes 3538948
  191.7 5.0 %copy-start.7 = (f32[416,768]{1,0:T(8,128)S(1)}, f32[416,768]{1,0:T(8,128)}, u32[]{:S(2)}) copy-start(f32[416,768]{1,0:T(8,128)} %shard_map.111) | copy-start | bytes 3833860
  204.3 8.3 %collective-permute-start.7 = (bf16[768,3072]{1,0:T(8,128)(2,1)}, bf16[768,3072]{1,0:T(8,128)(2,1)}, u32[]{:S(2)}, u32[]{:S(2)}) collective-permute-start(bf16[768,3072]{1,0:T(8,128)(2,1)} %shard_map.113), channel_id=1, source_target_pairs={{0,1},{1,0},{2,3},{3,2},{4,5},{5,4},{6,7},{7,6},{8,9},{9,8},{10,11... | collective-permute-start | bytes 14155784 | tf_op jit(solution)/shard_map/ppermute | solution.py:243
  210.4 9.3 %collective-permute-start.6 = (bf16[768,3072]{1,0:T(8,128)(2,1)}, bf16[768,3072]{1,0:T(8,128)(2,1)}, u32[]{:S(2)}, u32[]{:S(2)}) collective-permute-start(bf16[768,3072]{1,0:T(8,128)(2,1)} %shard_map.116), channel_id=1, source_target_pairs={{0,1},{1,0},{2,3},{3,2},{4,5},{5,4},{6,7},{7,6},{8,9},{9,8},{10,11... | collective-permute-start | bytes 14155784 | tf_op jit(solution)/shard_map/ppermute | solution.py:243
  226.8 6.5 %copy-start.5 = (bf16[384,768]{1,0:T(8,128)(2,1)S(1)}, bf16[384,768]{1,0:T(8,128)(2,1)}, u32[]{:S(2)}) copy-start(bf16[384,768]{1,0:T(8,128)(2,1)} %multiply_convert_fusion.refs_3_) | copy-start | bytes 1769476
  226.8 11.2 %collective-permute-start.5 = (bf16[8,768]{1,0:T(8,128)(2,1)S(1)}, bf16[8,768]{1,0:T(8,128)(2,1)S(1)}, u32[]{:S(2)}, u32[]{:S(2)}) collective-permute-start(bf16[8,768]{1,0:T(8,128)(2,1)S(1)} %get-tuple-element.28), channel_id=1, source_target_pairs={{4,0},{8,4},{12,8},{16,12},{20,16},{24,20},{28,24},{5,1},{9,5},{13... | collective-permute-start | bytes 36872 | tf_op jit(solution)/shard_map/ppermute | solution.py:22
  228.3 9.8 %collective-permute-start.4 = (bf16[8,768]{1,0:T(8,128)(2,1)S(1)}, bf16[8,768]{1,0:T(8,128)(2,1)S(1)}, u32[]{:S(2)}, u32[]{:S(2)}) collective-permute-start(bf16[8,768]{1,0:T(8,128)(2,1)S(1)} %get-tuple-element.27), channel_id=1, source_target_pairs={{0,4},{4,8},{8,12},{12,16},{16,20},{20,24},{24,28},{1,5},{5,9},{9,... | collective-permute-start | bytes 36872 | tf_op jit(solution)/shard_map/ppermute | solution.py:19
  238.9 7.4 %copy-start.1 = (f32[432,1536]{1,0:T(8,128)S(1)}, f32[432,1536]{1,0:T(8,128)}, u32[]{:S(2)}) copy-start(f32[432,1536]{1,0:T(8,128)} %get-tuple-element.23) | copy-start | bytes 7962628
  (5 other events, 10.1 us)
Sparse Core Ops, SparseCore 0:
  11.5 127.3 all-gather.1
  226.9 170.1 reduce-scatter.1

commit v16 on v15

--- a/solution.py
+++ b/solution.py
@@ -32,7 +32,7 @@
     return jax.vjp(gelu_value, pre_values)[1](upstream_gradient)[0]
 
 
-def conv_forward_kernel(dilation, out_rows, act_ref, w_ref, scale_ref, shift_ref, out_ref):
+def conv_forward_kernel(dilation, out_rows, act_ref, w_ref, scale_ref, shift_ref, out_ref, mid_ref):
     tap = pl.program_id(0)
     for kernel_tap in range(3):
 
@@ -47,7 +47,9 @@
             elif kernel_tap == 1:
                 out_ref[...] = out_ref[...] + term
             else:
-                out_ref[...] = (out_ref[...] + term) * scale_ref[...] + shift_ref[...]
+                pre = (out_ref[...] + term) * scale_ref[...] + shift_ref[...]
+                out_ref[...] = pre
+                mid_ref[...] = gelu_value(pre).astype(mid_ref.dtype)
 
 
 def conv_backward_kernel(dilation, out_rows, grad_ref, w_ref, out_ref):
@@ -81,8 +83,11 @@
             pl.BlockSpec((1, c2), lambda k: (0, 0)),
             pl.BlockSpec((1, c2), lambda k: (0, 0)),
         ],
-        out_specs=pl.BlockSpec((out_rows, c2), lambda k: (0, 0)),
-        out_shape=jax.ShapeDtypeStruct((out_rows, c2), jnp.float32),
+        out_specs=[pl.BlockSpec((out_rows, c2), lambda k: (0, 0))] * 2,
+        out_shape=[
+            jax.ShapeDtypeStruct((out_rows, c2), jnp.float32),
+            jax.ShapeDtypeStruct((out_rows, c2), jnp.bfloat16),
+        ],
     )(padded, gathered, scale.reshape(1, c2), shift.reshape(1, c2))
 
 
@@ -193,7 +198,7 @@
         inside = (position >= 0) & (position < window_len)
         activated = jnp.where(inside, gelu_value(pre_in), 0.0).astype(jnp.bfloat16)
         out_rows = row_count + 2 * (remaining - dilation)
-        pre_mid = conv_forward(
+        pre_mid, middle = conv_forward(
             activated,
             gathered,
             residual_block_index,
@@ -203,7 +208,6 @@
             dilation,
             out_rows,
         )
-        middle = gelu_value(pre_mid).astype(jnp.bfloat16)
         stream = stream[dilation : dilation + out_rows] + jnp.einsum(
             "pe,ce->pc", middle, w_out, preferred_element_type=jnp.float32
         )

time: 408 us -> 406 us (level)
  no operation moved by 1% of the time
where the time goes in v16:
time: 406 us; the launch traced here: 405 us
  waiting for transfers between devices  250 us (62%)
  Pallas kernels  56.1 us (14%)
  other arithmetic  24.3 us (6%)
  local copies, waits for them, and re-layouts  22 us (5%)
  starting transfers between devices  19.9 us (5%)
  matrix products  18 us (4%)
  between operations  14.5 us (4%)
    reduce_scatter x1, waiting for transfers between devices, per_device(): lax.psum_scatter(paired, ('seq', 'y'), scatter_dimension=0, tiled=True)  146 us
    all_gather x1, waiting for transfers between devices, fetch_weights(): gathered = lax.all_gather(local, ALL, axis=0, tiled=True)  103 us
    pallas_call x4, Pallas kernels, weight_gradient_buffer(): pl.pallas_call(lambda *refs: gradient_kernel(inverse_square_root, tuple(l...  26.5 us
    ppermute x3, starting transfers between devices, padded_2(): lax.ppermute(lax.slice_in_dim(block, block.shape[dim] - width, None, axis...  15.3 us
    pallas_call x2, Pallas kernels, conv_forward(): pl.pallas_call(lambda *refs: conv_forward_kernel(dilation, out_rows, *ref...  15 us
    pallas_call x2, Pallas kernels, conv_backward(): pl.pallas_call(lambda *refs: conv_backward_kernel(dilation, out_rows, *re...  14.6 us
    dot_general x2, matrix products, per_device(): jnp.einsum('pe,ce->pc', middle, w_out, preferred_element_type=jnp.float32)  11.1 us
  transfers between devices with their start and end apart: 10, of which 3 were waited for; matrix products, arithmetic and copies ran while one was open for 8% of the time, Pallas kernels for 7%

profile of v16, /device:TPU:0, one launch (start us, length us, event | category | flops | bytes accessed | tf_op | source)
XLA Modules:
  0.0 405.1 jit_solution(2948772965770036735)
XLA Ops:
  11.6 5.5 %collective-permute-start = (bf16[24,1536]{1,0:T(8,128)(2,1)S(1)}, bf16[24,1536]{1,0:T(8,128)(2,1)S(1)}, u32[]{:S(2)}, u32[]{:S(2)}) collective-permute-start(bf16[24,1536]{1,0:T(8,128)(2,1)S(1)} %get-tuple-element.33), channel_id=1, source_target_pairs={{0,4},{4,8},{8,12},{12,16},{16,20},{20,24},{24,28},{1,5},{5,9},{9,... | collective-permute-start | bytes 221192 | tf_op jit(solution)/shard_map/ppermute | solution.py:19
  17.1 1.7 copy.20
  20.0 2.1 gather_fusion.2
  24.7 3.0 multiply_add_fusion
  28.9 1.7 copy.22
  31.8 2.1 gather_fusion.1
  35.8 103.1 %all-gather.2.cloned.1.call-done.refs_1_ = bf16[1536,6144]{1,0:T(8,128)(2,1)} async-done(((bf16[48,6144]{1,0:T(8,128)(2,1)}), bf16[1536,6144]{1,0:T(8,128)(2,1)}) %all-gather.2.cloned.1.call-update) | async-done | bytes 18874384 | tf_op jit(solution)/shard_map/all_gather | solution.py:115
  138.9 7.6 %shard_map.111 = (f32[416,768]{1,0:T(8,128)}, bf16[416,768]{1,0:T(8,128)(2,1)}) custom-call(bf16[432,1536]{1,0:T(8,128)(2,1)} %copy-done, bf16[1536,6144]{1,0:T(8,128)(2,1)} %all-gather.2.cloned.1.call-done.refs_1_, f32[1,768]{1,0:T(1,128)} %get-tuple-element.40.refs_2_, f32[1,768]{1,0:T(1,128)} %get-tuple-element.42.refs_3_), custom_call_target="tpu_custom_call" | custom-call | tf_op jit(solution)/shard_map/pallas_call | solution.py:77
  146.5 6.5 %fusion.27 = (bf16[416,1536]{1,0:T(8,128)(2,1)}, f32[416,1536]{1,0:T(8,128)}, f32[416,1536]{1,0:T(8,128)}) fusion(pred[416]{0:T(512)(128)(4,1)S(1)} %fusion.90, f32[1536]{0:T(1024)S(1)} %get-tuple-element.23, f32[1536]{0:T(1024)S(1)} %get-tuple-element.45, bf16[416,768]{1,0:T(8,128)(2,1)} %get-tuple-element.11, ...), kind=kOutput, calls=%fused_computation.47 | convolution fusion | flops 989773824 | bytes 11956640 | tf_op jit(solution)/shard_map/pe,ce->pc/dot_general | solution.py:211
  152.9 7.4 %shard_map.112 = (f32[384,768]{1,0:T(8,128)}, bf16[384,768]{1,0:T(8,128)(2,1)}) custom-call(bf16[416,1536]{1,0:T(8,128)(2,1)} %get-tuple-element.29.refs_0_, bf16[1536,6144]{1,0:T(8,128)(2,1)} %all-gather.2.cloned.1.call-done.refs_1_, f32[1,768]{1,0:T(1,128)} %get-tuple-element.39.refs_2_, f32[1,768]{1,0:T(1,128)} %get-tuple-element.41.refs_3_), custom_call_target="tpu_custom_call" | custom-call | tf_op jit(solution)/shard_map/pallas_call | solution.py:77
  160.3 3.6 fusion.68
  166.7 4.7 %collective-permute-start.2 = (bf16[16,768]{1,0:T(8,128)(2,1)S(1)}, bf16[16,768]{1,0:T(8,128)(2,1)S(1)}, u32[]{:S(2)}, u32[]{:S(2)}) collective-permute-start(bf16[16,768]{1,0:T(8,128)(2,1)S(1)} %get-tuple-element.37), channel_id=1, source_target_pairs={{0,4},{4,8},{8,12},{12,16},{16,20},{20,24},{24,28},{1,5},{5,9},{9,... | collective-permute-start | bytes 73736 | tf_op jit(solution)/shard_map/ppermute | solution.py:19
  175.3 6.2 %shard_map.113 = bf16[768,3072]{1,0:T(8,128)(2,1)} custom-call(bf16[1536,416]{1,0:T(8,128)(2,1)} %bitcast.65, bf16[416,2304]{1,0:T(8,128)(2,1)} %fusion.55.refs_1_, bf16[1536,384]{1,0:T(8,128)(2,1)} %bitcast.69, bf16[384,768]{1,0:T(8,128)(2,1)} %get-tuple-element.12.refs_3_), custom_call_target="tpu_custom_call" | custom-call | tf_op jit(solution)/shard_map/pallas_call | solution.py:162
  182.4 7.2 %shard_map.114 = f32[384,1536]{1,0:T(8,128)} custom-call(bf16[416,768]{1,0:T(8,128)(2,1)} %pad_maximum_fusion.refs_0_, bf16[1536,6144]{1,0:T(8,128)(2,1)} %all-gather.2.cloned.1.call-done.refs_1_), custom_call_target="tpu_custom_call" | custom-call | tf_op jit(solution)/shard_map/pallas_call | solution.py:96
  189.6 3.6 convert_bitcast_fusion
  194.6 3.3 fusion.76
  202.1 6.1 %shard_map.116 = bf16[768,3072]{1,0:T(8,128)(2,1)} custom-call(bf16[1536,400]{1,0:T(8,128)(2,1)} %bitcast.67, bf16[400,2304]{1,0:T(8,128)(2,1)} %fusion.57.refs_1_, bf16[1536,384]{1,0:T(8,128)(2,1)} %bitcast.71, bf16[384,768]{1,0:T(8,128)(2,1)} %slice.109.refs_3_), custom_call_target="tpu_custom_call" | custom-call | tf_op jit(solution)/shard_map/pallas_call | solution.py:162
  210.4 7.1 %shard_map.117.refs_5_ = bf16[768,6144]{1,0:T(8,128)(2,1)} custom-call(bf16[1536,416]{1,0:T(8,128)(2,1)} %bitcast.66, bf16[416,2304]{1,0:T(8,128)(2,1)} %fusion.55.refs_1_, bf16[1536,384]{1,0:T(8,128)(2,1)} %bitcast.70, bf16[384,768]{1,0:T(8,128)(2,1)} %get-tuple-element.12.refs_3_, bf16[768,3072]{1,0:T(8,128)(2,1)} %collective-permute-done.7.refs_4_), custom_call_target="tpu_custom_call" | custom-call | tf_op jit(solution)/shard_map/pallas_call | solution.py:162
  217.5 7.2 %shard_map.118 = bf16[768,6144]{1,0:T(8,128)(2,1)} custom-call(bf16[1536,400]{1,0:T(8,128)(2,1)} %bitcast.68, bf16[400,2304]{1,0:T(8,128)(2,1)} %fusion.57.refs_1_, bf16[1536,384]{1,0:T(8,128)(2,1)} %bitcast.72, bf16[384,768]{1,0:T(8,128)(2,1)} %slice.109.refs_3_, bf16[768,3072]{1,0:T(8,128)(2,1)} %collective-permute-done.6.refs_4_, ...), custom_call_target="tpu_custom_call", output_to_operand_aliasing={{}: (5, {})} | custom-call | tf_op jit(solution)/shard_map/pallas_call | solution.py:162
  226.1 5.1 %collective-permute-start.4 = (bf16[8,768]{1,0:T(8,128)(2,1)S(1)}, bf16[8,768]{1,0:T(8,128)(2,1)S(1)}, u32[]{:S(2)}, u32[]{:S(2)}) collective-permute-start(bf16[8,768]{1,0:T(8,128)(2,1)S(1)} %get-tuple-element.35), channel_id=1, source_target_pairs={{0,4},{4,8},{8,12},{12,16},{16,20},{20,24},{24,28},{1,5},{5,9},{9,... | collective-permute-start | bytes 36872 | tf_op jit(solution)/shard_map/ppermute | solution.py:19
  231.2 4.7 %fusion.18 = bf16[1,384,1536]{2,1,0:T(8,128)(2,1)} fusion(bf16[384,768]{1,0:T(8,128)(2,1)S(1)} %copy-done.10, f32[416,1536]{1,0:T(8,128)} %get-tuple-element.43, bf16[1536,6144]{1,0:T(8,128)(2,1)} %all-gather.2.cloned.1.call-done.refs_1_), kind=kOutput, calls=%fused_computation.38 | convolution fusion | flops 907149312 | bytes 6488064 | tf_op jit(solution)/shard_map/pe,ce->pc/dot_general | solution.py:211
  236.8 7.4 %shard_map.115 = f32[384,1536]{1,0:T(8,128)} custom-call(bf16[400,768]{1,0:T(8,128)(2,1)} %pad_maximum_fusion.1.refs_0_, bf16[1536,6144]{1,0:T(8,128)(2,1)} %all-gather.2.cloned.1.call-done.refs_1_), custom_call_target="tpu_custom_call" | custom-call | tf_op jit(solution)/shard_map/pallas_call | solution.py:96
  244.2 5.5 %fusion.44 = f32[1,384,1536]{2,1,0:T(8,128)} fusion(f32[384,1536]{1,0:T(8,128)} %copy-done.2, f32[384,1536]{1,0:T(8,128)} %shard_map.115, f32[432,1536]{1,0:T(8,128)S(1)} %copy-done.1, f32[1536]{0:T(1024)S(1)} %get-tuple-element.44), kind=kLoop, calls=%fused_computation.66 | loop fusion | flops 12386304 | bytes 9443328 | tf_op jit(solution)/shard_map/broadcast_in_dim | solution.py:271
  249.7 145.6 %reduce-scatter.2.cloned.1.call-done = bf16[48,6144]{1,0:T(8,128)(2,1)} async-done(((bf16[768,6144]{1,0:T(8,128)(2,1)}), bf16[48,6144]{1,0:T(8,128)(2,1)}) %reduce-scatter.2.cloned.1.call-update) | async-done | bytes 589840 | tf_op jit(solution)/shard_map/reduce_scatter | solution.py:265
  (92 shorter events, 33.0 us)
Async XLA Ops:
  7.2 3.1 copy-start.3
  7.2 131.7 %all-gather.2.cloned.1.call-start = ((), (), s32[]{:S(2)}) async-start(), calls=%async_computation.1 | async-start | bytes 19464192 | tf_op jit(solution)/shard_map/all_gather | solution.py:115
  10.2 385.0 %reduce-scatter.2.cloned.1.call-start = ((), (), s32[]{:S(2)}) async-start(), calls=%async_computation.2 | async-start | bytes 10027008 | tf_op jit(solution)/shard_map/reduce_scatter | solution.py:265
  10.3 14.4 %collective-permute-start.1 = (bf16[24,1536]{1,0:T(8,128)(2,1)S(1)}, bf16[24,1536]{1,0:T(8,128)(2,1)S(1)}, u32[]{:S(2)}, u32[]{:S(2)}) collective-permute-start(bf16[24,1536]{1,0:T(8,128)(2,1)S(1)} %get-tuple-element.34), channel_id=1, source_target_pairs={{4,0},{8,4},{12,8},{16,12},{20,16},{24,20},{28,24},{5,1},{9,5},{13... | collective-permute-start | bytes 221192 | tf_op jit(solution)/shard_map/ppermute | solution.py:22
  11.6 13.1 %collective-permute-start = (bf16[24,1536]{1,0:T(8,128)(2,1)S(1)}, bf16[24,1536]{1,0:T(8,128)(2,1)S(1)}, u32[]{:S(2)}, u32[]{:S(2)}) collective-permute-start(bf16[24,1536]{1,0:T(8,128)(2,1)S(1)} %get-tuple-element.33), channel_id=1, source_target_pairs={{0,4},{4,8},{8,12},{12,16},{16,20},{20,24},{24,28},{1,5},{5,9},{9,... | collective-permute-start | bytes 221192 | tf_op jit(solution)/shard_map/ppermute | solution.py:19
  18.8 3.4 copy-start.12
  18.8 3.4 copy-start.13
  18.8 3.4 copy-start.15
  18.8 4.0 copy-start.14
  27.7 2.8 copy-start
  152.9 7.4 %copy-start.6 = (bf16[1,384,1536]{2,1,0:T(8,128)(2,1)S(1)}, bf16[1,384,1536]{2,1,0:T(8,128)(2,1)}, u32[]{:S(2)}) copy-start(bf16[1,384,1536]{2,1,0:T(8,128)(2,1)} %param.11) | copy-start | bytes 3538948
  163.9 7.5 %copy-start.8 = (bf16[384,768]{1,0:T(8,128)(2,1)}, bf16[384,768]{1,0:T(8,128)(2,1)S(1)}, u32[]{:S(2)}) copy-start(bf16[384,768]{1,0:T(8,128)(2,1)S(1)} %fusion.68) | copy-start | bytes 1769476
  163.9 7.5 %copy-start.5 = (bf16[416,1536]{1,0:T(8,128)(2,1)S(1)}, bf16[416,1536]{1,0:T(8,128)(2,1)}, u32[]{:S(2)}) copy-start(bf16[416,1536]{1,0:T(8,128)(2,1)} %get-tuple-element.29.refs_0_) | copy-start | bytes 3833860
  165.4 16.0 %collective-permute-start.3 = (bf16[16,768]{1,0:T(8,128)(2,1)S(1)}, bf16[16,768]{1,0:T(8,128)(2,1)S(1)}, u32[]{:S(2)}, u32[]{:S(2)}) collective-permute-start(bf16[16,768]{1,0:T(8,128)(2,1)S(1)} %get-tuple-element.38), channel_id=1, source_target_pairs={{4,0},{8,4},{12,8},{16,12},{20,16},{24,20},{28,24},{5,1},{9,5},{13... | collective-permute-start | bytes 73736 | tf_op jit(solution)/shard_map/ppermute | solution.py:22
  166.7 14.7 %collective-permute-start.2 = (bf16[16,768]{1,0:T(8,128)(2,1)S(1)}, bf16[16,768]{1,0:T(8,128)(2,1)S(1)}, u32[]{:S(2)}, u32[]{:S(2)}) collective-permute-start(bf16[16,768]{1,0:T(8,128)(2,1)S(1)} %get-tuple-element.37), channel_id=1, source_target_pairs={{0,4},{4,8},{8,12},{12,16},{16,20},{20,24},{24,28},{1,5},{5,9},{9,... | collective-permute-start | bytes 73736 | tf_op jit(solution)/shard_map/ppermute | solution.py:19
  175.3 6.2 %copy-start.9 = (bf16[384,768]{1,0:T(8,128)(2,1)S(1)}, bf16[384,768]{1,0:T(8,128)(2,1)}, u32[]{:S(2)}) copy-start(bf16[384,768]{1,0:T(8,128)(2,1)} %copy-done.8) | copy-start | bytes 1769476
  182.4 7.2 %copy-start.7 = (bf16[1,384,1536]{2,1,0:T(8,128)(2,1)S(1)}, bf16[1,384,1536]{2,1,0:T(8,128)(2,1)}, u32[]{:S(2)}) copy-start(bf16[1,384,1536]{2,1,0:T(8,128)(2,1)} %param.11) | copy-start | bytes 3538948
  189.6 5.0 %copy-start.16 = (f32[416,768]{1,0:T(8,128)S(1)}, f32[416,768]{1,0:T(8,128)}, u32[]{:S(2)}) copy-start(f32[416,768]{1,0:T(8,128)} %get-tuple-element.15) | copy-start | bytes 3833860
  202.1 8.3 %collective-permute-start.7 = (bf16[768,3072]{1,0:T(8,128)(2,1)}, bf16[768,3072]{1,0:T(8,128)(2,1)}, u32[]{:S(2)}, u32[]{:S(2)}) collective-permute-start(bf16[768,3072]{1,0:T(8,128)(2,1)} %shard_map.113), channel_id=1, source_target_pairs={{0,1},{1,0},{2,3},{3,2},{4,5},{5,4},{6,7},{7,6},{8,9},{9,8},{10,11... | collective-permute-start | bytes 14155784 | tf_op jit(solution)/shard_map/ppermute | solution.py:247
  208.3 9.2 %collective-permute-start.6 = (bf16[768,3072]{1,0:T(8,128)(2,1)}, bf16[768,3072]{1,0:T(8,128)(2,1)}, u32[]{:S(2)}, u32[]{:S(2)}) collective-permute-start(bf16[768,3072]{1,0:T(8,128)(2,1)} %shard_map.116), channel_id=1, source_target_pairs={{0,1},{1,0},{2,3},{3,2},{4,5},{5,4},{6,7},{7,6},{8,9},{9,8},{10,11... | collective-permute-start | bytes 14155784 | tf_op jit(solution)/shard_map/ppermute | solution.py:247
  224.7 6.6 %copy-start.10 = (bf16[384,768]{1,0:T(8,128)(2,1)S(1)}, bf16[384,768]{1,0:T(8,128)(2,1)}, u32[]{:S(2)}) copy-start(bf16[384,768]{1,0:T(8,128)(2,1)} %get-tuple-element.12.refs_3_) | copy-start | bytes 1769476
  224.7 11.2 %collective-permute-start.5 = (bf16[8,768]{1,0:T(8,128)(2,1)S(1)}, bf16[8,768]{1,0:T(8,128)(2,1)S(1)}, u32[]{:S(2)}, u32[]{:S(2)}) collective-permute-start(bf16[8,768]{1,0:T(8,128)(2,1)S(1)} %get-tuple-element.36), channel_id=1, source_target_pairs={{4,0},{8,4},{12,8},{16,12},{20,16},{24,20},{28,24},{5,1},{9,5},{13... | collective-permute-start | bytes 36872 | tf_op jit(solution)/shard_map/ppermute | solution.py:22
  226.1 9.8 %collective-permute-start.4 = (bf16[8,768]{1,0:T(8,128)(2,1)S(1)}, bf16[8,768]{1,0:T(8,128)(2,1)S(1)}, u32[]{:S(2)}, u32[]{:S(2)}) collective-permute-start(bf16[8,768]{1,0:T(8,128)(2,1)S(1)} %get-tuple-element.35), channel_id=1, source_target_pairs={{0,4},{4,8},{8,12},{12,16},{16,20},{20,24},{24,28},{1,5},{5,9},{9,... | collective-permute-start | bytes 36872 | tf_op jit(solution)/shard_map/ppermute | solution.py:19
  236.8 7.4 %copy-start.1 = (f32[432,1536]{1,0:T(8,128)S(1)}, f32[432,1536]{1,0:T(8,128)}, u32[]{:S(2)}) copy-start(f32[432,1536]{1,0:T(8,128)} %get-tuple-element.31) | copy-start | bytes 7962628
  (3 other events, 4.4 us)
Sparse Core Ops, SparseCore 0:
  11.5 127.3 all-gather.1
  224.8 170.3 reduce-scatter.1
